TPU v7x, 32 devices: a whole 2x2x4 slice. The times are simulated.
32 devices in a mesh: parts: 2 (over x), seq: 16 (over z, y, core).
Axes of the slice: x: 2, y: 2, z: 4, core: 2. Of those that a mesh axis runs over, the one named last changes fastest.
Arguments:
- queries: bfloat16 [4096, 2048], P(('parts', 'seq')), parts along dimension 0
- joined_keys_values: bfloat16 [4096, 2048], P(('parts', 'seq')), parts along dimension 0
- segment_ids: int32 [4096], P(('parts', 'seq')), parts along dimension 0, may hold values from 0 to 3, never falling along the last dimension, each value on 1 to 1024 neighbouring positions
- residual: bfloat16 [4096, 2688], P(('parts', 'seq')), parts along dimension 0, may hold values from -4 to 4
- norm_gain: float32 [2688], replicated, may hold values from 0.5 to 1.5
- out_proj: bfloat16 [2048, 2688], P('seq'), may hold values from -1 to 1
- head_weight: bfloat16 [16384, 2688], P('seq')
- next_ids: int32 [128], P('parts'), parts along dimension 0, may hold values from 0 to 16383
Outputs:
- layer_out: bfloat16 [4096, 2688], P(('parts', 'seq')), parts along dimension 0
- log_probs: float32 [128, 16384], P('parts', 'seq'), parts along dimension 0
- target_logp: float32 [128], P(('parts', 'seq')), parts along dimension 0
There are 2 independent parts, one for each index of `parts`. A program takes and returns all parts, laid end to end along the dimension named above; an argument that names none is the same for every part. Nothing has to cross between parts.
All inputs are finite; a program needn't handle non-finite values.
Results may differ from a plain program's by a relative error of at most 0.0056.
Values may be sent and summed in bfloat16 or wider, within the bound.
No kernel may reach another device: no remote copies, remote signals or barrier semaphores. Data moves between devices by JAX's collectives and lax.ppermute only.
A program may use at most 64 MiB of HBM per device.

v0:
```python
import jax
import jax.numpy as jnp
from jax import lax
from jax.sharding import PartitionSpec as P

QUERY_HEADS = 16
KEY_VALUE_HEADS = 8
HEAD_SIZE = 128
ATTENTION_SPAN = 1024
SCORE_DEV = 4


score_scale = 168.0 ** (-0.5)
masked_score = -1e30


def shifted(value, axis, steps):
    count = lax.axis_size(axis)
    leading, last = (max(0, -steps), min(count, count - steps))
    return lax.ppermute(value, axis, [(source, source + steps) for source in range(leading, last)])


def normalize(hidden, norm_gain):
    mean_square = jnp.mean(hidden * hidden, axis=1, keepdims=True)
    return (hidden * lax.rsqrt(mean_square + 1e-06) * norm_gain[None, :]).astype(jnp.bfloat16)


def local(
    queries, joined_keys_values, segment_ids, residual, norm_gain, out_proj, head_weight, next_ids
):
    token_rows = queries.shape[0]
    blocks = ATTENTION_SPAN // token_rows
    queries_per_group = QUERY_HEADS // KEY_VALUE_HEADS
    my_index = lax.axis_index("seq")
    first_row = my_index * token_rows
    rim_kv_parts = []
    rim_seg_parts = []
    for distance in range(blocks, 0, -1):
        moved_kv, moved_seg = shifted((joined_keys_values, segment_ids), "seq", distance)
        rim_kv_parts.append(moved_kv)
        rim_seg_parts.append(moved_seg)
    rim_kv = jnp.concatenate(rim_kv_parts, 0)
    rim_seg = jnp.concatenate(rim_seg_parts, 0)
    key_value_pair = jnp.concatenate([rim_kv, joined_keys_values], 0)
    key_seg = jnp.concatenate([rim_seg, segment_ids], 0)
    count_of_keys = key_value_pair.shape[0]
    query_pos = first_row + jnp.arange(token_rows, dtype=jnp.int32)
    key_pos = first_row - blocks * token_rows + jnp.arange(count_of_keys, dtype=jnp.int32)
    allowed = (segment_ids[:, None] == key_seg[None, :]) & (key_pos[None, :] >= 0)
    allowed = (
        allowed
        & (key_pos[None, :] <= query_pos[:, None])
        & (key_pos[None, :] > query_pos[:, None] - ATTENTION_SPAN)
    )
    heads_for_queries = queries.reshape(token_rows, KEY_VALUE_HEADS, queries_per_group, HEAD_SIZE)
    heads_for_keys = key_value_pair[:, : KEY_VALUE_HEADS * HEAD_SIZE].reshape(
        count_of_keys, KEY_VALUE_HEADS, HEAD_SIZE
    )
    heads_for_values = key_value_pair[:, KEY_VALUE_HEADS * HEAD_SIZE :].reshape(
        count_of_keys, KEY_VALUE_HEADS, HEAD_SIZE
    )
    scores = (
        jnp.einsum(
            "qhgd,khd->hgqk", heads_for_queries, heads_for_keys, preferred_element_type=jnp.float32
        )
        * score_scale
    )
    scores = jnp.where(allowed[None, None, :, :], scores, masked_score)
    row_max = jnp.max(scores, axis=-1, keepdims=True)
    raised = jnp.exp(scores - row_max)
    weights = (raised / jnp.sum(raised, axis=-1, keepdims=True)).astype(jnp.bfloat16)
    context = jnp.einsum(
        "hgqk,khd->qhgd", weights, heads_for_values, preferred_element_type=jnp.float32
    )
    context = context.reshape(token_rows, QUERY_HEADS * HEAD_SIZE).astype(jnp.bfloat16)
    width = residual.shape[1]
    projected = jnp.dot(
        context,
        lax.all_gather(out_proj, "seq", axis=0, tiled=True),
        preferred_element_type=jnp.float32,
    )
    hidden = residual.astype(jnp.float32) + projected
    layer_out = hidden.astype(jnp.bfloat16)
    score_count = SCORE_DEV
    stride = token_rows // score_count
    picked = hidden.reshape(score_count, stride, width)[:, stride - 1, :]
    normed = normalize(picked, norm_gain)
    logits = lax.dot_general(
        lax.all_gather(normed, "seq", axis=0, tiled=True),
        head_weight,
        (((1,), (1,)), ((), ())),
        preferred_element_type=jnp.float32,
    )
    global_max = lax.pmax(jnp.max(logits, axis=1), "seq")
    global_total = lax.psum(jnp.sum(jnp.exp(logits - global_max[:, None]), axis=1), "seq")
    log_total = global_max + jnp.log(global_total)
    log_probs = logits - log_total[:, None]
    vocab_width = head_weight.shape[0]
    local_ids = next_ids - my_index * vocab_width
    vocab_ids = jnp.arange(vocab_width, dtype=jnp.int32)
    picked_terms = jnp.sum(
        jnp.where(local_ids[:, None] == vocab_ids[None, :], log_probs, 0.0), axis=1
    )
    target_logp = lax.psum_scatter(picked_terms, "seq", scatter_dimension=0, tiled=True)
    return (layer_out, log_probs, target_logp)


def solution(mesh):
    in_specs = (
        P(("parts", "seq"), None),
        P(("parts", "seq"), None),
        P(("parts", "seq")),
        P(("parts", "seq"), None),
        P(),
        P("seq", None),
        P("seq", None),
        P("parts"),
    )
    out_specs = (P(("parts", "seq"), None), P("parts", "seq"), P(("parts", "seq")))
    return jax.shard_map(local, mesh=mesh, in_specs=in_specs, out_specs=out_specs, check_vma=False)
```

profile of v0, /device:TPU:0, one launch (start us, length us, event | category | flops | bytes accessed | tf_op | source)
XLA Modules:
  0.0 391.8 jit_solution(2573217400198368961)
XLA Ops:
  7.2 0.7 all-gather.3.cloned.1.call-update
  7.9 1.3 copy.26
  9.2 6.0 %collective-permute-start = (bf16[128,2048]{0,1:T(8,128)(2,1)S(1)}, bf16[128,2048]{0,1:T(8,128)(2,1)S(1)}, u32[]{:S(2)}, u32[]{:S(2)}) collective-permute-start(bf16[128,2048]{0,1:T(8,128)(2,1)S(1)} %copy.26), channel_id=1, source_target_pairs={{0,8},{1,9},{2,10},{3,11},{4,12},{5,13},{6,14},{7,15},{16,24},{17,... | collective-permute-start | bytes 1572872 | tf_op jit(solution)/shard_map/ppermute | solution.py:20
  15.2 3.6 collective-permute-start.1
  18.8 2.2 collective-permute-start.2
  21.0 1.3 collective-permute-start.3
  22.3 1.9 collective-permute-start.8
  24.3 1.2 broadcast_subtract_fusion.1
  25.4 1.4 reshape.150
  26.9 1.2 dynamic-slice
  28.8 53.5 %collective-permute-done.8 = s32[128]{0:T(128)S(1)} collective-permute-done((s32[128]{0:T(128)}, s32[128]{0:T(128)S(1)}, u32[]{:S(2)}, u32[]{:S(2)}) %collective-permute-start.8) | collective-permute-done | bytes 544 | tf_op jit(solution)/shard_map/ppermute | solution.py:20
  82.2 87.8 %collective-permute-start.9 = (s32[128]{0:T(128)}, s32[128]{0:T(128)S(1)}, u32[]{:S(2)}, u32[]{:S(2)}) collective-permute-start(s32[128]{0:T(128)} %param.10), channel_id=1, source_target_pairs={{0,7},{1,8},{2,9},{3,10},{4,11},{5,12},{6,13},{7,14},{8,15},{16,23... | collective-permute-start | bytes 1544 | tf_op jit(solution)/shard_map/ppermute | solution.py:20
  170.1 1.4 collective-permute-done.9
  171.5 1.7 collective-permute-start.10
  173.2 1.4 collective-permute-done.10
  174.6 1.3 collective-permute-start.11
  175.9 1.4 collective-permute-done.11
  177.3 8.0 %collective-permute-start.12 = (s32[128]{0:T(128)}, s32[128]{0:T(128)S(1)}, u32[]{:S(2)}, u32[]{:S(2)}) collective-permute-start(s32[128]{0:T(128)} %param.10), channel_id=1, source_target_pairs={{0,4},{1,5},{2,6},{3,7},{4,8},{5,9},{6,10},{7,11},{8,12},{9,13},{1... | collective-permute-start | bytes 1544 | tf_op jit(solution)/shard_map/ppermute | solution.py:20
  185.3 1.4 collective-permute-done.12
  186.7 3.1 collective-permute-start.13
  189.8 1.4 collective-permute-done.13
  191.2 5.1 %collective-permute-start.14 = (s32[128]{0:T(128)}, s32[128]{0:T(128)S(1)}, u32[]{:S(2)}, u32[]{:S(2)}) collective-permute-start(s32[128]{0:T(128)} %param.10), channel_id=1, source_target_pairs={{0,2},{1,3},{2,4},{3,5},{4,6},{5,7},{6,8},{7,9},{8,10},{9,11},{10,... | collective-permute-start | bytes 1544 | tf_op jit(solution)/shard_map/ppermute | solution.py:20
  196.4 1.4 collective-permute-done.14
  197.8 1.6 collective-permute-start.15
  199.4 0.9 collective-permute-done.15
  200.4 11.4 %collective-permute-start.4 = (bf16[128,2048]{0,1:T(8,128)(2,1)S(1)}, bf16[128,2048]{0,1:T(8,128)(2,1)S(1)}, u32[]{:S(2)}, u32[]{:S(2)}) collective-permute-start(bf16[128,2048]{0,1:T(8,128)(2,1)S(1)} %copy.26), channel_id=1, source_target_pairs={{0,4},{1,5},{2,6},{3,7},{4,8},{5,9},{6,10},{7,11},{8,12},{9,13},{1... | collective-permute-start | bytes 1572872 | tf_op jit(solution)/shard_map/ppermute | solution.py:20
  211.8 0.7 constant_dynamic-update-slice_fusion.10
  212.5 1.7 compare_and_fusion
  214.2 1.9 collective-permute-start.5
  216.3 2.2 collective-permute-start.6
  218.5 0.1 constant_dynamic-update-slice_fusion.7
  218.6 3.6 collective-permute-start.7
  222.5 0.1 constant_dynamic-update-slice_fusion.4
  222.6 2.7 collective-permute-done.5
  225.4 11.1 %collective-permute-done.6 = bf16[128,2048]{0,1:T(8,128)(2,1)S(1)} collective-permute-done((bf16[128,2048]{0,1:T(8,128)(2,1)S(1)}, bf16[128,2048]{0,1:T(8,128)(2,1)S(1)}, u32[]{:S(2)}, u32[]{:S(2)}) %collective-permute-start.6) | collective-permute-done | bytes 524320 | tf_op jit(solution)/shard_map/ppermute | solution.py:20
  236.9 1.8 fusion.27
  238.7 4.2 %fusion.28 = f32[8,2,128]{2,1,0:T(2,128)} fusion(pred[128,1152]{0,1:T(8,128)(4,1)S(1)} %compare_and_fusion, bf16[1152,8,128,1]{0,2,3,1:T(8,128)(2,1)S(1)} %bitcast.43, bf16[128,8,2,128]{3,2,1,0:T(2,128)(2,1)S(1)} %reshape.150), kind=kOutput, calls=%fused_computation.55 | convolution fusion | flops 613418112 | bytes 3039232 | tf_op jit(solution)/shard_map/sub | solution.py:70
  243.0 6.3 %fusion.6 = bf16[8,128,2,128]{3,1,2,0:T(8,128)(2,1)S(1)} fusion(bf16[1152,8,128,1]{0,2,3,1:T(8,128)(2,1)} %bitcast.45, f32[8,2,128]{2,1,0:T(2,128)} %fusion.28, pred[128,1152]{0,1:T(8,128)(4,1)S(1)} %compare_and_fusion, bf16[1152,8,128,1]{0,2,3,1:T(8,128)(2,1)S(1)} %bitcast.44, bf16[128,8,2,128]{3,2,1,0:T(2,128)(2,1)S(1)} %reshape.150), kind=kOutput, calls=%fused_computation.10 | convolution fusion | flops 1220021376 | bytes 5922816 | tf_op jit(solution)/shard_map/hgqk,khd->qhgd/dot_general | solution.py:72
  249.3 6.8 %fusion.31 = (bf16[128,2688]{1,0:T(8,128)(2,1)}, f32[128,2688]{1,0:T(8,128)S(1)}) fusion(bf16[128,2048]{0,1:T(8,128)(2,1)S(1)} %bitcast.47, bf16[2048,2688]{1,0:T(8,128)(2,1)} %all-gather.3.cloned.1.call-done, bf16[128,2688]{1,0:T(8,128)(2,1)} %param.11), kind=kOutput, calls=%fused_computation.56 | convolution fusion | flops 1410318336 | bytes 14286848 | tf_op jit(solution)/shard_map/dot_general | solution.py:77
  256.2 0.1 multiply_reduce_fusion
  256.4 31.9 %all-gather = bf16[16,4,2688]{2,1,0:T(4,128)(2,1)S(1)} all-gather(bf16[1,4,2688]{2,1,0:T(4,128)(2,1)S(1)} %fusion.19), channel_id=1, replica_groups=mesh['parts'=2,'seq'=16] {'seq'}, dimensions={0}, use_global_device_ids=true | all-gather | bytes 365568 | tf_op jit(solution)/shard_map/all_gather | solution.py:89
  288.4 4.4 %fusion.32 = (f32[64]{0:T(128)S(1)}, f32[64,1024]{1,0:T(8,128)S(1)}) fusion(bf16[64,2688]{1,0:T(8,128)(2,1)S(1)} %reshape.153, bf16[1024,2688]{1,0:T(8,128)(2,1)} %param.14), kind=kOutput, calls=%fused_computation.57 | convolution fusion | flops 352387008 | bytes 6111488 | tf_op jit(solution)/shard_map/dot_general | solution.py:88
  292.9 31.4 %pmax.7 = f32[64]{0:T(128)S(1)} all-reduce(f32[64]{0:T(128)S(1)} %get-tuple-element.9), channel_id=1, replica_groups=mesh['parts'=2,'seq'=16] {'seq'}, use_global_device_ids=true, to_apply=%region_4.5 | all-reduce | flops 64 | bytes 512 | tf_op jit(solution)/shard_map/pmax | solution.py:94
  324.3 0.2 exponential_reduce_fusion
  324.5 29.5 %psum.7 = f32[64]{0:T(128)S(1)} all-reduce(f32[64]{0:T(128)S(1)} %exponential_reduce_fusion), channel_id=1, replica_groups=mesh['parts'=2,'seq'=16] {'seq'}, use_global_device_ids=true, to_apply=%region_6.7 | all-reduce | flops 64 | bytes 512 | tf_op jit(solution)/shard_map/psum | solution.py:95
  354.0 0.9 select_reduce_fusion
  354.9 29.5 %all-reduce = f32[64]{0:T(128)S(1)} all-reduce(f32[64]{0:T(128)S(1)} %get-tuple-element.3), channel_id=2, replica_groups=mesh['parts'=2,'seq'=16] {'seq'}, use_global_device_ids=true, to_apply=%region_8.9.clone | all-reduce | flops 64 | bytes 512
  384.4 0.6 dynamic-slice.1
  (36 shorter events, 1.2 us)
Async XLA Ops:
  7.2 242.2 %all-gather.3.cloned.1.call-start = ((), (), s32[]{:S(2)}) async-start(), calls=%async_computation | async-start | bytes 11698176 | tf_op jit(solution)/shard_map/all_gather | solution.py:79
  9.2 205.0 %collective-permute-start = (bf16[128,2048]{0,1:T(8,128)(2,1)S(1)}, bf16[128,2048]{0,1:T(8,128)(2,1)S(1)}, u32[]{:S(2)}, u32[]{:S(2)}) collective-permute-start(bf16[128,2048]{0,1:T(8,128)(2,1)S(1)} %copy.26), channel_id=1, source_target_pairs={{0,8},{1,9},{2,10},{3,11},{4,12},{5,13},{6,14},{7,15},{16,24},{17,... | collective-permute-start | bytes 1572872 | tf_op jit(solution)/shard_map/ppermute | solution.py:20
  15.2 201.0 %collective-permute-start.1 = (bf16[128,2048]{0,1:T(8,128)(2,1)S(1)}, bf16[128,2048]{0,1:T(8,128)(2,1)S(1)}, u32[]{:S(2)}, u32[]{:S(2)}) collective-permute-start(bf16[128,2048]{0,1:T(8,128)(2,1)S(1)} %copy.26), channel_id=1, source_target_pairs={{0,7},{1,8},{2,9},{3,10},{4,11},{5,12},{6,13},{7,14},{8,15},{16,23... | collective-permute-start | bytes 1572872 | tf_op jit(solution)/shard_map/ppermute | solution.py:20
  18.8 199.8 %collective-permute-start.2 = (bf16[128,2048]{0,1:T(8,128)(2,1)S(1)}, bf16[128,2048]{0,1:T(8,128)(2,1)S(1)}, u32[]{:S(2)}, u32[]{:S(2)}) collective-permute-start(bf16[128,2048]{0,1:T(8,128)(2,1)S(1)} %copy.26), channel_id=1, source_target_pairs={{0,6},{1,7},{2,8},{3,9},{4,10},{5,11},{6,12},{7,13},{8,14},{9,15},... | collective-permute-start | bytes 1572872 | tf_op jit(solution)/shard_map/ppermute | solution.py:20
  21.0 201.3 %collective-permute-start.3 = (bf16[128,2048]{0,1:T(8,128)(2,1)S(1)}, bf16[128,2048]{0,1:T(8,128)(2,1)S(1)}, u32[]{:S(2)}, u32[]{:S(2)}) collective-permute-start(bf16[128,2048]{0,1:T(8,128)(2,1)S(1)} %copy.26), channel_id=1, source_target_pairs={{0,5},{1,6},{2,7},{3,8},{4,9},{5,10},{6,11},{7,12},{8,13},{9,14},{... | collective-permute-start | bytes 1572872 | tf_op jit(solution)/shard_map/ppermute | solution.py:20
  22.3 59.9 %collective-permute-start.8 = (s32[128]{0:T(128)}, s32[128]{0:T(128)S(1)}, u32[]{:S(2)}, u32[]{:S(2)}) collective-permute-start(s32[128]{0:T(128)} %param.10), channel_id=1, source_target_pairs={{0,8},{1,9},{2,10},{3,11},{4,12},{5,13},{6,14},{7,15},{16,24},{17,... | collective-permute-start | bytes 1544 | tf_op jit(solution)/shard_map/ppermute | solution.py:20
  82.2 89.3 %collective-permute-start.9 = (s32[128]{0:T(128)}, s32[128]{0:T(128)S(1)}, u32[]{:S(2)}, u32[]{:S(2)}) collective-permute-start(s32[128]{0:T(128)} %param.10), channel_id=1, source_target_pairs={{0,7},{1,8},{2,9},{3,10},{4,11},{5,12},{6,13},{7,14},{8,15},{16,23... | collective-permute-start | bytes 1544 | tf_op jit(solution)/shard_map/ppermute | solution.py:20
  171.5 3.1 collective-permute-start.10
  174.6 2.7 collective-permute-start.11
  177.3 9.5 %collective-permute-start.12 = (s32[128]{0:T(128)}, s32[128]{0:T(128)S(1)}, u32[]{:S(2)}, u32[]{:S(2)}) collective-permute-start(s32[128]{0:T(128)} %param.10), channel_id=1, source_target_pairs={{0,4},{1,5},{2,6},{3,7},{4,8},{5,9},{6,10},{7,11},{8,12},{9,13},{1... | collective-permute-start | bytes 1544 | tf_op jit(solution)/shard_map/ppermute | solution.py:20
  186.7 4.5 %collective-permute-start.13 = (s32[128]{0:T(128)}, s32[128]{0:T(128)S(1)}, u32[]{:S(2)}, u32[]{:S(2)}) collective-permute-start(s32[128]{0:T(128)} %param.10), channel_id=1, source_target_pairs={{0,3},{1,4},{2,5},{3,6},{4,7},{5,8},{6,9},{7,10},{8,11},{9,12},{10... | collective-permute-start | bytes 1544 | tf_op jit(solution)/shard_map/ppermute | solution.py:20
  191.2 6.6 %collective-permute-start.14 = (s32[128]{0:T(128)}, s32[128]{0:T(128)S(1)}, u32[]{:S(2)}, u32[]{:S(2)}) collective-permute-start(s32[128]{0:T(128)} %param.10), channel_id=1, source_target_pairs={{0,2},{1,3},{2,4},{3,5},{4,6},{5,7},{6,8},{7,9},{8,10},{9,11},{10,... | collective-permute-start | bytes 1544 | tf_op jit(solution)/shard_map/ppermute | solution.py:20
  197.8 2.6 collective-permute-start.15
  200.4 22.1 %collective-permute-start.4 = (bf16[128,2048]{0,1:T(8,128)(2,1)S(1)}, bf16[128,2048]{0,1:T(8,128)(2,1)S(1)}, u32[]{:S(2)}, u32[]{:S(2)}) collective-permute-start(bf16[128,2048]{0,1:T(8,128)(2,1)S(1)} %copy.26), channel_id=1, source_target_pairs={{0,4},{1,5},{2,6},{3,7},{4,8},{5,9},{6,10},{7,11},{8,12},{9,13},{1... | collective-permute-start | bytes 1572872 | tf_op jit(solution)/shard_map/ppermute | solution.py:20
  214.2 11.1 %collective-permute-start.5 = (bf16[128,2048]{0,1:T(8,128)(2,1)S(1)}, bf16[128,2048]{0,1:T(8,128)(2,1)S(1)}, u32[]{:S(2)}, u32[]{:S(2)}) collective-permute-start(bf16[128,2048]{0,1:T(8,128)(2,1)S(1)} %copy.26), channel_id=1, source_target_pairs={{0,3},{1,4},{2,5},{3,6},{4,7},{5,8},{6,9},{7,10},{8,11},{9,12},{10... | collective-permute-start | bytes 1572872 | tf_op jit(solution)/shard_map/ppermute | solution.py:20
  216.3 20.2 %collective-permute-start.6 = (bf16[128,2048]{0,1:T(8,128)(2,1)S(1)}, bf16[128,2048]{0,1:T(8,128)(2,1)S(1)}, u32[]{:S(2)}, u32[]{:S(2)}) collective-permute-start(bf16[128,2048]{0,1:T(8,128)(2,1)S(1)} %copy.26), channel_id=1, source_target_pairs={{0,2},{1,3},{2,4},{3,5},{4,6},{5,7},{6,8},{7,9},{8,10},{9,11},{10,... | collective-permute-start | bytes 1572872 | tf_op jit(solution)/shard_map/ppermute | solution.py:20
  218.6 18.0 %collective-permute-start.7 = (bf16[128,2048]{0,1:T(8,128)(2,1)S(1)}, bf16[128,2048]{0,1:T(8,128)(2,1)S(1)}, u32[]{:S(2)}, u32[]{:S(2)}) collective-permute-start(bf16[128,2048]{0,1:T(8,128)(2,1)S(1)} %copy.26), channel_id=1, source_target_pairs={{0,1},{1,2},{2,3},{3,4},{4,5},{5,6},{6,7},{7,8},{8,9},{9,10},{10,1... | collective-permute-start | bytes 1572872 | tf_op jit(solution)/shard_map/ppermute | solution.py:20
  249.3 7.0 %copy-start = (f32[2688]{0:T(1024)S(1)}, f32[2688]{0:T(1024)}, u32[]{:S(2)}) copy-start(f32[2688]{0:T(1024)} %param.12) | copy-start | bytes 32260
  256.1 97.9 %copy-start.1 = (s32[64]{0:T(128)S(1)}, s32[64]{0:T(128)}, u32[]{:S(2)}) copy-start(s32[64]{0:T(128)} %broadcast_subtract_fusion.1) | copy-start | bytes 772
Sparse Core Ops, SparseCore 0:
  10.3 136.2 all-gather.2
where the time goes:
time: 393 us; the launch traced here: 392 us
  starting transfers between devices  143 us (36%)
  blocking collectives  122 us (31%)
  waiting for transfers between devices  77.3 us (20%)
  matrix products  21.8 us (6%)
  between operations  15.1 us (4%)
  local copies, waits for them, and re-layouts  8.31 us (2%)
  other arithmetic  4.24 us (1%)
    ppermute x16, starting transfers between devices, shifted(): lax.ppermute(value, axis, [(source, source + steps) for source in range(l...  143 us
    ppermute x16, waiting for transfers between devices, shifted(): lax.ppermute(value, axis, [(source, source + steps) for source in range(l...  76.6 us
    all_gather x1, blocking collectives, local(): lax.all_gather(normed, 'seq', axis=0, tiled=True)  31.9 us
    pmax x1, blocking collectives, local(): global_max = lax.pmax(jnp.max(logits, axis=1), 'seq')  31.4 us
    unnamed x1, blocking collectives  29.5 us
    psum x1, blocking collectives, local(): lax.psum(jnp.sum(jnp.exp(logits - global_max[:, None]), axis=1), 'seq')  29.5 us
  transfers between devices with their start and end apart: 17, of which 10 were waited for; matrix products, arithmetic and copies ran while one was open for 5% of the time, Pallas kernels for 0%

commit v1 on v0

--- a/solution.py
+++ b/solution.py
@@ -8,16 +8,31 @@
 HEAD_SIZE = 128
 ATTENTION_SPAN = 1024
 SCORE_DEV = 4
+SEG_LANES = 128
 
 
 score_scale = 168.0 ** (-0.5)
 masked_score = -1e30
 
 
-def shifted(value, axis, steps):
+def forward_one(value, axis):
     count = lax.axis_size(axis)
-    leading, last = (max(0, -steps), min(count, count - steps))
-    return lax.ppermute(value, axis, [(source, source + steps) for source in range(leading, last)])
+    return lax.ppermute(value, axis, [(source, source + 1) for source in range(count - 1)])
+
+
+def gather_rows(value, axis):
+    count = lax.axis_size(axis)
+    bits = count.bit_length() - 1
+    me = lax.axis_index(axis)
+    data = value[None]
+    for bit in reversed(range(bits)):
+        step = 1 << bit
+        received = lax.ppermute(data, axis, [(i, i ^ step) for i in range(count)])
+        low = ((me >> bit) & 1) == 0
+        data = jnp.where(low, jnp.concatenate([data, received], 0), jnp.concatenate([received, data], 0))
+    data = data.reshape((2,) * bits + value.shape)
+    data = jnp.transpose(data, tuple(reversed(range(bits))) + tuple(range(bits, bits + value.ndim)))
+    return data.reshape((count * value.shape[0],) + value.shape[1:])
 
 
 def normalize(hidden, norm_gain):
@@ -31,16 +46,20 @@
     token_rows = queries.shape[0]
     blocks = ATTENTION_SPAN // token_rows
     queries_per_group = QUERY_HEADS // KEY_VALUE_HEADS
+    kv_width = joined_keys_values.shape[1]
     my_index = lax.axis_index("seq")
     first_row = my_index * token_rows
-    rim_kv_parts = []
-    rim_seg_parts = []
-    for distance in range(blocks, 0, -1):
-        moved_kv, moved_seg = shifted((joined_keys_values, segment_ids), "seq", distance)
-        rim_kv_parts.append(moved_kv)
-        rim_seg_parts.append(moved_seg)
-    rim_kv = jnp.concatenate(rim_kv_parts, 0)
-    rim_seg = jnp.concatenate(rim_seg_parts, 0)
+
+    seg_cols = jnp.broadcast_to(segment_ids.astype(jnp.bfloat16)[:, None], (token_rows, SEG_LANES))
+    own = jnp.concatenate([joined_keys_values, seg_cols], 1)
+    arrived = []
+    current = own
+    for _ in range(blocks):
+        current = forward_one(current, "seq")
+        arrived.append(current)
+    rim = jnp.concatenate(arrived[::-1], 0)
+    rim_kv = rim[:, :kv_width]
+    rim_seg = rim[:, kv_width].astype(jnp.int32)
     key_value_pair = jnp.concatenate([rim_kv, joined_keys_values], 0)
     key_seg = jnp.concatenate([rim_seg, segment_ids], 0)
     count_of_keys = key_value_pair.shape[0]
@@ -86,22 +105,26 @@
     picked = hidden.reshape(score_count, stride, width)[:, stride - 1, :]
     normed = normalize(picked, norm_gain)
     logits = lax.dot_general(
-        lax.all_gather(normed, "seq", axis=0, tiled=True),
+        gather_rows(normed, "seq"),
         head_weight,
         (((1,), (1,)), ((), ())),
         preferred_element_type=jnp.float32,
     )
-    global_max = lax.pmax(jnp.max(logits, axis=1), "seq")
-    global_total = lax.psum(jnp.sum(jnp.exp(logits - global_max[:, None]), axis=1), "seq")
-    log_total = global_max + jnp.log(global_total)
-    log_probs = logits - log_total[:, None]
     vocab_width = head_weight.shape[0]
     local_ids = next_ids - my_index * vocab_width
     vocab_ids = jnp.arange(vocab_width, dtype=jnp.int32)
-    picked_terms = jnp.sum(
-        jnp.where(local_ids[:, None] == vocab_ids[None, :], log_probs, 0.0), axis=1
-    )
-    target_logp = lax.psum_scatter(picked_terms, "seq", scatter_dimension=0, tiled=True)
+    shard_max = jnp.max(logits, axis=1)
+    shard_total = jnp.sum(jnp.exp(logits - shard_max[:, None]), axis=1)
+    shard_pick = jnp.sum(jnp.where(local_ids[:, None] == vocab_ids[None, :], logits, 0.0), axis=1)
+    stats = gather_rows(jnp.stack([shard_max, shard_total, shard_pick], 0), "seq")
+    stats = stats.reshape(-1, 3, shard_max.shape[0])
+    all_max, all_total, all_pick = stats[:, 0], stats[:, 1], stats[:, 2]
+    global_max = jnp.max(all_max, axis=0)
+    global_total = jnp.sum(all_total * jnp.exp(all_max - global_max[None, :]), axis=0)
+    log_total = global_max + jnp.log(global_total)
+    log_probs = logits - log_total[:, None]
+    target_all = jnp.sum(all_pick, axis=0) - log_total
+    target_logp = lax.dynamic_slice_in_dim(target_all, my_index * score_count, score_count, 0)
     return (layer_out, log_probs, target_logp)
 
 

time: 393 us -> 231 us (0.59)
  blocking collectives: 122 us -> 0 us
  waiting for transfers between devices: 77.3 us -> 28.3 us
  starting transfers between devices: 143 us -> 149 us
    ppermute x16, waiting for transfers between devices: 76.6 us -> 27.6 us  [the longest x8 17.6 us: gather_rows(): received = lax.ppermute(data, axis, [(i, i ^ step) for i in range(count)])]
    all_gather x1 -> x0, blocking collectives: 31.9 us -> none  [local(): lax.all_gather(normed, 'seq', axis=0, tiled=True)]
    pmax x1 -> x0, blocking collectives: 31.4 us -> none  [local(): global_max = lax.pmax(jnp.max(logits, axis=1), 'seq')]
    unnamed x1 -> x0, blocking collectives: 29.5 us -> none
    psum x1 -> x0, blocking collectives: 29.5 us -> none  [local(): lax.psum(jnp.sum(jnp.exp(logits - global_max[:, None]), axis=1), 'seq')]
    ppermute x16, starting transfers between devices: 143 us -> 149 us  [the longest x8 95.4 us: forward_one(): lax.ppermute(value, axis, [(source, source + 1) for source in range(count...]
  transfers between devices with their start and end apart: 17 -> 17, of which waited for: 10 -> 15; matrix products, arithmetic and copies ran while one was open for 5% -> 11% of each run, Pallas kernels for 0% -> 0%
where the time goes in v1:
time: 231 us
  starting transfers between devices  149 us (65%)
  waiting for transfers between devices  28.3 us (12%)
  matrix products  22 us (10%)
  between operations  14.4 us (6%)
  local copies, waits for them, and re-layouts  10.5 us (5%)
  other arithmetic  6.95 us (3%)
    ppermute x8, starting transfers between devices, forward_one(): lax.ppermute(value, axis, [(source, source + 1) for source in range(count...  95.4 us
    ppermute x8, starting transfers between devices, gather_rows(): received = lax.ppermute(data, axis, [(i, i ^ step) for i in range(count)])  53.1 us
    ppermute x8, waiting for transfers between devices, gather_rows(): received = lax.ppermute(data, axis, [(i, i ^ step) for i in range(count)])  17.6 us
    ppermute x8, waiting for transfers between devices, forward_one(): lax.ppermute(value, axis, [(source, source + 1) for source in range(count...  10.1 us
    dot_general x1, matrix products, local(): jnp.dot(context, lax.all_gather(out_proj, 'seq', axis=0, tiled=True), pre...  6.78 us
    unnamed x18, local copies, waits for them, and re-layouts  6.76 us
    dot_general x1, matrix products, local(): jnp.einsum('hgqk,khd->qhgd', weights, heads_for_values, preferred_element...  6.3 us
  transfers between devices with their start and end apart: 17, of which 15 were waited for; matrix products, arithmetic and copies ran while one was open for 11% of the time, Pallas kernels for 0%

profile of v1, /device:TPU:0, one launch (start us, length us, event | category | flops | bytes accessed | tf_op | source)
XLA Modules:
  0.0 230.7 jit_solution(1498826647229405836)
XLA Ops:
  7.2 0.7 all-gather.2.cloned.1.call-update
  7.9 1.3 copy.21
  9.2 0.7 convert_element_type.38
  9.9 2.4 %collective-permute-start = (bf16[128,2176]{0,1:T(8,128)(2,1)S(1)}, bf16[128,2176]{0,1:T(8,128)(2,1)S(1)}, u32[]{:S(2)}, u32[]{:S(2)}) collective-permute-start(bf16[128,2176]{0,1:T(8,128)(2,1)S(1)} %pad_maximum_fusion.1), channel_id=1, source_target_pairs={{0,1},{1,2},{2,3},{3,4},{4,5},{5,6},{6,7},{7,8},{8,9},{9,10},{10,1... | collective-permute-start | bytes 1671176 | tf_op jit(solution)/shard_map/ppermute | solution.py:20
  12.3 1.5 collective-permute-done
  13.9 9.4 %collective-permute-start.1 = (bf16[128,2176]{0,1:T(8,128)(2,1)S(1)}, bf16[128,2176]{0,1:T(8,128)(2,1)S(1)}, u32[]{:S(2)}, u32[]{:S(2)}) collective-permute-start(bf16[128,2176]{0,1:T(8,128)(2,1)S(1)} %collective-permute-done), channel_id=1, source_target_pairs={{0,1},{1,2},{2,3},{3,4},{4,5},{5,6},{6,7},{7,8},{8,9},{9,10},{10,1... | collective-permute-start | bytes 1671176 | tf_op jit(solution)/shard_map/ppermute | solution.py:20
  23.3 1.5 collective-permute-done.1
  24.9 12.2 %collective-permute-start.2 = (bf16[128,2176]{0,1:T(8,128)(2,1)S(1)}, bf16[128,2176]{0,1:T(8,128)(2,1)S(1)}, u32[]{:S(2)}, u32[]{:S(2)}) collective-permute-start(bf16[128,2176]{0,1:T(8,128)(2,1)S(1)} %collective-permute-done.1), channel_id=1, source_target_pairs={{0,1},{1,2},{2,3},{3,4},{4,5},{5,6},{6,7},{7,8},{8,9},{9,10},{10,1... | collective-permute-start | bytes 1671176 | tf_op jit(solution)/shard_map/ppermute | solution.py:20
  37.1 1.5 collective-permute-done.2
  38.6 9.3 %collective-permute-start.3 = (bf16[128,2176]{0,1:T(8,128)(2,1)S(1)}, bf16[128,2176]{0,1:T(8,128)(2,1)S(1)}, u32[]{:S(2)}, u32[]{:S(2)}) collective-permute-start(bf16[128,2176]{0,1:T(8,128)(2,1)S(1)} %collective-permute-done.2), channel_id=1, source_target_pairs={{0,1},{1,2},{2,3},{3,4},{4,5},{5,6},{6,7},{7,8},{8,9},{9,10},{10,1... | collective-permute-start | bytes 1671176 | tf_op jit(solution)/shard_map/ppermute | solution.py:20
  47.9 1.5 collective-permute-done.3
  49.5 14.9 %collective-permute-start.4 = (bf16[128,2176]{0,1:T(8,128)(2,1)S(1)}, bf16[128,2176]{0,1:T(8,128)(2,1)S(1)}, u32[]{:S(2)}, u32[]{:S(2)}) collective-permute-start(bf16[128,2176]{0,1:T(8,128)(2,1)S(1)} %collective-permute-done.3), channel_id=1, source_target_pairs={{0,1},{1,2},{2,3},{3,4},{4,5},{5,6},{6,7},{7,8},{8,9},{9,10},{10,1... | collective-permute-start | bytes 1671176 | tf_op jit(solution)/shard_map/ppermute | solution.py:20
  64.4 1.5 collective-permute-done.4
  65.9 21.2 %collective-permute-start.5 = (bf16[128,2176]{0,1:T(8,128)(2,1)S(1)}, bf16[128,2176]{0,1:T(8,128)(2,1)S(1)}, u32[]{:S(2)}, u32[]{:S(2)}) collective-permute-start(bf16[128,2176]{0,1:T(8,128)(2,1)S(1)} %collective-permute-done.4), channel_id=1, source_target_pairs={{0,1},{1,2},{2,3},{3,4},{4,5},{5,6},{6,7},{7,8},{8,9},{9,10},{10,1... | collective-permute-start | bytes 1671176 | tf_op jit(solution)/shard_map/ppermute | solution.py:20
  87.1 1.5 collective-permute-done.5
  88.7 0.8 copy-done
  89.5 14.0 %collective-permute-start.6 = (bf16[128,2176]{0,1:T(8,128)(2,1)S(1)}, bf16[128,2176]{0,1:T(8,128)(2,1)}, u32[]{:S(2)}, u32[]{:S(2)}) collective-permute-start(bf16[128,2176]{0,1:T(8,128)(2,1)S(1)} %collective-permute-done.5), channel_id=1, source_target_pairs={{0,1},{1,2},{2,3},{3,4},{4,5},{5,6},{6,7},{7,8},{8,9},{9,10},{10,1... | collective-permute-start | bytes 1671176 | tf_op jit(solution)/shard_map/ppermute | solution.py:20
  103.4 0.9 collective-permute-done.6
  104.3 12.0 %collective-permute-start.7 = (bf16[128,2176]{0,1:T(8,128)(2,1)}, bf16[128,2176]{0,1:T(8,128)(2,1)}, u32[]{:S(2)}, u32[]{:S(2)}) collective-permute-start(bf16[128,2176]{0,1:T(8,128)(2,1)} %collective-permute-done.6), channel_id=1, source_target_pairs={{0,1},{1,2},{2,3},{3,4},{4,5},{5,6},{6,7},{7,8},{8,9},{9,10},{10,1... | collective-permute-start | bytes 1671176 | tf_op jit(solution)/shard_map/ppermute | solution.py:20
  116.3 2.2 reshape.229
  118.5 1.2 constant_dynamic-update-slice_fusion.7
  119.7 1.2 constant_dynamic-update-slice_fusion.6
  121.0 1.2 constant_dynamic-update-slice_fusion.5
  122.8 0.2 constant_dynamic-update-slice_fusion.1
  123.2 0.4 slice.32
  123.9 3.1 %pad_maximum_fusion = (bf16[1152,1024]{0,1:T(8,128)(2,1)S(1)}, bf16[1152,1024]{0,1:T(8,128)(2,1)}) fusion(bf16[128,2048]{0,1:T(8,128)(2,1)S(1)} %copy.21, bf16[1024,2048]{0,1:T(8,128)(2,1)S(1)} %slice.32), kind=kLoop, calls=%fused_computation.13 | loop fusion | flops 9437184 | bytes 9437184 | tf_op jit(solution)/shard_map/concatenate | solution.py:63
  127.0 1.1 compare_and_fusion
  128.1 4.4 %fusion.33 = f32[8,2,128]{2,1,0:T(2,128)} fusion(pred[128,1152]{0,1:T(8,128)(4,1)S(1)} %compare_and_fusion, bf16[1152,8,128,1]{0,2,3,1:T(8,128)(2,1)S(1)} %bitcast.63, bf16[128,8,2,128]{3,2,1,0:T(2,128)(2,1)S(1)} %copy-done.1), kind=kOutput, calls=%fused_computation.68 | convolution fusion | flops 613418112 | bytes 3039232 | tf_op jit(solution)/shard_map/sub | solution.py:89
  132.5 6.3 %fusion.7 = bf16[8,128,2,128]{3,1,2,0:T(8,128)(2,1)S(1)} fusion(bf16[1152,8,128,1]{0,2,3,1:T(8,128)(2,1)} %bitcast.65, f32[8,2,128]{2,1,0:T(2,128)} %fusion.33, pred[128,1152]{0,1:T(8,128)(4,1)S(1)} %compare_and_fusion, bf16[1152,8,128,1]{0,2,3,1:T(8,128)(2,1)S(1)} %bitcast.64, bf16[128,8,2,128]{3,2,1,0:T(2,128)(2,1)S(1)} %copy-done.1), kind=kOutput, calls=%fused_computation.14 | convolution fusion | flops 1220021376 | bytes 5922816 | tf_op jit(solution)/shard_map/hgqk,khd->qhgd/dot_general | solution.py:91
  138.9 6.8 %fusion.36 = (bf16[128,2688]{1,0:T(8,128)(2,1)}, f32[128,2688]{1,0:T(8,128)S(1)}) fusion(bf16[128,2048]{0,1:T(8,128)(2,1)S(1)} %bitcast.68, bf16[2048,2688]{1,0:T(8,128)(2,1)} %all-gather.2.cloned.1.call-done, bf16[128,2688]{1,0:T(8,128)(2,1)} %param.11), kind=kOutput, calls=%fused_computation.69 | convolution fusion | flops 1410318336 | bytes 14286848 | tf_op jit(solution)/shard_map/dot_general | solution.py:96
  145.9 44.7 %collective-permute-start.8 = (bf16[1,4,2688]{2,1,0:T(4,128)(2,1)S(1)}, bf16[1,4,2688]{2,1,0:T(4,128)(2,1)S(1)}, u32[]{:S(2)}, u32[]{:S(2)}) collective-permute-start(bf16[1,4,2688]{2,1,0:T(4,128)(2,1)S(1)} %fusion.21), channel_id=1, source_target_pairs={{0,8},{1,9},{2,10},{3,11},{4,12},{5,13},{6,14},{7,15},{8,0},{9,1},... | collective-permute-start | bytes 64520 | tf_op jit(solution)/shard_map/ppermute | solution.py:30
  190.7 1.8 collective-permute-done.8
  192.5 3.2 %collective-permute-start.9 = (bf16[2,4,2688]{2,1,0:T(4,128)(2,1)S(1)}, bf16[2,4,2688]{2,1,0:T(4,128)(2,1)S(1)}, u32[]{:S(2)}, u32[]{:S(2)}) collective-permute-start(bf16[2,4,2688]{2,1,0:T(4,128)(2,1)S(1)} %maximum_select_fusion.3), channel_id=1, source_target_pairs={{0,4},{1,5},{2,6},{3,7},{4,0},{5,1},{6,2},{7,3},{8,12},{9,13},{10,... | collective-permute-start | bytes 129032 | tf_op jit(solution)/shard_map/ppermute | solution.py:30
  195.7 2.0 collective-permute-done.9
  197.8 4.5 %collective-permute-done.10 = bf16[4,4,2688]{2,1,0:T(4,128)(2,1)S(1)} collective-permute-done((bf16[4,4,2688]{2,1,0:T(4,128)(2,1)S(1)}, bf16[4,4,2688]{2,1,0:T(4,128)(2,1)S(1)}, u32[]{:S(2)}, u32[]{:S(2)}) %collective-permute-start.10) | collective-permute-done | bytes 86048 | tf_op jit(solution)/shard_map/ppermute | solution.py:30
  202.3 0.2 maximum_select_fusion.1
  202.6 1.4 collective-permute-done.11
  204.0 0.4 maximum_select_fusion
  204.6 4.4 %fusion.37 = (f32[64]{0:T(128)S(1)}, f32[64,1024]{1,0:T(8,128)S(1)}) fusion(bf16[64,2688]{1,0:T(8,128)(2,1)S(1)} %reshape.231, bf16[1024,2688]{1,0:T(8,128)(2,1)} %param.14), kind=kOutput, calls=%fused_computation.70 | convolution fusion | flops 352387008 | bytes 6111488 | tf_op jit(solution)/shard_map/dot_general | solution.py:107
  209.0 0.2 exponential_reduce_fusion
  209.3 3.0 %collective-permute-start.12 = (f32[1,3,64]{2,1,0:T(4,128)S(1)}, f32[1,3,64]{2,1,0:T(4,128)S(1)}, u32[]{:S(2)}, u32[]{:S(2)}) collective-permute-start(f32[1,3,64]{2,1,0:T(4,128)S(1)} %maximum_bitcast_fusion), channel_id=1, source_target_pairs={{0,8},{1,9},{2,10},{3,11},{4,12},{5,13},{6,14},{7,15},{8,0},{9,1},... | collective-permute-start | bytes 2312 | tf_op jit(solution)/shard_map/ppermute | solution.py:30
  212.3 1.6 collective-permute-done.12
  213.8 2.0 collective-permute-start.13
  215.8 1.6 collective-permute-done.13
  217.5 3.6 %collective-permute-done.14 = f32[4,3,64]{2,1,0:T(4,128)S(1)} collective-permute-done((f32[4,3,64]{2,1,0:T(4,128)S(1)}, f32[4,3,64]{2,1,0:T(4,128)S(1)}, u32[]{:S(2)}, u32[]{:S(2)}) %collective-permute-start.14) | collective-permute-done | bytes 3104 | tf_op jit(solution)/shard_map/ppermute | solution.py:30
  221.2 1.2 collective-permute-done.15
  222.5 0.8 broadcast_subtract_fusion
  223.3 0.6 dynamic_slice.3
  (44 shorter events, 2.0 us)
Async XLA Ops:
  7.2 131.7 %all-gather.2.cloned.1.call-start = ((), (), s32[]{:S(2)}) async-start(), calls=%async_computation | async-start | bytes 11698176 | tf_op jit(solution)/shard_map/all_gather | solution.py:98
  9.9 3.9 %collective-permute-start = (bf16[128,2176]{0,1:T(8,128)(2,1)S(1)}, bf16[128,2176]{0,1:T(8,128)(2,1)S(1)}, u32[]{:S(2)}, u32[]{:S(2)}) collective-permute-start(bf16[128,2176]{0,1:T(8,128)(2,1)S(1)} %pad_maximum_fusion.1), channel_id=1, source_target_pairs={{0,1},{1,2},{2,3},{3,4},{4,5},{5,6},{6,7},{7,8},{8,9},{9,10},{10,1... | collective-permute-start | bytes 1671176 | tf_op jit(solution)/shard_map/ppermute | solution.py:20
  13.9 11.0 %collective-permute-start.1 = (bf16[128,2176]{0,1:T(8,128)(2,1)S(1)}, bf16[128,2176]{0,1:T(8,128)(2,1)S(1)}, u32[]{:S(2)}, u32[]{:S(2)}) collective-permute-start(bf16[128,2176]{0,1:T(8,128)(2,1)S(1)} %collective-permute-done), channel_id=1, source_target_pairs={{0,1},{1,2},{2,3},{3,4},{4,5},{5,6},{6,7},{7,8},{8,9},{9,10},{10,1... | collective-permute-start | bytes 1671176 | tf_op jit(solution)/shard_map/ppermute | solution.py:20
  24.9 13.8 %collective-permute-start.2 = (bf16[128,2176]{0,1:T(8,128)(2,1)S(1)}, bf16[128,2176]{0,1:T(8,128)(2,1)S(1)}, u32[]{:S(2)}, u32[]{:S(2)}) collective-permute-start(bf16[128,2176]{0,1:T(8,128)(2,1)S(1)} %collective-permute-done.1), channel_id=1, source_target_pairs={{0,1},{1,2},{2,3},{3,4},{4,5},{5,6},{6,7},{7,8},{8,9},{9,10},{10,1... | collective-permute-start | bytes 1671176 | tf_op jit(solution)/shard_map/ppermute | solution.py:20
  38.6 10.8 %collective-permute-start.3 = (bf16[128,2176]{0,1:T(8,128)(2,1)S(1)}, bf16[128,2176]{0,1:T(8,128)(2,1)S(1)}, u32[]{:S(2)}, u32[]{:S(2)}) collective-permute-start(bf16[128,2176]{0,1:T(8,128)(2,1)S(1)} %collective-permute-done.2), channel_id=1, source_target_pairs={{0,1},{1,2},{2,3},{3,4},{4,5},{5,6},{6,7},{7,8},{8,9},{9,10},{10,1... | collective-permute-start | bytes 1671176 | tf_op jit(solution)/shard_map/ppermute | solution.py:20
  49.5 16.4 %collective-permute-start.4 = (bf16[128,2176]{0,1:T(8,128)(2,1)S(1)}, bf16[128,2176]{0,1:T(8,128)(2,1)S(1)}, u32[]{:S(2)}, u32[]{:S(2)}) collective-permute-start(bf16[128,2176]{0,1:T(8,128)(2,1)S(1)} %collective-permute-done.3), channel_id=1, source_target_pairs={{0,1},{1,2},{2,3},{3,4},{4,5},{5,6},{6,7},{7,8},{8,9},{9,10},{10,1... | collective-permute-start | bytes 1671176 | tf_op jit(solution)/shard_map/ppermute | solution.py:20
  65.9 22.7 %collective-permute-start.5 = (bf16[128,2176]{0,1:T(8,128)(2,1)S(1)}, bf16[128,2176]{0,1:T(8,128)(2,1)S(1)}, u32[]{:S(2)}, u32[]{:S(2)}) collective-permute-start(bf16[128,2176]{0,1:T(8,128)(2,1)S(1)} %collective-permute-done.4), channel_id=1, source_target_pairs={{0,1},{1,2},{2,3},{3,4},{4,5},{5,6},{6,7},{7,8},{8,9},{9,10},{10,1... | collective-permute-start | bytes 1671176 | tf_op jit(solution)/shard_map/ppermute | solution.py:20
  88.7 0.8 copy-start
  89.5 14.9 %collective-permute-start.6 = (bf16[128,2176]{0,1:T(8,128)(2,1)S(1)}, bf16[128,2176]{0,1:T(8,128)(2,1)}, u32[]{:S(2)}, u32[]{:S(2)}) collective-permute-start(bf16[128,2176]{0,1:T(8,128)(2,1)S(1)} %collective-permute-done.5), channel_id=1, source_target_pairs={{0,1},{1,2},{2,3},{3,4},{4,5},{5,6},{6,7},{7,8},{8,9},{9,10},{10,1... | collective-permute-start | bytes 1671176 | tf_op jit(solution)/shard_map/ppermute | solution.py:20
  104.3 14.2 %collective-permute-start.7 = (bf16[128,2176]{0,1:T(8,128)(2,1)}, bf16[128,2176]{0,1:T(8,128)(2,1)}, u32[]{:S(2)}, u32[]{:S(2)}) collective-permute-start(bf16[128,2176]{0,1:T(8,128)(2,1)} %collective-permute-done.6), channel_id=1, source_target_pairs={{0,1},{1,2},{2,3},{3,4},{4,5},{5,6},{6,7},{7,8},{8,9},{9,10},{10,1... | collective-permute-start | bytes 1671176 | tf_op jit(solution)/shard_map/ppermute | solution.py:20
  123.2 0.7 copy-start.3
  123.9 4.2 %copy-start.1 = (bf16[128,8,2,128]{3,2,1,0:T(2,128)(2,1)S(1)}, bf16[128,8,2,128]{3,2,1,0:T(2,128)(2,1)}, u32[]{:S(2)}) copy-start(bf16[128,8,2,128]{3,2,1,0:T(2,128)(2,1)} %reshape.229) | copy-start | bytes 1572868
  138.9 7.0 %copy-start.2 = (f32[2688]{0:T(1024)S(1)}, f32[2688]{0:T(1024)}, u32[]{:S(2)}) copy-start(f32[2688]{0:T(1024)} %param.12) | copy-start | bytes 32260
  138.9 63.7 %copy-start.4 = (s32[64]{0:T(128)S(1)}, s32[64]{0:T(128)}, u32[]{:S(2)}) copy-start(s32[64]{0:T(128)} %param.15) | copy-start | bytes 772
  145.9 46.5 %collective-permute-start.8 = (bf16[1,4,2688]{2,1,0:T(4,128)(2,1)S(1)}, bf16[1,4,2688]{2,1,0:T(4,128)(2,1)S(1)}, u32[]{:S(2)}, u32[]{:S(2)}) collective-permute-start(bf16[1,4,2688]{2,1,0:T(4,128)(2,1)S(1)} %fusion.21), channel_id=1, source_target_pairs={{0,8},{1,9},{2,10},{3,11},{4,12},{5,13},{6,14},{7,15},{8,0},{9,1},... | collective-permute-start | bytes 64520 | tf_op jit(solution)/shard_map/ppermute | solution.py:30
  192.5 5.2 %collective-permute-start.9 = (bf16[2,4,2688]{2,1,0:T(4,128)(2,1)S(1)}, bf16[2,4,2688]{2,1,0:T(4,128)(2,1)S(1)}, u32[]{:S(2)}, u32[]{:S(2)}) collective-permute-start(bf16[2,4,2688]{2,1,0:T(4,128)(2,1)S(1)} %maximum_select_fusion.3), channel_id=1, source_target_pairs={{0,4},{1,5},{2,6},{3,7},{4,0},{5,1},{6,2},{7,3},{8,12},{9,13},{10,... | collective-permute-start | bytes 129032 | tf_op jit(solution)/shard_map/ppermute | solution.py:30
  197.8 4.6 %collective-permute-start.10 = (bf16[4,4,2688]{2,1,0:T(4,128)(2,1)S(1)}, bf16[4,4,2688]{2,1,0:T(4,128)(2,1)S(1)}, u32[]{:S(2)}, u32[]{:S(2)}) collective-permute-start(bf16[4,4,2688]{2,1,0:T(4,128)(2,1)S(1)} %maximum_select_fusion.2), channel_id=1, source_target_pairs={{0,2},{1,3},{2,0},{3,1},{4,6},{5,7},{6,4},{7,5},{8,10},{9,11},{10,... | collective-permute-start | bytes 258056 | tf_op jit(solution)/shard_map/ppermute | solution.py:30
  202.5 1.5 collective-permute-start.11
  209.3 4.5 %collective-permute-start.12 = (f32[1,3,64]{2,1,0:T(4,128)S(1)}, f32[1,3,64]{2,1,0:T(4,128)S(1)}, u32[]{:S(2)}, u32[]{:S(2)}) collective-permute-start(f32[1,3,64]{2,1,0:T(4,128)S(1)} %maximum_bitcast_fusion), channel_id=1, source_target_pairs={{0,8},{1,9},{2,10},{3,11},{4,12},{5,13},{6,14},{7,15},{8,0},{9,1},... | collective-permute-start | bytes 2312 | tf_op jit(solution)/shard_map/ppermute | solution.py:30
  213.8 3.6 %collective-permute-start.13 = (f32[2,3,64]{2,1,0:T(4,128)S(1)}, f32[2,3,64]{2,1,0:T(4,128)S(1)}, u32[]{:S(2)}, u32[]{:S(2)}) collective-permute-start(f32[2,3,64]{2,1,0:T(4,128)S(1)} %maximum_select_fusion.7), channel_id=1, source_target_pairs={{0,4},{1,5},{2,6},{3,7},{4,0},{5,1},{6,2},{7,3},{8,12},{9,13},{10,... | collective-permute-start | bytes 4616 | tf_op jit(solution)/shard_map/ppermute | solution.py:30
  217.4 3.7 %collective-permute-start.14 = (f32[4,3,64]{2,1,0:T(4,128)S(1)}, f32[4,3,64]{2,1,0:T(4,128)S(1)}, u32[]{:S(2)}, u32[]{:S(2)}) collective-permute-start(f32[4,3,64]{2,1,0:T(4,128)S(1)} %maximum_select_fusion.6), channel_id=1, source_target_pairs={{0,2},{1,3},{2,0},{3,1},{4,6},{5,7},{6,4},{7,5},{8,10},{9,11},{10,... | collective-permute-start | bytes 9224 | tf_op jit(solution)/shard_map/ppermute | solution.py:30
  221.1 1.2 collective-permute-start.15
Sparse Core Ops, SparseCore 0:
  10.3 105.5 all-gather.1

commit v2 on v1

--- a/solution.py
+++ b/solution.py
@@ -1,6 +1,8 @@
 import jax
 import jax.numpy as jnp
+import numpy as np
 from jax import lax
+from jax.sharding import Mesh
 from jax.sharding import PartitionSpec as P
 
 QUERY_HEADS = 16
@@ -9,30 +11,49 @@
 ATTENTION_SPAN = 1024
 SCORE_DEV = 4
 SEG_LANES = 128
+LANES = 128
+CORES = 2
+SEQ = ("chip", "core")
 
 
 score_scale = 168.0 ** (-0.5)
 masked_score = -1e30
 
 
-def forward_one(value, axis):
-    count = lax.axis_size(axis)
-    return lax.ppermute(value, axis, [(source, source + 1) for source in range(count - 1)])
+def seq_count():
+    return lax.axis_size("chip") * lax.axis_size("core")
 
 
-def gather_rows(value, axis):
-    count = lax.axis_size(axis)
+def seq_index():
+    return lax.axis_index("chip") * lax.axis_size("core") + lax.axis_index("core")
+
+
+def forward_one(value):
+    count = seq_count()
+    return lax.ppermute(value, SEQ, [(source, source + 1) for source in range(count - 1)])
+
+
+def swap_cores(value):
+    return lax.ppermute(value, "core", [(0, 1), (1, 0)])
+
+
+def gather_rows(value):
+    count = seq_count()
     bits = count.bit_length() - 1
-    me = lax.axis_index(axis)
+    me = seq_index()
     data = value[None]
     for bit in reversed(range(bits)):
         step = 1 << bit
-        received = lax.ppermute(data, axis, [(i, i ^ step) for i in range(count)])
+        received = lax.ppermute(data, SEQ, [(i, i ^ step) for i in range(count)])
         low = ((me >> bit) & 1) == 0
         data = jnp.where(low, jnp.concatenate([data, received], 0), jnp.concatenate([received, data], 0))
     data = data.reshape((2,) * bits + value.shape)
     data = jnp.transpose(data, tuple(reversed(range(bits))) + tuple(range(bits, bits + value.ndim)))
     return data.reshape((count * value.shape[0],) + value.shape[1:])
+
+
+def in_core_order(mine, theirs, first):
+    return jnp.where(first, jnp.concatenate([mine, theirs], 0), jnp.concatenate([theirs, mine], 0))
 
 
 def normalize(hidden, norm_gain):
@@ -47,15 +68,25 @@
     blocks = ATTENTION_SPAN // token_rows
     queries_per_group = QUERY_HEADS // KEY_VALUE_HEADS
     kv_width = joined_keys_values.shape[1]
-    my_index = lax.axis_index("seq")
+    width = residual.shape[1]
+    my_index = seq_index()
+    core = lax.axis_index("core")
+    first_core = core == 0
     first_row = my_index * token_rows
+
+    half = -(-width // (CORES * LANES)) * LANES
+    padded_proj = jnp.pad(out_proj, ((0, 0), (0, CORES * half - width)))
+    my_half = lax.dynamic_slice_in_dim(padded_proj, core * half, half, 1)
+    other_half = lax.dynamic_slice_in_dim(padded_proj, (1 - core) * half, half, 1)
+    chip_proj = in_core_order(my_half, swap_cores(other_half), first_core)
+    proj_half = lax.all_gather(chip_proj, "chip", axis=0, tiled=True)
 
     seg_cols = jnp.broadcast_to(segment_ids.astype(jnp.bfloat16)[:, None], (token_rows, SEG_LANES))
     own = jnp.concatenate([joined_keys_values, seg_cols], 1)
     arrived = []
     current = own
     for _ in range(blocks):
-        current = forward_one(current, "seq")
+        current = forward_one(current)
         arrived.append(current)
     rim = jnp.concatenate(arrived[::-1], 0)
     rim_kv = rim[:, :kv_width]
@@ -92,12 +123,16 @@
         "hgqk,khd->qhgd", weights, heads_for_values, preferred_element_type=jnp.float32
     )
     context = context.reshape(token_rows, QUERY_HEADS * HEAD_SIZE).astype(jnp.bfloat16)
-    width = residual.shape[1]
-    projected = jnp.dot(
-        context,
-        lax.all_gather(out_proj, "seq", axis=0, tiled=True),
-        preferred_element_type=jnp.float32,
-    )
+
+    chip_context = in_core_order(context, swap_cores(context), first_core)
+    chip_projected = jnp.dot(chip_context, proj_half, preferred_element_type=jnp.float32)
+    mine = lax.dynamic_slice_in_dim(chip_projected, core * token_rows, token_rows, 0)
+    theirs = lax.dynamic_slice_in_dim(chip_projected, (1 - core) * token_rows, token_rows, 0)
+    returned = swap_cores(theirs)
+    projected = jnp.where(
+        first_core, jnp.concatenate([mine, returned], 1), jnp.concatenate([returned, mine], 1)
+    )[:, :width]
+
     hidden = residual.astype(jnp.float32) + projected
     layer_out = hidden.astype(jnp.bfloat16)
     score_count = SCORE_DEV
@@ -105,7 +140,7 @@
     picked = hidden.reshape(score_count, stride, width)[:, stride - 1, :]
     normed = normalize(picked, norm_gain)
     logits = lax.dot_general(
-        gather_rows(normed, "seq"),
+        gather_rows(normed),
         head_weight,
         (((1,), (1,)), ((), ())),
         preferred_element_type=jnp.float32,
@@ -116,7 +151,7 @@
     shard_max = jnp.max(logits, axis=1)
     shard_total = jnp.sum(jnp.exp(logits - shard_max[:, None]), axis=1)
     shard_pick = jnp.sum(jnp.where(local_ids[:, None] == vocab_ids[None, :], logits, 0.0), axis=1)
-    stats = gather_rows(jnp.stack([shard_max, shard_total, shard_pick], 0), "seq")
+    stats = gather_rows(jnp.stack([shard_max, shard_total, shard_pick], 0))
     stats = stats.reshape(-1, 3, shard_max.shape[0])
     all_max, all_total, all_pick = stats[:, 0], stats[:, 1], stats[:, 2]
     global_max = jnp.max(all_max, axis=0)
@@ -129,15 +164,19 @@
 
 
 def solution(mesh):
+    parts, seq = mesh.shape["parts"], mesh.shape["seq"]
+    devices = np.asarray(mesh.devices).reshape(parts, seq // CORES, CORES)
+    fine = Mesh(devices, ("parts",) + SEQ)
+    rows = ("parts",) + SEQ
     in_specs = (
-        P(("parts", "seq"), None),
-        P(("parts", "seq"), None),
-        P(("parts", "seq")),
-        P(("parts", "seq"), None),
+        P(rows, None),
+        P(rows, None),
+        P(rows),
+        P(rows, None),
         P(),
-        P("seq", None),
-        P("seq", None),
+        P(SEQ, None),
+        P(SEQ, None),
         P("parts"),
     )
-    out_specs = (P(("parts", "seq"), None), P("parts", "seq"), P(("parts", "seq")))
-    return jax.shard_map(local, mesh=mesh, in_specs=in_specs, out_specs=out_specs, check_vma=False)
+    out_specs = (P(rows, None), P("parts", SEQ), P(rows))
+    return jax.shard_map(local, mesh=fine, in_specs=in_specs, out_specs=out_specs, check_vma=False)

time: 231 us -> 238 us (1.030)
  waiting for transfers between devices: 28.3 us -> 31.2 us
    ppermute x16 -> x19, waiting for transfers between devices: 27.6 us -> 31.2 us  [the longest x8 17.6 us: gather_rows(): received = lax.ppermute(data, SEQ, [(i, i ^ step) for i in range(count)])]
    ppermute x16 -> x19, starting transfers between devices: 149 us -> 151 us  [the longest x8 96.4 us: forward_one(): lax.ppermute(value, SEQ, [(source, source + 1) for source in range(count...]
    unnamed x18 -> x20, local copies, waits for them, and re-layouts: 6.76 us -> 6.76 us
  transfers between devices with their start and end apart: 17 -> 20, of which waited for: 15 -> 17; matrix products, arithmetic and copies ran while one was open for 11% -> 10% of each run, Pallas kernels for 0% -> 0%
where the time goes in v2:
time: 238 us; the launch traced here: 237 us
  starting transfers between devices  151 us (63%)
  waiting for transfers between devices  31.2 us (13%)
  matrix products  20.2 us (8%)
  between operations  14.4 us (6%)
  local copies, waits for them, and re-layouts  11.7 us (5%)
  other arithmetic  9.03 us (4%)
    ppermute x8, starting transfers between devices, forward_one(): lax.ppermute(value, SEQ, [(source, source + 1) for source in range(count...  96.4 us
    ppermute x8, starting transfers between devices, gather_rows(): received = lax.ppermute(data, SEQ, [(i, i ^ step) for i in range(count)])  36.5 us
    ppermute x3, starting transfers between devices, swap_cores(): return lax.ppermute(value, 'core', [(0, 1), (1, 0)])  17.9 us
    ppermute x8, waiting for transfers between devices, gather_rows(): received = lax.ppermute(data, SEQ, [(i, i ^ step) for i in range(count)])  17.6 us
    ppermute x8, waiting for transfers between devices, forward_one(): lax.ppermute(value, SEQ, [(source, source + 1) for source in range(count...  10.1 us
    dot_general x1, matrix products, local(): jnp.einsum('hgqk,khd->qhgd', weights, heads_for_values, preferred_element...  7.1 us
    unnamed x20, local copies, waits for them, and re-layouts  6.76 us
    dot_general x1, matrix products, local(): jnp.dot(chip_context, proj_half, preferred_element_type=jnp.float32)  4.82 us
  transfers between devices with their start and end apart: 20, of which 17 were waited for; matrix products, arithmetic and copies ran while one was open for 10% of the time, Pallas kernels for 0%

profile of v2, /device:TPU:0, one launch (start us, length us, event | category | flops | bytes accessed | tf_op | source)
XLA Modules:
  0.0 237.4 jit_solution(1607828491789145454)
XLA Ops:
  7.2 1.1 pad_dynamic-slice_fusion.1
  8.9 1.3 copy.21
  10.2 0.7 convert_element_type.40
  10.9 1.1 maximum_select_fusion.2
  12.0 2.0 collective-permute-start
  14.0 1.5 collective-permute-done
  15.6 9.4 %collective-permute-start.1 = (bf16[128,2176]{0,1:T(8,128)(2,1)S(1)}, bf16[128,2176]{0,1:T(8,128)(2,1)S(1)}, u32[]{:S(2)}, u32[]{:S(2)}) collective-permute-start(bf16[128,2176]{0,1:T(8,128)(2,1)S(1)} %collective-permute-done), channel_id=1, source_target_pairs={{0,1},{1,2},{2,3},{3,4},{4,5},{5,6},{6,7},{7,8},{8,9},{9,10},{10,1... | collective-permute-start | bytes 1671176 | tf_op jit(solution)/shard_map/ppermute | solution.py:33
  25.0 1.5 collective-permute-done.1
  26.5 12.4 %collective-permute-start.2 = (bf16[128,2176]{0,1:T(8,128)(2,1)S(1)}, bf16[128,2176]{0,1:T(8,128)(2,1)S(1)}, u32[]{:S(2)}, u32[]{:S(2)}) collective-permute-start(bf16[128,2176]{0,1:T(8,128)(2,1)S(1)} %collective-permute-done.1), channel_id=1, source_target_pairs={{0,1},{1,2},{2,3},{3,4},{4,5},{5,6},{6,7},{7,8},{8,9},{9,10},{10,1... | collective-permute-start | bytes 1671176 | tf_op jit(solution)/shard_map/ppermute | solution.py:33
  39.0 1.5 collective-permute-done.2
  40.5 9.3 %collective-permute-start.3 = (bf16[128,2176]{0,1:T(8,128)(2,1)S(1)}, bf16[128,2176]{0,1:T(8,128)(2,1)S(1)}, u32[]{:S(2)}, u32[]{:S(2)}) collective-permute-start(bf16[128,2176]{0,1:T(8,128)(2,1)S(1)} %collective-permute-done.2), channel_id=1, source_target_pairs={{0,1},{1,2},{2,3},{3,4},{4,5},{5,6},{6,7},{7,8},{8,9},{9,10},{10,1... | collective-permute-start | bytes 1671176 | tf_op jit(solution)/shard_map/ppermute | solution.py:33
  49.8 1.5 collective-permute-done.3
  51.3 12.5 %collective-permute-start.4 = (bf16[128,2176]{0,1:T(8,128)(2,1)S(1)}, bf16[128,2176]{0,1:T(8,128)(2,1)S(1)}, u32[]{:S(2)}, u32[]{:S(2)}) collective-permute-start(bf16[128,2176]{0,1:T(8,128)(2,1)S(1)} %collective-permute-done.3), channel_id=1, source_target_pairs={{0,1},{1,2},{2,3},{3,4},{4,5},{5,6},{6,7},{7,8},{8,9},{9,10},{10,1... | collective-permute-start | bytes 1671176 | tf_op jit(solution)/shard_map/ppermute | solution.py:33
  63.9 1.5 collective-permute-done.4
  65.4 21.2 %collective-permute-start.5 = (bf16[128,2176]{0,1:T(8,128)(2,1)S(1)}, bf16[128,2176]{0,1:T(8,128)(2,1)S(1)}, u32[]{:S(2)}, u32[]{:S(2)}) collective-permute-start(bf16[128,2176]{0,1:T(8,128)(2,1)S(1)} %collective-permute-done.4), channel_id=1, source_target_pairs={{0,1},{1,2},{2,3},{3,4},{4,5},{5,6},{6,7},{7,8},{8,9},{9,10},{10,1... | collective-permute-start | bytes 1671176 | tf_op jit(solution)/shard_map/ppermute | solution.py:33
  86.6 1.5 collective-permute-done.5
  88.1 0.8 copy-done.1
  88.9 17.6 %collective-permute-start.6 = (bf16[128,2176]{0,1:T(8,128)(2,1)S(1)}, bf16[128,2176]{0,1:T(8,128)(2,1)}, u32[]{:S(2)}, u32[]{:S(2)}) collective-permute-start(bf16[128,2176]{0,1:T(8,128)(2,1)S(1)} %collective-permute-done.5), channel_id=1, source_target_pairs={{0,1},{1,2},{2,3},{3,4},{4,5},{5,6},{6,7},{7,8},{8,9},{9,10},{10,1... | collective-permute-start | bytes 1671176 | tf_op jit(solution)/shard_map/ppermute | solution.py:33
  106.5 0.9 collective-permute-done.6
  107.4 11.9 %collective-permute-start.7 = (bf16[128,2176]{0,1:T(8,128)(2,1)}, bf16[128,2176]{0,1:T(8,128)(2,1)}, u32[]{:S(2)}, u32[]{:S(2)}) collective-permute-start(bf16[128,2176]{0,1:T(8,128)(2,1)} %collective-permute-done.6), channel_id=1, source_target_pairs={{0,1},{1,2},{2,3},{3,4},{4,5},{5,6},{6,7},{7,8},{8,9},{9,10},{10,1... | collective-permute-start | bytes 1671176 | tf_op jit(solution)/shard_map/ppermute | solution.py:33
  119.3 2.2 reshape.229
  121.6 1.2 constant_dynamic-update-slice_fusion.7
  122.8 1.2 constant_dynamic-update-slice_fusion.6
  124.1 1.2 constant_dynamic-update-slice_fusion.5
  127.0 3.0 %pad_maximum_fusion = (bf16[1152,1024]{0,1:T(8,128)(2,1)S(1)}, bf16[1152,1024]{0,1:T(8,128)(2,1)}) fusion(bf16[128,2048]{0,1:T(8,128)(2,1)S(1)} %copy.21, bf16[1024,2048]{0,1:T(8,128)(2,1)S(1)} %slice.36), kind=kLoop, calls=%fused_computation.12 | loop fusion | flops 9437184 | bytes 9437184 | tf_op jit(solution)/shard_map/concatenate | solution.py:94
  130.0 1.1 compare_and_fusion
  131.1 3.8 %fusion.45 = f32[8,2,128]{2,1,0:T(2,128)S(1)} fusion(pred[128,1152]{0,1:T(8,128)(4,1)S(1)} %compare_and_fusion, bf16[1152,8,128,1]{0,2,3,1:T(8,128)(2,1)S(1)} %bitcast.62, bf16[128,8,2,128]{3,2,1,0:T(2,128)(2,1)S(1)} %copy-done.2), kind=kOutput, calls=%fused_computation.86 | convolution fusion | flops 613418112 | bytes 3039232 | tf_op jit(solution)/shard_map/sub | solution.py:120
  134.9 7.1 %fusion.9 = bf16[8,128,2,128]{3,1,2,0:T(8,128)(2,1)} fusion(bf16[1152,8,128,1]{0,2,3,1:T(8,128)(2,1)} %bitcast.64, f32[8,2,128]{2,1,0:T(2,128)S(1)} %fusion.45, pred[128,1152]{0,1:T(8,128)(4,1)S(1)} %compare_and_fusion, bf16[1152,8,128,1]{0,2,3,1:T(8,128)(2,1)S(1)} %bitcast.63, bf16[128,8,2,128]{3,2,1,0:T(2,128)(2,1)S(1)} %copy-done.2), kind=kOutput, calls=%fused_computation.17 | convolution fusion | flops 1220021376 | bytes 5922816 | tf_op jit(solution)/shard_map/hgqk,khd->qhgd/dot_general | solution.py:122
  142.0 17.0 %collective-permute-start.8 = (bf16[128,2048]{0,1:T(8,128)(2,1)}, bf16[128,2048]{0,1:T(8,128)(2,1)S(1)}, u32[]{:S(2)}, u32[]{:S(2)}) collective-permute-start(bf16[128,2048]{0,1:T(8,128)(2,1)} %bitcast.74), channel_id=1, source_target_pairs={{0,1},{1,0},{2,3},{3,2},{4,5},{5,4},{6,7},{7,6},{8,9},{9,8},{10,11... | collective-permute-start | bytes 1572872 | tf_op jit(solution)/shard_map/ppermute | solution.py:37
  159.0 1.7 collective-permute-done.8
  160.8 4.8 %fusion.12 = f32[256,1408]{1,0:T(8,128)S(1)} fusion(bf16[2048,1408]{1,0:T(8,128)(2,1)} %all-gather.2.cloned.1.call-done, bf16[128,2048]{0,1:T(8,128)(2,1)S(1)} %collective-permute-done.8, bf16[128,2048]{0,1:T(8,128)(2,1)} %bitcast.75, pred[]{:T(512)S(6)} %eq.49), kind=kOutput, calls=%fused_computation.20 | convolution fusion | flops 1481113600 | bytes 8257537 | tf_op jit(solution)/shard_map/dot_general | solution.py:128
  166.2 1.8 collective-permute-done.10
  168.0 1.1 fusion.43
  169.3 25.6 %collective-permute-start.11 = (bf16[1,4,2688]{2,1,0:T(4,128)(2,1)S(1)}, bf16[1,4,2688]{2,1,0:T(4,128)(2,1)S(1)}, u32[]{:S(2)}, u32[]{:S(2)}) collective-permute-start(bf16[1,4,2688]{2,1,0:T(4,128)(2,1)S(1)} %fusion.30), channel_id=1, source_target_pairs={{0,8},{1,9},{2,10},{3,11},{4,12},{5,13},{6,14},{7,15},{8,0},{9,1},... | collective-permute-start | bytes 64520 | tf_op jit(solution)/shard_map/ppermute | solution.py:47
  194.9 1.8 collective-permute-done.11
  196.7 5.7 %collective-permute-start.12 = (bf16[2,4,2688]{2,1,0:T(4,128)(2,1)S(1)}, bf16[2,4,2688]{2,1,0:T(4,128)(2,1)S(1)}, u32[]{:S(2)}, u32[]{:S(2)}) collective-permute-start(bf16[2,4,2688]{2,1,0:T(4,128)(2,1)S(1)} %maximum_select_fusion.6), channel_id=1, source_target_pairs={{0,4},{1,5},{2,6},{3,7},{4,0},{5,1},{6,2},{7,3},{8,12},{9,13},{10,... | collective-permute-start | bytes 129032 | tf_op jit(solution)/shard_map/ppermute | solution.py:47
  202.4 2.0 collective-permute-done.12
  204.6 4.5 %collective-permute-done.13 = bf16[4,4,2688]{2,1,0:T(4,128)(2,1)S(1)} collective-permute-done((bf16[4,4,2688]{2,1,0:T(4,128)(2,1)S(1)}, bf16[4,4,2688]{2,1,0:T(4,128)(2,1)S(1)}, u32[]{:S(2)}, u32[]{:S(2)}) %collective-permute-start.13) | collective-permute-done | bytes 86048 | tf_op jit(solution)/shard_map/ppermute | solution.py:47
  209.3 1.4 collective-permute-done.14
  211.3 4.4 %fusion.48 = (f32[64]{0:T(128)S(1)}, f32[64,1024]{1,0:T(8,128)S(1)}) fusion(bf16[64,2688]{1,0:T(8,128)(2,1)S(1)} %reshape.231, bf16[1024,2688]{1,0:T(8,128)(2,1)} %param.14), kind=kOutput, calls=%fused_computation.87 | convolution fusion | flops 352387008 | bytes 6111488 | tf_op jit(solution)/shard_map/dot_general | solution.py:142
  216.0 3.0 %collective-permute-start.15 = (f32[1,3,64]{2,1,0:T(4,128)S(1)}, f32[1,3,64]{2,1,0:T(4,128)S(1)}, u32[]{:S(2)}, u32[]{:S(2)}) collective-permute-start(f32[1,3,64]{2,1,0:T(4,128)S(1)} %maximum_bitcast_fusion), channel_id=1, source_target_pairs={{0,8},{1,9},{2,10},{3,11},{4,12},{5,13},{6,14},{7,15},{8,0},{9,1},... | collective-permute-start | bytes 2312 | tf_op jit(solution)/shard_map/ppermute | solution.py:47
  219.0 1.6 collective-permute-done.15
  220.6 2.0 collective-permute-start.16
  222.6 1.6 collective-permute-done.16
  224.2 3.6 %collective-permute-done.17 = f32[4,3,64]{2,1,0:T(4,128)S(1)} collective-permute-done((f32[4,3,64]{2,1,0:T(4,128)S(1)}, f32[4,3,64]{2,1,0:T(4,128)S(1)}, u32[]{:S(2)}, u32[]{:S(2)}) %collective-permute-start.17) | collective-permute-done | bytes 3104 | tf_op jit(solution)/shard_map/ppermute | solution.py:47
  227.9 1.2 collective-permute-done.18
  229.2 0.8 broadcast_subtract_fusion
  230.0 0.6 dynamic_slice.19
  (56 shorter events, 4.5 us)
Async XLA Ops:
  7.2 153.6 %all-gather.2.cloned.1.call-start = ((), (), s32[]{:S(2)}) async-start(), calls=%async_computation | async-start | bytes 6488064 | tf_op jit(solution)/shard_map/all_gather | solution.py:82
  8.4 2.5 %collective-permute-start.9 = (bf16[128,1408]{1,0:T(8,128)(2,1)S(1)}, bf16[128,1408]{1,0:T(8,128)(2,1)S(1)}, u32[]{:S(2)}, u32[]{:S(2)}) collective-permute-start(bf16[128,1408]{1,0:T(8,128)(2,1)S(1)} %get-tuple-element.16), channel_id=1, source_target_pairs={{0,1},{1,0},{2,3},{3,2},{4,5},{5,4},{6,7},{7,6},{8,9},{9,8},{10,11... | collective-permute-start | bytes 1081352 | tf_op jit(solution)/shard_map/ppermute | solution.py:37
  12.0 3.5 %collective-permute-start = (bf16[128,2176]{0,1:T(8,128)(2,1)S(1)}, bf16[128,2176]{0,1:T(8,128)(2,1)S(1)}, u32[]{:S(2)}, u32[]{:S(2)}) collective-permute-start(bf16[128,2176]{0,1:T(8,128)(2,1)S(1)} %pad_maximum_fusion.3), channel_id=1, source_target_pairs={{0,1},{1,2},{2,3},{3,4},{4,5},{5,6},{6,7},{7,8},{8,9},{9,10},{10,1... | collective-permute-start | bytes 1671176 | tf_op jit(solution)/shard_map/ppermute | solution.py:33
  15.6 11.0 %collective-permute-start.1 = (bf16[128,2176]{0,1:T(8,128)(2,1)S(1)}, bf16[128,2176]{0,1:T(8,128)(2,1)S(1)}, u32[]{:S(2)}, u32[]{:S(2)}) collective-permute-start(bf16[128,2176]{0,1:T(8,128)(2,1)S(1)} %collective-permute-done), channel_id=1, source_target_pairs={{0,1},{1,2},{2,3},{3,4},{4,5},{5,6},{6,7},{7,8},{8,9},{9,10},{10,1... | collective-permute-start | bytes 1671176 | tf_op jit(solution)/shard_map/ppermute | solution.py:33
  26.5 14.0 %collective-permute-start.2 = (bf16[128,2176]{0,1:T(8,128)(2,1)S(1)}, bf16[128,2176]{0,1:T(8,128)(2,1)S(1)}, u32[]{:S(2)}, u32[]{:S(2)}) collective-permute-start(bf16[128,2176]{0,1:T(8,128)(2,1)S(1)} %collective-permute-done.1), channel_id=1, source_target_pairs={{0,1},{1,2},{2,3},{3,4},{4,5},{5,6},{6,7},{7,8},{8,9},{9,10},{10,1... | collective-permute-start | bytes 1671176 | tf_op jit(solution)/shard_map/ppermute | solution.py:33
  40.5 10.8 %collective-permute-start.3 = (bf16[128,2176]{0,1:T(8,128)(2,1)S(1)}, bf16[128,2176]{0,1:T(8,128)(2,1)S(1)}, u32[]{:S(2)}, u32[]{:S(2)}) collective-permute-start(bf16[128,2176]{0,1:T(8,128)(2,1)S(1)} %collective-permute-done.2), channel_id=1, source_target_pairs={{0,1},{1,2},{2,3},{3,4},{4,5},{5,6},{6,7},{7,8},{8,9},{9,10},{10,1... | collective-permute-start | bytes 1671176 | tf_op jit(solution)/shard_map/ppermute | solution.py:33
  51.3 14.1 %collective-permute-start.4 = (bf16[128,2176]{0,1:T(8,128)(2,1)S(1)}, bf16[128,2176]{0,1:T(8,128)(2,1)S(1)}, u32[]{:S(2)}, u32[]{:S(2)}) collective-permute-start(bf16[128,2176]{0,1:T(8,128)(2,1)S(1)} %collective-permute-done.3), channel_id=1, source_target_pairs={{0,1},{1,2},{2,3},{3,4},{4,5},{5,6},{6,7},{7,8},{8,9},{9,10},{10,1... | collective-permute-start | bytes 1671176 | tf_op jit(solution)/shard_map/ppermute | solution.py:33
  65.4 22.7 %collective-permute-start.5 = (bf16[128,2176]{0,1:T(8,128)(2,1)S(1)}, bf16[128,2176]{0,1:T(8,128)(2,1)S(1)}, u32[]{:S(2)}, u32[]{:S(2)}) collective-permute-start(bf16[128,2176]{0,1:T(8,128)(2,1)S(1)} %collective-permute-done.4), channel_id=1, source_target_pairs={{0,1},{1,2},{2,3},{3,4},{4,5},{5,6},{6,7},{7,8},{8,9},{9,10},{10,1... | collective-permute-start | bytes 1671176 | tf_op jit(solution)/shard_map/ppermute | solution.py:33
  88.1 0.8 copy-start.1
  88.9 18.5 %collective-permute-start.6 = (bf16[128,2176]{0,1:T(8,128)(2,1)S(1)}, bf16[128,2176]{0,1:T(8,128)(2,1)}, u32[]{:S(2)}, u32[]{:S(2)}) collective-permute-start(bf16[128,2176]{0,1:T(8,128)(2,1)S(1)} %collective-permute-done.5), channel_id=1, source_target_pairs={{0,1},{1,2},{2,3},{3,4},{4,5},{5,6},{6,7},{7,8},{8,9},{9,10},{10,1... | collective-permute-start | bytes 1671176 | tf_op jit(solution)/shard_map/ppermute | solution.py:33
  107.4 14.2 %collective-permute-start.7 = (bf16[128,2176]{0,1:T(8,128)(2,1)}, bf16[128,2176]{0,1:T(8,128)(2,1)}, u32[]{:S(2)}, u32[]{:S(2)}) collective-permute-start(bf16[128,2176]{0,1:T(8,128)(2,1)} %collective-permute-done.6), channel_id=1, source_target_pairs={{0,1},{1,2},{2,3},{3,4},{4,5},{5,6},{6,7},{7,8},{8,9},{9,10},{10,1... | collective-permute-start | bytes 1671176 | tf_op jit(solution)/shard_map/ppermute | solution.py:33
  126.3 0.7 copy-start.4
  127.0 4.1 %copy-start.2 = (bf16[128,8,2,128]{3,2,1,0:T(2,128)(2,1)S(1)}, bf16[128,8,2,128]{3,2,1,0:T(2,128)(2,1)}, u32[]{:S(2)}) copy-start(bf16[128,8,2,128]{3,2,1,0:T(2,128)(2,1)} %reshape.229) | copy-start | bytes 1572868
  142.0 18.7 %collective-permute-start.8 = (bf16[128,2048]{0,1:T(8,128)(2,1)}, bf16[128,2048]{0,1:T(8,128)(2,1)S(1)}, u32[]{:S(2)}, u32[]{:S(2)}) collective-permute-start(bf16[128,2048]{0,1:T(8,128)(2,1)} %bitcast.74), channel_id=1, source_target_pairs={{0,1},{1,0},{2,3},{3,2},{4,5},{5,4},{6,7},{7,6},{8,9},{9,8},{10,11... | collective-permute-start | bytes 1572872 | tf_op jit(solution)/shard_map/ppermute | solution.py:37
  159.0 9.0 %copy-start = (bf16[128,2688]{1,0:T(8,128)(2,1)S(1)}, bf16[128,2688]{1,0:T(8,128)(2,1)}, u32[]{:S(2)}) copy-start(bf16[128,2688]{1,0:T(8,128)(2,1)} %param.11) | copy-start | bytes 2064388
  165.6 3.7 %copy-start.3 = (f32[2688]{0:T(1024)S(1)}, f32[2688]{0:T(1024)}, u32[]{:S(2)}) copy-start(f32[2688]{0:T(1024)} %param.12) | copy-start | bytes 32260
  165.6 43.7 %copy-start.5 = (s32[64]{0:T(128)S(1)}, s32[64]{0:T(128)}, u32[]{:S(2)}) copy-start(s32[64]{0:T(128)} %param.15) | copy-start | bytes 772
  165.7 2.3 collective-permute-start.10
  169.3 27.4 %collective-permute-start.11 = (bf16[1,4,2688]{2,1,0:T(4,128)(2,1)S(1)}, bf16[1,4,2688]{2,1,0:T(4,128)(2,1)S(1)}, u32[]{:S(2)}, u32[]{:S(2)}) collective-permute-start(bf16[1,4,2688]{2,1,0:T(4,128)(2,1)S(1)} %fusion.30), channel_id=1, source_target_pairs={{0,8},{1,9},{2,10},{3,11},{4,12},{5,13},{6,14},{7,15},{8,0},{9,1},... | collective-permute-start | bytes 64520 | tf_op jit(solution)/shard_map/ppermute | solution.py:47
  196.7 7.7 %collective-permute-start.12 = (bf16[2,4,2688]{2,1,0:T(4,128)(2,1)S(1)}, bf16[2,4,2688]{2,1,0:T(4,128)(2,1)S(1)}, u32[]{:S(2)}, u32[]{:S(2)}) collective-permute-start(bf16[2,4,2688]{2,1,0:T(4,128)(2,1)S(1)} %maximum_select_fusion.6), channel_id=1, source_target_pairs={{0,4},{1,5},{2,6},{3,7},{4,0},{5,1},{6,2},{7,3},{8,12},{9,13},{10,... | collective-permute-start | bytes 129032 | tf_op jit(solution)/shard_map/ppermute | solution.py:47
  204.5 4.6 %collective-permute-start.13 = (bf16[4,4,2688]{2,1,0:T(4,128)(2,1)S(1)}, bf16[4,4,2688]{2,1,0:T(4,128)(2,1)S(1)}, u32[]{:S(2)}, u32[]{:S(2)}) collective-permute-start(bf16[4,4,2688]{2,1,0:T(4,128)(2,1)S(1)} %maximum_select_fusion.5), channel_id=1, source_target_pairs={{0,2},{1,3},{2,0},{3,1},{4,6},{5,7},{6,4},{7,5},{8,10},{9,11},{10,... | collective-permute-start | bytes 258056 | tf_op jit(solution)/shard_map/ppermute | solution.py:47
  209.2 1.5 collective-permute-start.14
  216.0 4.5 %collective-permute-start.15 = (f32[1,3,64]{2,1,0:T(4,128)S(1)}, f32[1,3,64]{2,1,0:T(4,128)S(1)}, u32[]{:S(2)}, u32[]{:S(2)}) collective-permute-start(f32[1,3,64]{2,1,0:T(4,128)S(1)} %maximum_bitcast_fusion), channel_id=1, source_target_pairs={{0,8},{1,9},{2,10},{3,11},{4,12},{5,13},{6,14},{7,15},{8,0},{9,1},... | collective-permute-start | bytes 2312 | tf_op jit(solution)/shard_map/ppermute | solution.py:47
  220.6 3.6 %collective-permute-start.16 = (f32[2,3,64]{2,1,0:T(4,128)S(1)}, f32[2,3,64]{2,1,0:T(4,128)S(1)}, u32[]{:S(2)}, u32[]{:S(2)}) collective-permute-start(f32[2,3,64]{2,1,0:T(4,128)S(1)} %maximum_select_fusion.10), channel_id=1, source_target_pairs={{0,4},{1,5},{2,6},{3,7},{4,0},{5,1},{6,2},{7,3},{8,12},{9,13},{10,... | collective-permute-start | bytes 4616 | tf_op jit(solution)/shard_map/ppermute | solution.py:47
  224.2 3.7 %collective-permute-start.17 = (f32[4,3,64]{2,1,0:T(4,128)S(1)}, f32[4,3,64]{2,1,0:T(4,128)S(1)}, u32[]{:S(2)}, u32[]{:S(2)}) collective-permute-start(f32[4,3,64]{2,1,0:T(4,128)S(1)} %maximum_select_fusion.9), channel_id=1, source_target_pairs={{0,2},{1,3},{2,0},{3,1},{4,6},{5,7},{6,4},{7,5},{8,10},{9,11},{10,... | collective-permute-start | bytes 9224 | tf_op jit(solution)/shard_map/ppermute | solution.py:47
  227.8 1.2 collective-permute-start.18
Sparse Core Ops, SparseCore 0:
  12.1 107.9 all-gather.1

commit v3 on v2

--- a/solution.py
+++ b/solution.py
@@ -54,6 +54,42 @@
 
 def in_core_order(mine, theirs, first):
     return jnp.where(first, jnp.concatenate([mine, theirs], 0), jnp.concatenate([theirs, mine], 0))
+
+
+def shift_chips(value, chips):
+    count = seq_count()
+    step = chips * CORES
+    return lax.ppermute(value, SEQ, [(s, s + step) for s in range(count - step)])
+
+
+def across_pair(value, from_odd):
+    count = seq_count()
+    pairs = [(s, s ^ CORES) for s in range(count) if ((s // CORES) % 2 == 1) == from_odd]
+    return lax.ppermute(value, SEQ, pairs)
+
+
+def halo_window(own, kv_width, blocks, first_core):
+    assert blocks == 4 * CORES
+    odd = (lax.axis_index("chip") % 2) == 1
+    back2 = shift_chips(own, 2)
+    own_to_odd = across_pair(own, False)
+    partner_own = swap_cores(own)
+    back4 = shift_chips(back2, 2)
+    back2_to_even = across_pair(back2, True)
+    back2_to_odd = across_pair(back2, False)
+    back4_to_even = across_pair(back4, True)
+    back1 = jnp.where(odd, own_to_odd, back2_to_even)
+    back3 = jnp.where(odd, back2_to_odd, back4_to_even)
+    near = swap_cores(jnp.stack([back1, back2], 0))
+    far = swap_cores(jnp.stack([back3, back4], 0))
+    pieces = []
+    for mine, theirs in ((back4, far[1]), (back3, far[0]), (back2, near[1]), (back1, near[0]), (own, partner_own)):
+        pieces.append(in_core_order(mine, theirs, first_core))
+    sequence = jnp.concatenate(pieces, 0)
+    token_rows = own.shape[0]
+    core = lax.axis_index("core")
+    window = lax.dynamic_slice_in_dim(sequence, core * token_rows, (blocks + 1) * token_rows, 0)
+    return window[:, :kv_width], window[:, kv_width].astype(jnp.int32)
 
 
 def normalize(hidden, norm_gain):
@@ -83,16 +119,7 @@
 
     seg_cols = jnp.broadcast_to(segment_ids.astype(jnp.bfloat16)[:, None], (token_rows, SEG_LANES))
     own = jnp.concatenate([joined_keys_values, seg_cols], 1)
-    arrived = []
-    current = own
-    for _ in range(blocks):
-        current = forward_one(current)
-        arrived.append(current)
-    rim = jnp.concatenate(arrived[::-1], 0)
-    rim_kv = rim[:, :kv_width]
-    rim_seg = rim[:, kv_width].astype(jnp.int32)
-    key_value_pair = jnp.concatenate([rim_kv, joined_keys_values], 0)
-    key_seg = jnp.concatenate([rim_seg, segment_ids], 0)
+    key_value_pair, key_seg = halo_window(own, kv_width, blocks, first_core)
     count_of_keys = key_value_pair.shape[0]
     query_pos = first_row + jnp.arange(token_rows, dtype=jnp.int32)
     key_pos = first_row - blocks * token_rows + jnp.arange(count_of_keys, dtype=jnp.int32)

time: 238 us -> 182 us (0.76)
  starting transfers between devices: 151 us -> 30.6 us
  waiting for transfers between devices: 31.2 us -> 96.6 us
  local copies, waits for them, and re-layouts: 11.7 us -> 9.07 us
    ppermute x8 -> x6, starting transfers between devices: 96.4 us -> 24.6 us  [the longest x2 14 us: shift_chips(): lax.ppermute(value, SEQ, [(s, s + step) for s in range(count - step)])]
    ppermute x8 -> x6, waiting for transfers between devices: 10.1 us -> 51.4 us  [the longest x2 28.8 us: shift_chips(): lax.ppermute(value, SEQ, [(s, s + step) for s in range(count - step)])]
    ppermute x8, starting transfers between devices: 36.5 us -> 4.85 us  [gather_rows(): received = lax.ppermute(data, SEQ, [(i, i ^ step) for i in range(count)])]
    ppermute x3 -> x6, starting transfers between devices: 17.9 us -> 1.11 us  [swap_cores(): return lax.ppermute(value, 'core', [(0, 1), (1, 0)])]
    all_gather x1, waiting for transfers between devices: 0.01 us -> 16.5 us  [local(): proj_half = lax.all_gather(chip_proj, 'chip', axis=0, tiled=True)]
    unnamed x20 -> x17, local copies, waits for them, and re-layouts: 6.76 us -> 0.33 us
    ppermute x8, waiting for transfers between devices: 17.6 us -> 23 us  [gather_rows(): received = lax.ppermute(data, SEQ, [(i, i ^ step) for i in range(count)])]
    squeeze x0 -> x2, local copies, waits for them, and re-layouts: none -> 2.61 us  [the longest x1 1.32 us: halo_window(): far[0]]
  transfers between devices with their start and end apart: 20 -> 21, of which waited for: 17 -> 15; matrix products, arithmetic and copies ran while one was open for 10% -> 13% of each run, Pallas kernels for 0% -> 0%
where the time goes in v3:
time: 182 us
  waiting for transfers between devices  96.6 us (53%)
  starting transfers between devices  30.6 us (17%)
  matrix products  20.1 us (11%)
  between operations  14.5 us (8%)
  other arithmetic  10.8 us (6%)
  local copies, waits for them, and re-layouts  9.07 us (5%)
    ppermute x2, waiting for transfers between devices, shift_chips(): lax.ppermute(value, SEQ, [(s, s + step) for s in range(count - step)])  28.8 us
    ppermute x8, waiting for transfers between devices, gather_rows(): received = lax.ppermute(data, SEQ, [(i, i ^ step) for i in range(count)])  23 us
    ppermute x4, waiting for transfers between devices, across_pair(): return lax.ppermute(value, SEQ, pairs)  22.6 us
    all_gather x1, waiting for transfers between devices, local(): proj_half = lax.all_gather(chip_proj, 'chip', axis=0, tiled=True)  16.5 us
    ppermute x2, starting transfers between devices, shift_chips(): lax.ppermute(value, SEQ, [(s, s + step) for s in range(count - step)])  14 us
    ppermute x4, starting transfers between devices, across_pair(): return lax.ppermute(value, SEQ, pairs)  10.6 us
    dot_general x1, matrix products, local(): jnp.einsum('hgqk,khd->qhgd', weights, heads_for_values, preferred_element...  7.15 us
    ppermute x6, waiting for transfers between devices, swap_cores(): return lax.ppermute(value, 'core', [(0, 1), (1, 0)])  5.6 us
  transfers between devices with their start and end apart: 21, of which 15 were waited for; matrix products, arithmetic and copies ran while one was open for 13% of the time, Pallas kernels for 0%

profile of v3, /device:TPU:0, one launch (start us, length us, event | category | flops | bytes accessed | tf_op | source)
XLA Modules:
  0.0 181.5 jit_solution(754245742252989557)
XLA Ops:
  7.2 1.2 pad_dynamic-slice_fusion.1
  8.4 0.5 collective-permute-start.10
  9.0 1.3 collective-permute-done.10
  10.3 1.0 maximum_select_fusion.7
  11.7 4.9 %collective-permute-start = (bf16[128,2176]{0,1:T(8,128)(2,1)S(1)}, bf16[128,2176]{0,1:T(8,128)(2,1)S(1)}, u32[]{:S(2)}, u32[]{:S(2)}) collective-permute-start(bf16[128,2176]{0,1:T(8,128)(2,1)S(1)} %pad_maximum_fusion.4), channel_id=1, source_target_pairs={{0,4},{1,5},{2,6},{3,7},{4,8},{5,9},{6,10},{7,11},{8,12},{9,13},{1... | collective-permute-start | bytes 1671176 | tf_op jit(solution)/shard_map/ppermute | solution.py:62
  16.6 18.4 %collective-permute-done = bf16[128,2176]{0,1:T(8,128)(2,1)S(1)} collective-permute-done((bf16[128,2176]{0,1:T(8,128)(2,1)S(1)}, bf16[128,2176]{0,1:T(8,128)(2,1)S(1)}, u32[]{:S(2)}, u32[]{:S(2)}) %collective-permute-start) | collective-permute-done | bytes 557088 | tf_op jit(solution)/shard_map/ppermute | solution.py:62
  35.0 9.1 %collective-permute-start.1 = (bf16[128,2176]{0,1:T(8,128)(2,1)S(1)}, bf16[128,2176]{0,1:T(8,128)(2,1)S(1)}, u32[]{:S(2)}, u32[]{:S(2)}) collective-permute-start(bf16[128,2176]{0,1:T(8,128)(2,1)S(1)} %collective-permute-done), channel_id=1, source_target_pairs={{0,4},{1,5},{2,6},{3,7},{4,8},{5,9},{6,10},{7,11},{8,12},{9,13},{1... | collective-permute-start | bytes 1671176 | tf_op jit(solution)/shard_map/ppermute | solution.py:62
  44.1 3.4 %collective-permute-start.5 = (bf16[128,2176]{0,1:T(8,128)(2,1)S(1)}, bf16[128,2176]{0,1:T(8,128)(2,1)S(1)}, u32[]{:S(2)}, u32[]{:S(2)}) collective-permute-start(bf16[128,2176]{0,1:T(8,128)(2,1)S(1)} %pad_maximum_fusion.4), channel_id=1, source_target_pairs={{0,2},{1,3},{4,6},{5,7},{8,10},{9,11},{12,14},{13,15},{16,18},{17,... | collective-permute-start | bytes 1671176 | tf_op jit(solution)/shard_map/ppermute | solution.py:68
  47.5 1.3 collective-permute-start.6
  48.8 4.6 %collective-permute-start.2 = (bf16[128,2176]{0,1:T(8,128)(2,1)S(1)}, bf16[128,2176]{0,1:T(8,128)(2,1)S(1)}, u32[]{:S(2)}, u32[]{:S(2)}) collective-permute-start(bf16[128,2176]{0,1:T(8,128)(2,1)S(1)} %collective-permute-done), channel_id=1, source_target_pairs={{0,2},{1,3},{4,6},{5,7},{8,10},{9,11},{12,14},{13,15},{16,18},{17,... | collective-permute-start | bytes 1671176 | tf_op jit(solution)/shard_map/ppermute | solution.py:68
  53.4 10.4 %collective-permute-done.1 = bf16[128,2176]{0,1:T(8,128)(2,1)S(1)} collective-permute-done((bf16[128,2176]{0,1:T(8,128)(2,1)S(1)}, bf16[128,2176]{0,1:T(8,128)(2,1)S(1)}, u32[]{:S(2)}, u32[]{:S(2)}) %collective-permute-start.1) | collective-permute-done | bytes 557088 | tf_op jit(solution)/shard_map/ppermute | solution.py:62
  63.9 1.3 collective-permute-start.3
  65.2 1.2 pad_maximum_fusion.3
  66.4 22.6 %collective-permute-done.3 = bf16[128,2176]{0,1:T(8,128)(2,1)S(1)} collective-permute-done((bf16[128,2176]{0,1:T(8,128)(2,1)S(1)}, bf16[128,2176]{0,1:T(8,128)(2,1)S(1)}, u32[]{:S(2)}, u32[]{:S(2)}) %collective-permute-start.3) | collective-permute-done | bytes 557088 | tf_op jit(solution)/shard_map/ppermute | solution.py:68
  89.1 1.1 pad_maximum_fusion.2
  90.2 0.5 collective-permute-start.8
  90.7 2.2 %reshape.233 = bf16[128,8,2,128]{3,2,1,0:T(2,128)(2,1)} reshape(bf16[128,2048]{1,0:T(8,128)(2,1)} %param.8) | data formatting | bytes 1048576 | tf_op jit(solution)/shard_map/reshape | solution.py:132
  92.9 1.3 slice_bitcast_fusion
  94.2 1.3 slice_bitcast_fusion.2
  95.9 0.4 fusion.12
  96.3 0.4 fusion.13
  96.7 0.4 fusion.14
  97.1 1.6 fusion.15
  98.8 1.8 constant_dynamic-slice_fusion.2
  100.6 1.1 compare_and_fusion
  101.6 3.7 %fusion.50 = f32[8,2,128]{2,1,0:T(2,128)S(1)} fusion(pred[128,1152]{0,1:T(8,128)(4,1)S(1)} %compare_and_fusion, bf16[1152,8,128,1]{0,2,3,1:T(8,128)(2,1)S(1)} %bitcast.75, bf16[128,8,2,128]{3,2,1,0:T(2,128)(2,1)S(1)} %copy-done.4), kind=kOutput, calls=%fused_computation.93 | convolution fusion | flops 613418112 | bytes 3039232 | tf_op jit(solution)/shard_map/sub | solution.py:147
  105.3 7.2 %fusion.8 = bf16[8,128,2,128]{3,1,2,0:T(8,128)(2,1)} fusion(bf16[1152,8,128,1]{0,2,3,1:T(8,128)(2,1)} %bitcast.77, f32[8,2,128]{2,1,0:T(2,128)S(1)} %fusion.50, pred[128,1152]{0,1:T(8,128)(4,1)S(1)} %compare_and_fusion, bf16[1152,8,128,1]{0,2,3,1:T(8,128)(2,1)S(1)} %bitcast.76, bf16[128,8,2,128]{3,2,1,0:T(2,128)(2,1)S(1)} %copy-done.4), kind=kOutput, calls=%fused_computation.13 | convolution fusion | flops 1220021376 | bytes 5922816 | tf_op jit(solution)/shard_map/hgqk,khd->qhgd/dot_general | solution.py:149
  112.5 2.1 %collective-permute-done.9 = bf16[128,2048]{0,1:T(8,128)(2,1)S(1)} collective-permute-done((bf16[128,2048]{0,1:T(8,128)(2,1)}, bf16[128,2048]{0,1:T(8,128)(2,1)S(1)}, u32[]{:S(2)}, u32[]{:S(2)}) %collective-permute-start.9) | collective-permute-done | bytes 524320 | tf_op jit(solution)/shard_map/ppermute | solution.py:37
  114.6 16.5 %all-gather.2.cloned.1.call-done = bf16[2048,1408]{1,0:T(8,128)(2,1)} async-done(((bf16[256,1408]{1,0:T(8,128)(2,1)}), bf16[2048,1408]{1,0:T(8,128)(2,1)}) %all-gather.2.cloned.1.call-update) | async-done | bytes 5767184 | tf_op jit(solution)/shard_map/all_gather | solution.py:118
  131.1 4.8 %fusion.16 = f32[256,1408]{1,0:T(8,128)S(1)} fusion(bf16[2048,1408]{1,0:T(8,128)(2,1)} %all-gather.2.cloned.1.call-done, bf16[128,2048]{0,1:T(8,128)(2,1)S(1)} %collective-permute-done.9, bf16[128,2048]{0,1:T(8,128)(2,1)} %bitcast.89, pred[]{:T(512)S(6)} %eq.54), kind=kOutput, calls=%fused_computation.28 | convolution fusion | flops 1481113600 | bytes 8257537 | tf_op jit(solution)/shard_map/dot_general | solution.py:155
  136.2 2.2 %collective-permute-done.11 = f32[128,1408]{1,0:T(8,128)S(1)} collective-permute-done((f32[128,1408]{1,0:T(8,128)S(1)}, f32[128,1408]{1,0:T(8,128)S(1)}, u32[]{:S(2)}, u32[]{:S(2)}) %collective-permute-start.11) | collective-permute-done | bytes 720928 | tf_op jit(solution)/shard_map/ppermute | solution.py:37
  138.3 1.0 fusion.48
  139.7 1.9 %collective-permute-start.12 = (bf16[1,4,2688]{2,1,0:T(4,128)(2,1)S(1)}, bf16[1,4,2688]{2,1,0:T(4,128)(2,1)S(1)}, u32[]{:S(2)}, u32[]{:S(2)}) collective-permute-start(bf16[1,4,2688]{2,1,0:T(4,128)(2,1)S(1)} %fusion.34), channel_id=1, source_target_pairs={{0,8},{1,9},{2,10},{3,11},{4,12},{5,13},{6,14},{7,15},{8,0},{9,1},... | collective-permute-start | bytes 64520 | tf_op jit(solution)/shard_map/ppermute | solution.py:47
  141.6 2.8 %collective-permute-done.12 = bf16[1,4,2688]{2,1,0:T(4,128)(2,1)S(1)} collective-permute-done((bf16[1,4,2688]{2,1,0:T(4,128)(2,1)S(1)}, bf16[1,4,2688]{2,1,0:T(4,128)(2,1)S(1)}, u32[]{:S(2)}, u32[]{:S(2)}) %collective-permute-start.12) | collective-permute-done | bytes 21536 | tf_op jit(solution)/shard_map/ppermute | solution.py:47
  144.5 0.4 collective-permute-start.13
  144.9 3.7 %collective-permute-done.13 = bf16[2,4,2688]{2,1,0:T(4,128)(2,1)S(1)} collective-permute-done((bf16[2,4,2688]{2,1,0:T(4,128)(2,1)S(1)}, bf16[2,4,2688]{2,1,0:T(4,128)(2,1)S(1)}, u32[]{:S(2)}, u32[]{:S(2)}) %collective-permute-start.13) | collective-permute-done | bytes 43040 | tf_op jit(solution)/shard_map/ppermute | solution.py:47
  148.7 4.5 %collective-permute-done.14 = bf16[4,4,2688]{2,1,0:T(4,128)(2,1)S(1)} collective-permute-done((bf16[4,4,2688]{2,1,0:T(4,128)(2,1)S(1)}, bf16[4,4,2688]{2,1,0:T(4,128)(2,1)S(1)}, u32[]{:S(2)}, u32[]{:S(2)}) %collective-permute-start.14) | collective-permute-done | bytes 86048 | tf_op jit(solution)/shard_map/ppermute | solution.py:47
  153.5 1.4 collective-permute-done.15
  154.8 0.4 maximum_select_fusion.8
  155.4 4.4 %fusion.53 = (f32[64]{0:T(128)S(1)}, f32[64,1024]{1,0:T(8,128)S(1)}) fusion(bf16[64,2688]{1,0:T(8,128)(2,1)S(1)} %reshape.235, bf16[1024,2688]{1,0:T(8,128)(2,1)} %param.14), kind=kOutput, calls=%fused_computation.94 | convolution fusion | flops 352387008 | bytes 6111488 | tf_op jit(solution)/shard_map/dot_general | solution.py:169
  160.1 1.9 %collective-permute-start.16 = (f32[1,3,64]{2,1,0:T(4,128)S(1)}, f32[1,3,64]{2,1,0:T(4,128)S(1)}, u32[]{:S(2)}, u32[]{:S(2)}) collective-permute-start(f32[1,3,64]{2,1,0:T(4,128)S(1)} %maximum_bitcast_fusion), channel_id=1, source_target_pairs={{0,8},{1,9},{2,10},{3,11},{4,12},{5,13},{6,14},{7,15},{8,0},{9,1},... | collective-permute-start | bytes 2312 | tf_op jit(solution)/shard_map/ppermute | solution.py:47
  162.1 2.6 %collective-permute-done.16 = f32[1,3,64]{2,1,0:T(4,128)S(1)} collective-permute-done((f32[1,3,64]{2,1,0:T(4,128)S(1)}, f32[1,3,64]{2,1,0:T(4,128)S(1)}, u32[]{:S(2)}, u32[]{:S(2)}) %collective-permute-start.16) | collective-permute-done | bytes 800 | tf_op jit(solution)/shard_map/ppermute | solution.py:47
  164.7 0.3 collective-permute-start.17
  165.0 3.3 %collective-permute-done.17 = f32[2,3,64]{2,1,0:T(4,128)S(1)} collective-permute-done((f32[2,3,64]{2,1,0:T(4,128)S(1)}, f32[2,3,64]{2,1,0:T(4,128)S(1)}, u32[]{:S(2)}, u32[]{:S(2)}) %collective-permute-start.17) | collective-permute-done | bytes 1568 | tf_op jit(solution)/shard_map/ppermute | solution.py:47
  168.3 3.6 %collective-permute-done.18 = f32[4,3,64]{2,1,0:T(4,128)S(1)} collective-permute-done((f32[4,3,64]{2,1,0:T(4,128)S(1)}, f32[4,3,64]{2,1,0:T(4,128)S(1)}, u32[]{:S(2)}, u32[]{:S(2)}) %collective-permute-start.18) | collective-permute-done | bytes 3104 | tf_op jit(solution)/shard_map/ppermute | solution.py:47
  172.0 1.2 collective-permute-done.19
  173.3 0.8 broadcast_subtract_fusion
  174.1 0.6 dynamic_slice.23
  (64 shorter events, 2.5 us)
Async XLA Ops:
  7.2 4.2 %copy-start.3 = (bf16[128,2048]{1,0:T(8,128)(2,1)S(1)}, bf16[128,2048]{1,0:T(8,128)(2,1)}, u32[]{:S(2)}) copy-start(bf16[128,2048]{1,0:T(8,128)(2,1)} %param.9) | copy-start | bytes 1572868
  7.2 123.9 %all-gather.2.cloned.1.call-start = ((), (), s32[]{:S(2)}) async-start(), calls=%async_computation | async-start | bytes 6488064 | tf_op jit(solution)/shard_map/all_gather | solution.py:118
  7.2 4.4 %copy-start.6 = (s32[128]{0:T(128)S(1)}, s32[128]{0:T(128)}, u32[]{:S(2)}) copy-start(s32[128]{0:T(128)} %param.10) | copy-start | bytes 1540
  8.4 1.8 %collective-permute-start.10 = (bf16[128,1408]{1,0:T(8,128)(2,1)S(1)}, bf16[128,1408]{1,0:T(8,128)(2,1)S(1)}, u32[]{:S(2)}, u32[]{:S(2)}) collective-permute-start(bf16[128,1408]{1,0:T(8,128)(2,1)S(1)} %get-tuple-element.20), channel_id=1, source_target_pairs={{0,1},{1,0},{2,3},{3,2},{4,5},{5,4},{6,7},{7,6},{8,9},{9,8},{10,11... | collective-permute-start | bytes 1081352 | tf_op jit(solution)/shard_map/ppermute | solution.py:37
  11.7 53.4 %copy-start.1 = (bf16[128,2176]{0,1:T(8,128)(2,1)}, bf16[128,2176]{0,1:T(8,128)(2,1)S(1)}, u32[]{:S(2)}) copy-start(bf16[128,2176]{0,1:T(8,128)(2,1)S(1)} %pad_maximum_fusion.4) | copy-start | bytes 1671172
  11.7 23.3 %collective-permute-start = (bf16[128,2176]{0,1:T(8,128)(2,1)S(1)}, bf16[128,2176]{0,1:T(8,128)(2,1)S(1)}, u32[]{:S(2)}, u32[]{:S(2)}) collective-permute-start(bf16[128,2176]{0,1:T(8,128)(2,1)S(1)} %pad_maximum_fusion.4), channel_id=1, source_target_pairs={{0,4},{1,5},{2,6},{3,7},{4,8},{5,9},{6,10},{7,11},{8,12},{9,13},{1... | collective-permute-start | bytes 1671176 | tf_op jit(solution)/shard_map/ppermute | solution.py:62
  35.0 28.9 %collective-permute-start.1 = (bf16[128,2176]{0,1:T(8,128)(2,1)S(1)}, bf16[128,2176]{0,1:T(8,128)(2,1)S(1)}, u32[]{:S(2)}, u32[]{:S(2)}) collective-permute-start(bf16[128,2176]{0,1:T(8,128)(2,1)S(1)} %collective-permute-done), channel_id=1, source_target_pairs={{0,4},{1,5},{2,6},{3,7},{4,8},{5,9},{6,10},{7,11},{8,12},{9,13},{1... | collective-permute-start | bytes 1671176 | tf_op jit(solution)/shard_map/ppermute | solution.py:62
  44.1 21.1 %collective-permute-start.5 = (bf16[128,2176]{0,1:T(8,128)(2,1)S(1)}, bf16[128,2176]{0,1:T(8,128)(2,1)S(1)}, u32[]{:S(2)}, u32[]{:S(2)}) collective-permute-start(bf16[128,2176]{0,1:T(8,128)(2,1)S(1)} %pad_maximum_fusion.4), channel_id=1, source_target_pairs={{0,2},{1,3},{4,6},{5,7},{8,10},{9,11},{12,14},{13,15},{16,18},{17,... | collective-permute-start | bytes 1671176 | tf_op jit(solution)/shard_map/ppermute | solution.py:68
  47.5 17.7 %collective-permute-start.6 = (bf16[128,2176]{0,1:T(8,128)(2,1)S(1)}, bf16[128,2176]{0,1:T(8,128)(2,1)S(1)}, u32[]{:S(2)}, u32[]{:S(2)}) collective-permute-start(bf16[128,2176]{0,1:T(8,128)(2,1)S(1)} %collective-permute-done), channel_id=1, source_target_pairs={{2,0},{3,1},{6,4},{7,5},{10,8},{11,9},{14,12},{15,13},{18,16},{19,... | collective-permute-start | bytes 1671176 | tf_op jit(solution)/shard_map/ppermute | solution.py:68
  48.8 17.6 %collective-permute-start.2 = (bf16[128,2176]{0,1:T(8,128)(2,1)S(1)}, bf16[128,2176]{0,1:T(8,128)(2,1)S(1)}, u32[]{:S(2)}, u32[]{:S(2)}) collective-permute-start(bf16[128,2176]{0,1:T(8,128)(2,1)S(1)} %collective-permute-done), channel_id=1, source_target_pairs={{0,2},{1,3},{4,6},{5,7},{8,10},{9,11},{12,14},{13,15},{16,18},{17,... | collective-permute-start | bytes 1671176 | tf_op jit(solution)/shard_map/ppermute | solution.py:68
  63.9 25.2 %collective-permute-start.3 = (bf16[128,2176]{0,1:T(8,128)(2,1)S(1)}, bf16[128,2176]{0,1:T(8,128)(2,1)S(1)}, u32[]{:S(2)}, u32[]{:S(2)}) collective-permute-start(bf16[128,2176]{0,1:T(8,128)(2,1)S(1)} %collective-permute-done.1), channel_id=1, source_target_pairs={{2,0},{3,1},{6,4},{7,5},{10,8},{11,9},{14,12},{15,13},{18,16},{19,... | collective-permute-start | bytes 1671176 | tf_op jit(solution)/shard_map/ppermute | solution.py:68
  66.4 23.8 %copy-start.2 = (bf16[128,2176]{0,1:T(8,128)(2,1)S(1)}, bf16[128,2176]{0,1:T(8,128)(2,1)}, u32[]{:S(2)}) copy-start(bf16[128,2176]{0,1:T(8,128)(2,1)} %copy-done.1) | copy-start | bytes 1671172
  66.4 26.5 %collective-permute-start.7 = (bf16[2,128,2176]{1,2,0:T(8,128)(2,1)}, bf16[2,128,2176]{1,2,0:T(8,128)(2,1)}, u32[]{:S(2)}, u32[]{:S(2)}) collective-permute-start(bf16[2,128,2176]{1,2,0:T(8,128)(2,1)} %pad_maximum_fusion.3), channel_id=1, source_target_pairs={{0,1},{1,0},{2,3},{3,2},{4,5},{5,4},{6,7},{7,6},{8,9},{9,8},{10,11... | collective-permute-start | bytes 3342344 | tf_op jit(solution)/shard_map/ppermute | solution.py:37
  90.2 4.0 %collective-permute-start.4 = (bf16[2,128,2176]{1,2,0:T(8,128)(2,1)}, bf16[2,128,2176]{1,2,0:T(8,128)(2,1)}, u32[]{:S(2)}, u32[]{:S(2)}) collective-permute-start(bf16[2,128,2176]{1,2,0:T(8,128)(2,1)} %pad_maximum_fusion.2), channel_id=1, source_target_pairs={{0,1},{1,0},{2,3},{3,2},{4,5},{5,4},{6,7},{7,6},{8,9},{9,8},{10,11... | collective-permute-start | bytes 3342344 | tf_op jit(solution)/shard_map/ppermute | solution.py:37
  90.2 6.9 %collective-permute-start.8 = (bf16[128,2176]{0,1:T(8,128)(2,1)S(1)}, bf16[128,2176]{0,1:T(8,128)(2,1)}, u32[]{:S(2)}, u32[]{:S(2)}) collective-permute-start(bf16[128,2176]{0,1:T(8,128)(2,1)S(1)} %copy-done.2), channel_id=1, source_target_pairs={{0,1},{1,0},{2,3},{3,2},{4,5},{5,4},{6,7},{7,6},{8,9},{9,8},{10,11... | collective-permute-start | bytes 1671176 | tf_op jit(solution)/shard_map/ppermute | solution.py:37
  98.8 2.9 %copy-start.4 = (bf16[128,8,2,128]{3,2,1,0:T(2,128)(2,1)S(1)}, bf16[128,8,2,128]{3,2,1,0:T(2,128)(2,1)}, u32[]{:S(2)}) copy-start(bf16[128,8,2,128]{3,2,1,0:T(2,128)(2,1)} %reshape.233) | copy-start | bytes 1572868
  112.5 2.1 %collective-permute-start.9 = (bf16[128,2048]{0,1:T(8,128)(2,1)}, bf16[128,2048]{0,1:T(8,128)(2,1)S(1)}, u32[]{:S(2)}, u32[]{:S(2)}) collective-permute-start(bf16[128,2048]{0,1:T(8,128)(2,1)} %bitcast.88), channel_id=1, source_target_pairs={{0,1},{1,0},{2,3},{3,2},{4,5},{5,4},{6,7},{7,6},{8,9},{9,8},{10,11... | collective-permute-start | bytes 1572872 | tf_op jit(solution)/shard_map/ppermute | solution.py:37
  135.9 2.4 %copy-start = (bf16[128,2688]{1,0:T(8,128)(2,1)S(1)}, bf16[128,2688]{1,0:T(8,128)(2,1)}, u32[]{:S(2)}) copy-start(bf16[128,2688]{1,0:T(8,128)(2,1)} %param.11) | copy-start | bytes 2064388
  136.1 3.5 %copy-start.5 = (f32[2688]{0:T(1024)S(1)}, f32[2688]{0:T(1024)}, u32[]{:S(2)}) copy-start(f32[2688]{0:T(1024)} %param.12) | copy-start | bytes 32260
  136.1 2.3 %collective-permute-start.11 = (f32[128,1408]{1,0:T(8,128)S(1)}, f32[128,1408]{1,0:T(8,128)S(1)}, u32[]{:S(2)}, u32[]{:S(2)}) collective-permute-start(f32[128,1408]{1,0:T(8,128)S(1)} %get-tuple-element.13), channel_id=1, source_target_pairs={{0,1},{1,0},{2,3},{3,2},{4,5},{5,4},{6,7},{7,6},{8,9},{9,8},{10,11... | collective-permute-start | bytes 2162696 | tf_op jit(solution)/shard_map/ppermute | solution.py:37
  138.3 15.1 %copy-start.7 = (s32[64]{0:T(128)S(1)}, s32[64]{0:T(128)}, u32[]{:S(2)}) copy-start(s32[64]{0:T(128)} %param.15) | copy-start | bytes 772
  139.7 4.8 %collective-permute-start.12 = (bf16[1,4,2688]{2,1,0:T(4,128)(2,1)S(1)}, bf16[1,4,2688]{2,1,0:T(4,128)(2,1)S(1)}, u32[]{:S(2)}, u32[]{:S(2)}) collective-permute-start(bf16[1,4,2688]{2,1,0:T(4,128)(2,1)S(1)} %fusion.34), channel_id=1, source_target_pairs={{0,8},{1,9},{2,10},{3,11},{4,12},{5,13},{6,14},{7,15},{8,0},{9,1},... | collective-permute-start | bytes 64520 | tf_op jit(solution)/shard_map/ppermute | solution.py:47
  144.5 4.1 %collective-permute-start.13 = (bf16[2,4,2688]{2,1,0:T(4,128)(2,1)S(1)}, bf16[2,4,2688]{2,1,0:T(4,128)(2,1)S(1)}, u32[]{:S(2)}, u32[]{:S(2)}) collective-permute-start(bf16[2,4,2688]{2,1,0:T(4,128)(2,1)S(1)} %maximum_select_fusion.11), channel_id=1, source_target_pairs={{0,4},{1,5},{2,6},{3,7},{4,0},{5,1},{6,2},{7,3},{8,12},{9,13},{10,... | collective-permute-start | bytes 129032 | tf_op jit(solution)/shard_map/ppermute | solution.py:47
  148.6 4.6 %collective-permute-start.14 = (bf16[4,4,2688]{2,1,0:T(4,128)(2,1)S(1)}, bf16[4,4,2688]{2,1,0:T(4,128)(2,1)S(1)}, u32[]{:S(2)}, u32[]{:S(2)}) collective-permute-start(bf16[4,4,2688]{2,1,0:T(4,128)(2,1)S(1)} %maximum_select_fusion.10), channel_id=1, source_target_pairs={{0,2},{1,3},{2,0},{3,1},{4,6},{5,7},{6,4},{7,5},{8,10},{9,11},{10,... | collective-permute-start | bytes 258056 | tf_op jit(solution)/shard_map/ppermute | solution.py:47
  153.4 1.5 collective-permute-start.15
  160.1 4.5 %collective-permute-start.16 = (f32[1,3,64]{2,1,0:T(4,128)S(1)}, f32[1,3,64]{2,1,0:T(4,128)S(1)}, u32[]{:S(2)}, u32[]{:S(2)}) collective-permute-start(f32[1,3,64]{2,1,0:T(4,128)S(1)} %maximum_bitcast_fusion), channel_id=1, source_target_pairs={{0,8},{1,9},{2,10},{3,11},{4,12},{5,13},{6,14},{7,15},{8,0},{9,1},... | collective-permute-start | bytes 2312 | tf_op jit(solution)/shard_map/ppermute | solution.py:47
  164.7 3.6 %collective-permute-start.17 = (f32[2,3,64]{2,1,0:T(4,128)S(1)}, f32[2,3,64]{2,1,0:T(4,128)S(1)}, u32[]{:S(2)}, u32[]{:S(2)}) collective-permute-start(f32[2,3,64]{2,1,0:T(4,128)S(1)} %maximum_select_fusion.15), channel_id=1, source_target_pairs={{0,4},{1,5},{2,6},{3,7},{4,0},{5,1},{6,2},{7,3},{8,12},{9,13},{10,... | collective-permute-start | bytes 4616 | tf_op jit(solution)/shard_map/ppermute | solution.py:47
  168.3 3.7 %collective-permute-start.18 = (f32[4,3,64]{2,1,0:T(4,128)S(1)}, f32[4,3,64]{2,1,0:T(4,128)S(1)}, u32[]{:S(2)}, u32[]{:S(2)}) collective-permute-start(f32[4,3,64]{2,1,0:T(4,128)S(1)} %maximum_select_fusion.14), channel_id=1, source_target_pairs={{0,2},{1,3},{2,0},{3,1},{4,6},{5,7},{6,4},{7,5},{8,10},{9,11},{10,... | collective-permute-start | bytes 9224 | tf_op jit(solution)/shard_map/ppermute | solution.py:47
  172.0 1.2 collective-permute-start.19
Sparse Core Ops, SparseCore 0:
  11.4 119.6 all-gather.1

commit v4 on v3

--- a/solution.py
+++ b/solution.py
@@ -92,6 +92,15 @@
     return window[:, :kv_width], window[:, kv_width].astype(jnp.int32)
 
 
+def spread_over_chips(piece):
+    chips = lax.axis_size("chip")
+    count = seq_count()
+    pieces = [piece]
+    for d in range(1, chips):
+        pieces.append(lax.ppermute(piece, SEQ, [(s, (s + CORES * d) % count) for s in range(count)]))
+    return jnp.stack(pieces, 0)
+
+
 def normalize(hidden, norm_gain):
     mean_square = jnp.mean(hidden * hidden, axis=1, keepdims=True)
     return (hidden * lax.rsqrt(mean_square + 1e-06) * norm_gain[None, :]).astype(jnp.bfloat16)
@@ -115,7 +124,7 @@
     my_half = lax.dynamic_slice_in_dim(padded_proj, core * half, half, 1)
     other_half = lax.dynamic_slice_in_dim(padded_proj, (1 - core) * half, half, 1)
     chip_proj = in_core_order(my_half, swap_cores(other_half), first_core)
-    proj_half = lax.all_gather(chip_proj, "chip", axis=0, tiled=True)
+    proj_pieces = spread_over_chips(chip_proj)
 
     seg_cols = jnp.broadcast_to(segment_ids.astype(jnp.bfloat16)[:, None], (token_rows, SEG_LANES))
     own = jnp.concatenate([joined_keys_values, seg_cols], 1)
@@ -152,7 +161,21 @@
     context = context.reshape(token_rows, QUERY_HEADS * HEAD_SIZE).astype(jnp.bfloat16)
 
     chip_context = in_core_order(context, swap_cores(context), first_core)
-    chip_projected = jnp.dot(chip_context, proj_half, preferred_element_type=jnp.float32)
+    chips = lax.axis_size("chip")
+    chip_cols = proj_pieces.shape[1]
+    chip = lax.axis_index("chip")
+    permuted_context = jnp.concatenate(
+        [
+            lax.dynamic_slice_in_dim(chip_context, ((chip - d) % chips) * chip_cols, chip_cols, 1)
+            for d in range(chips)
+        ],
+        1,
+    )
+    chip_projected = jnp.dot(
+        permuted_context,
+        proj_pieces.reshape(chips * proj_pieces.shape[1], proj_pieces.shape[2]),
+        preferred_element_type=jnp.float32,
+    )
     mine = lax.dynamic_slice_in_dim(chip_projected, core * token_rows, token_rows, 0)
     theirs = lax.dynamic_slice_in_dim(chip_projected, (1 - core) * token_rows, token_rows, 0)
     returned = swap_cores(theirs)

time: 182 us -> 253 us (1.39)
  starting transfers between devices: 30.6 us -> 102 us
  between operations: 14.5 us -> 1.32 us
  local copies, waits for them, and re-layouts: 9.07 us -> 16.4 us
  waiting for transfers between devices: 96.6 us -> 102 us
    ppermute x0 -> x7, starting transfers between devices: none -> 82.9 us  [spread_over_chips(): lax.ppermute(piece, SEQ, [(s, (s + CORES * d) % count) for s in range(cou...]
    ppermute x0 -> x7, waiting for transfers between devices: none -> 60.3 us  [spread_over_chips(): lax.ppermute(piece, SEQ, [(s, (s + CORES * d) % count) for s in range(cou...]
    ppermute x2, waiting for transfers between devices: 28.8 us -> 0.01 us  [shift_chips(): lax.ppermute(value, SEQ, [(s, s + step) for s in range(count - step)])]
    all_gather x1 -> x0, waiting for transfers between devices: 16.5 us -> none  [local(): proj_half = lax.all_gather(chip_proj, 'chip', axis=0, tiled=True)]
    ppermute x4, waiting for transfers between devices: 22.6 us -> 9.54 us  [across_pair(): return lax.ppermute(value, SEQ, pairs)]
    unnamed x17 -> x26, local copies, waits for them, and re-layouts: 0.33 us -> 8.1 us
    ppermute x2, starting transfers between devices: 14 us -> 7.81 us  [shift_chips(): lax.ppermute(value, SEQ, [(s, s + step) for s in range(count - step)])]
    ppermute x8, starting transfers between devices: 4.85 us -> 0.43 us  [gather_rows(): received = lax.ppermute(data, SEQ, [(i, i ^ step) for i in range(count)])]
  transfers between devices with their start and end apart: 21 -> 27, of which waited for: 15 -> 15; matrix products, arithmetic and copies ran while one was open for 13% -> 12% of each run, Pallas kernels for 0% -> 0%
where the time goes in v4:
time: 253 us; the launch traced here: 252 us
  starting transfers between devices  102 us (40%)
  waiting for transfers between devices  102 us (40%)
  matrix products  19 us (8%)
  local copies, waits for them, and re-layouts  16.4 us (6%)
  other arithmetic  11.6 us (5%)
    ppermute x7, starting transfers between devices, spread_over_chips(): lax.ppermute(piece, SEQ, [(s, (s + CORES * d) % count) for s in range(cou...  82.9 us
    ppermute x7, waiting for transfers between devices, spread_over_chips(): lax.ppermute(piece, SEQ, [(s, (s + CORES * d) % count) for s in range(cou...  60.3 us
    ppermute x8, waiting for transfers between devices, gather_rows(): received = lax.ppermute(data, SEQ, [(i, i ^ step) for i in range(count)])  27.4 us
    ppermute x4, waiting for transfers between devices, across_pair(): return lax.ppermute(value, SEQ, pairs)  9.54 us
    ppermute x4, starting transfers between devices, across_pair(): return lax.ppermute(value, SEQ, pairs)  8.88 us
    unnamed x26, local copies, waits for them, and re-layouts  8.1 us
    ppermute x2, starting transfers between devices, shift_chips(): lax.ppermute(value, SEQ, [(s, s + step) for s in range(count - step)])  7.81 us
    dot_general x1, matrix products, local(): jnp.einsum('hgqk,khd->qhgd', weights, heads_for_values, preferred_element...  6.31 us
  transfers between devices with their start and end apart: 27, of which 15 were waited for; matrix products, arithmetic and copies ran while one was open for 12% of the time, Pallas kernels for 0%

profile of v4, /device:TPU:0, one launch (start us, length us, event | category | flops | bytes accessed | tf_op | source)
XLA Modules:
  0.0 252.0 jit_solution(16423137229562093926)
XLA Ops:
  0.6 1.1 pad_dynamic-slice_fusion.1
  3.0 1.3 copy.20
  4.3 1.1 maximum_select_fusion.7
  5.4 2.5 %collective-permute-start.11 = (bf16[256,1408]{1,0:T(8,128)(2,1)}, bf16[256,1408]{1,0:T(8,128)(2,1)S(1)}, u32[]{:S(2)}, u32[]{:S(2)}) collective-permute-start(bf16[256,1408]{1,0:T(8,128)(2,1)} %maximum_select_fusion.7), channel_id=1, source_target_pairs={{0,2},{1,3},{2,4},{3,5},{4,6},{5,7},{6,8},{7,9},{8,10},{9,11},{10,... | collective-permute-start | bytes 2162696 | tf_op jit(solution)/shard_map/ppermute | solution.py:100
  7.9 0.8 pad_maximum_fusion.4
  8.7 3.5 %collective-permute-start = (bf16[128,2176]{0,1:T(8,128)(2,1)}, bf16[128,2176]{0,1:T(8,128)(2,1)S(1)}, u32[]{:S(2)}, u32[]{:S(2)}) collective-permute-start(bf16[128,2176]{0,1:T(8,128)(2,1)} %pad_maximum_fusion.4), channel_id=1, source_target_pairs={{0,4},{1,5},{2,6},{3,7},{4,8},{5,9},{6,10},{7,11},{8,12},{9,13},{1... | collective-permute-start | bytes 1671176 | tf_op jit(solution)/shard_map/ppermute | solution.py:62
  12.3 3.5 %collective-permute-start.5 = (bf16[128,2176]{0,1:T(8,128)(2,1)}, bf16[128,2176]{0,1:T(8,128)(2,1)S(1)}, u32[]{:S(2)}, u32[]{:S(2)}) collective-permute-start(bf16[128,2176]{0,1:T(8,128)(2,1)} %pad_maximum_fusion.4), channel_id=1, source_target_pairs={{0,2},{1,3},{4,6},{5,7},{8,10},{9,11},{12,14},{13,15},{16,18},{17,... | collective-permute-start | bytes 1671176 | tf_op jit(solution)/shard_map/ppermute | solution.py:68
  16.0 2.2 reshape.291
  18.2 1.6 collective-permute-start.12
  19.8 1.0 fusion.16
  20.8 7.3 %collective-permute-done.11 = bf16[256,1408]{1,0:T(8,128)(2,1)S(1)} collective-permute-done((bf16[256,1408]{1,0:T(8,128)(2,1)}, bf16[256,1408]{1,0:T(8,128)(2,1)S(1)}, u32[]{:S(2)}, u32[]{:S(2)}) %collective-permute-start.11) | collective-permute-done | bytes 720928 | tf_op jit(solution)/shard_map/ppermute | solution.py:100
  28.1 0.9 bitcast_dynamic-update-slice_fusion.6
  29.1 2.5 collective-permute-start.14
  31.6 9.4 %collective-permute-done.12 = bf16[256,1408]{1,0:T(8,128)(2,1)S(1)} collective-permute-done((bf16[256,1408]{1,0:T(8,128)(2,1)}, bf16[256,1408]{1,0:T(8,128)(2,1)S(1)}, u32[]{:S(2)}, u32[]{:S(2)}) %collective-permute-start.12) | collective-permute-done | bytes 720928 | tf_op jit(solution)/shard_map/ppermute | solution.py:100
  40.9 4.3 %collective-permute-start.1 = (bf16[128,2176]{0,1:T(8,128)(2,1)S(1)}, bf16[128,2176]{0,1:T(8,128)(2,1)S(1)}, u32[]{:S(2)}, u32[]{:S(2)}) collective-permute-start(bf16[128,2176]{0,1:T(8,128)(2,1)S(1)} %collective-permute-done), channel_id=1, source_target_pairs={{0,4},{1,5},{2,6},{3,7},{4,8},{5,9},{6,10},{7,11},{8,12},{9,13},{1... | collective-permute-start | bytes 1671176 | tf_op jit(solution)/shard_map/ppermute | solution.py:62
  45.3 0.9 bitcast_dynamic-update-slice_fusion.5
  46.2 43.6 %collective-permute-done.13 = bf16[256,1408]{1,0:T(8,128)(2,1)S(1)} collective-permute-done((bf16[256,1408]{1,0:T(8,128)(2,1)}, bf16[256,1408]{1,0:T(8,128)(2,1)S(1)}, u32[]{:S(2)}, u32[]{:S(2)}) %collective-permute-start.13) | collective-permute-done | bytes 720928 | tf_op jit(solution)/shard_map/ppermute | solution.py:100
  89.8 1.3 collective-permute-start.6
  91.1 0.9 bitcast_dynamic-update-slice_fusion.4
  92.0 12.8 %collective-permute-start.15 = (bf16[256,1408]{1,0:T(8,128)(2,1)}, bf16[256,1408]{1,0:T(8,128)(2,1)S(1)}, u32[]{:S(2)}, u32[]{:S(2)}) collective-permute-start(bf16[256,1408]{1,0:T(8,128)(2,1)} %maximum_select_fusion.7), channel_id=1, source_target_pairs={{0,10},{1,11},{2,12},{3,13},{4,14},{5,15},{6,0},{7,1},{8,2},{9,3},... | collective-permute-start | bytes 2162696 | tf_op jit(solution)/shard_map/ppermute | solution.py:100
  104.8 0.9 bitcast_dynamic-update-slice_fusion.3
  105.8 29.4 %collective-permute-start.16 = (bf16[256,1408]{1,0:T(8,128)(2,1)}, bf16[256,1408]{1,0:T(8,128)(2,1)}, u32[]{:S(2)}, u32[]{:S(2)}) collective-permute-start(bf16[256,1408]{1,0:T(8,128)(2,1)} %maximum_select_fusion.7), channel_id=1, source_target_pairs={{0,12},{1,13},{2,14},{3,15},{4,0},{5,1},{6,2},{7,3},{8,4},{9,5},{1... | collective-permute-start | bytes 2162696 | tf_op jit(solution)/shard_map/ppermute | solution.py:100
  135.2 2.8 %collective-permute-start.2 = (bf16[128,2176]{0,1:T(8,128)(2,1)S(1)}, bf16[128,2176]{0,1:T(8,128)(2,1)S(1)}, u32[]{:S(2)}, u32[]{:S(2)}) collective-permute-start(bf16[128,2176]{0,1:T(8,128)(2,1)S(1)} %collective-permute-done), channel_id=1, source_target_pairs={{0,2},{1,3},{4,6},{5,7},{8,10},{9,11},{12,14},{13,15},{16,18},{17,... | collective-permute-start | bytes 1671176 | tf_op jit(solution)/shard_map/ppermute | solution.py:68
  138.0 1.3 collective-permute-start.3
  139.5 9.5 %collective-permute-done.2 = bf16[128,2176]{0,1:T(8,128)(2,1)S(1)} collective-permute-done((bf16[128,2176]{0,1:T(8,128)(2,1)S(1)}, bf16[128,2176]{0,1:T(8,128)(2,1)S(1)}, u32[]{:S(2)}, u32[]{:S(2)}) %collective-permute-start.2) | collective-permute-done | bytes 557088 | tf_op jit(solution)/shard_map/ppermute | solution.py:68
  149.0 34.0 %collective-permute-start.17 = (bf16[256,1408]{1,0:T(8,128)(2,1)}, bf16[256,1408]{1,0:T(8,128)(2,1)}, u32[]{:S(2)}, u32[]{:S(2)}) collective-permute-start(bf16[256,1408]{1,0:T(8,128)(2,1)} %maximum_select_fusion.7), channel_id=1, source_target_pairs={{0,14},{1,15},{2,0},{3,1},{4,2},{5,3},{6,4},{7,5},{8,6},{9,7},{10,... | collective-permute-start | bytes 2162696 | tf_op jit(solution)/shard_map/ppermute | solution.py:100
  183.9 0.9 bitcast_dynamic-update-slice_fusion.2
  184.8 1.1 collective-permute-done.7
  185.9 1.5 collective-permute-done.4
  189.0 1.6 fusion.15
  190.6 1.8 constant_dynamic-slice_fusion.2
  192.5 1.1 compare_and_fusion
  193.6 3.8 %fusion.43 = f32[8,2,128]{2,1,0:T(2,128)S(1)} fusion(pred[128,1152]{0,1:T(8,128)(4,1)S(1)} %compare_and_fusion, bf16[1152,8,128,1]{0,2,3,1:T(8,128)(2,1)S(1)} %bitcast.94, bf16[128,8,2,128]{3,2,1,0:T(2,128)(2,1)S(1)} %copy-done.1), kind=kOutput, calls=%fused_computation.102 | convolution fusion | flops 613418112 | bytes 3039232 | tf_op jit(solution)/shard_map/sub | solution.py:156
  197.4 6.3 %fusion.8 = bf16[8,128,2,128]{3,1,2,0:T(8,128)(2,1)S(1)} fusion(bf16[1152,8,128,1]{0,2,3,1:T(8,128)(2,1)} %bitcast.96, f32[8,2,128]{2,1,0:T(2,128)S(1)} %fusion.43, pred[128,1152]{0,1:T(8,128)(4,1)} %copy-done.2, bf16[1152,8,128,1]{0,2,3,1:T(8,128)(2,1)S(1)} %bitcast.95, bf16[128,8,2,128]{3,2,1,0:T(2,128)(2,1)S(1)} %copy-done.1), kind=kOutput, calls=%fused_computation.13 | convolution fusion | flops 1220021376 | bytes 5922816 | tf_op jit(solution)/shard_map/hgqk,khd->qhgd/dot_general | solution.py:158
  204.0 2.0 bitcast_dynamic-update-slice_fusion.1
  206.0 2.1 bitcast_dynamic-update-slice_fusion
  208.7 4.5 %fusion.47 = f32[256,1408]{1,0:T(8,128)S(1)} fusion(bf16[256,2048]{0,1:T(8,128)(2,1)S(1)} %dynamic-slice_dynamic-update-slice_fusion, bf16[2048,1408]{1,0:T(8,128)(2,1)} %bitcast.26), kind=kOutput, calls=%fused_computation.104 | convolution fusion | flops 1476395008 | bytes 8257536 | tf_op jit(solution)/shard_map/dot_general | solution.py:174
  213.7 1.8 collective-permute-done.18
  215.5 1.1 fusion.41
  217.0 4.7 %collective-permute-done.19 = bf16[1,4,2688]{2,1,0:T(4,128)(2,1)S(1)} collective-permute-done((bf16[1,4,2688]{2,1,0:T(4,128)(2,1)S(1)}, bf16[1,4,2688]{2,1,0:T(4,128)(2,1)S(1)}, u32[]{:S(2)}, u32[]{:S(2)}) %collective-permute-start.19) | collective-permute-done | bytes 21536 | tf_op jit(solution)/shard_map/ppermute | solution.py:47
  221.8 4.0 %collective-permute-done.20 = bf16[2,4,2688]{2,1,0:T(4,128)(2,1)S(1)} collective-permute-done((bf16[2,4,2688]{2,1,0:T(4,128)(2,1)S(1)}, bf16[2,4,2688]{2,1,0:T(4,128)(2,1)S(1)}, u32[]{:S(2)}, u32[]{:S(2)}) %collective-permute-start.20) | collective-permute-done | bytes 43040 | tf_op jit(solution)/shard_map/ppermute | solution.py:47
  226.0 4.5 %collective-permute-done.21 = bf16[4,4,2688]{2,1,0:T(4,128)(2,1)S(1)} collective-permute-done((bf16[4,4,2688]{2,1,0:T(4,128)(2,1)S(1)}, bf16[4,4,2688]{2,1,0:T(4,128)(2,1)S(1)}, u32[]{:S(2)}, u32[]{:S(2)}) %collective-permute-start.21) | collective-permute-done | bytes 86048 | tf_op jit(solution)/shard_map/ppermute | solution.py:47
  230.7 1.4 collective-permute-done.22
  232.7 4.4 %fusion.46 = (f32[64]{0:T(128)S(1)}, f32[64,1024]{1,0:T(8,128)S(1)}) fusion(bf16[64,2688]{1,0:T(8,128)(2,1)S(1)} %reshape.294, bf16[1024,2688]{1,0:T(8,128)(2,1)} %param.14), kind=kOutput, calls=%fused_computation.103 | convolution fusion | flops 352387008 | bytes 6111488 | tf_op jit(solution)/shard_map/dot_general | solution.py:192
  237.5 4.5 %collective-permute-done.23 = f32[1,3,64]{2,1,0:T(4,128)S(1)} collective-permute-done((f32[1,3,64]{2,1,0:T(4,128)S(1)}, f32[1,3,64]{2,1,0:T(4,128)S(1)}, u32[]{:S(2)}, u32[]{:S(2)}) %collective-permute-start.23) | collective-permute-done | bytes 800 | tf_op jit(solution)/shard_map/ppermute | solution.py:47
  242.0 3.6 %collective-permute-done.24 = f32[2,3,64]{2,1,0:T(4,128)S(1)} collective-permute-done((f32[2,3,64]{2,1,0:T(4,128)S(1)}, f32[2,3,64]{2,1,0:T(4,128)S(1)}, u32[]{:S(2)}, u32[]{:S(2)}) %collective-permute-start.24) | collective-permute-done | bytes 1568 | tf_op jit(solution)/shard_map/ppermute | solution.py:47
  245.6 3.6 %collective-permute-done.25 = f32[4,3,64]{2,1,0:T(4,128)S(1)} collective-permute-done((f32[4,3,64]{2,1,0:T(4,128)S(1)}, f32[4,3,64]{2,1,0:T(4,128)S(1)}, u32[]{:S(2)}, u32[]{:S(2)}) %collective-permute-start.25) | collective-permute-done | bytes 3104 | tf_op jit(solution)/shard_map/ppermute | solution.py:47
  249.3 1.2 collective-permute-done.26
  (88 shorter events, 8.5 us)
Async XLA Ops:
  1.8 2.5 collective-permute-start.10
  5.4 22.8 %collective-permute-start.11 = (bf16[256,1408]{1,0:T(8,128)(2,1)}, bf16[256,1408]{1,0:T(8,128)(2,1)S(1)}, u32[]{:S(2)}, u32[]{:S(2)}) collective-permute-start(bf16[256,1408]{1,0:T(8,128)(2,1)} %maximum_select_fusion.7), channel_id=1, source_target_pairs={{0,2},{1,3},{2,4},{3,5},{4,6},{5,7},{6,8},{7,9},{8,10},{9,11},{10,... | collective-permute-start | bytes 2162696 | tf_op jit(solution)/shard_map/ppermute | solution.py:100
  8.7 20.3 %collective-permute-start = (bf16[128,2176]{0,1:T(8,128)(2,1)}, bf16[128,2176]{0,1:T(8,128)(2,1)S(1)}, u32[]{:S(2)}, u32[]{:S(2)}) collective-permute-start(bf16[128,2176]{0,1:T(8,128)(2,1)} %pad_maximum_fusion.4), channel_id=1, source_target_pairs={{0,4},{1,5},{2,6},{3,7},{4,8},{5,9},{6,10},{7,11},{8,12},{9,13},{1... | collective-permute-start | bytes 1671176 | tf_op jit(solution)/shard_map/ppermute | solution.py:62
  12.3 93.5 %collective-permute-start.5 = (bf16[128,2176]{0,1:T(8,128)(2,1)}, bf16[128,2176]{0,1:T(8,128)(2,1)S(1)}, u32[]{:S(2)}, u32[]{:S(2)}) collective-permute-start(bf16[128,2176]{0,1:T(8,128)(2,1)} %pad_maximum_fusion.4), channel_id=1, source_target_pairs={{0,2},{1,3},{4,6},{5,7},{8,10},{9,11},{12,14},{13,15},{16,18},{17,... | collective-permute-start | bytes 1671176 | tf_op jit(solution)/shard_map/ppermute | solution.py:68
  15.7 173.3 %collective-permute-start.8 = (bf16[128,2176]{0,1:T(8,128)(2,1)}, bf16[128,2176]{0,1:T(8,128)(2,1)}, u32[]{:S(2)}, u32[]{:S(2)}) collective-permute-start(bf16[128,2176]{0,1:T(8,128)(2,1)} %pad_maximum_fusion.4), channel_id=1, source_target_pairs={{0,1},{1,0},{2,3},{3,2},{4,5},{5,4},{6,7},{7,6},{8,9},{9,8},{10,11... | collective-permute-start | bytes 1671176 | tf_op jit(solution)/shard_map/ppermute | solution.py:37
  18.2 22.7 %collective-permute-start.12 = (bf16[256,1408]{1,0:T(8,128)(2,1)}, bf16[256,1408]{1,0:T(8,128)(2,1)S(1)}, u32[]{:S(2)}, u32[]{:S(2)}) collective-permute-start(bf16[256,1408]{1,0:T(8,128)(2,1)} %maximum_select_fusion.7), channel_id=1, source_target_pairs={{0,4},{1,5},{2,6},{3,7},{4,8},{5,9},{6,10},{7,11},{8,12},{9,13},{1... | collective-permute-start | bytes 2162696 | tf_op jit(solution)/shard_map/ppermute | solution.py:100
  28.1 61.7 %collective-permute-start.13 = (bf16[256,1408]{1,0:T(8,128)(2,1)}, bf16[256,1408]{1,0:T(8,128)(2,1)S(1)}, u32[]{:S(2)}, u32[]{:S(2)}) collective-permute-start(bf16[256,1408]{1,0:T(8,128)(2,1)} %maximum_select_fusion.7), channel_id=1, source_target_pairs={{0,6},{1,7},{2,8},{3,9},{4,10},{5,11},{6,12},{7,13},{8,14},{9,15},... | collective-permute-start | bytes 2162696 | tf_op jit(solution)/shard_map/ppermute | solution.py:100
  29.1 63.0 %collective-permute-start.14 = (bf16[256,1408]{1,0:T(8,128)(2,1)}, bf16[256,1408]{1,0:T(8,128)(2,1)S(1)}, u32[]{:S(2)}, u32[]{:S(2)}) collective-permute-start(bf16[256,1408]{1,0:T(8,128)(2,1)} %maximum_select_fusion.7), channel_id=1, source_target_pairs={{0,8},{1,9},{2,10},{3,11},{4,12},{5,13},{6,14},{7,15},{8,0},{9,1},... | collective-permute-start | bytes 2162696 | tf_op jit(solution)/shard_map/ppermute | solution.py:100
  40.9 94.2 %collective-permute-start.1 = (bf16[128,2176]{0,1:T(8,128)(2,1)S(1)}, bf16[128,2176]{0,1:T(8,128)(2,1)S(1)}, u32[]{:S(2)}, u32[]{:S(2)}) collective-permute-start(bf16[128,2176]{0,1:T(8,128)(2,1)S(1)} %collective-permute-done), channel_id=1, source_target_pairs={{0,4},{1,5},{2,6},{3,7},{4,8},{5,9},{6,10},{7,11},{8,12},{9,13},{1... | collective-permute-start | bytes 1671176 | tf_op jit(solution)/shard_map/ppermute | solution.py:62
  89.8 48.2 %collective-permute-start.6 = (bf16[128,2176]{0,1:T(8,128)(2,1)S(1)}, bf16[128,2176]{0,1:T(8,128)(2,1)S(1)}, u32[]{:S(2)}, u32[]{:S(2)}) collective-permute-start(bf16[128,2176]{0,1:T(8,128)(2,1)S(1)} %collective-permute-done), channel_id=1, source_target_pairs={{2,0},{3,1},{6,4},{7,5},{10,8},{11,9},{14,12},{15,13},{18,16},{19,... | collective-permute-start | bytes 1671176 | tf_op jit(solution)/shard_map/ppermute | solution.py:68
  92.0 91.2 %collective-permute-start.15 = (bf16[256,1408]{1,0:T(8,128)(2,1)}, bf16[256,1408]{1,0:T(8,128)(2,1)S(1)}, u32[]{:S(2)}, u32[]{:S(2)}) collective-permute-start(bf16[256,1408]{1,0:T(8,128)(2,1)} %maximum_select_fusion.7), channel_id=1, source_target_pairs={{0,10},{1,11},{2,12},{3,13},{4,14},{5,15},{6,0},{7,1},{8,2},{9,3},... | collective-permute-start | bytes 2162696 | tf_op jit(solution)/shard_map/ppermute | solution.py:100
  105.8 98.2 %collective-permute-start.16 = (bf16[256,1408]{1,0:T(8,128)(2,1)}, bf16[256,1408]{1,0:T(8,128)(2,1)}, u32[]{:S(2)}, u32[]{:S(2)}) collective-permute-start(bf16[256,1408]{1,0:T(8,128)(2,1)} %maximum_select_fusion.7), channel_id=1, source_target_pairs={{0,12},{1,13},{2,14},{3,15},{4,0},{5,1},{6,2},{7,3},{8,4},{9,5},{1... | collective-permute-start | bytes 2162696 | tf_op jit(solution)/shard_map/ppermute | solution.py:100
  135.2 13.9 %collective-permute-start.2 = (bf16[128,2176]{0,1:T(8,128)(2,1)S(1)}, bf16[128,2176]{0,1:T(8,128)(2,1)S(1)}, u32[]{:S(2)}, u32[]{:S(2)}) collective-permute-start(bf16[128,2176]{0,1:T(8,128)(2,1)S(1)} %collective-permute-done), channel_id=1, source_target_pairs={{0,2},{1,3},{4,6},{5,7},{8,10},{9,11},{12,14},{13,15},{16,18},{17,... | collective-permute-start | bytes 1671176 | tf_op jit(solution)/shard_map/ppermute | solution.py:68
  138.0 45.1 %collective-permute-start.3 = (bf16[128,2176]{0,1:T(8,128)(2,1)S(1)}, bf16[128,2176]{0,1:T(8,128)(2,1)S(1)}, u32[]{:S(2)}, u32[]{:S(2)}) collective-permute-start(bf16[128,2176]{0,1:T(8,128)(2,1)S(1)} %collective-permute-done.1), channel_id=1, source_target_pairs={{2,0},{3,1},{6,4},{7,5},{10,8},{11,9},{14,12},{15,13},{18,16},{19,... | collective-permute-start | bytes 1671176 | tf_op jit(solution)/shard_map/ppermute | solution.py:68
  149.0 57.0 %collective-permute-start.17 = (bf16[256,1408]{1,0:T(8,128)(2,1)}, bf16[256,1408]{1,0:T(8,128)(2,1)}, u32[]{:S(2)}, u32[]{:S(2)}) collective-permute-start(bf16[256,1408]{1,0:T(8,128)(2,1)} %maximum_select_fusion.7), channel_id=1, source_target_pairs={{0,14},{1,15},{2,0},{3,1},{4,2},{5,3},{6,4},{7,5},{8,6},{9,7},{10,... | collective-permute-start | bytes 2162696 | tf_op jit(solution)/shard_map/ppermute | solution.py:100
  183.1 2.8 %collective-permute-start.7 = (bf16[2,128,2176]{1,2,0:T(8,128)(2,1)S(1)}, bf16[2,128,2176]{1,2,0:T(8,128)(2,1)S(1)}, u32[]{:S(2)}, u32[]{:S(2)}) collective-permute-start(bf16[2,128,2176]{1,2,0:T(8,128)(2,1)S(1)} %pad_maximum_fusion.3), channel_id=1, source_target_pairs={{0,1},{1,0},{2,3},{3,2},{4,5},{5,4},{6,7},{7,6},{8,9},{9,8},{10,11... | collective-permute-start | bytes 3342344 | tf_op jit(solution)/shard_map/ppermute | solution.py:37
  183.3 4.2 %collective-permute-start.4 = (bf16[2,128,2176]{1,2,0:T(8,128)(2,1)S(1)}, bf16[2,128,2176]{1,2,0:T(8,128)(2,1)S(1)}, u32[]{:S(2)}, u32[]{:S(2)}) collective-permute-start(bf16[2,128,2176]{1,2,0:T(8,128)(2,1)S(1)} %pad_maximum_fusion.2), channel_id=1, source_target_pairs={{0,1},{1,0},{2,3},{3,2},{4,5},{5,4},{6,7},{7,6},{8,9},{9,8},{10,11... | collective-permute-start | bytes 3342344 | tf_op jit(solution)/shard_map/ppermute | solution.py:37
  190.6 1.8 copy-start.4
  190.6 2.9 %copy-start.1 = (bf16[128,8,2,128]{3,2,1,0:T(2,128)(2,1)S(1)}, bf16[128,8,2,128]{3,2,1,0:T(2,128)(2,1)}, u32[]{:S(2)}) copy-start(bf16[128,8,2,128]{3,2,1,0:T(2,128)(2,1)} %reshape.291) | copy-start | bytes 1572868
  193.6 3.9 %copy-start.2 = (pred[128,1152]{0,1:T(8,128)(4,1)}, pred[128,1152]{0,1:T(8,128)(4,1)S(1)}, u32[]{:S(2)}) copy-start(pred[128,1152]{0,1:T(8,128)(4,1)S(1)} %compare_and_fusion) | copy-start | bytes 442372
  203.7 4.3 %collective-permute-start.9 = (bf16[128,2048]{0,1:T(8,128)(2,1)S(1)}, bf16[128,2048]{0,1:T(8,128)(2,1)S(1)}, u32[]{:S(2)}, u32[]{:S(2)}) collective-permute-start(bf16[128,2048]{0,1:T(8,128)(2,1)S(1)} %bitcast.102), channel_id=1, source_target_pairs={{0,1},{1,0},{2,3},{3,2},{4,5},{5,4},{6,7},{7,6},{8,9},{9,8},{10,11... | collective-permute-start | bytes 1572872 | tf_op jit(solution)/shard_map/ppermute | solution.py:37
  213.1 2.4 copy-start
  213.2 3.6 %copy-start.3 = (f32[2688]{0:T(1024)S(1)}, f32[2688]{0:T(1024)}, u32[]{:S(2)}) copy-start(f32[2688]{0:T(1024)} %param.12) | copy-start | bytes 32260
  213.3 2.3 collective-permute-start.18
  215.5 15.2 %copy-start.5 = (s32[64]{0:T(128)S(1)}, s32[64]{0:T(128)}, u32[]{:S(2)}) copy-start(s32[64]{0:T(128)} %param.15) | copy-start | bytes 772
  216.9 4.8 %collective-permute-start.19 = (bf16[1,4,2688]{2,1,0:T(4,128)(2,1)S(1)}, bf16[1,4,2688]{2,1,0:T(4,128)(2,1)S(1)}, u32[]{:S(2)}, u32[]{:S(2)}) collective-permute-start(bf16[1,4,2688]{2,1,0:T(4,128)(2,1)S(1)} %fusion.28), channel_id=1, source_target_pairs={{0,8},{1,9},{2,10},{3,11},{4,12},{5,13},{6,14},{7,15},{8,0},{9,1},... | collective-permute-start | bytes 64520 | tf_op jit(solution)/shard_map/ppermute | solution.py:47
  221.7 4.1 %collective-permute-start.20 = (bf16[2,4,2688]{2,1,0:T(4,128)(2,1)S(1)}, bf16[2,4,2688]{2,1,0:T(4,128)(2,1)S(1)}, u32[]{:S(2)}, u32[]{:S(2)}) collective-permute-start(bf16[2,4,2688]{2,1,0:T(4,128)(2,1)S(1)} %maximum_select_fusion.11), channel_id=1, source_target_pairs={{0,4},{1,5},{2,6},{3,7},{4,0},{5,1},{6,2},{7,3},{8,12},{9,13},{10,... | collective-permute-start | bytes 129032 | tf_op jit(solution)/shard_map/ppermute | solution.py:47
  225.9 4.6 %collective-permute-start.21 = (bf16[4,4,2688]{2,1,0:T(4,128)(2,1)S(1)}, bf16[4,4,2688]{2,1,0:T(4,128)(2,1)S(1)}, u32[]{:S(2)}, u32[]{:S(2)}) collective-permute-start(bf16[4,4,2688]{2,1,0:T(4,128)(2,1)S(1)} %maximum_select_fusion.10), channel_id=1, source_target_pairs={{0,2},{1,3},{2,0},{3,1},{4,6},{5,7},{6,4},{7,5},{8,10},{9,11},{10,... | collective-permute-start | bytes 258056 | tf_op jit(solution)/shard_map/ppermute | solution.py:47
  230.6 1.5 collective-permute-start.22
  237.4 4.5 %collective-permute-start.23 = (f32[1,3,64]{2,1,0:T(4,128)S(1)}, f32[1,3,64]{2,1,0:T(4,128)S(1)}, u32[]{:S(2)}, u32[]{:S(2)}) collective-permute-start(f32[1,3,64]{2,1,0:T(4,128)S(1)} %maximum_bitcast_fusion), channel_id=1, source_target_pairs={{0,8},{1,9},{2,10},{3,11},{4,12},{5,13},{6,14},{7,15},{8,0},{9,1},... | collective-permute-start | bytes 2312 | tf_op jit(solution)/shard_map/ppermute | solution.py:47
  242.0 3.6 %collective-permute-start.24 = (f32[2,3,64]{2,1,0:T(4,128)S(1)}, f32[2,3,64]{2,1,0:T(4,128)S(1)}, u32[]{:S(2)}, u32[]{:S(2)}) collective-permute-start(f32[2,3,64]{2,1,0:T(4,128)S(1)} %maximum_select_fusion.15), channel_id=1, source_target_pairs={{0,4},{1,5},{2,6},{3,7},{4,0},{5,1},{6,2},{7,3},{8,12},{9,13},{10,... | collective-permute-start | bytes 4616 | tf_op jit(solution)/shard_map/ppermute | solution.py:47
  245.6 3.7 %collective-permute-start.25 = (f32[4,3,64]{2,1,0:T(4,128)S(1)}, f32[4,3,64]{2,1,0:T(4,128)S(1)}, u32[]{:S(2)}, u32[]{:S(2)}) collective-permute-start(f32[4,3,64]{2,1,0:T(4,128)S(1)} %maximum_select_fusion.14), channel_id=1, source_target_pairs={{0,2},{1,3},{2,0},{3,1},{4,6},{5,7},{6,4},{7,5},{8,10},{9,11},{10,... | collective-permute-start | bytes 9224 | tf_op jit(solution)/shard_map/ppermute | solution.py:47
  249.2 1.2 collective-permute-start.26

commit v5 on v3

--- a/solution.py
+++ b/solution.py
@@ -110,12 +110,7 @@
     first_core = core == 0
     first_row = my_index * token_rows
 
-    half = -(-width // (CORES * LANES)) * LANES
-    padded_proj = jnp.pad(out_proj, ((0, 0), (0, CORES * half - width)))
-    my_half = lax.dynamic_slice_in_dim(padded_proj, core * half, half, 1)
-    other_half = lax.dynamic_slice_in_dim(padded_proj, (1 - core) * half, half, 1)
-    chip_proj = in_core_order(my_half, swap_cores(other_half), first_core)
-    proj_half = lax.all_gather(chip_proj, "chip", axis=0, tiled=True)
+    full_proj = lax.all_gather(out_proj, SEQ, axis=0, tiled=True)
 
     seg_cols = jnp.broadcast_to(segment_ids.astype(jnp.bfloat16)[:, None], (token_rows, SEG_LANES))
     own = jnp.concatenate([joined_keys_values, seg_cols], 1)
@@ -151,21 +146,17 @@
     )
     context = context.reshape(token_rows, QUERY_HEADS * HEAD_SIZE).astype(jnp.bfloat16)
 
-    chip_context = in_core_order(context, swap_cores(context), first_core)
-    chip_projected = jnp.dot(chip_context, proj_half, preferred_element_type=jnp.float32)
-    mine = lax.dynamic_slice_in_dim(chip_projected, core * token_rows, token_rows, 0)
-    theirs = lax.dynamic_slice_in_dim(chip_projected, (1 - core) * token_rows, token_rows, 0)
-    returned = swap_cores(theirs)
-    projected = jnp.where(
-        first_core, jnp.concatenate([mine, returned], 1), jnp.concatenate([returned, mine], 1)
-    )[:, :width]
-
+    score_count = SCORE_DEV
+    stride = token_rows // score_count
+    scored_context = context.reshape(score_count, stride, -1)[:, stride - 1, :]
+    scored_residual = residual.reshape(score_count, stride, width)[:, stride - 1, :]
+    picked = scored_residual.astype(jnp.float32) + jnp.dot(
+        scored_context, full_proj, preferred_element_type=jnp.float32
+    )
+    normed = normalize(picked, norm_gain)
+    projected = jnp.dot(context, full_proj, preferred_element_type=jnp.float32)
     hidden = residual.astype(jnp.float32) + projected
     layer_out = hidden.astype(jnp.bfloat16)
-    score_count = SCORE_DEV
-    stride = token_rows // score_count
-    picked = hidden.reshape(score_count, stride, width)[:, stride - 1, :]
-    normed = normalize(picked, norm_gain)
     logits = lax.dot_general(
         gather_rows(normed),
         head_weight,

time: 182 us -> 181 us (level)
  matrix products: 20.1 us -> 27.5 us
  waiting for transfers between devices: 96.6 us -> 89.3 us
  local copies, waits for them, and re-layouts: 9.07 us -> 11.5 us
    dot_general x1 -> x2, matrix products: 4.82 us -> 12.4 us  [the longest x1 6.67 us: local(): projected = jnp.dot(context, full_proj, preferred_element_type=jnp.float32)]
    ppermute x6 -> x3, waiting for transfers between devices: 5.6 us -> 0.01 us  [swap_cores(): return lax.ppermute(value, 'core', [(0, 1), (1, 0)])]
    ppermute x4, waiting for transfers between devices: 22.6 us -> 20.1 us  [across_pair(): return lax.ppermute(value, SEQ, pairs)]
  transfers between devices with their start and end apart: 21 -> 18, of which waited for: 15 -> 11; matrix products, arithmetic and copies ran while one was open for 13% -> 19% of each run, Pallas kernels for 0% -> 0%
where the time goes in v5:
time: 181 us
  waiting for transfers between devices  89.3 us (49%)
  starting transfers between devices  28.9 us (16%)
  matrix products  27.5 us (15%)
  between operations  14.4 us (8%)
  local copies, waits for them, and re-layouts  11.5 us (6%)
  other arithmetic  9.06 us (5%)
    ppermute x2, waiting for transfers between devices, shift_chips(): lax.ppermute(value, SEQ, [(s, s + step) for s in range(count - step)])  28.7 us
    ppermute x8, waiting for transfers between devices, gather_rows(): received = lax.ppermute(data, SEQ, [(i, i ^ step) for i in range(count)])  21.9 us
    ppermute x4, waiting for transfers between devices, across_pair(): return lax.ppermute(value, SEQ, pairs)  20.1 us
    all_gather x1, waiting for transfers between devices, local(): full_proj = lax.all_gather(out_proj, SEQ, axis=0, tiled=True)  17.9 us
    ppermute x2, starting transfers between devices, shift_chips(): lax.ppermute(value, SEQ, [(s, s + step) for s in range(count - step)])  12.7 us
    ppermute x4, starting transfers between devices, across_pair(): return lax.ppermute(value, SEQ, pairs)  10.7 us
    dot_general x1, matrix products, local(): projected = jnp.dot(context, full_proj, preferred_element_type=jnp.float32)  6.67 us
    dot_general x1, matrix products, local(): jnp.einsum('hgqk,khd->qhgd', weights, heads_for_values, preferred_element...  6.31 us
  transfers between devices with their start and end apart: 18, of which 11 were waited for; matrix products, arithmetic and copies ran while one was open for 19% of the time, Pallas kernels for 0%

profile of v5, /device:TPU:0, one launch (start us, length us, event | category | flops | bytes accessed | tf_op | source)
XLA Modules:
  0.0 180.7 jit_solution(3568010816587637594)
XLA Ops:
  7.2 0.7 all-gather.2.cloned.1.call-update
  7.9 1.3 copy.15
  9.2 0.7 convert_element_type.46
  9.9 5.0 %collective-permute-start = (bf16[128,2176]{0,1:T(8,128)(2,1)S(1)}, bf16[128,2176]{0,1:T(8,128)(2,1)S(1)}, u32[]{:S(2)}, u32[]{:S(2)}) collective-permute-start(bf16[128,2176]{0,1:T(8,128)(2,1)S(1)} %pad_maximum_fusion.2), channel_id=1, source_target_pairs={{0,4},{1,5},{2,6},{3,7},{4,8},{5,9},{6,10},{7,11},{8,12},{9,13},{1... | collective-permute-start | bytes 1671176 | tf_op jit(solution)/shard_map/ppermute | solution.py:62
  14.9 17.5 %collective-permute-done = bf16[128,2176]{0,1:T(8,128)(2,1)S(1)} collective-permute-done((bf16[128,2176]{0,1:T(8,128)(2,1)S(1)}, bf16[128,2176]{0,1:T(8,128)(2,1)S(1)}, u32[]{:S(2)}, u32[]{:S(2)}) %collective-permute-start) | collective-permute-done | bytes 557088 | tf_op jit(solution)/shard_map/ppermute | solution.py:62
  32.5 7.7 %collective-permute-start.1 = (bf16[128,2176]{0,1:T(8,128)(2,1)S(1)}, bf16[128,2176]{0,1:T(8,128)(2,1)S(1)}, u32[]{:S(2)}, u32[]{:S(2)}) collective-permute-start(bf16[128,2176]{0,1:T(8,128)(2,1)S(1)} %collective-permute-done), channel_id=1, source_target_pairs={{0,4},{1,5},{2,6},{3,7},{4,8},{5,9},{6,10},{7,11},{8,12},{9,13},{1... | collective-permute-start | bytes 1671176 | tf_op jit(solution)/shard_map/ppermute | solution.py:62
  40.2 3.5 %collective-permute-start.5 = (bf16[128,2176]{0,1:T(8,128)(2,1)S(1)}, bf16[128,2176]{0,1:T(8,128)(2,1)S(1)}, u32[]{:S(2)}, u32[]{:S(2)}) collective-permute-start(bf16[128,2176]{0,1:T(8,128)(2,1)S(1)} %pad_maximum_fusion.2), channel_id=1, source_target_pairs={{0,2},{1,3},{4,6},{5,7},{8,10},{9,11},{12,14},{13,15},{16,18},{17,... | collective-permute-start | bytes 1671176 | tf_op jit(solution)/shard_map/ppermute | solution.py:68
  43.7 1.3 collective-permute-start.6
  45.0 4.6 %collective-permute-start.2 = (bf16[128,2176]{0,1:T(8,128)(2,1)S(1)}, bf16[128,2176]{0,1:T(8,128)(2,1)S(1)}, u32[]{:S(2)}, u32[]{:S(2)}) collective-permute-start(bf16[128,2176]{0,1:T(8,128)(2,1)S(1)} %collective-permute-done), channel_id=1, source_target_pairs={{0,2},{1,3},{4,6},{5,7},{8,10},{9,11},{12,14},{13,15},{16,18},{17,... | collective-permute-start | bytes 1671176 | tf_op jit(solution)/shard_map/ppermute | solution.py:68
  49.6 11.2 %collective-permute-done.1 = bf16[128,2176]{0,1:T(8,128)(2,1)S(1)} collective-permute-done((bf16[128,2176]{0,1:T(8,128)(2,1)S(1)}, bf16[128,2176]{0,1:T(8,128)(2,1)S(1)}, u32[]{:S(2)}, u32[]{:S(2)}) %collective-permute-start.1) | collective-permute-done | bytes 557088 | tf_op jit(solution)/shard_map/ppermute | solution.py:62
  60.8 1.3 collective-permute-start.3
  62.2 1.1 pad_maximum_fusion.1
  63.3 20.0 %collective-permute-done.3 = bf16[128,2176]{0,1:T(8,128)(2,1)S(1)} collective-permute-done((bf16[128,2176]{0,1:T(8,128)(2,1)S(1)}, bf16[128,2176]{0,1:T(8,128)(2,1)S(1)}, u32[]{:S(2)}, u32[]{:S(2)}) %collective-permute-start.3) | collective-permute-done | bytes 557088 | tf_op jit(solution)/shard_map/ppermute | solution.py:68
  83.4 1.1 pad_maximum_fusion
  84.5 0.5 collective-permute-start.8
  85.0 2.2 %reshape.181 = bf16[128,8,2,128]{3,2,1,0:T(2,128)(2,1)} reshape(bf16[128,2048]{1,0:T(8,128)(2,1)} %param.8) | data formatting | bytes 1048576 | tf_op jit(solution)/shard_map/reshape | solution.py:127
  87.2 1.6 slice.55
  88.8 1.3 slice_bitcast_fusion
  90.1 1.3 slice_bitcast_fusion.2
  91.4 0.3 fusion.10
  91.8 0.4 fusion.11
  92.2 0.4 fusion.12
  92.6 0.4 fusion.13
  93.0 1.5 fusion.14
  94.6 1.9 %constant_dynamic-slice_fusion = (bf16[1152,1024]{0,1:T(8,128)(2,1)S(1)}, bf16[1152,1024]{0,1:T(8,128)(2,1)}) fusion(bf16[1280,2176]{0,1:T(8,128)(2,1)S(1)} %fusion.14, s32[]{:T(128)S(6)} %select_n.139, s32[]{:T(128)S(6)} %add.82), kind=kLoop, calls=%fused_computation.74 | loop fusion | bytes 9437192 | tf_op jit(solution)/shard_map/slice | solution.py:128
  96.4 1.1 compare_and_fusion
  97.5 4.3 %fusion.40 = f32[8,2,128]{2,1,0:T(2,128)} fusion(pred[128,1152]{0,1:T(8,128)(4,1)S(1)} %compare_and_fusion, bf16[1152,8,128,1]{0,2,3,1:T(8,128)(2,1)S(1)} %bitcast.86, bf16[128,8,2,128]{3,2,1,0:T(2,128)(2,1)S(1)} %copy-done.3), kind=kOutput, calls=%fused_computation.80 | convolution fusion | flops 613418112 | bytes 3039232 | tf_op jit(solution)/shard_map/sub | solution.py:142
  101.8 6.3 %fusion.7 = bf16[8,128,2,128]{3,1,2,0:T(8,128)(2,1)S(1)} fusion(bf16[1152,8,128,1]{0,2,3,1:T(8,128)(2,1)} %bitcast.88, f32[8,2,128]{2,1,0:T(2,128)} %fusion.40, pred[128,1152]{0,1:T(8,128)(4,1)S(1)} %compare_and_fusion, bf16[1152,8,128,1]{0,2,3,1:T(8,128)(2,1)S(1)} %bitcast.87, bf16[128,8,2,128]{3,2,1,0:T(2,128)(2,1)S(1)} %copy-done.3), kind=kOutput, calls=%fused_computation.12 | convolution fusion | flops 1220021376 | bytes 5922816 | tf_op jit(solution)/shard_map/hgqk,khd->qhgd/dot_general | solution.py:144
  108.1 0.7 copy.20
  108.8 0.4 convert_element_type.56
  109.3 17.9 %all-gather.2.cloned.1.call-done = bf16[2048,2688]{1,0:T(8,128)(2,1)} async-done(((bf16[128,2688]{1,0:T(8,128)(2,1)}), bf16[2048,2688]{1,0:T(8,128)(2,1)}) %all-gather.2.cloned.1.call-update) | async-done | bytes 11010064 | tf_op jit(solution)/shard_map/all_gather | solution.py:113
  127.2 5.8 %multiply_reduce_fusion = (f32[4]{0:T(128)S(1)}, f32[4,2688]{1,0:T(4,128)S(1)}) fusion(bf16[2048,2688]{1,0:T(8,128)(2,1)} %all-gather.2.cloned.1.call-done, bf16[4,1,2048]{2,1,0:T(2,128)(2,1)S(1)} %slice.56, bf16[4,1,2688]{2,1,0:T(2,128)(2,1)} %slice.55), kind=kOutput, calls=%fused_computation.47 | convolution fusion | flops 44083196 | bytes 11090960 | tf_op jit(solution)/shard_map/dot_general | solution.py:153
  133.0 2.0 %collective-permute-start.9 = (bf16[1,4,2688]{2,1,0:T(4,128)(2,1)S(1)}, bf16[1,4,2688]{2,1,0:T(4,128)(2,1)S(1)}, u32[]{:S(2)}, u32[]{:S(2)}) collective-permute-start(bf16[1,4,2688]{2,1,0:T(4,128)(2,1)S(1)} %fusion.25), channel_id=1, source_target_pairs={{0,8},{1,9},{2,10},{3,11},{4,12},{5,13},{6,14},{7,15},{8,0},{9,1},... | collective-permute-start | bytes 64520 | tf_op jit(solution)/shard_map/ppermute | solution.py:47
  135.1 2.9 %collective-permute-done.9 = bf16[1,4,2688]{2,1,0:T(4,128)(2,1)S(1)} collective-permute-done((bf16[1,4,2688]{2,1,0:T(4,128)(2,1)S(1)}, bf16[1,4,2688]{2,1,0:T(4,128)(2,1)S(1)}, u32[]{:S(2)}, u32[]{:S(2)}) %collective-permute-start.9) | collective-permute-done | bytes 21536 | tf_op jit(solution)/shard_map/ppermute | solution.py:47
  138.1 0.5 collective-permute-start.10
  138.5 3.6 %collective-permute-done.10 = bf16[2,4,2688]{2,1,0:T(4,128)(2,1)S(1)} collective-permute-done((bf16[2,4,2688]{2,1,0:T(4,128)(2,1)S(1)}, bf16[2,4,2688]{2,1,0:T(4,128)(2,1)S(1)}, u32[]{:S(2)}, u32[]{:S(2)}) %collective-permute-start.10) | collective-permute-done | bytes 43040 | tf_op jit(solution)/shard_map/ppermute | solution.py:47
  142.3 4.5 %collective-permute-done.11 = bf16[4,4,2688]{2,1,0:T(4,128)(2,1)S(1)} collective-permute-done((bf16[4,4,2688]{2,1,0:T(4,128)(2,1)S(1)}, bf16[4,4,2688]{2,1,0:T(4,128)(2,1)S(1)}, u32[]{:S(2)}, u32[]{:S(2)}) %collective-permute-start.11) | collective-permute-done | bytes 86048 | tf_op jit(solution)/shard_map/ppermute | solution.py:47
  147.1 1.4 collective-permute-done.12
  148.5 0.4 maximum_select_fusion.5
  149.1 4.5 %fusion.43 = (f32[64]{0:T(128)S(1)}, f32[64,1024]{1,0:T(8,128)S(1)}) fusion(bf16[64,2688]{1,0:T(8,128)(2,1)S(1)} %reshape.183, bf16[1024,2688]{1,0:T(8,128)(2,1)} %param.14), kind=kOutput, calls=%fused_computation.81 | convolution fusion | flops 352387008 | bytes 6111488 | tf_op jit(solution)/shard_map/dot_general | solution.py:160
  153.8 1.8 %collective-permute-start.13 = (f32[1,3,64]{2,1,0:T(4,128)S(1)}, f32[1,3,64]{2,1,0:T(4,128)S(1)}, u32[]{:S(2)}, u32[]{:S(2)}) collective-permute-start(f32[1,3,64]{2,1,0:T(4,128)S(1)} %maximum_bitcast_fusion), channel_id=1, source_target_pairs={{0,8},{1,9},{2,10},{3,11},{4,12},{5,13},{6,14},{7,15},{8,0},{9,1},... | collective-permute-start | bytes 2312 | tf_op jit(solution)/shard_map/ppermute | solution.py:47
  155.6 2.7 %collective-permute-done.13 = f32[1,3,64]{2,1,0:T(4,128)S(1)} collective-permute-done((f32[1,3,64]{2,1,0:T(4,128)S(1)}, f32[1,3,64]{2,1,0:T(4,128)S(1)}, u32[]{:S(2)}, u32[]{:S(2)}) %collective-permute-start.13) | collective-permute-done | bytes 800 | tf_op jit(solution)/shard_map/ppermute | solution.py:47
  158.4 0.4 collective-permute-start.14
  158.8 3.2 %collective-permute-done.14 = f32[2,3,64]{2,1,0:T(4,128)S(1)} collective-permute-done((f32[2,3,64]{2,1,0:T(4,128)S(1)}, f32[2,3,64]{2,1,0:T(4,128)S(1)}, u32[]{:S(2)}, u32[]{:S(2)}) %collective-permute-start.14) | collective-permute-done | bytes 1568 | tf_op jit(solution)/shard_map/ppermute | solution.py:47
  162.0 3.6 %collective-permute-done.15 = f32[4,3,64]{2,1,0:T(4,128)S(1)} collective-permute-done((f32[4,3,64]{2,1,0:T(4,128)S(1)}, f32[4,3,64]{2,1,0:T(4,128)S(1)}, u32[]{:S(2)}, u32[]{:S(2)}) %collective-permute-start.15) | collective-permute-done | bytes 3104 | tf_op jit(solution)/shard_map/ppermute | solution.py:47
  165.7 6.7 %fusion.6 = bf16[128,2688]{1,0:T(8,128)(2,1)} fusion(bf16[128,2048]{0,1:T(8,128)(2,1)S(1)} %bitcast.85, bf16[2048,2688]{1,0:T(8,128)(2,1)} %all-gather.2.cloned.1.call-done, bf16[128,2688]{1,0:T(8,128)(2,1)S(1)} %copy-done), kind=kOutput, calls=%fused_computation.10 | convolution fusion | flops 1410318336 | bytes 12910592 | tf_op jit(solution)/shard_map/dot_general | solution.py:157
  172.5 0.8 broadcast_subtract_fusion
  173.3 0.6 dynamic_slice.7
  (55 shorter events, 1.5 us)
Async XLA Ops:
  7.2 120.0 %all-gather.2.cloned.1.call-start = ((), (), s32[]{:S(2)}) async-start(), calls=%async_computation | async-start | bytes 11698176 | tf_op jit(solution)/shard_map/all_gather | solution.py:113
  9.9 52.2 %copy-start.1 = (bf16[128,2176]{0,1:T(8,128)(2,1)}, bf16[128,2176]{0,1:T(8,128)(2,1)S(1)}, u32[]{:S(2)}) copy-start(bf16[128,2176]{0,1:T(8,128)(2,1)S(1)} %pad_maximum_fusion.2) | copy-start | bytes 1671172
  9.9 22.5 %collective-permute-start = (bf16[128,2176]{0,1:T(8,128)(2,1)S(1)}, bf16[128,2176]{0,1:T(8,128)(2,1)S(1)}, u32[]{:S(2)}, u32[]{:S(2)}) collective-permute-start(bf16[128,2176]{0,1:T(8,128)(2,1)S(1)} %pad_maximum_fusion.2), channel_id=1, source_target_pairs={{0,4},{1,5},{2,6},{3,7},{4,8},{5,9},{6,10},{7,11},{8,12},{9,13},{1... | collective-permute-start | bytes 1671176 | tf_op jit(solution)/shard_map/ppermute | solution.py:62
  32.5 28.4 %collective-permute-start.1 = (bf16[128,2176]{0,1:T(8,128)(2,1)S(1)}, bf16[128,2176]{0,1:T(8,128)(2,1)S(1)}, u32[]{:S(2)}, u32[]{:S(2)}) collective-permute-start(bf16[128,2176]{0,1:T(8,128)(2,1)S(1)} %collective-permute-done), channel_id=1, source_target_pairs={{0,4},{1,5},{2,6},{3,7},{4,8},{5,9},{6,10},{7,11},{8,12},{9,13},{1... | collective-permute-start | bytes 1671176 | tf_op jit(solution)/shard_map/ppermute | solution.py:62
  40.2 21.9 %collective-permute-start.5 = (bf16[128,2176]{0,1:T(8,128)(2,1)S(1)}, bf16[128,2176]{0,1:T(8,128)(2,1)S(1)}, u32[]{:S(2)}, u32[]{:S(2)}) collective-permute-start(bf16[128,2176]{0,1:T(8,128)(2,1)S(1)} %pad_maximum_fusion.2), channel_id=1, source_target_pairs={{0,2},{1,3},{4,6},{5,7},{8,10},{9,11},{12,14},{13,15},{16,18},{17,... | collective-permute-start | bytes 1671176 | tf_op jit(solution)/shard_map/ppermute | solution.py:68
  43.7 18.4 %collective-permute-start.6 = (bf16[128,2176]{0,1:T(8,128)(2,1)S(1)}, bf16[128,2176]{0,1:T(8,128)(2,1)S(1)}, u32[]{:S(2)}, u32[]{:S(2)}) collective-permute-start(bf16[128,2176]{0,1:T(8,128)(2,1)S(1)} %collective-permute-done), channel_id=1, source_target_pairs={{2,0},{3,1},{6,4},{7,5},{10,8},{11,9},{14,12},{15,13},{18,16},{19,... | collective-permute-start | bytes 1671176 | tf_op jit(solution)/shard_map/ppermute | solution.py:68
  45.0 18.3 %collective-permute-start.2 = (bf16[128,2176]{0,1:T(8,128)(2,1)S(1)}, bf16[128,2176]{0,1:T(8,128)(2,1)S(1)}, u32[]{:S(2)}, u32[]{:S(2)}) collective-permute-start(bf16[128,2176]{0,1:T(8,128)(2,1)S(1)} %collective-permute-done), channel_id=1, source_target_pairs={{0,2},{1,3},{4,6},{5,7},{8,10},{9,11},{12,14},{13,15},{16,18},{17,... | collective-permute-start | bytes 1671176 | tf_op jit(solution)/shard_map/ppermute | solution.py:68
  60.8 22.5 %collective-permute-start.3 = (bf16[128,2176]{0,1:T(8,128)(2,1)S(1)}, bf16[128,2176]{0,1:T(8,128)(2,1)S(1)}, u32[]{:S(2)}, u32[]{:S(2)}) collective-permute-start(bf16[128,2176]{0,1:T(8,128)(2,1)S(1)} %collective-permute-done.1), channel_id=1, source_target_pairs={{2,0},{3,1},{6,4},{7,5},{10,8},{11,9},{14,12},{15,13},{18,16},{19,... | collective-permute-start | bytes 1671176 | tf_op jit(solution)/shard_map/ppermute | solution.py:68
  63.3 21.2 %copy-start.2 = (bf16[128,2176]{0,1:T(8,128)(2,1)S(1)}, bf16[128,2176]{0,1:T(8,128)(2,1)}, u32[]{:S(2)}) copy-start(bf16[128,2176]{0,1:T(8,128)(2,1)} %copy-done.1) | copy-start | bytes 1671172
  63.3 25.5 %collective-permute-start.7 = (bf16[2,128,2176]{1,2,0:T(8,128)(2,1)}, bf16[2,128,2176]{1,2,0:T(8,128)(2,1)}, u32[]{:S(2)}, u32[]{:S(2)}) collective-permute-start(bf16[2,128,2176]{1,2,0:T(8,128)(2,1)} %pad_maximum_fusion.1), channel_id=1, source_target_pairs={{0,1},{1,0},{2,3},{3,2},{4,5},{5,4},{6,7},{7,6},{8,9},{9,8},{10,11... | collective-permute-start | bytes 3342344 | tf_op jit(solution)/shard_map/ppermute | solution.py:37
  84.5 5.6 %collective-permute-start.4 = (bf16[2,128,2176]{1,2,0:T(8,128)(2,1)}, bf16[2,128,2176]{1,2,0:T(8,128)(2,1)}, u32[]{:S(2)}, u32[]{:S(2)}) collective-permute-start(bf16[2,128,2176]{1,2,0:T(8,128)(2,1)} %pad_maximum_fusion), channel_id=1, source_target_pairs={{0,1},{1,0},{2,3},{3,2},{4,5},{5,4},{6,7},{7,6},{8,9},{9,8},{10,11... | collective-permute-start | bytes 3342344 | tf_op jit(solution)/shard_map/ppermute | solution.py:37
  84.5 8.5 %collective-permute-start.8 = (bf16[128,2176]{0,1:T(8,128)(2,1)S(1)}, bf16[128,2176]{0,1:T(8,128)(2,1)}, u32[]{:S(2)}, u32[]{:S(2)}) collective-permute-start(bf16[128,2176]{0,1:T(8,128)(2,1)S(1)} %copy-done.2), channel_id=1, source_target_pairs={{0,1},{1,0},{2,3},{3,2},{4,5},{5,4},{6,7},{7,6},{8,9},{9,8},{10,11... | collective-permute-start | bytes 1671176 | tf_op jit(solution)/shard_map/ppermute | solution.py:37
  94.5 1.9 %copy-start.5 = (s32[128]{0:T(128)S(1)}, s32[128]{0:T(128)}, u32[]{:S(2)}) copy-start(s32[128]{0:T(128)} %param.10) | copy-start | bytes 1540
  94.6 3.0 %copy-start.3 = (bf16[128,8,2,128]{3,2,1,0:T(2,128)(2,1)S(1)}, bf16[128,8,2,128]{3,2,1,0:T(2,128)(2,1)}, u32[]{:S(2)}) copy-start(bf16[128,8,2,128]{3,2,1,0:T(2,128)(2,1)} %reshape.181) | copy-start | bytes 1572868
  109.2 23.7 %copy-start.4 = (f32[2688]{0:T(1024)S(1)}, f32[2688]{0:T(1024)}, u32[]{:S(2)}) copy-start(f32[2688]{0:T(1024)} %param.12) | copy-start | bytes 32260
  109.2 37.8 %copy-start.6 = (s32[64]{0:T(128)S(1)}, s32[64]{0:T(128)}, u32[]{:S(2)}) copy-start(s32[64]{0:T(128)} %param.15) | copy-start | bytes 772
  133.0 5.0 %collective-permute-start.9 = (bf16[1,4,2688]{2,1,0:T(4,128)(2,1)S(1)}, bf16[1,4,2688]{2,1,0:T(4,128)(2,1)S(1)}, u32[]{:S(2)}, u32[]{:S(2)}) collective-permute-start(bf16[1,4,2688]{2,1,0:T(4,128)(2,1)S(1)} %fusion.25), channel_id=1, source_target_pairs={{0,8},{1,9},{2,10},{3,11},{4,12},{5,13},{6,14},{7,15},{8,0},{9,1},... | collective-permute-start | bytes 64520 | tf_op jit(solution)/shard_map/ppermute | solution.py:47
  138.1 4.1 %collective-permute-start.10 = (bf16[2,4,2688]{2,1,0:T(4,128)(2,1)S(1)}, bf16[2,4,2688]{2,1,0:T(4,128)(2,1)S(1)}, u32[]{:S(2)}, u32[]{:S(2)}) collective-permute-start(bf16[2,4,2688]{2,1,0:T(4,128)(2,1)S(1)} %maximum_select_fusion.8), channel_id=1, source_target_pairs={{0,4},{1,5},{2,6},{3,7},{4,0},{5,1},{6,2},{7,3},{8,12},{9,13},{10,... | collective-permute-start | bytes 129032 | tf_op jit(solution)/shard_map/ppermute | solution.py:47
  142.2 4.6 %collective-permute-start.11 = (bf16[4,4,2688]{2,1,0:T(4,128)(2,1)S(1)}, bf16[4,4,2688]{2,1,0:T(4,128)(2,1)S(1)}, u32[]{:S(2)}, u32[]{:S(2)}) collective-permute-start(bf16[4,4,2688]{2,1,0:T(4,128)(2,1)S(1)} %maximum_select_fusion.7), channel_id=1, source_target_pairs={{0,2},{1,3},{2,0},{3,1},{4,6},{5,7},{6,4},{7,5},{8,10},{9,11},{10,... | collective-permute-start | bytes 258056 | tf_op jit(solution)/shard_map/ppermute | solution.py:47
  147.0 1.5 collective-permute-start.12
  149.1 16.7 %copy-start = (bf16[128,2688]{1,0:T(8,128)(2,1)S(1)}, bf16[128,2688]{1,0:T(8,128)(2,1)}, u32[]{:S(2)}) copy-start(bf16[128,2688]{1,0:T(8,128)(2,1)} %param.11) | copy-start | bytes 2064388
  153.8 4.5 %collective-permute-start.13 = (f32[1,3,64]{2,1,0:T(4,128)S(1)}, f32[1,3,64]{2,1,0:T(4,128)S(1)}, u32[]{:S(2)}, u32[]{:S(2)}) collective-permute-start(f32[1,3,64]{2,1,0:T(4,128)S(1)} %maximum_bitcast_fusion), channel_id=1, source_target_pairs={{0,8},{1,9},{2,10},{3,11},{4,12},{5,13},{6,14},{7,15},{8,0},{9,1},... | collective-permute-start | bytes 2312 | tf_op jit(solution)/shard_map/ppermute | solution.py:47
  158.4 3.6 %collective-permute-start.14 = (f32[2,3,64]{2,1,0:T(4,128)S(1)}, f32[2,3,64]{2,1,0:T(4,128)S(1)}, u32[]{:S(2)}, u32[]{:S(2)}) collective-permute-start(f32[2,3,64]{2,1,0:T(4,128)S(1)} %maximum_select_fusion.12), channel_id=1, source_target_pairs={{0,4},{1,5},{2,6},{3,7},{4,0},{5,1},{6,2},{7,3},{8,12},{9,13},{10,... | collective-permute-start | bytes 4616 | tf_op jit(solution)/shard_map/ppermute | solution.py:47
  162.0 3.7 %collective-permute-start.15 = (f32[4,3,64]{2,1,0:T(4,128)S(1)}, f32[4,3,64]{2,1,0:T(4,128)S(1)}, u32[]{:S(2)}, u32[]{:S(2)}) collective-permute-start(f32[4,3,64]{2,1,0:T(4,128)S(1)} %maximum_select_fusion.11), channel_id=1, source_target_pairs={{0,2},{1,3},{2,0},{3,1},{4,6},{5,7},{6,4},{7,5},{8,10},{9,11},{10,... | collective-permute-start | bytes 9224 | tf_op jit(solution)/shard_map/ppermute | solution.py:47
  165.7 6.8 %collective-permute-start.16 = (f32[8,3,64]{2,1,0:T(4,128)S(1)}, f32[8,3,64]{2,1,0:T(4,128)S(1)}, u32[]{:S(2)}, u32[]{:S(2)}) collective-permute-start(f32[8,3,64]{2,1,0:T(4,128)S(1)} %maximum_select_fusion.10), channel_id=1, source_target_pairs={{0,1},{1,0},{2,3},{3,2},{4,5},{5,4},{6,7},{7,6},{8,9},{9,8},{10,11... | collective-permute-start | bytes 18440 | tf_op jit(solution)/shard_map/ppermute | solution.py:47
Sparse Core Ops, SparseCore 0:
  10.3 116.8 all-gather.1

commit v6 on v5

--- a/solution.py
+++ b/solution.py
@@ -37,18 +37,26 @@
     return lax.ppermute(value, "core", [(0, 1), (1, 0)])
 
 
-def gather_rows(value):
-    count = seq_count()
-    bits = count.bit_length() - 1
+def gather_rows(value, radix=4):
+    count = seq_count()
     me = seq_index()
     data = value[None]
-    for bit in reversed(range(bits)):
-        step = 1 << bit
-        received = lax.ppermute(data, SEQ, [(i, i ^ step) for i in range(count)])
-        low = ((me >> bit) & 1) == 0
-        data = jnp.where(low, jnp.concatenate([data, received], 0), jnp.concatenate([received, data], 0))
-    data = data.reshape((2,) * bits + value.shape)
-    data = jnp.transpose(data, tuple(reversed(range(bits))) + tuple(range(bits, bits + value.ndim)))
+    stride = 1
+    while stride < count:
+        digits = min(radix, count // stride)
+        mine = (me // stride) % digits
+        received = [data]
+        for offset in range(1, digits):
+            pairs = []
+            for i in range(count):
+                d = (i // stride) % digits
+                pairs.append((i, i + (((d + offset) % digits) - d) * stride))
+            received.append(lax.ppermute(data, SEQ, pairs))
+        stacked = jnp.stack(received, 0)
+        order = (mine - jnp.arange(digits)) % digits
+        data = jnp.take(stacked, order, axis=0)
+        data = data.reshape((digits * data.shape[1],) + data.shape[2:])
+        stride *= digits
     return data.reshape((count * value.shape[0],) + value.shape[1:])
 
 
@@ -148,15 +156,11 @@
 
     score_count = SCORE_DEV
     stride = token_rows // score_count
-    scored_context = context.reshape(score_count, stride, -1)[:, stride - 1, :]
-    scored_residual = residual.reshape(score_count, stride, width)[:, stride - 1, :]
-    picked = scored_residual.astype(jnp.float32) + jnp.dot(
-        scored_context, full_proj, preferred_element_type=jnp.float32
-    )
-    normed = normalize(picked, norm_gain)
     projected = jnp.dot(context, full_proj, preferred_element_type=jnp.float32)
     hidden = residual.astype(jnp.float32) + projected
     layer_out = hidden.astype(jnp.bfloat16)
+    picked = hidden.reshape(score_count, stride, width)[:, stride - 1, :]
+    normed = normalize(picked, norm_gain)
     logits = lax.dot_general(
         gather_rows(normed),
         head_weight,

time: 181 us -> 177 us (0.978)
  waiting for transfers between devices: 89.3 us -> 77.7 us
  starting transfers between devices: 28.9 us -> 36.9 us
  matrix products: 27.5 us -> 21.9 us
  other arithmetic: 9.06 us -> 13.1 us
    ppermute x8 -> x12, waiting for transfers between devices: 21.9 us -> 11.7 us  [gather_rows(): received.append(lax.ppermute(data, SEQ, pairs))]
    ppermute x8 -> x12, starting transfers between devices: 4.98 us -> 13.5 us  [gather_rows(): received.append(lax.ppermute(data, SEQ, pairs))]
    dot_general x1 -> x0, matrix products: 5.77 us -> none  [local(): jnp.dot(scored_context, full_proj, preferred_element_type=jnp.float32)]
    gather x0 -> x5, local copies, waits for them, and re-layouts: none -> 3.2 us  [gather_rows(): data = jnp.take(stacked, order, axis=0)]
    ppermute x2, waiting for transfers between devices: 28.7 us -> 25.8 us  [shift_chips(): lax.ppermute(value, SEQ, [(s, s + step) for s in range(count - step)])]
  transfers between devices with their start and end apart: 18 -> 22, of which waited for: 11 -> 13; matrix products, arithmetic and copies ran while one was open for 19% -> 17% of each run, Pallas kernels for 0% -> 0%
where the time goes in v6:
time: 177 us
  waiting for transfers between devices  77.7 us (44%)
  starting transfers between devices  36.9 us (21%)
  matrix products  21.9 us (12%)
  between operations  14.5 us (8%)
  other arithmetic  13.1 us (7%)
  local copies, waits for them, and re-layouts  12.8 us (7%)
    ppermute x2, waiting for transfers between devices, shift_chips(): lax.ppermute(value, SEQ, [(s, s + step) for s in range(count - step)])  25.8 us
    ppermute x4, waiting for transfers between devices, across_pair(): return lax.ppermute(value, SEQ, pairs)  20 us
    all_gather x1, waiting for transfers between devices, local(): full_proj = lax.all_gather(out_proj, SEQ, axis=0, tiled=True)  19.6 us
    ppermute x12, starting transfers between devices, gather_rows(): received.append(lax.ppermute(data, SEQ, pairs))  13.5 us
    ppermute x2, starting transfers between devices, shift_chips(): lax.ppermute(value, SEQ, [(s, s + step) for s in range(count - step)])  12.7 us
    ppermute x12, waiting for transfers between devices, gather_rows(): received.append(lax.ppermute(data, SEQ, pairs))  11.7 us
    ppermute x4, starting transfers between devices, across_pair(): return lax.ppermute(value, SEQ, pairs)  10.6 us
    dot_general x1, matrix products, local(): projected = jnp.dot(context, full_proj, preferred_element_type=jnp.float32)  6.84 us
  transfers between devices with their start and end apart: 22, of which 13 were waited for; matrix products, arithmetic and copies ran while one was open for 17% of the time, Pallas kernels for 0%

profile of v6, /device:TPU:0, one launch (start us, length us, event | category | flops | bytes accessed | tf_op | source)
XLA Modules:
  0.0 176.9 jit_solution(11667877224894218139)
XLA Ops:
  7.2 0.7 all-gather.2.cloned.1.call-update
  7.9 1.3 copy.17
  9.2 0.7 convert_element_type.51
  9.9 5.0 %collective-permute-start = (bf16[128,2176]{0,1:T(8,128)(2,1)S(1)}, bf16[128,2176]{0,1:T(8,128)(2,1)S(1)}, u32[]{:S(2)}, u32[]{:S(2)}) collective-permute-start(bf16[128,2176]{0,1:T(8,128)(2,1)S(1)} %pad_maximum_fusion.2), channel_id=1, source_target_pairs={{0,4},{1,5},{2,6},{3,7},{4,8},{5,9},{6,10},{7,11},{8,12},{9,13},{1... | collective-permute-start | bytes 1671176 | tf_op jit(solution)/shard_map/ppermute | solution.py:70
  14.9 3.5 %collective-permute-start.5 = (bf16[128,2176]{0,1:T(8,128)(2,1)S(1)}, bf16[128,2176]{0,1:T(8,128)(2,1)S(1)}, u32[]{:S(2)}, u32[]{:S(2)}) collective-permute-start(bf16[128,2176]{0,1:T(8,128)(2,1)S(1)} %pad_maximum_fusion.2), channel_id=1, source_target_pairs={{0,2},{1,3},{4,6},{5,7},{8,10},{9,11},{12,14},{13,15},{16,18},{17,... | collective-permute-start | bytes 1671176 | tf_op jit(solution)/shard_map/ppermute | solution.py:76
  19.0 13.4 %collective-permute-done = bf16[128,2176]{0,1:T(8,128)(2,1)S(1)} collective-permute-done((bf16[128,2176]{0,1:T(8,128)(2,1)S(1)}, bf16[128,2176]{0,1:T(8,128)(2,1)S(1)}, u32[]{:S(2)}, u32[]{:S(2)}) %collective-permute-start) | collective-permute-done | bytes 557088 | tf_op jit(solution)/shard_map/ppermute | solution.py:70
  32.4 7.7 %collective-permute-start.1 = (bf16[128,2176]{0,1:T(8,128)(2,1)S(1)}, bf16[128,2176]{0,1:T(8,128)(2,1)S(1)}, u32[]{:S(2)}, u32[]{:S(2)}) collective-permute-start(bf16[128,2176]{0,1:T(8,128)(2,1)S(1)} %collective-permute-done), channel_id=1, source_target_pairs={{0,4},{1,5},{2,6},{3,7},{4,8},{5,9},{6,10},{7,11},{8,12},{9,13},{1... | collective-permute-start | bytes 1671176 | tf_op jit(solution)/shard_map/ppermute | solution.py:70
  40.2 1.3 collective-permute-start.6
  43.8 4.6 %collective-permute-start.2 = (bf16[128,2176]{0,1:T(8,128)(2,1)S(1)}, bf16[128,2176]{0,1:T(8,128)(2,1)S(1)}, u32[]{:S(2)}, u32[]{:S(2)}) collective-permute-start(bf16[128,2176]{0,1:T(8,128)(2,1)S(1)} %collective-permute-done), channel_id=1, source_target_pairs={{0,2},{1,3},{4,6},{5,7},{8,10},{9,11},{12,14},{13,15},{16,18},{17,... | collective-permute-start | bytes 1671176 | tf_op jit(solution)/shard_map/ppermute | solution.py:76
  48.4 12.4 %collective-permute-done.1 = bf16[128,2176]{0,1:T(8,128)(2,1)S(1)} collective-permute-done((bf16[128,2176]{0,1:T(8,128)(2,1)S(1)}, bf16[128,2176]{0,1:T(8,128)(2,1)S(1)}, u32[]{:S(2)}, u32[]{:S(2)}) %collective-permute-start.1) | collective-permute-done | bytes 557088 | tf_op jit(solution)/shard_map/ppermute | solution.py:70
  60.8 1.3 collective-permute-start.3
  62.2 1.1 pad_maximum_fusion.1
  63.3 20.0 %collective-permute-done.3 = bf16[128,2176]{0,1:T(8,128)(2,1)S(1)} collective-permute-done((bf16[128,2176]{0,1:T(8,128)(2,1)S(1)}, bf16[128,2176]{0,1:T(8,128)(2,1)S(1)}, u32[]{:S(2)}, u32[]{:S(2)}) %collective-permute-start.3) | collective-permute-done | bytes 557088 | tf_op jit(solution)/shard_map/ppermute | solution.py:76
  83.3 1.1 pad_maximum_fusion
  84.5 2.2 %reshape.415 = bf16[128,8,2,128]{3,2,1,0:T(2,128)(2,1)} reshape(bf16[128,2048]{1,0:T(8,128)(2,1)} %param.8) | data formatting | bytes 1048576 | tf_op jit(solution)/shard_map/reshape | solution.py:135
  87.9 1.3 slice_bitcast_fusion
  89.3 1.3 slice_bitcast_fusion.2
  92.1 1.6 fusion.13
  93.8 1.9 %constant_dynamic-slice_fusion = (bf16[1152,1024]{0,1:T(8,128)(2,1)S(1)}, bf16[1152,1024]{0,1:T(8,128)(2,1)}) fusion(bf16[1280,2176]{0,1:T(8,128)(2,1)S(1)} %fusion.13, s32[]{:T(128)S(6)} %select_n.199, s32[]{:T(128)S(6)} %add.168), kind=kLoop, calls=%fused_computation.105 | loop fusion | bytes 9437192 | tf_op jit(solution)/shard_map/slice | solution.py:136
  95.7 1.3 compare_and_fusion
  97.0 4.3 %fusion.52 = f32[8,2,128]{2,1,0:T(2,128)} fusion(pred[128,1152]{0,1:T(8,128)(4,1)S(1)} %compare_and_fusion, bf16[1152,8,128,1]{0,2,3,1:T(8,128)(2,1)S(1)} %bitcast.96, bf16[128,8,2,128]{3,2,1,0:T(2,128)(2,1)S(1)} %copy-done), kind=kOutput, calls=%fused_computation.114 | convolution fusion | flops 613418112 | bytes 3039232 | tf_op jit(solution)/shard_map/sub | solution.py:150
  101.3 6.3 %fusion.6 = bf16[8,128,2,128]{3,1,2,0:T(8,128)(2,1)S(1)} fusion(bf16[1152,8,128,1]{0,2,3,1:T(8,128)(2,1)} %bitcast.98, f32[8,2,128]{2,1,0:T(2,128)} %fusion.52, pred[128,1152]{0,1:T(8,128)(4,1)S(1)} %compare_and_fusion, bf16[1152,8,128,1]{0,2,3,1:T(8,128)(2,1)S(1)} %bitcast.97, bf16[128,8,2,128]{3,2,1,0:T(2,128)(2,1)S(1)} %copy-done), kind=kOutput, calls=%fused_computation.14 | convolution fusion | flops 1220021376 | bytes 5922816 | tf_op jit(solution)/shard_map/hgqk,khd->qhgd/dot_general | solution.py:152
  107.6 19.6 %all-gather.2.cloned.1.call-done = bf16[2048,2688]{1,0:T(8,128)(2,1)} async-done(((bf16[128,2688]{1,0:T(8,128)(2,1)}), bf16[2048,2688]{1,0:T(8,128)(2,1)}) %all-gather.2.cloned.1.call-update) | async-done | bytes 11010064 | tf_op jit(solution)/shard_map/all_gather | solution.py:121
  127.1 6.8 %fusion.55 = (bf16[128,2688]{1,0:T(8,128)(2,1)}, f32[128,2688]{1,0:T(8,128)S(1)}) fusion(bf16[128,2048]{0,1:T(8,128)(2,1)S(1)} %bitcast.103, bf16[2048,2688]{1,0:T(8,128)(2,1)} %all-gather.2.cloned.1.call-done, bf16[128,2688]{1,0:T(8,128)(2,1)} %param.11), kind=kOutput, calls=%fused_computation.115 | convolution fusion | flops 1410318336 | bytes 14286848 | tf_op jit(solution)/shard_map/dot_general | solution.py:159
  134.9 1.5 collective-permute-start.10
  136.5 1.2 collective-permute-done.9
  137.6 1.1 collective-permute-done.10
  138.8 0.7 gather_fusion
  139.7 0.7 collective-permute-start.12
  140.4 1.4 collective-permute-start.13
  141.8 2.8 %collective-permute-start.14 = (bf16[4,4,2688]{2,1,0:T(4,128)(2,1)S(1)}, bf16[4,4,2688]{2,1,0:T(4,128)(2,1)S(1)}, u32[]{:S(2)}, u32[]{:S(2)}) collective-permute-start(bf16[4,4,2688]{2,1,0:T(4,128)(2,1)S(1)} %broadcast_select_fusion.2), channel_id=1, source_target_pairs={{0,12},{1,13},{2,14},{3,15},{4,0},{5,1},{6,2},{7,3},{8,4},{9,5},{1... | collective-permute-start | bytes 258056 | tf_op jit(solution)/shard_map/ppermute | solution.py:54
  144.7 2.2 %collective-permute-done.12 = bf16[4,4,2688]{2,1,0:T(4,128)(2,1)S(1)} collective-permute-done((bf16[4,4,2688]{2,1,0:T(4,128)(2,1)S(1)}, bf16[4,4,2688]{2,1,0:T(4,128)(2,1)S(1)}, u32[]{:S(2)}, u32[]{:S(2)}) %collective-permute-start.12) | collective-permute-done | bytes 86048 | tf_op jit(solution)/shard_map/ppermute | solution.py:54
  147.0 3.1 %collective-permute-done.13 = bf16[4,4,2688]{2,1,0:T(4,128)(2,1)S(1)} collective-permute-done((bf16[4,4,2688]{2,1,0:T(4,128)(2,1)S(1)}, bf16[4,4,2688]{2,1,0:T(4,128)(2,1)S(1)}, u32[]{:S(2)}, u32[]{:S(2)}) %collective-permute-start.13) | collective-permute-done | bytes 86048 | tf_op jit(solution)/shard_map/ppermute | solution.py:54
  150.4 1.0 gather_fusion.1
  151.5 4.5 %fusion.56 = (f32[64]{0:T(128)S(1)}, f32[64,1024]{1,0:T(8,128)S(1)}) fusion(bf16[1024,2688]{1,0:T(8,128)(2,1)} %param.14, bf16[64,2688]{1,0:T(8,128)(2,1)S(1)} %gather.32, pred[64]{0:T(512)(128)(4,1)S(1)} %copy-done.4), kind=kOutput, calls=%fused_computation.116 | convolution fusion | flops 352559040 | bytes 6111552 | tf_op jit(solution)/shard_map/dot_general | solution.py:164
  156.3 0.8 collective-permute-start.16
  157.0 1.4 collective-permute-start.17
  158.6 0.7 collective-permute-done.15
  159.3 0.7 collective-permute-done.16
  159.9 0.7 gather_fusion.2
  160.7 1.8 %collective-permute-start.18 = (f32[4,3,64]{2,1,0:T(4,128)S(1)}, f32[4,3,64]{2,1,0:T(4,128)S(1)}, u32[]{:S(2)}, u32[]{:S(2)}) collective-permute-start(f32[4,3,64]{2,1,0:T(4,128)S(1)} %broadcast_select_fusion.3), channel_id=1, source_target_pairs={{0,4},{1,5},{2,6},{3,7},{4,8},{5,9},{6,10},{7,11},{8,12},{9,13},{1... | collective-permute-start | bytes 9224 | tf_op jit(solution)/shard_map/ppermute | solution.py:54
  162.5 1.6 collective-permute-start.19
  164.1 0.8 collective-permute-start.20
  165.0 1.2 collective-permute-done.18
  166.1 0.9 collective-permute-done.19
  167.1 0.7 collective-permute-done.20
  167.8 0.7 gather_fusion.3
  168.7 0.8 broadcast_subtract_fusion
  (86 shorter events, 9.0 us)
Async XLA Ops:
  7.2 120.0 %all-gather.2.cloned.1.call-start = ((), (), s32[]{:S(2)}) async-start(), calls=%async_computation | async-start | bytes 11698176 | tf_op jit(solution)/shard_map/all_gather | solution.py:121
  9.9 22.5 %collective-permute-start = (bf16[128,2176]{0,1:T(8,128)(2,1)S(1)}, bf16[128,2176]{0,1:T(8,128)(2,1)S(1)}, u32[]{:S(2)}, u32[]{:S(2)}) collective-permute-start(bf16[128,2176]{0,1:T(8,128)(2,1)S(1)} %pad_maximum_fusion.2), channel_id=1, source_target_pairs={{0,4},{1,5},{2,6},{3,7},{4,8},{5,9},{6,10},{7,11},{8,12},{9,13},{1... | collective-permute-start | bytes 1671176 | tf_op jit(solution)/shard_map/ppermute | solution.py:70
  14.9 47.2 %collective-permute-start.5 = (bf16[128,2176]{0,1:T(8,128)(2,1)S(1)}, bf16[128,2176]{0,1:T(8,128)(2,1)S(1)}, u32[]{:S(2)}, u32[]{:S(2)}) collective-permute-start(bf16[128,2176]{0,1:T(8,128)(2,1)S(1)} %pad_maximum_fusion.2), channel_id=1, source_target_pairs={{0,2},{1,3},{4,6},{5,7},{8,10},{9,11},{12,14},{13,15},{16,18},{17,... | collective-permute-start | bytes 1671176 | tf_op jit(solution)/shard_map/ppermute | solution.py:76
  18.4 73.7 %collective-permute-start.8 = (bf16[128,2176]{0,1:T(8,128)(2,1)S(1)}, bf16[128,2176]{0,1:T(8,128)(2,1)}, u32[]{:S(2)}, u32[]{:S(2)}) collective-permute-start(bf16[128,2176]{0,1:T(8,128)(2,1)S(1)} %pad_maximum_fusion.2), channel_id=1, source_target_pairs={{0,1},{1,0},{2,3},{3,2},{4,5},{5,4},{6,7},{7,6},{8,9},{9,8},{10,11... | collective-permute-start | bytes 1671176 | tf_op jit(solution)/shard_map/ppermute | solution.py:37
  32.4 28.4 %collective-permute-start.1 = (bf16[128,2176]{0,1:T(8,128)(2,1)S(1)}, bf16[128,2176]{0,1:T(8,128)(2,1)S(1)}, u32[]{:S(2)}, u32[]{:S(2)}) collective-permute-start(bf16[128,2176]{0,1:T(8,128)(2,1)S(1)} %collective-permute-done), channel_id=1, source_target_pairs={{0,4},{1,5},{2,6},{3,7},{4,8},{5,9},{6,10},{7,11},{8,12},{9,13},{1... | collective-permute-start | bytes 1671176 | tf_op jit(solution)/shard_map/ppermute | solution.py:70
  40.2 21.9 %collective-permute-start.6 = (bf16[128,2176]{0,1:T(8,128)(2,1)S(1)}, bf16[128,2176]{0,1:T(8,128)(2,1)S(1)}, u32[]{:S(2)}, u32[]{:S(2)}) collective-permute-start(bf16[128,2176]{0,1:T(8,128)(2,1)S(1)} %collective-permute-done), channel_id=1, source_target_pairs={{2,0},{3,1},{6,4},{7,5},{10,8},{11,9},{14,12},{15,13},{18,16},{19,... | collective-permute-start | bytes 1671176 | tf_op jit(solution)/shard_map/ppermute | solution.py:76
  43.8 19.5 %collective-permute-start.2 = (bf16[128,2176]{0,1:T(8,128)(2,1)S(1)}, bf16[128,2176]{0,1:T(8,128)(2,1)S(1)}, u32[]{:S(2)}, u32[]{:S(2)}) collective-permute-start(bf16[128,2176]{0,1:T(8,128)(2,1)S(1)} %collective-permute-done), channel_id=1, source_target_pairs={{0,2},{1,3},{4,6},{5,7},{8,10},{9,11},{12,14},{13,15},{16,18},{17,... | collective-permute-start | bytes 1671176 | tf_op jit(solution)/shard_map/ppermute | solution.py:76
  60.8 22.5 %collective-permute-start.3 = (bf16[128,2176]{0,1:T(8,128)(2,1)S(1)}, bf16[128,2176]{0,1:T(8,128)(2,1)S(1)}, u32[]{:S(2)}, u32[]{:S(2)}) collective-permute-start(bf16[128,2176]{0,1:T(8,128)(2,1)S(1)} %collective-permute-done.1), channel_id=1, source_target_pairs={{2,0},{3,1},{6,4},{7,5},{10,8},{11,9},{14,12},{15,13},{18,16},{19,... | collective-permute-start | bytes 1671176 | tf_op jit(solution)/shard_map/ppermute | solution.py:76
  63.3 24.1 %copy-start.11 = (s32[64]{0:T(128)S(1)}, s32[64]{0:T(128)}, u32[]{:S(2)}) copy-start(s32[64]{0:T(128)} %param.15) | copy-start | bytes 772
  63.3 24.6 %collective-permute-start.7 = (bf16[2,128,2176]{1,2,0:T(8,128)(2,1)}, bf16[2,128,2176]{1,2,0:T(8,128)(2,1)}, u32[]{:S(2)}, u32[]{:S(2)}) collective-permute-start(bf16[2,128,2176]{1,2,0:T(8,128)(2,1)} %pad_maximum_fusion.1), channel_id=1, source_target_pairs={{0,1},{1,0},{2,3},{3,2},{4,5},{5,4},{6,7},{7,6},{8,9},{9,8},{10,11... | collective-permute-start | bytes 3342344 | tf_op jit(solution)/shard_map/ppermute | solution.py:37
  84.4 4.8 %collective-permute-start.4 = (bf16[2,128,2176]{1,2,0:T(8,128)(2,1)}, bf16[2,128,2176]{1,2,0:T(8,128)(2,1)}, u32[]{:S(2)}, u32[]{:S(2)}) collective-permute-start(bf16[2,128,2176]{1,2,0:T(8,128)(2,1)} %pad_maximum_fusion), channel_id=1, source_target_pairs={{0,1},{1,0},{2,3},{3,2},{4,5},{5,4},{6,7},{7,6},{8,9},{9,8},{10,11... | collective-permute-start | bytes 3342344 | tf_op jit(solution)/shard_map/ppermute | solution.py:37
  84.4 6.1 %copy-start.9 = (pred[4]{0:T(512)(128)(4,1)}, pred[4]{0:T(512)(128)(4,1)S(1)}, u32[]{:S(2)}) copy-start(pred[4]{0:T(512)(128)(4,1)S(1)} %compare_and_fusion.2) | copy-start | bytes 16
  93.8 1.9 %copy-start.3 = (pred[1152]{0:T(1024)(128)(4,1)S(1)}, pred[1152]{0:T(1024)(128)(4,1)}, u32[]{:S(2)}) copy-start(pred[1152]{0:T(1024)(128)(4,1)} %broadcast_compare_fusion) | copy-start | bytes 3460
  93.8 1.9 %copy-start.5 = (s32[128]{0:T(128)S(1)}, s32[128]{0:T(128)}, u32[]{:S(2)}) copy-start(s32[128]{0:T(128)} %param.10) | copy-start | bytes 1540
  93.8 1.9 %copy-start.7 = (s32[128]{0:T(128)S(1)}, s32[128]{0:T(128)}, u32[]{:S(2)}) copy-start(s32[128]{0:T(128)} %get-tuple-element.24) | copy-start | bytes 1540
  93.8 1.9 %copy-start.8 = (s32[128]{0:T(128)S(1)}, s32[128]{0:T(128)}, u32[]{:S(2)}) copy-start(s32[128]{0:T(128)} %get-tuple-element.25) | copy-start | bytes 1540
  93.8 3.2 %copy-start = (bf16[128,8,2,128]{3,2,1,0:T(2,128)(2,1)S(1)}, bf16[128,8,2,128]{3,2,1,0:T(2,128)(2,1)}, u32[]{:S(2)}) copy-start(bf16[128,8,2,128]{3,2,1,0:T(2,128)(2,1)} %reshape.415) | copy-start | bytes 1572868
  127.1 7.0 %copy-start.1 = (f32[2688]{0:T(1024)S(1)}, f32[2688]{0:T(1024)}, u32[]{:S(2)}) copy-start(f32[2688]{0:T(1024)} %param.12) | copy-start | bytes 32260
  127.1 12.4 %copy-start.2 = (pred[4]{0:T(512)(128)(4,1)S(1)}, pred[4]{0:T(512)(128)(4,1)}, u32[]{:S(2)}) copy-start(pred[4]{0:T(512)(128)(4,1)} %compare_and_fusion.1) | copy-start | bytes 16
  134.0 17.5 %copy-start.4 = (pred[64]{0:T(512)(128)(4,1)S(1)}, pred[64]{0:T(512)(128)(4,1)}, u32[]{:S(2)}) copy-start(pred[64]{0:T(512)(128)(4,1)} %broadcast_in_dim.103) | copy-start | bytes 196
  134.3 2.2 %collective-permute-start.11 = (bf16[1,4,2688]{2,0,1:T(2,128)(2,1)S(1)}, bf16[1,4,2688]{2,0,1:T(2,128)(2,1)S(1)}, u32[]{:S(2)}, u32[]{:S(2)}) collective-permute-start(bf16[1,4,2688]{2,0,1:T(2,128)(2,1)S(1)} %fusion.31), channel_id=1, source_target_pairs={{0,3},{1,0},{2,1},{3,2},{4,7},{5,4},{6,5},{7,6},{8,11},{9,8},{10,9... | collective-permute-start | bytes 64520 | tf_op jit(solution)/shard_map/ppermute | solution.py:54
  134.4 3.3 %collective-permute-start.9 = (bf16[1,4,2688]{2,1,0:T(4,128)(2,1)S(1)}, bf16[1,4,2688]{2,1,0:T(4,128)(2,1)S(1)}, u32[]{:S(2)}, u32[]{:S(2)}) collective-permute-start(bf16[1,4,2688]{2,1,0:T(4,128)(2,1)S(1)} %copy.21), channel_id=1, source_target_pairs={{0,1},{1,2},{2,3},{3,0},{4,5},{5,6},{6,7},{7,4},{8,9},{9,10},{10,1... | collective-permute-start | bytes 64520 | tf_op jit(solution)/shard_map/ppermute | solution.py:54
  134.9 3.8 %collective-permute-start.10 = (bf16[1,4,2688]{2,1,0:T(4,128)(2,1)S(1)}, bf16[1,4,2688]{2,1,0:T(4,128)(2,1)S(1)}, u32[]{:S(2)}, u32[]{:S(2)}) collective-permute-start(bf16[1,4,2688]{2,1,0:T(4,128)(2,1)S(1)} %copy.21), channel_id=1, source_target_pairs={{0,2},{1,3},{2,0},{3,1},{4,6},{5,7},{6,4},{7,5},{8,10},{9,11},{10,... | collective-permute-start | bytes 64520 | tf_op jit(solution)/shard_map/ppermute | solution.py:54
  139.7 7.3 %collective-permute-start.12 = (bf16[4,4,2688]{2,1,0:T(4,128)(2,1)S(1)}, bf16[4,4,2688]{2,1,0:T(4,128)(2,1)S(1)}, u32[]{:S(2)}, u32[]{:S(2)}) collective-permute-start(bf16[4,4,2688]{2,1,0:T(4,128)(2,1)S(1)} %broadcast_select_fusion.2), channel_id=1, source_target_pairs={{0,4},{1,5},{2,6},{3,7},{4,8},{5,9},{6,10},{7,11},{8,12},{9,13},{1... | collective-permute-start | bytes 258056 | tf_op jit(solution)/shard_map/ppermute | solution.py:54
  140.4 9.7 %collective-permute-start.13 = (bf16[4,4,2688]{2,1,0:T(4,128)(2,1)S(1)}, bf16[4,4,2688]{2,1,0:T(4,128)(2,1)S(1)}, u32[]{:S(2)}, u32[]{:S(2)}) collective-permute-start(bf16[4,4,2688]{2,1,0:T(4,128)(2,1)S(1)} %broadcast_select_fusion.2), channel_id=1, source_target_pairs={{0,8},{1,9},{2,10},{3,11},{4,12},{5,13},{6,14},{7,15},{8,0},{9,1},... | collective-permute-start | bytes 258056 | tf_op jit(solution)/shard_map/ppermute | solution.py:54
  141.8 8.3 %collective-permute-start.14 = (bf16[4,4,2688]{2,1,0:T(4,128)(2,1)S(1)}, bf16[4,4,2688]{2,1,0:T(4,128)(2,1)S(1)}, u32[]{:S(2)}, u32[]{:S(2)}) collective-permute-start(bf16[4,4,2688]{2,1,0:T(4,128)(2,1)S(1)} %broadcast_select_fusion.2), channel_id=1, source_target_pairs={{0,12},{1,13},{2,14},{3,15},{4,0},{5,1},{6,2},{7,3},{8,4},{9,5},{1... | collective-permute-start | bytes 258056 | tf_op jit(solution)/shard_map/ppermute | solution.py:54
  151.4 4.5 %copy-start.6 = (s32[64]{0:T(128)S(1)}, s32[64]{0:T(128)}, u32[]{:S(2)}) copy-start(s32[64]{0:T(128)} %broadcast_subtract_fusion.1) | copy-start | bytes 772
  151.5 7.0 %copy-start.10 = (pred[4]{0:T(512)(128)(4,1)S(1)}, pred[4]{0:T(512)(128)(4,1)}, u32[]{:S(2)}) copy-start(pred[4]{0:T(512)(128)(4,1)} %copy-done.9) | copy-start | bytes 16
  156.2 3.1 %collective-permute-start.15 = (f32[1,3,64]{2,1,0:T(4,128)S(1)}, f32[1,3,64]{2,1,0:T(4,128)S(1)}, u32[]{:S(2)}, u32[]{:S(2)}) collective-permute-start(f32[1,3,64]{2,1,0:T(4,128)S(1)} %get-tuple-element.19), channel_id=1, source_target_pairs={{0,1},{1,2},{2,3},{3,0},{4,5},{5,6},{6,7},{7,4},{8,9},{9,10},{10,1... | collective-permute-start | bytes 2312 | tf_op jit(solution)/shard_map/ppermute | solution.py:54
  156.3 3.7 %collective-permute-start.16 = (f32[1,3,64]{2,1,0:T(4,128)S(1)}, f32[1,3,64]{2,1,0:T(4,128)S(1)}, u32[]{:S(2)}, u32[]{:S(2)}) collective-permute-start(f32[1,3,64]{2,1,0:T(4,128)S(1)} %get-tuple-element.19), channel_id=1, source_target_pairs={{0,2},{1,3},{2,0},{3,1},{4,6},{5,7},{6,4},{7,5},{8,10},{9,11},{10,... | collective-permute-start | bytes 2312 | tf_op jit(solution)/shard_map/ppermute | solution.py:54
  157.0 2.9 %collective-permute-start.17 = (f32[1,3,64]{2,1,0:T(4,128)S(1)}, f32[1,3,64]{2,1,0:T(4,128)S(1)}, u32[]{:S(2)}, u32[]{:S(2)}) collective-permute-start(f32[1,3,64]{2,1,0:T(4,128)S(1)} %get-tuple-element.19), channel_id=1, source_target_pairs={{0,3},{1,0},{2,1},{3,2},{4,7},{5,4},{6,5},{7,6},{8,11},{9,8},{10,9... | collective-permute-start | bytes 2312 | tf_op jit(solution)/shard_map/ppermute | solution.py:54
  160.7 5.5 %collective-permute-start.18 = (f32[4,3,64]{2,1,0:T(4,128)S(1)}, f32[4,3,64]{2,1,0:T(4,128)S(1)}, u32[]{:S(2)}, u32[]{:S(2)}) collective-permute-start(f32[4,3,64]{2,1,0:T(4,128)S(1)} %broadcast_select_fusion.3), channel_id=1, source_target_pairs={{0,4},{1,5},{2,6},{3,7},{4,8},{5,9},{6,10},{7,11},{8,12},{9,13},{1... | collective-permute-start | bytes 9224 | tf_op jit(solution)/shard_map/ppermute | solution.py:54
  162.5 4.6 %collective-permute-start.19 = (f32[4,3,64]{2,1,0:T(4,128)S(1)}, f32[4,3,64]{2,1,0:T(4,128)S(1)}, u32[]{:S(2)}, u32[]{:S(2)}) collective-permute-start(f32[4,3,64]{2,1,0:T(4,128)S(1)} %broadcast_select_fusion.3), channel_id=1, source_target_pairs={{0,8},{1,9},{2,10},{3,11},{4,12},{5,13},{6,14},{7,15},{8,0},{9,1},... | collective-permute-start | bytes 9224 | tf_op jit(solution)/shard_map/ppermute | solution.py:54
  164.1 3.7 %collective-permute-start.20 = (f32[4,3,64]{2,1,0:T(4,128)S(1)}, f32[4,3,64]{2,1,0:T(4,128)S(1)}, u32[]{:S(2)}, u32[]{:S(2)}) collective-permute-start(f32[4,3,64]{2,1,0:T(4,128)S(1)} %broadcast_select_fusion.3), channel_id=1, source_target_pairs={{0,12},{1,13},{2,14},{3,15},{4,0},{5,1},{6,2},{7,3},{8,4},{9,5},{1... | collective-permute-start | bytes 9224 | tf_op jit(solution)/shard_map/ppermute | solution.py:54
Sparse Core Ops, SparseCore 0:
  10.3 116.8 all-gather.1

commit v7 on v6

--- a/solution.py
+++ b/solution.py
@@ -119,6 +119,9 @@
     first_row = my_index * token_rows
 
     full_proj = lax.all_gather(out_proj, SEQ, axis=0, tiled=True)
+    score_count = SCORE_DEV
+    stride = token_rows // score_count
+    scored_residual = gather_rows(residual.reshape(score_count, stride, width)[:, stride - 1, :])
 
     seg_cols = jnp.broadcast_to(segment_ids.astype(jnp.bfloat16)[:, None], (token_rows, SEG_LANES))
     own = jnp.concatenate([joined_keys_values, seg_cols], 1)
@@ -154,15 +157,16 @@
     )
     context = context.reshape(token_rows, QUERY_HEADS * HEAD_SIZE).astype(jnp.bfloat16)
 
-    score_count = SCORE_DEV
-    stride = token_rows // score_count
+    scored_context = gather_rows(context.reshape(score_count, stride, -1)[:, stride - 1, :])
+    picked = scored_residual.astype(jnp.float32) + jnp.dot(
+        scored_context, full_proj, preferred_element_type=jnp.float32
+    )
+    normed = normalize(picked, norm_gain)
     projected = jnp.dot(context, full_proj, preferred_element_type=jnp.float32)
     hidden = residual.astype(jnp.float32) + projected
     layer_out = hidden.astype(jnp.bfloat16)
-    picked = hidden.reshape(score_count, stride, width)[:, stride - 1, :]
-    normed = normalize(picked, norm_gain)
     logits = lax.dot_general(
-        gather_rows(normed),
+        normed,
         head_weight,
         (((1,), (1,)), ((), ())),
         preferred_element_type=jnp.float32,

time: 177 us -> 164 us (0.927)
  waiting for transfers between devices: 77.7 us -> 53.2 us
  starting transfers between devices: 36.9 us -> 49 us
  other arithmetic: 13.1 us -> 10.5 us
    all_gather x1, waiting for transfers between devices: 19.6 us -> 0.02 us  [local(): full_proj = lax.all_gather(out_proj, SEQ, axis=0, tiled=True)]
    ppermute x3, starting transfers between devices: 0.08 us -> 10.9 us  [swap_cores(): return lax.ppermute(value, 'core', [(0, 1), (1, 0)])]
    ppermute x2, waiting for transfers between devices: 25.8 us -> 15.4 us  [shift_chips(): lax.ppermute(value, SEQ, [(s, s + step) for s in range(count - step)])]
    ppermute x12 -> x18, starting transfers between devices: 13.5 us -> 21.6 us  [gather_rows(): received.append(lax.ppermute(data, SEQ, pairs))]
    ppermute x4, waiting for transfers between devices: 20 us -> 27.3 us  [across_pair(): return lax.ppermute(value, SEQ, pairs)]
    dot_general x1 -> x2, matrix products: 4.46 us -> 11 us  [the longest x1 6.49 us: local(): jnp.dot(scored_context, full_proj, preferred_element_type=jnp.float32)]
    dot_general x1, matrix products: 6.84 us -> 2.54 us  [local(): projected = jnp.dot(context, full_proj, preferred_element_type=jnp.float32)]
    ppermute x2, starting transfers between devices: 12.7 us -> 8.45 us  [shift_chips(): lax.ppermute(value, SEQ, [(s, s + step) for s in range(count - step)])]
  transfers between devices with their start and end apart: 22 -> 28, of which waited for: 13 -> 10; matrix products, arithmetic and copies ran while one was open for 17% -> 20% of each run, Pallas kernels for 0% -> 0%
where the time goes in v7:
time: 164 us; the launch traced here: 163 us
  waiting for transfers between devices  53.2 us (32%)
  starting transfers between devices  49 us (30%)
  matrix products  23.5 us (14%)
  between operations  14.6 us (9%)
  local copies, waits for them, and re-layouts  12.5 us (8%)
  other arithmetic  10.5 us (6%)
    ppermute x4, waiting for transfers between devices, across_pair(): return lax.ppermute(value, SEQ, pairs)  27.3 us
    ppermute x18, starting transfers between devices, gather_rows(): received.append(lax.ppermute(data, SEQ, pairs))  21.6 us
    ppermute x2, waiting for transfers between devices, shift_chips(): lax.ppermute(value, SEQ, [(s, s + step) for s in range(count - step)])  15.4 us
    ppermute x3, starting transfers between devices, swap_cores(): return lax.ppermute(value, 'core', [(0, 1), (1, 0)])  10.9 us
    ppermute x18, waiting for transfers between devices, gather_rows(): received.append(lax.ppermute(data, SEQ, pairs))  9.72 us
    ppermute x2, starting transfers between devices, shift_chips(): lax.ppermute(value, SEQ, [(s, s + step) for s in range(count - step)])  8.45 us
    ppermute x4, starting transfers between devices, across_pair(): return lax.ppermute(value, SEQ, pairs)  8.1 us
    dot_general x1, matrix products, local(): jnp.dot(scored_context, full_proj, preferred_element_type=jnp.float32)  6.49 us
  transfers between devices with their start and end apart: 28, of which 10 were waited for; matrix products, arithmetic and copies ran while one was open for 20% of the time, Pallas kernels for 0%

profile of v7, /device:TPU:0, one launch (start us, length us, event | category | flops | bytes accessed | tf_op | source)
XLA Modules:
  0.0 163.2 jit_solution(218271479622996861)
XLA Ops:
  7.2 0.7 all-gather.2.cloned.1.call-update
  7.9 1.3 copy.15
  9.2 0.7 convert_element_type.43
  10.0 5.0 %collective-permute-start = (bf16[128,2176]{0,1:T(8,128)(2,1)S(1)}, bf16[128,2176]{0,1:T(8,128)(2,1)S(1)}, u32[]{:S(2)}, u32[]{:S(2)}) collective-permute-start(bf16[128,2176]{0,1:T(8,128)(2,1)S(1)} %pad_maximum_fusion.2), channel_id=1, source_target_pairs={{0,4},{1,5},{2,6},{3,7},{4,8},{5,9},{6,10},{7,11},{8,12},{9,13},{1... | collective-permute-start | bytes 1671176 | tf_op jit(solution)/shard_map/ppermute | solution.py:70
  14.9 3.5 %collective-permute-start.5 = (bf16[128,2176]{0,1:T(8,128)(2,1)S(1)}, bf16[128,2176]{0,1:T(8,128)(2,1)S(1)}, u32[]{:S(2)}, u32[]{:S(2)}) collective-permute-start(bf16[128,2176]{0,1:T(8,128)(2,1)S(1)} %pad_maximum_fusion.2), channel_id=1, source_target_pairs={{0,2},{1,3},{4,6},{5,7},{8,10},{9,11},{12,14},{13,15},{16,18},{17,... | collective-permute-start | bytes 1671176 | tf_op jit(solution)/shard_map/ppermute | solution.py:76
  18.4 1.0 slice.67
  19.5 1.7 %collective-permute-start.11 = (bf16[1,4,2688]{2,1,0:T(4,128)(2,1)S(1)}, bf16[1,4,2688]{2,1,0:T(4,128)(2,1)S(1)}, u32[]{:S(2)}, u32[]{:S(2)}) collective-permute-start(bf16[1,4,2688]{2,1,0:T(4,128)(2,1)S(1)} %bitcast.113), channel_id=1, source_target_pairs={{0,3},{1,0},{2,1},{3,2},{4,7},{5,4},{6,5},{7,6},{8,11},{9,8},{10,9... | collective-permute-start | bytes 64520 | tf_op jit(solution)/shard_map/ppermute | solution.py:54
  24.0 0.7 broadcast_in_dim.126
  25.4 10.8 %collective-permute-start.8 = (bf16[128,2176]{0,1:T(8,128)(2,1)S(1)}, bf16[128,2176]{0,1:T(8,128)(2,1)S(1)}, u32[]{:S(2)}, u32[]{:S(2)}) collective-permute-start(bf16[128,2176]{0,1:T(8,128)(2,1)S(1)} %pad_maximum_fusion.2), channel_id=1, source_target_pairs={{0,1},{1,0},{2,3},{3,2},{4,5},{5,4},{6,7},{7,6},{8,9},{9,8},{10,11... | collective-permute-start | bytes 1671176 | tf_op jit(solution)/shard_map/ppermute | solution.py:37
  36.1 1.9 %collective-permute-done.10 = bf16[1,4,2688]{2,1,0:T(4,128)(2,1)S(1)} collective-permute-done((bf16[1,4,2688]{2,1,0:T(4,128)(2,1)S(1)}, bf16[1,4,2688]{2,1,0:T(4,128)(2,1)S(1)}, u32[]{:S(2)}, u32[]{:S(2)}) %collective-permute-start.10) | collective-permute-done | bytes 21536 | tf_op jit(solution)/shard_map/ppermute | solution.py:54
  38.3 0.6 gather_fusion
  39.0 3.5 %collective-permute-start.1 = (bf16[128,2176]{0,1:T(8,128)(2,1)S(1)}, bf16[128,2176]{0,1:T(8,128)(2,1)S(1)}, u32[]{:S(2)}, u32[]{:S(2)}) collective-permute-start(bf16[128,2176]{0,1:T(8,128)(2,1)S(1)} %collective-permute-done), channel_id=1, source_target_pairs={{0,4},{1,5},{2,6},{3,7},{4,8},{5,9},{6,10},{7,11},{8,12},{9,13},{1... | collective-permute-start | bytes 1671176 | tf_op jit(solution)/shard_map/ppermute | solution.py:70
  42.4 1.3 collective-permute-start.6
  43.7 0.7 broadcast_select_fusion.2
  44.5 1.5 collective-permute-start.12
  46.0 0.9 collective-permute-start.13
  46.9 15.4 %collective-permute-done.1 = bf16[128,2176]{0,1:T(8,128)(2,1)S(1)} collective-permute-done((bf16[128,2176]{0,1:T(8,128)(2,1)S(1)}, bf16[128,2176]{0,1:T(8,128)(2,1)S(1)}, u32[]{:S(2)}, u32[]{:S(2)}) %collective-permute-start.1) | collective-permute-done | bytes 557088 | tf_op jit(solution)/shard_map/ppermute | solution.py:70
  62.4 2.1 %collective-permute-start.2 = (bf16[128,2176]{0,1:T(8,128)(2,1)S(1)}, bf16[128,2176]{0,1:T(8,128)(2,1)S(1)}, u32[]{:S(2)}, u32[]{:S(2)}) collective-permute-start(bf16[128,2176]{0,1:T(8,128)(2,1)S(1)} %collective-permute-done), channel_id=1, source_target_pairs={{0,2},{1,3},{4,6},{5,7},{8,10},{9,11},{12,14},{13,15},{16,18},{17,... | collective-permute-start | bytes 1671176 | tf_op jit(solution)/shard_map/ppermute | solution.py:76
  64.5 1.3 collective-permute-start.3
  66.0 22.9 %collective-permute-done.2 = bf16[128,2176]{0,1:T(8,128)(2,1)S(1)} collective-permute-done((bf16[128,2176]{0,1:T(8,128)(2,1)S(1)}, bf16[128,2176]{0,1:T(8,128)(2,1)S(1)}, u32[]{:S(2)}, u32[]{:S(2)}) %collective-permute-start.2) | collective-permute-done | bytes 557088 | tf_op jit(solution)/shard_map/ppermute | solution.py:76
  88.9 4.3 %collective-permute-done.3 = bf16[128,2176]{0,1:T(8,128)(2,1)S(1)} collective-permute-done((bf16[128,2176]{0,1:T(8,128)(2,1)S(1)}, bf16[128,2176]{0,1:T(8,128)(2,1)S(1)}, u32[]{:S(2)}, u32[]{:S(2)}) %collective-permute-start.3) | collective-permute-done | bytes 557088 | tf_op jit(solution)/shard_map/ppermute | solution.py:76
  93.6 4.7 %collective-permute-start.14 = (bf16[4,4,2688]{2,1,0:T(4,128)(2,1)}, bf16[4,4,2688]{2,1,0:T(4,128)(2,1)}, u32[]{:S(2)}, u32[]{:S(2)}) collective-permute-start(bf16[4,4,2688]{2,1,0:T(4,128)(2,1)} %broadcast_select_fusion.2), channel_id=1, source_target_pairs={{0,12},{1,13},{2,14},{3,15},{4,0},{5,1},{6,2},{7,3},{8,4},{9,5},{1... | collective-permute-start | bytes 258056 | tf_op jit(solution)/shard_map/ppermute | solution.py:54
  100.5 1.9 %constant_dynamic-slice_fusion = (bf16[1152,1024]{0,1:T(8,128)(2,1)S(1)}, bf16[1152,1024]{0,1:T(8,128)(2,1)}) fusion(bf16[1280,2176]{0,1:T(8,128)(2,1)S(1)} %fusion.14, s32[]{:T(128)S(6)} %select_n.234, s32[]{:T(128)S(6)} %add.187), kind=kLoop, calls=%fused_computation.113 | loop fusion | bytes 9437192 | tf_op jit(solution)/shard_map/slice | solution.py:139
  102.4 1.1 compare_and_fusion
  103.5 3.7 %fusion.50 = f32[8,2,128]{2,1,0:T(2,128)S(1)} fusion(pred[128,1152]{0,1:T(8,128)(4,1)S(1)} %compare_and_fusion, bf16[1152,8,128,1]{0,2,3,1:T(8,128)(2,1)S(1)} %bitcast.105, bf16[128,8,2,128]{3,2,1,0:T(2,128)(2,1)S(1)} %reshape.322), kind=kOutput, calls=%fused_computation.121 | convolution fusion | flops 613418112 | bytes 3039232 | tf_op jit(solution)/shard_map/sub | solution.py:153
  107.2 6.3 %fusion.7 = bf16[8,128,2,128]{3,1,2,0:T(8,128)(2,1)S(1)} fusion(bf16[1152,8,128,1]{0,2,3,1:T(8,128)(2,1)} %bitcast.107, f32[8,2,128]{2,1,0:T(2,128)S(1)} %fusion.50, pred[128,1152]{0,1:T(8,128)(4,1)} %copy-done.3, bf16[1152,8,128,1]{0,2,3,1:T(8,128)(2,1)S(1)} %bitcast.106, bf16[128,8,2,128]{3,2,1,0:T(2,128)(2,1)S(1)} %reshape.322), kind=kOutput, calls=%fused_computation.18 | convolution fusion | flops 1220021376 | bytes 5922816 | tf_op jit(solution)/shard_map/hgqk,khd->qhgd/dot_general | solution.py:155
  114.9 1.4 collective-permute-start.17
  116.4 1.3 pad_maximum_fusion.3
  117.6 1.0 gather_fusion.1
  118.8 0.7 gather_fusion.2
  120.0 2.5 %collective-permute-start.19 = (bf16[4,4,2048]{2,1,0:T(4,128)(2,1)S(1)}, bf16[4,4,2048]{2,1,0:T(4,128)(2,1)S(1)}, u32[]{:S(2)}, u32[]{:S(2)}) collective-permute-start(bf16[4,4,2048]{2,1,0:T(4,128)(2,1)S(1)} %broadcast_select_fusion.3), channel_id=1, source_target_pairs={{0,8},{1,9},{2,10},{3,11},{4,12},{5,13},{6,14},{7,15},{8,0},{9,1},... | collective-permute-start | bytes 196616 | tf_op jit(solution)/shard_map/ppermute | solution.py:54
  122.5 1.3 collective-permute-start.20
  124.0 2.4 %collective-permute-done.18 = bf16[4,4,2048]{2,1,0:T(4,128)(2,1)S(1)} collective-permute-done((bf16[4,4,2048]{2,1,0:T(4,128)(2,1)S(1)}, bf16[4,4,2048]{2,1,0:T(4,128)(2,1)S(1)}, u32[]{:S(2)}, u32[]{:S(2)}) %collective-permute-start.18) | collective-permute-done | bytes 65568 | tf_op jit(solution)/shard_map/ppermute | solution.py:54
  126.3 2.3 %collective-permute-done.19 = bf16[4,4,2048]{2,1,0:T(4,128)(2,1)S(1)} collective-permute-done((bf16[4,4,2048]{2,1,0:T(4,128)(2,1)S(1)}, bf16[4,4,2048]{2,1,0:T(4,128)(2,1)S(1)}, u32[]{:S(2)}, u32[]{:S(2)}) %collective-permute-start.19) | collective-permute-done | bytes 65568 | tf_op jit(solution)/shard_map/ppermute | solution.py:54
  128.8 0.9 gather_fusion.3
  129.9 6.5 %multiply_reduce_fusion = (f32[64]{0:T(128)S(1)}, f32[64,2688]{1,0:T(8,128)S(1)}) fusion(bf16[2048,2688]{1,0:T(8,128)(2,1)} %all-gather.2.cloned.1.call-done, bf16[64,2048]{1,0:T(8,128)(2,1)S(1)} %gather.51, pred[64]{0:T(512)(128)(4,1)S(1)} %copy-done.7, bf16[64,2688]{1,0:T(8,128)(2,1)S(1)} %gather.46), kind=kOutput, calls=%fused_computation.33 | convolution fusion | flops 705634240 | bytes 12304704 | tf_op jit(solution)/shard_map/dot_general | solution.py:161
  136.4 4.5 %fusion.53 = (f32[64]{0:T(128)S(1)}, f32[64,1024]{1,0:T(8,128)S(1)}) fusion(bf16[1024,2688]{1,0:T(8,128)(2,1)} %param.14, f32[64,2688]{1,0:T(8,128)S(1)} %get-tuple-element.23, f32[2688]{0:T(1024)S(1)} %copy-done.4, f32[64]{0:T(128)S(1)} %add_rsqrt_fusion), kind=kOutput, calls=%fused_computation.122 | convolution fusion | flops 352903104 | bytes 6466560 | tf_op jit(solution)/shard_map/dot_general | solution.py:168
  141.4 1.1 collective-permute-start.22
  142.5 1.4 collective-permute-start.23
  143.9 2.5 %fusion.6 = bf16[128,2688]{1,0:T(8,128)(2,1)} fusion(bf16[128,2048]{0,1:T(8,128)(2,1)S(1)} %bitcast.104, bf16[2048,2688]{1,0:T(8,128)(2,1)S(1)} %copy-done, bf16[128,2688]{1,0:T(8,128)(2,1)S(1)} %copy-done.1), kind=kOutput, calls=%fused_computation.16 | convolution fusion | flops 1410318336 | bytes 12910592 | tf_op jit(solution)/shard_map/dot_general | solution.py:165
  146.5 0.7 gather_fusion.4
  147.2 1.4 collective-permute-start.24
  148.6 1.9 %collective-permute-start.25 = (f32[4,3,64]{2,1,0:T(4,128)S(1)}, f32[4,3,64]{2,1,0:T(4,128)S(1)}, u32[]{:S(2)}, u32[]{:S(2)}) collective-permute-start(f32[4,3,64]{2,1,0:T(4,128)S(1)} %broadcast_select_fusion.4), channel_id=1, source_target_pairs={{0,8},{1,9},{2,10},{3,11},{4,12},{5,13},{6,14},{7,15},{8,0},{9,1},... | collective-permute-start | bytes 9224 | tf_op jit(solution)/shard_map/ppermute | solution.py:54
  150.5 0.6 collective-permute-start.26
  151.1 1.5 collective-permute-done.24
  153.2 0.9 collective-permute-done.26
  154.1 0.7 gather_fusion.5
  155.0 0.8 broadcast_subtract_fusion
  (111 shorter events, 10.9 us)
Async XLA Ops:
  7.2 15.8 %copy-start.13 = (s32[64]{0:T(128)S(1)}, s32[64]{0:T(128)}, u32[]{:S(2)}) copy-start(s32[64]{0:T(128)} %param.15) | copy-start | bytes 772
  7.2 16.4 %copy-start.2 = (bf16[128,2048]{1,0:T(8,128)(2,1)S(1)}, bf16[128,2048]{1,0:T(8,128)(2,1)}, u32[]{:S(2)}) copy-start(bf16[128,2048]{1,0:T(8,128)(2,1)} %param.8) | copy-start | bytes 1572868
  7.2 122.7 %all-gather.2.cloned.1.call-start = ((), (), s32[]{:S(2)}) async-start(), calls=%async_computation | async-start | bytes 11698176 | tf_op jit(solution)/shard_map/all_gather | solution.py:121
  10.0 29.0 %collective-permute-start = (bf16[128,2176]{0,1:T(8,128)(2,1)S(1)}, bf16[128,2176]{0,1:T(8,128)(2,1)S(1)}, u32[]{:S(2)}, u32[]{:S(2)}) collective-permute-start(bf16[128,2176]{0,1:T(8,128)(2,1)S(1)} %pad_maximum_fusion.2), channel_id=1, source_target_pairs={{0,4},{1,5},{2,6},{3,7},{4,8},{5,9},{6,10},{7,11},{8,12},{9,13},{1... | collective-permute-start | bytes 1671176 | tf_op jit(solution)/shard_map/ppermute | solution.py:70
  14.9 31.1 %collective-permute-start.5 = (bf16[128,2176]{0,1:T(8,128)(2,1)S(1)}, bf16[128,2176]{0,1:T(8,128)(2,1)S(1)}, u32[]{:S(2)}, u32[]{:S(2)}) collective-permute-start(bf16[128,2176]{0,1:T(8,128)(2,1)S(1)} %pad_maximum_fusion.2), channel_id=1, source_target_pairs={{0,2},{1,3},{4,6},{5,7},{8,10},{9,11},{12,14},{13,15},{16,18},{17,... | collective-permute-start | bytes 1671176 | tf_op jit(solution)/shard_map/ppermute | solution.py:76
  19.4 6.0 %collective-permute-start.9 = (bf16[1,4,2688]{2,1,0:T(4,128)(2,1)S(1)}, bf16[1,4,2688]{2,1,0:T(4,128)(2,1)S(1)}, u32[]{:S(2)}, u32[]{:S(2)}) collective-permute-start(bf16[1,4,2688]{2,1,0:T(4,128)(2,1)S(1)} %bitcast.111), channel_id=1, source_target_pairs={{0,1},{1,2},{2,3},{3,0},{4,5},{5,6},{6,7},{7,4},{8,9},{9,10},{10,1... | collective-permute-start | bytes 64520 | tf_op jit(solution)/shard_map/ppermute | solution.py:54
  19.4 18.6 %collective-permute-start.10 = (bf16[1,4,2688]{2,1,0:T(4,128)(2,1)S(1)}, bf16[1,4,2688]{2,1,0:T(4,128)(2,1)S(1)}, u32[]{:S(2)}, u32[]{:S(2)}) collective-permute-start(bf16[1,4,2688]{2,1,0:T(4,128)(2,1)S(1)} %bitcast.112), channel_id=1, source_target_pairs={{0,2},{1,3},{2,0},{3,1},{4,6},{5,7},{6,4},{7,5},{8,10},{9,11},{10,... | collective-permute-start | bytes 64520 | tf_op jit(solution)/shard_map/ppermute | solution.py:54
  19.5 18.7 %collective-permute-start.11 = (bf16[1,4,2688]{2,1,0:T(4,128)(2,1)S(1)}, bf16[1,4,2688]{2,1,0:T(4,128)(2,1)S(1)}, u32[]{:S(2)}, u32[]{:S(2)}) collective-permute-start(bf16[1,4,2688]{2,1,0:T(4,128)(2,1)S(1)} %bitcast.113), channel_id=1, source_target_pairs={{0,3},{1,0},{2,1},{3,2},{4,7},{5,4},{6,5},{7,6},{8,11},{9,8},{10,9... | collective-permute-start | bytes 64520 | tf_op jit(solution)/shard_map/ppermute | solution.py:54
  22.4 43.6 %copy-start.6 = (s32[1024]{0:T(1024)}, s32[1024]{0:T(1024)S(1)}, u32[]{:S(2)}) copy-start(s32[1024]{0:T(1024)S(1)} %pad_clamp_fusion.1) | copy-start | bytes 12292
  25.4 74.7 %collective-permute-start.8 = (bf16[128,2176]{0,1:T(8,128)(2,1)S(1)}, bf16[128,2176]{0,1:T(8,128)(2,1)S(1)}, u32[]{:S(2)}, u32[]{:S(2)}) collective-permute-start(bf16[128,2176]{0,1:T(8,128)(2,1)S(1)} %pad_maximum_fusion.2), channel_id=1, source_target_pairs={{0,1},{1,0},{2,3},{3,2},{4,5},{5,4},{6,7},{7,6},{8,9},{9,8},{10,11... | collective-permute-start | bytes 1671176 | tf_op jit(solution)/shard_map/ppermute | solution.py:37
  39.0 23.4 %collective-permute-start.1 = (bf16[128,2176]{0,1:T(8,128)(2,1)S(1)}, bf16[128,2176]{0,1:T(8,128)(2,1)S(1)}, u32[]{:S(2)}, u32[]{:S(2)}) collective-permute-start(bf16[128,2176]{0,1:T(8,128)(2,1)S(1)} %collective-permute-done), channel_id=1, source_target_pairs={{0,4},{1,5},{2,6},{3,7},{4,8},{5,9},{6,10},{7,11},{8,12},{9,13},{1... | collective-permute-start | bytes 1671176 | tf_op jit(solution)/shard_map/ppermute | solution.py:70
  42.4 22.0 %collective-permute-start.6 = (bf16[128,2176]{0,1:T(8,128)(2,1)S(1)}, bf16[128,2176]{0,1:T(8,128)(2,1)S(1)}, u32[]{:S(2)}, u32[]{:S(2)}) collective-permute-start(bf16[128,2176]{0,1:T(8,128)(2,1)S(1)} %collective-permute-done), channel_id=1, source_target_pairs={{2,0},{3,1},{6,4},{7,5},{10,8},{11,9},{14,12},{15,13},{18,16},{19,... | collective-permute-start | bytes 1671176 | tf_op jit(solution)/shard_map/ppermute | solution.py:76
  44.5 70.4 %collective-permute-start.12 = (bf16[4,4,2688]{2,1,0:T(4,128)(2,1)}, bf16[4,4,2688]{2,1,0:T(4,128)(2,1)}, u32[]{:S(2)}, u32[]{:S(2)}) collective-permute-start(bf16[4,4,2688]{2,1,0:T(4,128)(2,1)} %broadcast_select_fusion.2), channel_id=1, source_target_pairs={{0,4},{1,5},{2,6},{3,7},{4,8},{5,9},{6,10},{7,11},{8,12},{9,13},{1... | collective-permute-start | bytes 258056 | tf_op jit(solution)/shard_map/ppermute | solution.py:54
  46.0 70.3 %collective-permute-start.13 = (bf16[4,4,2688]{2,1,0:T(4,128)(2,1)}, bf16[4,4,2688]{2,1,0:T(4,128)(2,1)}, u32[]{:S(2)}, u32[]{:S(2)}) collective-permute-start(bf16[4,4,2688]{2,1,0:T(4,128)(2,1)} %broadcast_select_fusion.2), channel_id=1, source_target_pairs={{0,8},{1,9},{2,10},{3,11},{4,12},{5,13},{6,14},{7,15},{8,0},{9,1},... | collective-permute-start | bytes 258056 | tf_op jit(solution)/shard_map/ppermute | solution.py:54
  62.4 26.5 %collective-permute-start.2 = (bf16[128,2176]{0,1:T(8,128)(2,1)S(1)}, bf16[128,2176]{0,1:T(8,128)(2,1)S(1)}, u32[]{:S(2)}, u32[]{:S(2)}) collective-permute-start(bf16[128,2176]{0,1:T(8,128)(2,1)S(1)} %collective-permute-done), channel_id=1, source_target_pairs={{0,2},{1,3},{4,6},{5,7},{8,10},{9,11},{12,14},{13,15},{16,18},{17,... | collective-permute-start | bytes 1671176 | tf_op jit(solution)/shard_map/ppermute | solution.py:76
  64.5 28.8 %collective-permute-start.3 = (bf16[128,2176]{0,1:T(8,128)(2,1)S(1)}, bf16[128,2176]{0,1:T(8,128)(2,1)S(1)}, u32[]{:S(2)}, u32[]{:S(2)}) collective-permute-start(bf16[128,2176]{0,1:T(8,128)(2,1)S(1)} %collective-permute-done.1), channel_id=1, source_target_pairs={{2,0},{3,1},{6,4},{7,5},{10,8},{11,9},{14,12},{15,13},{18,16},{19,... | collective-permute-start | bytes 1671176 | tf_op jit(solution)/shard_map/ppermute | solution.py:76
  88.9 4.7 %collective-permute-start.7 = (bf16[2,128,2176]{1,2,0:T(8,128)(2,1)S(1)}, bf16[2,128,2176]{1,2,0:T(8,128)(2,1)S(1)}, u32[]{:S(2)}, u32[]{:S(2)}) collective-permute-start(bf16[2,128,2176]{1,2,0:T(8,128)(2,1)S(1)} %pad_maximum_fusion.1), channel_id=1, source_target_pairs={{0,1},{1,0},{2,3},{3,2},{4,5},{5,4},{6,7},{7,6},{8,9},{9,8},{10,11... | collective-permute-start | bytes 3342344 | tf_op jit(solution)/shard_map/ppermute | solution.py:37
  93.4 5.0 %collective-permute-start.4 = (bf16[2,128,2176]{1,2,0:T(8,128)(2,1)S(1)}, bf16[2,128,2176]{1,2,0:T(8,128)(2,1)S(1)}, u32[]{:S(2)}, u32[]{:S(2)}) collective-permute-start(bf16[2,128,2176]{1,2,0:T(8,128)(2,1)S(1)} %pad_maximum_fusion), channel_id=1, source_target_pairs={{0,1},{1,0},{2,3},{3,2},{4,5},{5,4},{6,7},{7,6},{8,9},{9,8},{10,11... | collective-permute-start | bytes 3342344 | tf_op jit(solution)/shard_map/ppermute | solution.py:37
  93.6 22.7 %collective-permute-start.14 = (bf16[4,4,2688]{2,1,0:T(4,128)(2,1)}, bf16[4,4,2688]{2,1,0:T(4,128)(2,1)}, u32[]{:S(2)}, u32[]{:S(2)}) collective-permute-start(bf16[4,4,2688]{2,1,0:T(4,128)(2,1)} %broadcast_select_fusion.2), channel_id=1, source_target_pairs={{0,12},{1,13},{2,14},{3,15},{4,0},{5,1},{6,2},{7,3},{8,4},{9,5},{1... | collective-permute-start | bytes 258056 | tf_op jit(solution)/shard_map/ppermute | solution.py:54
  100.5 1.9 %copy-start.5 = (pred[1152]{0:T(1024)(128)(4,1)S(1)}, pred[1152]{0:T(1024)(128)(4,1)}, u32[]{:S(2)}) copy-start(pred[1152]{0:T(1024)(128)(4,1)} %broadcast_compare_fusion) | copy-start | bytes 3460
  100.5 1.9 %copy-start.8 = (s32[128]{0:T(128)S(1)}, s32[128]{0:T(128)}, u32[]{:S(2)}) copy-start(s32[128]{0:T(128)} %param.10) | copy-start | bytes 1540
  100.5 1.9 %copy-start.11 = (s32[128]{0:T(128)S(1)}, s32[128]{0:T(128)}, u32[]{:S(2)}) copy-start(s32[128]{0:T(128)} %get-tuple-element.26) | copy-start | bytes 1540
  100.5 1.9 %copy-start.12 = (s32[128]{0:T(128)S(1)}, s32[128]{0:T(128)}, u32[]{:S(2)}) copy-start(s32[128]{0:T(128)} %get-tuple-element.27) | copy-start | bytes 1540
  103.5 3.7 %copy-start.3 = (pred[128,1152]{0,1:T(8,128)(4,1)}, pred[128,1152]{0,1:T(8,128)(4,1)S(1)}, u32[]{:S(2)}) copy-start(pred[128,1152]{0,1:T(8,128)(4,1)S(1)} %compare_and_fusion) | copy-start | bytes 442372
  114.4 15.4 %copy-start.7 = (pred[64]{0:T(512)(128)(4,1)S(1)}, pred[64]{0:T(512)(128)(4,1)}, u32[]{:S(2)}) copy-start(pred[64]{0:T(512)(128)(4,1)} %broadcast_in_dim.126) | copy-start | bytes 196
  114.5 4.2 %collective-permute-start.15 = (bf16[1,4,2048]{2,1,0:T(4,128)(2,1)S(1)}, bf16[1,4,2048]{2,1,0:T(4,128)(2,1)S(1)}, u32[]{:S(2)}, u32[]{:S(2)}) collective-permute-start(bf16[1,4,2048]{2,1,0:T(4,128)(2,1)S(1)} %bitcast.117), channel_id=1, source_target_pairs={{0,1},{1,2},{2,3},{3,0},{4,5},{5,6},{6,7},{7,4},{8,9},{9,10},{10,1... | collective-permute-start | bytes 49160 | tf_op jit(solution)/shard_map/ppermute | solution.py:54
  114.8 3.9 %collective-permute-start.16 = (bf16[1,4,2048]{2,1,0:T(4,128)(2,1)S(1)}, bf16[1,4,2048]{2,1,0:T(4,128)(2,1)S(1)}, u32[]{:S(2)}, u32[]{:S(2)}) collective-permute-start(bf16[1,4,2048]{2,1,0:T(4,128)(2,1)S(1)} %bitcast.118), channel_id=1, source_target_pairs={{0,2},{1,3},{2,0},{3,1},{4,6},{5,7},{6,4},{7,5},{8,10},{9,11},{10,... | collective-permute-start | bytes 49160 | tf_op jit(solution)/shard_map/ppermute | solution.py:54
  114.9 3.8 %collective-permute-start.17 = (bf16[1,4,2048]{2,1,0:T(4,128)(2,1)S(1)}, bf16[1,4,2048]{2,1,0:T(4,128)(2,1)S(1)}, u32[]{:S(2)}, u32[]{:S(2)}) collective-permute-start(bf16[1,4,2048]{2,1,0:T(4,128)(2,1)S(1)} %bitcast.119), channel_id=1, source_target_pairs={{0,3},{1,0},{2,1},{3,2},{4,7},{5,4},{6,5},{7,6},{8,11},{9,8},{10,9... | collective-permute-start | bytes 49160 | tf_op jit(solution)/shard_map/ppermute | solution.py:54
  119.6 6.7 %collective-permute-start.18 = (bf16[4,4,2048]{2,1,0:T(4,128)(2,1)S(1)}, bf16[4,4,2048]{2,1,0:T(4,128)(2,1)S(1)}, u32[]{:S(2)}, u32[]{:S(2)}) collective-permute-start(bf16[4,4,2048]{2,1,0:T(4,128)(2,1)S(1)} %broadcast_select_fusion.3), channel_id=1, source_target_pairs={{0,4},{1,5},{2,6},{3,7},{4,8},{5,9},{6,10},{7,11},{8,12},{9,13},{1... | collective-permute-start | bytes 196616 | tf_op jit(solution)/shard_map/ppermute | solution.py:54
  120.0 8.6 %collective-permute-start.19 = (bf16[4,4,2048]{2,1,0:T(4,128)(2,1)S(1)}, bf16[4,4,2048]{2,1,0:T(4,128)(2,1)S(1)}, u32[]{:S(2)}, u32[]{:S(2)}) collective-permute-start(bf16[4,4,2048]{2,1,0:T(4,128)(2,1)S(1)} %broadcast_select_fusion.3), channel_id=1, source_target_pairs={{0,8},{1,9},{2,10},{3,11},{4,12},{5,13},{6,14},{7,15},{8,0},{9,1},... | collective-permute-start | bytes 196616 | tf_op jit(solution)/shard_map/ppermute | solution.py:54
  122.5 6.1 %collective-permute-start.20 = (bf16[4,4,2048]{2,1,0:T(4,128)(2,1)S(1)}, bf16[4,4,2048]{2,1,0:T(4,128)(2,1)S(1)}, u32[]{:S(2)}, u32[]{:S(2)}) collective-permute-start(bf16[4,4,2048]{2,1,0:T(4,128)(2,1)S(1)} %broadcast_select_fusion.3), channel_id=1, source_target_pairs={{0,12},{1,13},{2,14},{3,15},{4,0},{5,1},{6,2},{7,3},{8,4},{9,5},{1... | collective-permute-start | bytes 196616 | tf_op jit(solution)/shard_map/ppermute | solution.py:54
  129.8 6.6 %copy-start.4 = (f32[2688]{0:T(1024)S(1)}, f32[2688]{0:T(1024)}, u32[]{:S(2)}) copy-start(f32[2688]{0:T(1024)} %param.12) | copy-start | bytes 32260
  129.9 14.0 %copy-start = (bf16[2048,2688]{1,0:T(8,128)(2,1)S(1)}, bf16[2048,2688]{1,0:T(8,128)(2,1)}, u32[]{:S(2)}) copy-start(bf16[2048,2688]{1,0:T(8,128)(2,1)} %all-gather.2.cloned.1.call-done) | copy-start | bytes 33030148
  136.4 4.5 %copy-start.10 = (s32[64]{0:T(128)S(1)}, s32[64]{0:T(128)}, u32[]{:S(2)}) copy-start(s32[64]{0:T(128)} %broadcast_subtract_fusion.1) | copy-start | bytes 772
  136.4 7.5 %copy-start.1 = (bf16[128,2688]{1,0:T(8,128)(2,1)S(1)}, bf16[128,2688]{1,0:T(8,128)(2,1)}, u32[]{:S(2)}) copy-start(bf16[128,2688]{1,0:T(8,128)(2,1)} %param.11) | copy-start | bytes 2064388
  141.2 5.2 %collective-permute-start.21 = (f32[1,3,64]{2,1,0:T(4,128)S(1)}, f32[1,3,64]{2,1,0:T(4,128)S(1)}, u32[]{:S(2)}, u32[]{:S(2)}) collective-permute-start(f32[1,3,64]{2,1,0:T(4,128)S(1)} %get-tuple-element.21), channel_id=1, source_target_pairs={{0,1},{1,2},{2,3},{3,0},{4,5},{5,6},{6,7},{7,4},{8,9},{9,10},{10,1... | collective-permute-start | bytes 2312 | tf_op jit(solution)/shard_map/ppermute | solution.py:54
  141.4 5.1 %collective-permute-start.22 = (f32[1,3,64]{2,1,0:T(4,128)S(1)}, f32[1,3,64]{2,1,0:T(4,128)S(1)}, u32[]{:S(2)}, u32[]{:S(2)}) collective-permute-start(f32[1,3,64]{2,1,0:T(4,128)S(1)} %get-tuple-element.21), channel_id=1, source_target_pairs={{0,2},{1,3},{2,0},{3,1},{4,6},{5,7},{6,4},{7,5},{8,10},{9,11},{10,... | collective-permute-start | bytes 2312 | tf_op jit(solution)/shard_map/ppermute | solution.py:54
  142.5 3.9 %collective-permute-start.23 = (f32[1,3,64]{2,1,0:T(4,128)S(1)}, f32[1,3,64]{2,1,0:T(4,128)S(1)}, u32[]{:S(2)}, u32[]{:S(2)}) collective-permute-start(f32[1,3,64]{2,1,0:T(4,128)S(1)} %get-tuple-element.21), channel_id=1, source_target_pairs={{0,3},{1,0},{2,1},{3,2},{4,7},{5,4},{6,5},{7,6},{8,11},{9,8},{10,9... | collective-permute-start | bytes 2312 | tf_op jit(solution)/shard_map/ppermute | solution.py:54
  143.9 10.9 %copy-start.9 = (pred[16]{0:T(512)(128)(4,1)S(1)}, pred[16]{0:T(512)(128)(4,1)}, u32[]{:S(2)}) copy-start(pred[16]{0:T(512)(128)(4,1)} %broadcast_in_dim.140) | copy-start | bytes 52
  147.2 5.5 %collective-permute-start.24 = (f32[4,3,64]{2,1,0:T(4,128)S(1)}, f32[4,3,64]{2,1,0:T(4,128)S(1)}, u32[]{:S(2)}, u32[]{:S(2)}) collective-permute-start(f32[4,3,64]{2,1,0:T(4,128)S(1)} %broadcast_select_fusion.4), channel_id=1, source_target_pairs={{0,4},{1,5},{2,6},{3,7},{4,8},{5,9},{6,10},{7,11},{8,12},{9,13},{1... | collective-permute-start | bytes 9224 | tf_op jit(solution)/shard_map/ppermute | solution.py:54
  148.6 4.6 %collective-permute-start.25 = (f32[4,3,64]{2,1,0:T(4,128)S(1)}, f32[4,3,64]{2,1,0:T(4,128)S(1)}, u32[]{:S(2)}, u32[]{:S(2)}) collective-permute-start(f32[4,3,64]{2,1,0:T(4,128)S(1)} %broadcast_select_fusion.4), channel_id=1, source_target_pairs={{0,8},{1,9},{2,10},{3,11},{4,12},{5,13},{6,14},{7,15},{8,0},{9,1},... | collective-permute-start | bytes 9224 | tf_op jit(solution)/shard_map/ppermute | solution.py:54
  150.5 3.7 %collective-permute-start.26 = (f32[4,3,64]{2,1,0:T(4,128)S(1)}, f32[4,3,64]{2,1,0:T(4,128)S(1)}, u32[]{:S(2)}, u32[]{:S(2)}) collective-permute-start(f32[4,3,64]{2,1,0:T(4,128)S(1)} %broadcast_select_fusion.4), channel_id=1, source_target_pairs={{0,12},{1,13},{2,14},{3,15},{4,0},{5,1},{6,2},{7,3},{8,4},{9,5},{1... | collective-permute-start | bytes 9224 | tf_op jit(solution)/shard_map/ppermute | solution.py:54
Sparse Core Ops, SparseCore 0:
  10.3 114.3 all-gather.1

commit v8 on v7

--- a/solution.py
+++ b/solution.py
@@ -1,3 +1,5 @@
+import functools
+
 import jax
 import jax.numpy as jnp
 import numpy as np
@@ -14,6 +16,7 @@
 LANES = 128
 CORES = 2
 SEQ = ("chip", "core")
+RING_CHIPS = 8
 
 
 score_scale = 168.0 ** (-0.5)
@@ -100,12 +103,65 @@
     return window[:, :kv_width], window[:, kv_width].astype(jnp.int32)
 
 
+def chip_cycle(mesh):
+    chips = mesh.shape["seq"] // CORES
+    try:
+        coords = [tuple(d.coords) for d in np.asarray(mesh.devices)[0, ::CORES]]
+        moving = [a for a in range(len(coords[0])) if coords[0][a] != coords[1][a]][0]
+        fast = 1
+        while fast < chips and coords[fast][moving] != coords[0][moving]:
+            fast += 1
+    except Exception:
+        fast = 2
+    slow = chips // fast
+    if chips % fast or (slow % 2 and fast % 2) or fast < 2:
+        return list(range(chips))
+    if slow % 2:
+        path = [c for c in range(fast)]
+        for c in range(fast - 1, -1, -1):
+            rows = range(1, slow) if (fast - 1 - c) % 2 == 0 else range(slow - 1, 0, -1)
+            path += [r * fast + c for r in rows]
+        return path
+    path = [r * fast for r in range(slow)]
+    for r in range(slow - 1, -1, -1):
+        cols = range(1, fast) if (slow - 1 - r) % 2 == 0 else range(fast - 1, 0, -1)
+        path += [r * fast + c for c in cols]
+    return path
+
+
+def ring_gather(piece, cycle):
+    chips = len(cycle)
+    count = seq_count()
+    position = [0] * chips
+    for p, k in enumerate(cycle):
+        position[k] = p
+    ahead = {k: cycle[(position[k] + 1) % chips] for k in range(chips)}
+    behind = {k: cycle[(position[k] - 1) % chips] for k in range(chips)}
+    forward = [(s, ahead[s // CORES] * CORES + s % CORES) for s in range(count)]
+    backward = [(s, behind[s // CORES] * CORES + s % CORES) for s in range(count)]
+    me = jnp.asarray(position, jnp.int32)[lax.axis_index("chip")]
+    order = jnp.asarray(cycle, jnp.int32)
+    slots, sources = [piece], [order[me]]
+    current = piece
+    for step in range(1, chips // 2 + 1):
+        current = lax.ppermute(current, SEQ, forward)
+        slots.append(current)
+        sources.append(order[(me - step) % chips])
+    current = piece
+    for step in range(1, (chips - 1) // 2 + 1):
+        current = lax.ppermute(current, SEQ, backward)
+        slots.append(current)
+        sources.append(order[(me + step) % chips])
+    return slots, sources
+
+
 def normalize(hidden, norm_gain):
     mean_square = jnp.mean(hidden * hidden, axis=1, keepdims=True)
     return (hidden * lax.rsqrt(mean_square + 1e-06) * norm_gain[None, :]).astype(jnp.bfloat16)
 
 
 def local(
+    cycle,
     queries, joined_keys_values, segment_ids, residual, norm_gain, out_proj, head_weight, next_ids
 ):
     token_rows = queries.shape[0]
@@ -118,7 +174,24 @@
     first_core = core == 0
     first_row = my_index * token_rows
 
-    full_proj = lax.all_gather(out_proj, SEQ, axis=0, tiled=True)
+    if len(cycle) <= RING_CHIPS:
+        slots, sources = ring_gather(out_proj, cycle)
+        partner_slots = [swap_cores(s) for s in slots]
+        chip_rows = CORES * out_proj.shape[0]
+        full_proj = jnp.concatenate(
+            [in_core_order(m, t, first_core) for m, t in zip(slots, partner_slots)], 0
+        )
+
+        def slot_columns(rows_of_context):
+            return jnp.concatenate(
+                [lax.dynamic_slice_in_dim(rows_of_context, s * chip_rows, chip_rows, 1) for s in sources], 1
+            )
+
+    else:
+        full_proj = lax.all_gather(out_proj, SEQ, axis=0, tiled=True)
+
+        def slot_columns(rows_of_context):
+            return rows_of_context
     score_count = SCORE_DEV
     stride = token_rows // score_count
     scored_residual = gather_rows(residual.reshape(score_count, stride, width)[:, stride - 1, :])
@@ -159,10 +232,10 @@
 
     scored_context = gather_rows(context.reshape(score_count, stride, -1)[:, stride - 1, :])
     picked = scored_residual.astype(jnp.float32) + jnp.dot(
-        scored_context, full_proj, preferred_element_type=jnp.float32
+        slot_columns(scored_context), full_proj, preferred_element_type=jnp.float32
     )
     normed = normalize(picked, norm_gain)
-    projected = jnp.dot(context, full_proj, preferred_element_type=jnp.float32)
+    projected = jnp.dot(slot_columns(context), full_proj, preferred_element_type=jnp.float32)
     hidden = residual.astype(jnp.float32) + projected
     layer_out = hidden.astype(jnp.bfloat16)
     logits = lax.dot_general(
@@ -205,4 +278,5 @@
         P("parts"),
     )
     out_specs = (P(rows, None), P("parts", SEQ), P(rows))
-    return jax.shard_map(local, mesh=fine, in_specs=in_specs, out_specs=out_specs, check_vma=False)
+    cycle = chip_cycle(mesh)
+    return jax.shard_map(functools.partial(local, cycle), mesh=fine, in_specs=in_specs, out_specs=out_specs, check_vma=False)

time: 164 us -> 187 us (1.14)
  other arithmetic: 10.5 us -> 30.9 us
  waiting for transfers between devices: 53.2 us -> 67 us
  starting transfers between devices: 49 us -> 36.9 us
    ppermute x0 -> x7, waiting for transfers between devices: none -> 35 us  [the longest x4 25.4 us: ring_gather(): current = lax.ppermute(current, SEQ, forward)]
    unnamed x4 -> x12, other arithmetic: 1.49 us -> 21 us
    ppermute x4, waiting for transfers between devices: 27.3 us -> 9.93 us  [across_pair(): return lax.ppermute(value, SEQ, pairs)]
    ppermute x2, waiting for transfers between devices: 15.4 us -> 3.62 us  [shift_chips(): lax.ppermute(value, SEQ, [(s, s + step) for s in range(count - step)])]
    ppermute x3 -> x11, starting transfers between devices: 10.9 us -> 2.11 us  [swap_cores(): return lax.ppermute(value, 'core', [(0, 1), (1, 0)])]
    ppermute x18, waiting for transfers between devices: 9.72 us -> 16.4 us  [gather_rows(): received.append(lax.ppermute(data, SEQ, pairs))]
    ppermute x18, starting transfers between devices: 21.6 us -> 15.9 us  [gather_rows(): received.append(lax.ppermute(data, SEQ, pairs))]
    dot_general x2, matrix products: 9.03 us -> 13 us  [the longest x1 6.67 us: local(): jnp.dot(slot_columns(context), full_proj, preferred_element_type=jnp.floa...]
  transfers between devices with their start and end apart: 28 -> 42, of which waited for: 10 -> 20; matrix products, arithmetic and copies ran while one was open for 20% -> 29% of each run, Pallas kernels for 0% -> 0%
where the time goes in v8:
time: 187 us; the launch traced here: 186 us
  waiting for transfers between devices  67 us (36%)
  starting transfers between devices  36.9 us (20%)
  other arithmetic  30.9 us (17%)
  matrix products  25 us (13%)
  local copies, waits for them, and re-layouts  13.2 us (7%)
  between operations  13 us (7%)
    ppermute x4, waiting for transfers between devices, ring_gather(): current = lax.ppermute(current, SEQ, forward)  25.4 us
    unnamed x12, other arithmetic  21 us
    ppermute x18, waiting for transfers between devices, gather_rows(): received.append(lax.ppermute(data, SEQ, pairs))  16.4 us
    ppermute x18, starting transfers between devices, gather_rows(): received.append(lax.ppermute(data, SEQ, pairs))  15.9 us
    ppermute x4, starting transfers between devices, across_pair(): return lax.ppermute(value, SEQ, pairs)  10.6 us
    ppermute x4, waiting for transfers between devices, across_pair(): return lax.ppermute(value, SEQ, pairs)  9.93 us
    ppermute x3, waiting for transfers between devices, ring_gather(): current = lax.ppermute(current, SEQ, backward)  9.67 us
    dot_general x1, matrix products, local(): jnp.dot(slot_columns(context), full_proj, preferred_element_type=jnp.floa...  6.67 us
  transfers between devices with their start and end apart: 42, of which 20 were waited for; matrix products, arithmetic and copies ran while one was open for 29% of the time, Pallas kernels for 0%

profile of v8, /device:TPU:0, one launch (start us, length us, event | category | flops | bytes accessed | tf_op | source)
XLA Modules:
  0.0 186.0 jit_solution(17112451128889617885)
XLA Ops:
  1.7 2.5 %collective-permute-start.26 = (bf16[1,4,2688]{2,1,0:T(4,128)(2,1)S(1)}, bf16[1,4,2688]{2,1,0:T(4,128)(2,1)S(1)}, u32[]{:S(2)}, u32[]{:S(2)}) collective-permute-start(bf16[1,4,2688]{2,1,0:T(4,128)(2,1)S(1)} %bitcast.130), channel_id=1, source_target_pairs={{0,3},{1,0},{2,1},{3,2},{4,7},{5,4},{6,5},{7,6},{8,11},{9,8},{10,9... | collective-permute-start | bytes 64520 | tf_op jit(solution)/shard_map/ppermute | solution.py:57
  5.6 1.3 copy.17
  7.8 3.5 %collective-permute-start = (bf16[128,2176]{0,1:T(8,128)(2,1)}, bf16[128,2176]{0,1:T(8,128)(2,1)S(1)}, u32[]{:S(2)}, u32[]{:S(2)}) collective-permute-start(bf16[128,2176]{0,1:T(8,128)(2,1)} %pad_maximum_fusion.2), channel_id=1, source_target_pairs={{0,4},{1,5},{2,6},{3,7},{4,8},{5,9},{6,10},{7,11},{8,12},{9,13},{1... | collective-permute-start | bytes 1671176 | tf_op jit(solution)/shard_map/ppermute | solution.py:73
  11.3 1.1 collective-permute-start.9
  25.6 1.1 reshape.338
  27.9 1.7 collective-permute-start.29
  29.6 1.3 collective-permute-start.28
  31.0 1.6 collective-permute-start.27
  32.7 2.6 %collective-permute-start.5 = (bf16[128,2176]{0,1:T(8,128)(2,1)}, bf16[128,2176]{0,1:T(8,128)(2,1)S(1)}, u32[]{:S(2)}, u32[]{:S(2)}) collective-permute-start(bf16[128,2176]{0,1:T(8,128)(2,1)} %pad_maximum_fusion.2), channel_id=1, source_target_pairs={{0,2},{1,3},{4,6},{5,7},{8,10},{9,11},{12,14},{13,15},{16,18},{17,... | collective-permute-start | bytes 1671176 | tf_op jit(solution)/shard_map/ppermute | solution.py:79
  35.3 3.7 %collective-permute-done.28 = bf16[4,4,2688]{2,1,0:T(4,128)(2,1)S(1)} collective-permute-done((bf16[4,4,2688]{2,1,0:T(4,128)(2,1)S(1)}, bf16[4,4,2688]{2,1,0:T(4,128)(2,1)S(1)}, u32[]{:S(2)}, u32[]{:S(2)}) %collective-permute-start.28) | collective-permute-done | bytes 86048 | tf_op jit(solution)/shard_map/ppermute | solution.py:57
  39.0 2.0 %collective-permute-start.18 = (bf16[128,2688]{1,0:T(8,128)(2,1)}, bf16[128,2688]{1,0:T(8,128)(2,1)}, u32[]{:S(2)}, u32[]{:S(2)}) collective-permute-start(bf16[128,2688]{1,0:T(8,128)(2,1)} %param.15), channel_id=1, source_target_pairs={{0,2},{1,3},{2,6},{3,7},{4,0},{5,1},{6,10},{7,11},{8,4},{9,5},{10,... | collective-permute-start | bytes 2064392 | tf_op jit(solution)/shard_map/ppermute | solution.py:152
  41.0 1.9 %collective-permute-start.1 = (bf16[128,2176]{0,1:T(8,128)(2,1)S(1)}, bf16[128,2176]{0,1:T(8,128)(2,1)S(1)}, u32[]{:S(2)}, u32[]{:S(2)}) collective-permute-start(bf16[128,2176]{0,1:T(8,128)(2,1)S(1)} %collective-permute-done), channel_id=1, source_target_pairs={{0,4},{1,5},{2,6},{3,7},{4,8},{5,9},{6,10},{7,11},{8,12},{9,13},{1... | collective-permute-start | bytes 1671176 | tf_op jit(solution)/shard_map/ppermute | solution.py:73
  43.0 1.3 collective-permute-start.6
  45.5 3.2 %fusion.7 = bf16[2048,2688]{1,0:T(8,128)(2,1)} fusion(bf16[128,2688]{1,0:T(8,128)(2,1)} %collective-permute-done.9, bf16[128,2688]{1,0:T(8,128)(2,1)} %param.15, pred[]{:T(512)S(6)} %eq.58), kind=kLoop, calls=%fused_computation.19 | loop fusion | flops 6193151 | bytes 2752513
  48.7 5.4 %collective-permute-start.2 = (bf16[128,2176]{0,1:T(8,128)(2,1)S(1)}, bf16[128,2176]{0,1:T(8,128)(2,1)S(1)}, u32[]{:S(2)}, u32[]{:S(2)}) collective-permute-start(bf16[128,2176]{0,1:T(8,128)(2,1)S(1)} %collective-permute-done), channel_id=1, source_target_pairs={{0,2},{1,3},{4,6},{5,7},{8,10},{9,11},{12,14},{13,15},{16,18},{17,... | collective-permute-start | bytes 1671176 | tf_op jit(solution)/shard_map/ppermute | solution.py:79
  54.1 3.6 %collective-permute-done.10 = bf16[128,2688]{1,0:T(8,128)(2,1)} collective-permute-done((bf16[128,2688]{1,0:T(8,128)(2,1)}, bf16[128,2688]{1,0:T(8,128)(2,1)}, u32[]{:S(2)}, u32[]{:S(2)}) %collective-permute-start.10) | collective-permute-done | bytes 688160 | tf_op jit(solution)/shard_map/ppermute | solution.py:147
  57.7 5.7 %collective-permute-done.18 = bf16[128,2688]{1,0:T(8,128)(2,1)} collective-permute-done((bf16[128,2688]{1,0:T(8,128)(2,1)}, bf16[128,2688]{1,0:T(8,128)(2,1)}, u32[]{:S(2)}, u32[]{:S(2)}) %collective-permute-start.18) | collective-permute-done | bytes 688160 | tf_op jit(solution)/shard_map/ppermute | solution.py:152
  63.4 3.6 %collective-permute-done.1 = bf16[128,2176]{0,1:T(8,128)(2,1)S(1)} collective-permute-done((bf16[128,2176]{0,1:T(8,128)(2,1)S(1)}, bf16[128,2176]{0,1:T(8,128)(2,1)S(1)}, u32[]{:S(2)}, u32[]{:S(2)}) %collective-permute-start.1) | collective-permute-done | bytes 557088 | tf_op jit(solution)/shard_map/ppermute | solution.py:73
  67.9 1.7 collective-permute-done.6
  69.6 1.3 collective-permute-start.3
  70.9 1.1 broadcast_select_fusion
  72.2 2.8 %fusion.8 = bf16[2048,2688]{1,0:T(8,128)(2,1)} fusion(bf16[2048,2688]{1,0:T(8,128)(2,1)} %fusion.7, bf16[128,2688]{1,0:T(8,128)(2,1)S(1)} %collective-permute-done.11, bf16[128,2688]{1,0:T(8,128)(2,1)} %collective-permute-done.10, pred[]{:T(512)S(6)} %eq.58), kind=kLoop, calls=%fused_computation.21 | loop fusion | flops 6193152 | bytes 2752513
  75.5 8.8 %collective-permute-done.12 = bf16[128,2688]{1,0:T(8,128)(2,1)S(1)} collective-permute-done((bf16[128,2688]{1,0:T(8,128)(2,1)}, bf16[128,2688]{1,0:T(8,128)(2,1)S(1)}, u32[]{:S(2)}, u32[]{:S(2)}) %collective-permute-start.12) | collective-permute-done | bytes 688160 | tf_op jit(solution)/shard_map/ppermute | solution.py:147
  84.3 4.0 %collective-permute-done.20 = bf16[128,2688]{1,0:T(8,128)(2,1)} collective-permute-done((bf16[128,2688]{1,0:T(8,128)(2,1)}, bf16[128,2688]{1,0:T(8,128)(2,1)}, u32[]{:S(2)}, u32[]{:S(2)}) %collective-permute-start.20) | collective-permute-done | bytes 688160 | tf_op jit(solution)/shard_map/ppermute | solution.py:152
  88.2 8.0 %collective-permute-done.3 = bf16[128,2176]{0,1:T(8,128)(2,1)S(1)} collective-permute-done((bf16[128,2176]{0,1:T(8,128)(2,1)S(1)}, bf16[128,2176]{0,1:T(8,128)(2,1)S(1)}, u32[]{:S(2)}, u32[]{:S(2)}) %collective-permute-start.3) | collective-permute-done | bytes 557088 | tf_op jit(solution)/shard_map/ppermute | solution.py:79
  96.5 13.0 %collective-permute-done.14 = bf16[128,2688]{1,0:T(8,128)(2,1)} collective-permute-done((bf16[128,2688]{1,0:T(8,128)(2,1)S(1)}, bf16[128,2688]{1,0:T(8,128)(2,1)}, u32[]{:S(2)}, u32[]{:S(2)}) %collective-permute-start.14) | collective-permute-done | bytes 688160 | tf_op jit(solution)/shard_map/ppermute | solution.py:147
  109.5 1.4 fusion.9
  111.8 2.8 %fusion.10 = bf16[2048,2688]{1,0:T(8,128)(2,1)} fusion(bf16[2048,2688]{1,0:T(8,128)(2,1)} %fusion.9, bf16[128,2688]{1,0:T(8,128)(2,1)S(1)} %collective-permute-done.15, bf16[128,2688]{1,0:T(8,128)(2,1)} %collective-permute-done.14, pred[]{:T(512)S(6)} %eq.58), kind=kLoop, calls=%fused_computation.25 | loop fusion | flops 6193152 | bytes 2752513
  116.8 1.9 %constant_dynamic-slice_fusion = (bf16[1152,1024]{0,1:T(8,128)(2,1)S(1)}, bf16[1152,1024]{0,1:T(8,128)(2,1)}) fusion(bf16[1280,2176]{0,1:T(8,128)(2,1)S(1)} %fusion.22, s32[]{:T(128)S(6)} %select_n.357, s32[]{:T(128)S(6)} %add.307), kind=kLoop, calls=%fused_computation.104 | loop fusion | bytes 9437192 | tf_op jit(solution)/shard_map/slice | solution.py:212
  118.7 1.1 compare_and_fusion
  119.8 3.7 %fusion.55 = f32[8,2,128]{2,1,0:T(2,128)S(1)} fusion(pred[128,1152]{0,1:T(8,128)(4,1)S(1)} %compare_and_fusion, bf16[1152,8,128,1]{0,2,3,1:T(8,128)(2,1)S(1)} %bitcast.115, bf16[128,8,2,128]{3,2,1,0:T(2,128)(2,1)S(1)} %copy-done.2), kind=kOutput, calls=%fused_computation.151 | convolution fusion | flops 613418112 | bytes 3039232 | tf_op jit(solution)/shard_map/sub | solution.py:226
  123.5 6.4 %fusion.15 = bf16[8,128,2,128]{3,1,2,0:T(8,128)(2,1)S(1)} fusion(bf16[1152,8,128,1]{0,2,3,1:T(8,128)(2,1)} %bitcast.117, f32[8,2,128]{2,1,0:T(2,128)S(1)} %fusion.55, pred[128,1152]{0,1:T(8,128)(4,1)S(1)} %compare_and_fusion, bf16[1152,8,128,1]{0,2,3,1:T(8,128)(2,1)S(1)} %bitcast.116, bf16[128,8,2,128]{3,2,1,0:T(2,128)(2,1)} %reshape.338), kind=kOutput, calls=%fused_computation.34 | convolution fusion | flops 1220021376 | bytes 5922816 | tf_op jit(solution)/shard_map/hgqk,khd->qhgd/dot_general | solution.py:228
  133.4 2.3 %collective-permute-done.31 = bf16[1,4,2048]{2,1,0:T(4,128)(2,1)S(1)} collective-permute-done((bf16[1,4,2048]{2,1,0:T(4,128)(2,1)S(1)}, bf16[1,4,2048]{2,1,0:T(4,128)(2,1)S(1)}, u32[]{:S(2)}, u32[]{:S(2)}) %collective-permute-start.31) | collective-permute-done | bytes 16416 | tf_op jit(solution)/shard_map/ppermute | solution.py:57
  136.6 1.3 collective-permute-start.35
  139.4 1.8 collective-permute-done.35
  141.2 3.3 %collective-permute-done.34 = bf16[4,4,2048]{2,1,0:T(4,128)(2,1)S(1)} collective-permute-done((bf16[4,4,2048]{2,1,0:T(4,128)(2,1)S(1)}, bf16[4,4,2048]{2,1,0:T(4,128)(2,1)S(1)}, u32[]{:S(2)}, u32[]{:S(2)}) %collective-permute-start.34) | collective-permute-done | bytes 65568 | tf_op jit(solution)/shard_map/ppermute | solution.py:57
  145.9 1.1 collective-permute-done.17
  147.0 3.2 %fusion.11 = bf16[2048,2688]{1,0:T(8,128)(2,1)} fusion(bf16[2048,2688]{1,0:T(8,128)(2,1)} %fusion.10, bf16[128,2688]{1,0:T(8,128)(2,1)} %collective-permute-done.17, bf16[128,2688]{1,0:T(8,128)(2,1)} %collective-permute-done.16, pred[]{:T(512)S(6)} %eq.58), kind=kLoop, calls=%fused_computation.27 | loop fusion | flops 6193152 | bytes 2752513
  150.2 2.8 %fusion.12 = bf16[2048,2688]{1,0:T(8,128)(2,1)} fusion(bf16[2048,2688]{1,0:T(8,128)(2,1)} %fusion.11, bf16[128,2688]{1,0:T(8,128)(2,1)S(1)} %collective-permute-done.19, bf16[128,2688]{1,0:T(8,128)(2,1)} %collective-permute-done.18, pred[]{:T(512)S(6)} %eq.58), kind=kLoop, calls=%fused_computation.29 | loop fusion | flops 6193152 | bytes 2752513
  153.0 3.3 %fusion.13 = bf16[2048,2688]{1,0:T(8,128)(2,1)} fusion(bf16[2048,2688]{1,0:T(8,128)(2,1)} %fusion.12, bf16[128,2688]{1,0:T(8,128)(2,1)} %collective-permute-done.21, bf16[128,2688]{1,0:T(8,128)(2,1)} %collective-permute-done.20, pred[]{:T(512)S(6)} %eq.58), kind=kLoop, calls=%fused_computation.31 | loop fusion | flops 6193152 | bytes 2752513
  156.3 2.9 %fusion.14 = bf16[2048,2688]{1,0:T(8,128)(2,1)} fusion(bf16[2048,2688]{1,0:T(8,128)(2,1)} %fusion.13, bf16[128,2688]{1,0:T(8,128)(2,1)S(1)} %collective-permute-done.23, bf16[128,2688]{1,0:T(8,128)(2,1)} %collective-permute-done.22, pred[]{:T(512)S(6)} %eq.58), kind=kLoop, calls=%fused_computation.33 | loop fusion | flops 6193152 | bytes 2752513 | tf_op jit(solution)/shard_map/concatenate | solution.py:181
  159.2 6.3 %multiply_reduce_fusion = (f32[64]{0:T(128)S(1)}, f32[64,2688]{1,0:T(8,128)S(1)}) fusion(bf16[64,2048]{1,0:T(8,128)(2,1)S(1)} %constant_dynamic-update-slice_fusion, bf16[2048,2688]{1,0:T(8,128)(2,1)} %fusion.14, bf16[64,2688]{1,0:T(8,128)(2,1)S(1)} %gather.46, pred[64]{0:T(512)(128)(4,1)S(1)} %broadcast_in_dim.126), kind=kOutput, calls=%fused_computation.49 | convolution fusion | flops 705503168 | bytes 12304704 | tf_op jit(solution)/shard_map/dot_general | solution.py:234
  165.6 1.9 %fusion.58 = (f32[64]{0:T(128)S(1)}, f32[64,1024]{1,0:T(8,128)S(1)}) fusion(bf16[1024,2688]{1,0:T(8,128)(2,1)S(1)} %bitcast.112, f32[64,2688]{1,0:T(8,128)S(1)} %get-tuple-element.31, f32[2688]{0:T(1024)S(1)} %copy-done.4, f32[64]{0:T(128)S(1)} %add_rsqrt_fusion), kind=kOutput, calls=%fused_computation.152 | convolution fusion | flops 352903104 | bytes 6466560 | tf_op jit(solution)/shard_map/dot_general | solution.py:241
  168.0 1.5 collective-permute-start.37
  169.6 6.7 %fusion.6 = bf16[128,2688]{1,0:T(8,128)(2,1)} fusion(bf16[128,2048]{0,1:T(8,128)(2,1)S(1)} %dynamic-slice_dynamic-update-slice_fusion, bf16[2048,2688]{1,0:T(8,128)(2,1)} %fusion.14, bf16[128,2688]{1,0:T(8,128)(2,1)S(1)} %copy-done), kind=kOutput, calls=%fused_computation.16 | convolution fusion | flops 1410318336 | bytes 12910592 | tf_op jit(solution)/shard_map/dot_general | solution.py:238
  179.3 1.3 collective-permute-done.41
  180.6 1.9 %collective-permute-done.40 = f32[4,3,64]{2,1,0:T(4,128)S(1)} collective-permute-done((f32[4,3,64]{2,1,0:T(4,128)S(1)}, f32[4,3,64]{2,1,0:T(4,128)S(1)}, u32[]{:S(2)}, u32[]{:S(2)}) %collective-permute-start.40) | collective-permute-done | bytes 3104 | tf_op jit(solution)/shard_map/ppermute | solution.py:57
  182.5 1.4 collective-permute-done.39
  (157 shorter events, 24.9 us)
Async XLA Ops:
  0.6 12.0 %copy-start.7 = (s32[8]{0:T(128)S(1)}, s32[8]{0:T(128)}, u32[]{:S(2)}) copy-start(s32[8]{0:T(128)} %constant.259.clone) | copy-start | bytes 100
  0.6 19.2 %copy-start.3 = (s32[8]{0:T(128)S(1)}, s32[8]{0:T(128)}, u32[]{:S(2)}) copy-start(s32[8]{0:T(128)} %constant.260.clone) | copy-start | bytes 100
  0.7 11.9 %copy-start.6 = (s32[64]{0:T(128)S(1)}, s32[64]{0:T(128)}, u32[]{:S(2)}) copy-start(s32[64]{0:T(128)} %param.17) | copy-start | bytes 772
  0.7 24.9 %copy-start.1 = (bf16[128,2048]{1,0:T(8,128)(2,1)S(1)}, bf16[128,2048]{1,0:T(8,128)(2,1)}, u32[]{:S(2)}) copy-start(bf16[128,2048]{1,0:T(8,128)(2,1)} %param.10) | copy-start | bytes 1572868
  1.7 25.4 %collective-permute-start.26 = (bf16[1,4,2688]{2,1,0:T(4,128)(2,1)S(1)}, bf16[1,4,2688]{2,1,0:T(4,128)(2,1)S(1)}, u32[]{:S(2)}, u32[]{:S(2)}) collective-permute-start(bf16[1,4,2688]{2,1,0:T(4,128)(2,1)S(1)} %bitcast.130), channel_id=1, source_target_pairs={{0,3},{1,0},{2,1},{3,2},{4,7},{5,4},{6,5},{7,6},{8,11},{9,8},{10,9... | collective-permute-start | bytes 64520 | tf_op jit(solution)/shard_map/ppermute | solution.py:57
  4.2 22.9 %collective-permute-start.25 = (bf16[1,4,2688]{2,1,0:T(4,128)(2,1)S(1)}, bf16[1,4,2688]{2,1,0:T(4,128)(2,1)S(1)}, u32[]{:S(2)}, u32[]{:S(2)}) collective-permute-start(bf16[1,4,2688]{2,1,0:T(4,128)(2,1)S(1)} %bitcast.131), channel_id=1, source_target_pairs={{0,2},{1,3},{2,0},{3,1},{4,6},{5,7},{6,4},{7,5},{8,10},{9,11},{10,... | collective-permute-start | bytes 64520 | tf_op jit(solution)/shard_map/ppermute | solution.py:57
  4.8 22.3 %collective-permute-start.24 = (bf16[1,4,2688]{2,1,0:T(4,128)(2,1)S(1)}, bf16[1,4,2688]{2,1,0:T(4,128)(2,1)S(1)}, u32[]{:S(2)}, u32[]{:S(2)}) collective-permute-start(bf16[1,4,2688]{2,1,0:T(4,128)(2,1)S(1)} %bitcast.132), channel_id=1, source_target_pairs={{0,1},{1,2},{2,3},{3,0},{4,5},{5,6},{6,7},{7,4},{8,9},{9,10},{10,1... | collective-permute-start | bytes 64520 | tf_op jit(solution)/shard_map/ppermute | solution.py:57
  7.8 33.2 %collective-permute-start = (bf16[128,2176]{0,1:T(8,128)(2,1)}, bf16[128,2176]{0,1:T(8,128)(2,1)S(1)}, u32[]{:S(2)}, u32[]{:S(2)}) collective-permute-start(bf16[128,2176]{0,1:T(8,128)(2,1)} %pad_maximum_fusion.2), channel_id=1, source_target_pairs={{0,4},{1,5},{2,6},{3,7},{4,8},{5,9},{6,10},{7,11},{8,12},{9,13},{1... | collective-permute-start | bytes 1671176 | tf_op jit(solution)/shard_map/ppermute | solution.py:73
  11.3 31.6 %collective-permute-start.9 = (bf16[128,2688]{1,0:T(8,128)(2,1)}, bf16[128,2688]{1,0:T(8,128)(2,1)}, u32[]{:S(2)}, u32[]{:S(2)}) collective-permute-start(bf16[128,2688]{1,0:T(8,128)(2,1)} %param.15), channel_id=1, source_target_pairs={{0,1},{1,0},{2,3},{3,2},{4,5},{5,4},{6,7},{7,6},{8,9},{9,8},{10,11... | collective-permute-start | bytes 2064392 | tf_op jit(solution)/shard_map/ppermute | solution.py:40
  27.9 4.8 %collective-permute-start.29 = (bf16[4,4,2688]{2,1,0:T(4,128)(2,1)S(1)}, bf16[4,4,2688]{2,1,0:T(4,128)(2,1)S(1)}, u32[]{:S(2)}, u32[]{:S(2)}) collective-permute-start(bf16[4,4,2688]{2,1,0:T(4,128)(2,1)S(1)} %broadcast_select_fusion.3), channel_id=1, source_target_pairs={{0,12},{1,13},{2,14},{3,15},{4,0},{5,1},{6,2},{7,3},{8,4},{9,5},{1... | collective-permute-start | bytes 258056 | tf_op jit(solution)/shard_map/ppermute | solution.py:57
  29.6 9.3 %collective-permute-start.28 = (bf16[4,4,2688]{2,1,0:T(4,128)(2,1)S(1)}, bf16[4,4,2688]{2,1,0:T(4,128)(2,1)S(1)}, u32[]{:S(2)}, u32[]{:S(2)}) collective-permute-start(bf16[4,4,2688]{2,1,0:T(4,128)(2,1)S(1)} %broadcast_select_fusion.3), channel_id=1, source_target_pairs={{0,8},{1,9},{2,10},{3,11},{4,12},{5,13},{6,14},{7,15},{8,0},{9,1},... | collective-permute-start | bytes 258056 | tf_op jit(solution)/shard_map/ppermute | solution.py:57
  31.0 8.0 %collective-permute-start.27 = (bf16[4,4,2688]{2,1,0:T(4,128)(2,1)S(1)}, bf16[4,4,2688]{2,1,0:T(4,128)(2,1)S(1)}, u32[]{:S(2)}, u32[]{:S(2)}) collective-permute-start(bf16[4,4,2688]{2,1,0:T(4,128)(2,1)S(1)} %broadcast_select_fusion.3), channel_id=1, source_target_pairs={{0,4},{1,5},{2,6},{3,7},{4,8},{5,9},{6,10},{7,11},{8,12},{9,13},{1... | collective-permute-start | bytes 258056 | tf_op jit(solution)/shard_map/ppermute | solution.py:57
  32.7 16.0 %collective-permute-start.5 = (bf16[128,2176]{0,1:T(8,128)(2,1)}, bf16[128,2176]{0,1:T(8,128)(2,1)S(1)}, u32[]{:S(2)}, u32[]{:S(2)}) collective-permute-start(bf16[128,2176]{0,1:T(8,128)(2,1)} %pad_maximum_fusion.2), channel_id=1, source_target_pairs={{0,2},{1,3},{4,6},{5,7},{8,10},{9,11},{12,14},{13,15},{16,18},{17,... | collective-permute-start | bytes 1671176 | tf_op jit(solution)/shard_map/ppermute | solution.py:79
  39.0 18.7 %collective-permute-start.10 = (bf16[128,2688]{1,0:T(8,128)(2,1)}, bf16[128,2688]{1,0:T(8,128)(2,1)}, u32[]{:S(2)}, u32[]{:S(2)}) collective-permute-start(bf16[128,2688]{1,0:T(8,128)(2,1)} %param.15), channel_id=1, source_target_pairs={{0,4},{1,5},{2,0},{3,1},{4,8},{5,9},{6,2},{7,3},{8,12},{9,13},{10,... | collective-permute-start | bytes 2064392 | tf_op jit(solution)/shard_map/ppermute | solution.py:147
  39.0 24.4 %collective-permute-start.18 = (bf16[128,2688]{1,0:T(8,128)(2,1)}, bf16[128,2688]{1,0:T(8,128)(2,1)}, u32[]{:S(2)}, u32[]{:S(2)}) collective-permute-start(bf16[128,2688]{1,0:T(8,128)(2,1)} %param.15), channel_id=1, source_target_pairs={{0,2},{1,3},{2,6},{3,7},{4,0},{5,1},{6,10},{7,11},{8,4},{9,5},{10,... | collective-permute-start | bytes 2064392 | tf_op jit(solution)/shard_map/ppermute | solution.py:152
  41.0 26.0 %collective-permute-start.1 = (bf16[128,2176]{0,1:T(8,128)(2,1)S(1)}, bf16[128,2176]{0,1:T(8,128)(2,1)S(1)}, u32[]{:S(2)}, u32[]{:S(2)}) collective-permute-start(bf16[128,2176]{0,1:T(8,128)(2,1)S(1)} %collective-permute-done), channel_id=1, source_target_pairs={{0,4},{1,5},{2,6},{3,7},{4,8},{5,9},{6,10},{7,11},{8,12},{9,13},{1... | collective-permute-start | bytes 1671176 | tf_op jit(solution)/shard_map/ppermute | solution.py:73
  43.0 26.6 %collective-permute-start.6 = (bf16[128,2176]{0,1:T(8,128)(2,1)S(1)}, bf16[128,2176]{0,1:T(8,128)(2,1)}, u32[]{:S(2)}, u32[]{:S(2)}) collective-permute-start(bf16[128,2176]{0,1:T(8,128)(2,1)S(1)} %collective-permute-done), channel_id=1, source_target_pairs={{2,0},{3,1},{6,4},{7,5},{10,8},{11,9},{14,12},{15,13},{18,16},{19,... | collective-permute-start | bytes 1671176 | tf_op jit(solution)/shard_map/ppermute | solution.py:79
  48.7 26.5 %collective-permute-start.2 = (bf16[128,2176]{0,1:T(8,128)(2,1)S(1)}, bf16[128,2176]{0,1:T(8,128)(2,1)S(1)}, u32[]{:S(2)}, u32[]{:S(2)}) collective-permute-start(bf16[128,2176]{0,1:T(8,128)(2,1)S(1)} %collective-permute-done), channel_id=1, source_target_pairs={{0,2},{1,3},{4,6},{5,7},{8,10},{9,11},{12,14},{13,15},{16,18},{17,... | collective-permute-start | bytes 1671176 | tf_op jit(solution)/shard_map/ppermute | solution.py:79
  57.7 14.5 %collective-permute-start.11 = (bf16[128,2688]{1,0:T(8,128)(2,1)}, bf16[128,2688]{1,0:T(8,128)(2,1)S(1)}, u32[]{:S(2)}, u32[]{:S(2)}) collective-permute-start(bf16[128,2688]{1,0:T(8,128)(2,1)} %collective-permute-done.10), channel_id=1, source_target_pairs={{0,1},{1,0},{2,3},{3,2},{4,5},{5,4},{6,7},{7,6},{8,9},{9,8},{10,11... | collective-permute-start | bytes 2064392 | tf_op jit(solution)/shard_map/ppermute | solution.py:40
  63.4 20.9 %collective-permute-start.12 = (bf16[128,2688]{1,0:T(8,128)(2,1)}, bf16[128,2688]{1,0:T(8,128)(2,1)S(1)}, u32[]{:S(2)}, u32[]{:S(2)}) collective-permute-start(bf16[128,2688]{1,0:T(8,128)(2,1)} %collective-permute-done.10), channel_id=1, source_target_pairs={{0,4},{1,5},{2,0},{3,1},{4,8},{5,9},{6,2},{7,3},{8,12},{9,13},{10,... | collective-permute-start | bytes 2064392 | tf_op jit(solution)/shard_map/ppermute | solution.py:147
  67.0 21.2 %collective-permute-start.20 = (bf16[128,2688]{1,0:T(8,128)(2,1)}, bf16[128,2688]{1,0:T(8,128)(2,1)}, u32[]{:S(2)}, u32[]{:S(2)}) collective-permute-start(bf16[128,2688]{1,0:T(8,128)(2,1)} %collective-permute-done.18), channel_id=1, source_target_pairs={{0,2},{1,3},{2,6},{3,7},{4,0},{5,1},{6,10},{7,11},{8,4},{9,5},{10,... | collective-permute-start | bytes 2064392 | tf_op jit(solution)/shard_map/ppermute | solution.py:152
  69.6 26.6 %collective-permute-start.3 = (bf16[128,2176]{0,1:T(8,128)(2,1)S(1)}, bf16[128,2176]{0,1:T(8,128)(2,1)S(1)}, u32[]{:S(2)}, u32[]{:S(2)}) collective-permute-start(bf16[128,2176]{0,1:T(8,128)(2,1)S(1)} %collective-permute-done.1), channel_id=1, source_target_pairs={{2,0},{3,1},{6,4},{7,5},{10,8},{11,9},{14,12},{15,13},{18,16},{19,... | collective-permute-start | bytes 1671176 | tf_op jit(solution)/shard_map/ppermute | solution.py:79
  72.2 44.2 %collective-permute-start.8 = (bf16[128,2176]{0,1:T(8,128)(2,1)}, bf16[128,2176]{0,1:T(8,128)(2,1)S(1)}, u32[]{:S(2)}, u32[]{:S(2)}) collective-permute-start(bf16[128,2176]{0,1:T(8,128)(2,1)} %pad_maximum_fusion.2), channel_id=1, source_target_pairs={{0,1},{1,0},{2,3},{3,2},{4,5},{5,4},{6,7},{7,6},{8,9},{9,8},{10,11... | collective-permute-start | bytes 1671176 | tf_op jit(solution)/shard_map/ppermute | solution.py:40
  75.2 35.7 %collective-permute-start.7 = (bf16[2,128,2176]{1,2,0:T(8,128)(2,1)S(1)}, bf16[2,128,2176]{1,2,0:T(8,128)(2,1)S(1)}, u32[]{:S(2)}, u32[]{:S(2)}) collective-permute-start(bf16[2,128,2176]{1,2,0:T(8,128)(2,1)S(1)} %pad_maximum_fusion.1), channel_id=1, source_target_pairs={{0,1},{1,0},{2,3},{3,2},{4,5},{5,4},{6,7},{7,6},{8,9},{9,8},{10,11... | collective-permute-start | bytes 3342344 | tf_op jit(solution)/shard_map/ppermute | solution.py:40
  84.3 12.1 %collective-permute-start.13 = (bf16[128,2688]{1,0:T(8,128)(2,1)S(1)}, bf16[128,2688]{1,0:T(8,128)(2,1)S(1)}, u32[]{:S(2)}, u32[]{:S(2)}) collective-permute-start(bf16[128,2688]{1,0:T(8,128)(2,1)S(1)} %collective-permute-done.12), channel_id=1, source_target_pairs={{0,1},{1,0},{2,3},{3,2},{4,5},{5,4},{6,7},{7,6},{8,9},{9,8},{10,11... | collective-permute-start | bytes 2064392 | tf_op jit(solution)/shard_map/ppermute | solution.py:40
  88.2 21.3 %collective-permute-start.14 = (bf16[128,2688]{1,0:T(8,128)(2,1)S(1)}, bf16[128,2688]{1,0:T(8,128)(2,1)}, u32[]{:S(2)}, u32[]{:S(2)}) collective-permute-start(bf16[128,2688]{1,0:T(8,128)(2,1)S(1)} %collective-permute-done.12), channel_id=1, source_target_pairs={{0,4},{1,5},{2,0},{3,1},{4,8},{5,9},{6,2},{7,3},{8,12},{9,13},{10,... | collective-permute-start | bytes 2064392 | tf_op jit(solution)/shard_map/ppermute | solution.py:147
  96.2 42.6 %collective-permute-start.22 = (bf16[128,2688]{1,0:T(8,128)(2,1)}, bf16[128,2688]{1,0:T(8,128)(2,1)}, u32[]{:S(2)}, u32[]{:S(2)}) collective-permute-start(bf16[128,2688]{1,0:T(8,128)(2,1)} %collective-permute-done.20), channel_id=1, source_target_pairs={{0,2},{1,3},{2,6},{3,7},{4,0},{5,1},{6,10},{7,11},{8,4},{9,5},{10,... | collective-permute-start | bytes 2064392 | tf_op jit(solution)/shard_map/ppermute | solution.py:152
  96.4 18.3 %collective-permute-start.4 = (bf16[2,128,2176]{1,2,0:T(8,128)(2,1)S(1)}, bf16[2,128,2176]{1,2,0:T(8,128)(2,1)S(1)}, u32[]{:S(2)}, u32[]{:S(2)}) collective-permute-start(bf16[2,128,2176]{1,2,0:T(8,128)(2,1)S(1)} %pad_maximum_fusion), channel_id=1, source_target_pairs={{0,1},{1,0},{2,3},{3,2},{4,5},{5,4},{6,7},{7,6},{8,9},{9,8},{10,11... | collective-permute-start | bytes 3342344 | tf_op jit(solution)/shard_map/ppermute | solution.py:40
  109.5 2.4 %collective-permute-start.15 = (bf16[128,2688]{1,0:T(8,128)(2,1)}, bf16[128,2688]{1,0:T(8,128)(2,1)S(1)}, u32[]{:S(2)}, u32[]{:S(2)}) collective-permute-start(bf16[128,2688]{1,0:T(8,128)(2,1)} %collective-permute-done.14), channel_id=1, source_target_pairs={{0,1},{1,0},{2,3},{3,2},{4,5},{5,4},{6,7},{7,6},{8,9},{9,8},{10,11... | collective-permute-start | bytes 2064392 | tf_op jit(solution)/shard_map/ppermute | solution.py:40
  110.9 28.1 %collective-permute-start.16 = (bf16[128,2688]{1,0:T(8,128)(2,1)}, bf16[128,2688]{1,0:T(8,128)(2,1)}, u32[]{:S(2)}, u32[]{:S(2)}) collective-permute-start(bf16[128,2688]{1,0:T(8,128)(2,1)} %collective-permute-done.14), channel_id=1, source_target_pairs={{0,4},{1,5},{2,0},{3,1},{4,8},{5,9},{6,2},{7,3},{8,12},{9,13},{10,... | collective-permute-start | bytes 2064392 | tf_op jit(solution)/shard_map/ppermute | solution.py:147
  130.9 2.5 %collective-permute-start.32 = (bf16[1,4,2048]{2,1,0:T(4,128)(2,1)S(1)}, bf16[1,4,2048]{2,1,0:T(4,128)(2,1)S(1)}, u32[]{:S(2)}, u32[]{:S(2)}) collective-permute-start(bf16[1,4,2048]{2,1,0:T(4,128)(2,1)S(1)} %bitcast.139), channel_id=1, source_target_pairs={{0,3},{1,0},{2,1},{3,2},{4,7},{5,4},{6,5},{7,6},{8,11},{9,8},{10,9... | collective-permute-start | bytes 49160 | tf_op jit(solution)/shard_map/ppermute | solution.py:57
  131.9 3.7 %collective-permute-start.31 = (bf16[1,4,2048]{2,1,0:T(4,128)(2,1)S(1)}, bf16[1,4,2048]{2,1,0:T(4,128)(2,1)S(1)}, u32[]{:S(2)}, u32[]{:S(2)}) collective-permute-start(bf16[1,4,2048]{2,1,0:T(4,128)(2,1)S(1)} %bitcast.140), channel_id=1, source_target_pairs={{0,2},{1,3},{2,0},{3,1},{4,6},{5,7},{6,4},{7,5},{8,10},{9,11},{10,... | collective-permute-start | bytes 49160 | tf_op jit(solution)/shard_map/ppermute | solution.py:57
  132.7 3.2 %collective-permute-start.30 = (bf16[1,4,2048]{2,1,0:T(4,128)(2,1)S(1)}, bf16[1,4,2048]{2,1,0:T(4,128)(2,1)S(1)}, u32[]{:S(2)}, u32[]{:S(2)}) collective-permute-start(bf16[1,4,2048]{2,1,0:T(4,128)(2,1)S(1)} %bitcast.141), channel_id=1, source_target_pairs={{0,1},{1,2},{2,3},{3,0},{4,5},{5,6},{6,7},{7,4},{8,9},{9,10},{10,1... | collective-permute-start | bytes 49160 | tf_op jit(solution)/shard_map/ppermute | solution.py:57
  136.6 4.5 %collective-permute-start.35 = (bf16[4,4,2048]{2,1,0:T(4,128)(2,1)S(1)}, bf16[4,4,2048]{2,1,0:T(4,128)(2,1)S(1)}, u32[]{:S(2)}, u32[]{:S(2)}) collective-permute-start(bf16[4,4,2048]{2,1,0:T(4,128)(2,1)S(1)} %broadcast_select_fusion.4), channel_id=1, source_target_pairs={{0,12},{1,13},{2,14},{3,15},{4,0},{5,1},{6,2},{7,3},{8,4},{9,5},{1... | collective-permute-start | bytes 196616 | tf_op jit(solution)/shard_map/ppermute | solution.py:57
  138.0 6.6 %collective-permute-start.34 = (bf16[4,4,2048]{2,1,0:T(4,128)(2,1)S(1)}, bf16[4,4,2048]{2,1,0:T(4,128)(2,1)S(1)}, u32[]{:S(2)}, u32[]{:S(2)}) collective-permute-start(bf16[4,4,2048]{2,1,0:T(4,128)(2,1)S(1)} %broadcast_select_fusion.4), channel_id=1, source_target_pairs={{0,8},{1,9},{2,10},{3,11},{4,12},{5,13},{6,14},{7,15},{8,0},{9,1},... | collective-permute-start | bytes 196616 | tf_op jit(solution)/shard_map/ppermute | solution.py:57
  138.0 6.6 %collective-permute-start.33 = (bf16[4,4,2048]{2,1,0:T(4,128)(2,1)S(1)}, bf16[4,4,2048]{2,1,0:T(4,128)(2,1)S(1)}, u32[]{:S(2)}, u32[]{:S(2)}) collective-permute-start(bf16[4,4,2048]{2,1,0:T(4,128)(2,1)S(1)} %broadcast_select_fusion.4), channel_id=1, source_target_pairs={{0,4},{1,5},{2,6},{3,7},{4,8},{5,9},{6,10},{7,11},{8,12},{9,13},{1... | collective-permute-start | bytes 196616 | tf_op jit(solution)/shard_map/ppermute | solution.py:57
  138.8 11.4 %collective-permute-start.19 = (bf16[128,2688]{1,0:T(8,128)(2,1)}, bf16[128,2688]{1,0:T(8,128)(2,1)S(1)}, u32[]{:S(2)}, u32[]{:S(2)}) collective-permute-start(bf16[128,2688]{1,0:T(8,128)(2,1)} %collective-permute-done.18), channel_id=1, source_target_pairs={{0,1},{1,0},{2,3},{3,2},{4,5},{5,4},{6,7},{7,6},{8,9},{9,8},{10,11... | collective-permute-start | bytes 2064392 | tf_op jit(solution)/shard_map/ppermute | solution.py:40
  138.9 14.1 %collective-permute-start.21 = (bf16[128,2688]{1,0:T(8,128)(2,1)}, bf16[128,2688]{1,0:T(8,128)(2,1)}, u32[]{:S(2)}, u32[]{:S(2)}) collective-permute-start(bf16[128,2688]{1,0:T(8,128)(2,1)} %collective-permute-done.20), channel_id=1, source_target_pairs={{0,1},{1,0},{2,3},{3,2},{4,5},{5,4},{6,7},{7,6},{8,9},{9,8},{10,11... | collective-permute-start | bytes 2064392 | tf_op jit(solution)/shard_map/ppermute | solution.py:40
  141.2 15.1 %collective-permute-start.23 = (bf16[128,2688]{1,0:T(8,128)(2,1)}, bf16[128,2688]{1,0:T(8,128)(2,1)S(1)}, u32[]{:S(2)}, u32[]{:S(2)}) collective-permute-start(bf16[128,2688]{1,0:T(8,128)(2,1)} %collective-permute-done.22), channel_id=1, source_target_pairs={{0,1},{1,0},{2,3},{3,2},{4,5},{5,4},{6,7},{7,6},{8,9},{9,8},{10,11... | collective-permute-start | bytes 2064392 | tf_op jit(solution)/shard_map/ppermute | solution.py:40
  144.5 2.5 %collective-permute-start.17 = (bf16[128,2688]{1,0:T(8,128)(2,1)}, bf16[128,2688]{1,0:T(8,128)(2,1)}, u32[]{:S(2)}, u32[]{:S(2)}) collective-permute-start(bf16[128,2688]{1,0:T(8,128)(2,1)} %collective-permute-done.16), channel_id=1, source_target_pairs={{0,1},{1,0},{2,3},{3,2},{4,5},{5,4},{6,7},{7,6},{8,9},{9,8},{10,11... | collective-permute-start | bytes 2064392 | tf_op jit(solution)/shard_map/ppermute | solution.py:40
  156.3 9.2 %slice-start = ((s8[5505024]{0:T(1024)(128)(4,1)}), s8[4194304]{0:T(1024)(128)(4,1)S(1)}, s32[]{:S(2)}) async-start(s8[5505024]{0:T(1024)(128)(4,1)} %bitcast.111), calls=%async_computation | async-start | bytes 8388608
  159.2 6.4 %copy-start.4 = (f32[2688]{0:T(1024)S(1)}, f32[2688]{0:T(1024)}, u32[]{:S(2)}) copy-start(f32[2688]{0:T(1024)} %param.14) | copy-start | bytes 32260
  167.7 8.5 %collective-permute-start.38 = (f32[1,3,64]{2,1,0:T(4,128)S(1)}, f32[1,3,64]{2,1,0:T(4,128)S(1)}, u32[]{:S(2)}, u32[]{:S(2)}) collective-permute-start(f32[1,3,64]{2,1,0:T(4,128)S(1)} %get-tuple-element.21), channel_id=1, source_target_pairs={{0,3},{1,0},{2,1},{3,2},{4,7},{5,4},{6,5},{7,6},{8,11},{9,8},{10,9... | collective-permute-start | bytes 2312 | tf_op jit(solution)/shard_map/ppermute | solution.py:57
  168.0 8.2 %collective-permute-start.37 = (f32[1,3,64]{2,1,0:T(4,128)S(1)}, f32[1,3,64]{2,1,0:T(4,128)S(1)}, u32[]{:S(2)}, u32[]{:S(2)}) collective-permute-start(f32[1,3,64]{2,1,0:T(4,128)S(1)} %get-tuple-element.21), channel_id=1, source_target_pairs={{0,2},{1,3},{2,0},{3,1},{4,6},{5,7},{6,4},{7,5},{8,10},{9,11},{10,... | collective-permute-start | bytes 2312 | tf_op jit(solution)/shard_map/ppermute | solution.py:57
  169.6 6.7 %collective-permute-start.36 = (f32[1,3,64]{2,1,0:T(4,128)S(1)}, f32[1,3,64]{2,1,0:T(4,128)S(1)}, u32[]{:S(2)}, u32[]{:S(2)}) collective-permute-start(f32[1,3,64]{2,1,0:T(4,128)S(1)} %get-tuple-element.21), channel_id=1, source_target_pairs={{0,1},{1,2},{2,3},{3,0},{4,5},{5,6},{6,7},{7,4},{8,9},{9,10},{10,1... | collective-permute-start | bytes 2312 | tf_op jit(solution)/shard_map/ppermute | solution.py:57
  176.9 3.7 %collective-permute-start.41 = (f32[4,3,64]{2,1,0:T(4,128)S(1)}, f32[4,3,64]{2,1,0:T(4,128)S(1)}, u32[]{:S(2)}, u32[]{:S(2)}) collective-permute-start(f32[4,3,64]{2,1,0:T(4,128)S(1)} %broadcast_select_fusion.5), channel_id=1, source_target_pairs={{0,12},{1,13},{2,14},{3,15},{4,0},{5,1},{6,2},{7,3},{8,4},{9,5},{1... | collective-permute-start | bytes 9224 | tf_op jit(solution)/shard_map/ppermute | solution.py:57
  177.9 4.6 %collective-permute-start.40 = (f32[4,3,64]{2,1,0:T(4,128)S(1)}, f32[4,3,64]{2,1,0:T(4,128)S(1)}, u32[]{:S(2)}, u32[]{:S(2)}) collective-permute-start(f32[4,3,64]{2,1,0:T(4,128)S(1)} %broadcast_select_fusion.5), channel_id=1, source_target_pairs={{0,8},{1,9},{2,10},{3,11},{4,12},{5,13},{6,14},{7,15},{8,0},{9,1},... | collective-permute-start | bytes 9224 | tf_op jit(solution)/shard_map/ppermute | solution.py:57
  178.4 5.5 %collective-permute-start.39 = (f32[4,3,64]{2,1,0:T(4,128)S(1)}, f32[4,3,64]{2,1,0:T(4,128)S(1)}, u32[]{:S(2)}, u32[]{:S(2)}) collective-permute-start(f32[4,3,64]{2,1,0:T(4,128)S(1)} %broadcast_select_fusion.5), channel_id=1, source_target_pairs={{0,4},{1,5},{2,6},{3,7},{4,8},{5,9},{6,10},{7,11},{8,12},{9,13},{1... | collective-permute-start | bytes 9224 | tf_op jit(solution)/shard_map/ppermute | solution.py:57
  (4 other events, 15.3 us)

commit v9 on v7

--- a/solution.py
+++ b/solution.py
@@ -135,29 +135,35 @@
         & (key_pos[None, :] <= query_pos[:, None])
         & (key_pos[None, :] > query_pos[:, None] - ATTENTION_SPAN)
     )
-    heads_for_queries = queries.reshape(token_rows, KEY_VALUE_HEADS, queries_per_group, HEAD_SIZE)
     heads_for_keys = key_value_pair[:, : KEY_VALUE_HEADS * HEAD_SIZE].reshape(
         count_of_keys, KEY_VALUE_HEADS, HEAD_SIZE
     )
     heads_for_values = key_value_pair[:, KEY_VALUE_HEADS * HEAD_SIZE :].reshape(
         count_of_keys, KEY_VALUE_HEADS, HEAD_SIZE
     )
-    scores = (
-        jnp.einsum(
-            "qhgd,khd->hgqk", heads_for_queries, heads_for_keys, preferred_element_type=jnp.float32
+
+    def attend(rows_of_queries, rows_allowed):
+        rows = rows_of_queries.shape[0]
+        heads_for_queries = rows_of_queries.reshape(rows, KEY_VALUE_HEADS, queries_per_group, HEAD_SIZE)
+        scores = (
+            jnp.einsum(
+                "qhgd,khd->hgqk", heads_for_queries, heads_for_keys, preferred_element_type=jnp.float32
+            )
+            * score_scale
         )
-        * score_scale
-    )
-    scores = jnp.where(allowed[None, None, :, :], scores, masked_score)
-    row_max = jnp.max(scores, axis=-1, keepdims=True)
-    raised = jnp.exp(scores - row_max)
-    weights = (raised / jnp.sum(raised, axis=-1, keepdims=True)).astype(jnp.bfloat16)
-    context = jnp.einsum(
-        "hgqk,khd->qhgd", weights, heads_for_values, preferred_element_type=jnp.float32
-    )
-    context = context.reshape(token_rows, QUERY_HEADS * HEAD_SIZE).astype(jnp.bfloat16)
-
-    scored_context = gather_rows(context.reshape(score_count, stride, -1)[:, stride - 1, :])
+        scores = jnp.where(rows_allowed[None, None, :, :], scores, masked_score)
+        row_max = jnp.max(scores, axis=-1, keepdims=True)
+        raised = jnp.exp(scores - row_max)
+        weights = (raised / jnp.sum(raised, axis=-1, keepdims=True)).astype(jnp.bfloat16)
+        context = jnp.einsum(
+            "hgqk,khd->qhgd", weights, heads_for_values, preferred_element_type=jnp.float32
+        )
+        return context.reshape(rows, QUERY_HEADS * HEAD_SIZE).astype(jnp.bfloat16)
+
+    scored_rows = slice(stride - 1, token_rows, stride)
+    scored_context = gather_rows(attend(queries[scored_rows], allowed[scored_rows]))
+    context = attend(queries, allowed)
+
     picked = scored_residual.astype(jnp.float32) + jnp.dot(
         scored_context, full_proj, preferred_element_type=jnp.float32
     )

time: 164 us -> 182 us (1.11)
  waiting for transfers between devices: 53.2 us -> 64.8 us
  local copies, waits for them, and re-layouts: 12.5 us -> 21.4 us
  starting transfers between devices: 49 us -> 41.4 us
  matrix products: 23.5 us -> 28.2 us
    ppermute x18, waiting for transfers between devices: 9.72 us -> 25.4 us  [gather_rows(): received.append(lax.ppermute(data, SEQ, pairs))]
    ppermute x3, starting transfers between devices: 10.9 us -> 0.58 us  [swap_cores(): return lax.ppermute(value, 'core', [(0, 1), (1, 0)])]
    dot_general x1 -> x3, matrix products: 6.31 us -> 10.2 us  [the longest x2 9.75 us: attend(): jnp.einsum('hgqk,khd->qhgd', weights, heads_for_values, preferred_element...]
    ppermute x2, waiting for transfers between devices: 15.4 us -> 12.6 us  [shift_chips(): lax.ppermute(value, SEQ, [(s, s + step) for s in range(count - step)])]
    slice x1, local copies, waits for them, and re-layouts: 1.86 us -> 4.2 us  [local(): key_value_pair[:, :KEY_VALUE_HEADS * HEAD_SIZE]]
    unnamed x31 -> x18, local copies, waits for them, and re-layouts: 1.41 us -> 3.73 us
    ppermute x18, starting transfers between devices: 21.6 us -> 23.7 us  [gather_rows(): received.append(lax.ppermute(data, SEQ, pairs))]
    slice x1 -> x3, local copies, waits for them, and re-layouts: 0.04 us -> 1.96 us  [the longest x2 1.9 us: local(): allowed[scored_rows]]
  transfers between devices with their start and end apart: 28 -> 28, of which waited for: 10 -> 10; matrix products, arithmetic and copies ran while one was open for 20% -> 24% of each run, Pallas kernels for 0% -> 0%
where the time goes in v9:
time: 182 us; the launch traced here: 181 us
  waiting for transfers between devices  64.8 us (36%)
  starting transfers between devices  41.4 us (23%)
  matrix products  28.2 us (15%)
  local copies, waits for them, and re-layouts  21.4 us (12%)
  between operations  14.5 us (8%)
  other arithmetic  10.8 us (6%)
    ppermute x4, waiting for transfers between devices, across_pair(): return lax.ppermute(value, SEQ, pairs)  26.1 us
    ppermute x18, waiting for transfers between devices, gather_rows(): received.append(lax.ppermute(data, SEQ, pairs))  25.4 us
    ppermute x18, starting transfers between devices, gather_rows(): received.append(lax.ppermute(data, SEQ, pairs))  23.7 us
    ppermute x2, waiting for transfers between devices, shift_chips(): lax.ppermute(value, SEQ, [(s, s + step) for s in range(count - step)])  12.6 us
    dot_general x2, matrix products, attend(): jnp.einsum('hgqk,khd->qhgd', weights, heads_for_values, preferred_element...  9.75 us
    ppermute x2, starting transfers between devices, shift_chips(): lax.ppermute(value, SEQ, [(s, s + step) for s in range(count - step)])  8.96 us
    ppermute x4, starting transfers between devices, across_pair(): return lax.ppermute(value, SEQ, pairs)  8.12 us
    dot_general x1, matrix products, local(): jnp.dot(scored_context, full_proj, preferred_element_type=jnp.float32)  6.49 us
  transfers between devices with their start and end apart: 28, of which 10 were waited for; matrix products, arithmetic and copies ran while one was open for 24% of the time, Pallas kernels for 0%

profile of v9, /device:TPU:0, one launch (start us, length us, event | category | flops | bytes accessed | tf_op | source)
XLA Modules:
  0.0 181.2 jit_solution(5919909037738829863)
XLA Ops:
  7.2 0.7 all-gather.2.cloned.1.call-update
  8.6 1.3 copy.17
  9.9 0.8 pad_maximum_fusion.2
  10.8 5.0 %collective-permute-start = (bf16[128,2176]{0,1:T(8,128)(2,1)}, bf16[128,2176]{0,1:T(8,128)(2,1)S(1)}, u32[]{:S(2)}, u32[]{:S(2)}) collective-permute-start(bf16[128,2176]{0,1:T(8,128)(2,1)} %pad_maximum_fusion.2), channel_id=1, source_target_pairs={{0,4},{1,5},{2,6},{3,7},{4,8},{5,9},{6,10},{7,11},{8,12},{9,13},{1... | collective-permute-start | bytes 1671176 | tf_op jit(solution)/shard_map/ppermute | solution.py:70
  15.7 3.5 %collective-permute-start.5 = (bf16[128,2176]{0,1:T(8,128)(2,1)}, bf16[128,2176]{0,1:T(8,128)(2,1)S(1)}, u32[]{:S(2)}, u32[]{:S(2)}) collective-permute-start(bf16[128,2176]{0,1:T(8,128)(2,1)} %pad_maximum_fusion.2), channel_id=1, source_target_pairs={{0,2},{1,3},{4,6},{5,7},{8,10},{9,11},{12,14},{13,15},{16,18},{17,... | collective-permute-start | bytes 1671176 | tf_op jit(solution)/shard_map/ppermute | solution.py:76
  19.2 1.0 slice.71
  20.3 0.9 collective-permute-start.10
  21.3 1.2 reshape.348
  22.9 16.1 %collective-permute-done.11 = bf16[1,4,2688]{2,1,0:T(4,128)(2,1)S(1)} collective-permute-done((bf16[1,4,2688]{2,1,0:T(4,128)(2,1)S(1)}, bf16[1,4,2688]{2,1,0:T(4,128)(2,1)S(1)}, u32[]{:S(2)}, u32[]{:S(2)}) %collective-permute-start.11) | collective-permute-done | bytes 21536 | tf_op jit(solution)/shard_map/ppermute | solution.py:54
  40.0 4.0 %collective-permute-start.1 = (bf16[128,2176]{0,1:T(8,128)(2,1)S(1)}, bf16[128,2176]{0,1:T(8,128)(2,1)S(1)}, u32[]{:S(2)}, u32[]{:S(2)}) collective-permute-start(bf16[128,2176]{0,1:T(8,128)(2,1)S(1)} %collective-permute-done), channel_id=1, source_target_pairs={{0,4},{1,5},{2,6},{3,7},{4,8},{5,9},{6,10},{7,11},{8,12},{9,13},{1... | collective-permute-start | bytes 1671176 | tf_op jit(solution)/shard_map/ppermute | solution.py:70
  44.0 1.3 collective-permute-start.6
  45.4 2.7 %collective-permute-start.14 = (bf16[4,4,2688]{2,1,0:T(4,128)(2,1)S(1)}, bf16[4,4,2688]{2,1,0:T(4,128)(2,1)S(1)}, u32[]{:S(2)}, u32[]{:S(2)}) collective-permute-start(bf16[4,4,2688]{2,1,0:T(4,128)(2,1)S(1)} %broadcast_select_fusion.2), channel_id=1, source_target_pairs={{0,12},{1,13},{2,14},{3,15},{4,0},{5,1},{6,2},{7,3},{8,4},{9,5},{1... | collective-permute-start | bytes 258056 | tf_op jit(solution)/shard_map/ppermute | solution.py:54
  48.1 2.4 %collective-permute-start.13 = (bf16[4,4,2688]{2,1,0:T(4,128)(2,1)S(1)}, bf16[4,4,2688]{2,1,0:T(4,128)(2,1)S(1)}, u32[]{:S(2)}, u32[]{:S(2)}) collective-permute-start(bf16[4,4,2688]{2,1,0:T(4,128)(2,1)S(1)} %broadcast_select_fusion.2), channel_id=1, source_target_pairs={{0,8},{1,9},{2,10},{3,11},{4,12},{5,13},{6,14},{7,15},{8,0},{9,1},... | collective-permute-start | bytes 258056 | tf_op jit(solution)/shard_map/ppermute | solution.py:54
  50.5 0.8 collective-permute-start.12
  51.3 12.6 %collective-permute-done.1 = bf16[128,2176]{0,1:T(8,128)(2,1)S(1)} collective-permute-done((bf16[128,2176]{0,1:T(8,128)(2,1)S(1)}, bf16[128,2176]{0,1:T(8,128)(2,1)S(1)}, u32[]{:S(2)}, u32[]{:S(2)}) %collective-permute-start.1) | collective-permute-done | bytes 557088 | tf_op jit(solution)/shard_map/ppermute | solution.py:70
  63.9 2.1 %collective-permute-start.2 = (bf16[128,2176]{0,1:T(8,128)(2,1)S(1)}, bf16[128,2176]{0,1:T(8,128)(2,1)S(1)}, u32[]{:S(2)}, u32[]{:S(2)}) collective-permute-start(bf16[128,2176]{0,1:T(8,128)(2,1)S(1)} %collective-permute-done), channel_id=1, source_target_pairs={{0,2},{1,3},{4,6},{5,7},{8,10},{9,11},{12,14},{13,15},{16,18},{17,... | collective-permute-start | bytes 1671176 | tf_op jit(solution)/shard_map/ppermute | solution.py:76
  66.0 1.3 collective-permute-start.3
  67.3 1.1 pad_maximum_fusion.1
  68.4 21.7 %collective-permute-done.2 = bf16[128,2176]{0,1:T(8,128)(2,1)S(1)} collective-permute-done((bf16[128,2176]{0,1:T(8,128)(2,1)S(1)}, bf16[128,2176]{0,1:T(8,128)(2,1)S(1)}, u32[]{:S(2)}, u32[]{:S(2)}) %collective-permute-start.2) | collective-permute-done | bytes 557088 | tf_op jit(solution)/shard_map/ppermute | solution.py:76
  90.2 4.3 %collective-permute-done.3 = bf16[128,2176]{0,1:T(8,128)(2,1)S(1)} collective-permute-done((bf16[128,2176]{0,1:T(8,128)(2,1)S(1)}, bf16[128,2176]{0,1:T(8,128)(2,1)S(1)}, u32[]{:S(2)}, u32[]{:S(2)}) %collective-permute-start.3) | collective-permute-done | bytes 557088 | tf_op jit(solution)/shard_map/ppermute | solution.py:76
  94.6 1.1 pad_maximum_fusion
  96.7 1.6 gather_fusion.1
  98.3 1.1 gather.46
  99.4 1.3 slice_bitcast_fusion
  100.7 1.3 slice_bitcast_fusion.2
  103.5 1.6 fusion.19
  105.1 2.4 %copy-done.1 = bf16[1280,2176]{0,1:T(8,128)(2,1)} copy-done((bf16[1280,2176]{0,1:T(8,128)(2,1)}, bf16[1280,2176]{0,1:T(8,128)(2,1)S(1)}, u32[]{:S(2)}) %copy-start.1) | copy-done | bytes 5570584
  107.5 1.1 compare_and_fusion
  108.6 1.7 slice.50
  110.5 4.2 %constant_dynamic-slice_fusion = (bf16[1152,1024]{0,1:T(8,128)(2,1)S(1)}, bf16[1152,1024]{0,1:T(8,128)(2,1)}) fusion(bf16[1280,2176]{0,1:T(8,128)(2,1)} %copy-done.1, s32[]{:T(128)S(6)} %select_n.238, s32[]{:T(128)S(6)} %add.187), kind=kLoop, calls=%fused_computation.120 | loop fusion | bytes 9437192 | tf_op jit(solution)/shard_map/slice | solution.py:138
  115.4 2.5 %convolution_convert_fusion = bf16[8,128,2,4]{1,3,2,0:T(4,128)(2,1)S(1)} fusion(bf16[1152,8,128,1]{0,2,3,1:T(8,128)(2,1)} %bitcast.120, f32[8,2,4]{2,1,0:T(2,128)S(1)} %fusion.59, f32[8,2,4,1152]{3,2,1,0:T(4,128)S(1)} %fusion.11), kind=kOutput, calls=%fused_computation.38 | convolution fusion | flops 19104960 | bytes 2670848 | tf_op jit(solution)/shard_map/hgqk,khd->qhgd/dot_general | solution.py:158
  118.0 1.8 collective-permute-start.16
  119.8 4.4 %fusion.56 = f32[8,2,128]{2,1,0:T(2,128)S(1)} fusion(pred[128,1152]{0,1:T(8,128)(4,1)S(1)} %compare_and_fusion, bf16[1152,8,128,1]{0,2,3,1:T(8,128)(2,1)S(1)} %bitcast.116, bf16[128,8,2,128]{3,2,1,0:T(2,128)(2,1)} %reshape.348), kind=kOutput, calls=%fused_computation.128 | convolution fusion | flops 613418112 | bytes 3039232 | tf_op jit(solution)/shard_map/sub | solution.py:156
  124.1 7.2 %fusion.12 = bf16[8,128,2,128]{3,1,2,0:T(8,128)(2,1)} fusion(bf16[1152,8,128,1]{0,2,3,1:T(8,128)(2,1)} %bitcast.121, f32[8,2,128]{2,1,0:T(2,128)S(1)} %fusion.56, pred[128,1152]{0,1:T(8,128)(4,1)S(1)} %compare_and_fusion, bf16[1152,8,128,1]{0,2,3,1:T(8,128)(2,1)S(1)} %bitcast.117, bf16[128,8,2,128]{3,2,1,0:T(2,128)(2,1)} %reshape.348), kind=kOutput, calls=%fused_computation.24 | convolution fusion | flops 1220021376 | bytes 5922816 | tf_op jit(solution)/shard_map/hgqk,khd->qhgd/dot_general | solution.py:158
  132.2 7.0 %collective-permute-start.20 = (bf16[4,4,2048]{2,1,0:T(4,128)(2,1)S(1)}, bf16[4,4,2048]{2,1,0:T(4,128)(2,1)S(1)}, u32[]{:S(2)}, u32[]{:S(2)}) collective-permute-start(bf16[4,4,2048]{2,1,0:T(4,128)(2,1)S(1)} %broadcast_select_fusion.3), channel_id=1, source_target_pairs={{0,12},{1,13},{2,14},{3,15},{4,0},{5,1},{6,2},{7,3},{8,4},{9,5},{1... | collective-permute-start | bytes 196616 | tf_op jit(solution)/shard_map/ppermute | solution.py:54
  139.1 0.7 collective-permute-start.19
  139.8 1.9 %collective-permute-start.18 = (bf16[4,4,2048]{2,1,0:T(4,128)(2,1)S(1)}, bf16[4,4,2048]{2,1,0:T(4,128)(2,1)S(1)}, u32[]{:S(2)}, u32[]{:S(2)}) collective-permute-start(bf16[4,4,2048]{2,1,0:T(4,128)(2,1)S(1)} %broadcast_select_fusion.3), channel_id=1, source_target_pairs={{0,4},{1,5},{2,6},{3,7},{4,8},{5,9},{6,10},{7,11},{8,12},{9,13},{1... | collective-permute-start | bytes 196616 | tf_op jit(solution)/shard_map/ppermute | solution.py:54
  141.9 5.2 %collective-permute-done.19 = bf16[4,4,2048]{2,1,0:T(4,128)(2,1)S(1)} collective-permute-done((bf16[4,4,2048]{2,1,0:T(4,128)(2,1)S(1)}, bf16[4,4,2048]{2,1,0:T(4,128)(2,1)S(1)}, u32[]{:S(2)}, u32[]{:S(2)}) %collective-permute-start.19) | collective-permute-done | bytes 65568 | tf_op jit(solution)/shard_map/ppermute | solution.py:54
  147.3 0.8 gather_fusion.3
  148.2 6.5 %multiply_reduce_fusion = (f32[64]{0:T(128)S(1)}, f32[64,2688]{1,0:T(8,128)S(1)}) fusion(bf16[2048,2688]{1,0:T(8,128)(2,1)} %all-gather.2.cloned.1.call-done, bf16[64,2048]{1,0:T(8,128)(2,1)S(1)} %gather.51, pred[64]{0:T(512)(128)(4,1)S(1)} %broadcast_in_dim.142, bf16[64,2688]{1,0:T(8,128)(2,1)S(1)} %gather.46), kind=kOutput, calls=%fused_computation.40 | convolution fusion | flops 705634240 | bytes 12304704 | tf_op jit(solution)/shard_map/dot_general | solution.py:167
  154.8 4.5 %fusion.60 = (f32[64]{0:T(128)S(1)}, f32[64,1024]{1,0:T(8,128)S(1)}) fusion(bf16[1024,2688]{1,0:T(8,128)(2,1)} %param.14, f32[64,2688]{1,0:T(8,128)S(1)} %get-tuple-element.21, f32[2688]{0:T(1024)S(1)} %copy-done.5, f32[64]{0:T(128)S(1)} %add_rsqrt_fusion), kind=kOutput, calls=%fused_computation.130 | convolution fusion | flops 352903104 | bytes 6466560 | tf_op jit(solution)/shard_map/dot_general | solution.py:174
  159.6 0.8 collective-permute-start.23
  161.0 2.5 %fusion.7 = bf16[128,2688]{1,0:T(8,128)(2,1)} fusion(bf16[128,2048]{0,1:T(8,128)(2,1)S(1)} %bitcast.124, bf16[2048,2688]{1,0:T(8,128)(2,1)S(1)} %copy-done, bf16[128,2688]{1,0:T(8,128)(2,1)S(1)} %copy-done.3), kind=kOutput, calls=%fused_computation.17 | convolution fusion | flops 1410318336 | bytes 12910592 | tf_op jit(solution)/shard_map/dot_general | solution.py:171
  164.7 1.5 collective-permute-start.26
  166.7 2.0 %collective-permute-start.24 = (f32[4,3,64]{2,1,0:T(4,128)S(1)}, f32[4,3,64]{2,1,0:T(4,128)S(1)}, u32[]{:S(2)}, u32[]{:S(2)}) collective-permute-start(f32[4,3,64]{2,1,0:T(4,128)S(1)} %broadcast_select_fusion.4), channel_id=1, source_target_pairs={{0,4},{1,5},{2,6},{3,7},{4,8},{5,9},{6,10},{7,11},{8,12},{9,13},{1... | collective-permute-start | bytes 9224 | tf_op jit(solution)/shard_map/ppermute | solution.py:54
  168.8 2.0 %collective-permute-done.25 = f32[4,3,64]{2,1,0:T(4,128)S(1)} collective-permute-done((f32[4,3,64]{2,1,0:T(4,128)S(1)}, f32[4,3,64]{2,1,0:T(4,128)S(1)}, u32[]{:S(2)}, u32[]{:S(2)}) %collective-permute-start.25) | collective-permute-done | bytes 3104 | tf_op jit(solution)/shard_map/ppermute | solution.py:54
  170.8 1.4 collective-permute-done.24
  173.0 0.8 broadcast_subtract_fusion
  (101 shorter events, 11.2 us)
Async XLA Ops:
  7.2 14.1 %copy-start.7 = (s32[64]{0:T(128)S(1)}, s32[64]{0:T(128)}, u32[]{:S(2)}) copy-start(s32[64]{0:T(128)} %param.15) | copy-start | bytes 772
  7.2 14.1 %copy-start.4 = (bf16[128,2048]{1,0:T(8,128)(2,1)S(1)}, bf16[128,2048]{1,0:T(8,128)(2,1)}, u32[]{:S(2)}) copy-start(bf16[128,2048]{1,0:T(8,128)(2,1)} %param.8) | copy-start | bytes 1572868
  7.2 141.0 %all-gather.2.cloned.1.call-start = ((), (), s32[]{:S(2)}) async-start(), calls=%async_computation | async-start | bytes 11698176 | tf_op jit(solution)/shard_map/all_gather | solution.py:121
  10.8 29.2 %collective-permute-start = (bf16[128,2176]{0,1:T(8,128)(2,1)}, bf16[128,2176]{0,1:T(8,128)(2,1)S(1)}, u32[]{:S(2)}, u32[]{:S(2)}) collective-permute-start(bf16[128,2176]{0,1:T(8,128)(2,1)} %pad_maximum_fusion.2), channel_id=1, source_target_pairs={{0,4},{1,5},{2,6},{3,7},{4,8},{5,9},{6,10},{7,11},{8,12},{9,13},{1... | collective-permute-start | bytes 1671176 | tf_op jit(solution)/shard_map/ppermute | solution.py:70
  15.7 34.8 %collective-permute-start.5 = (bf16[128,2176]{0,1:T(8,128)(2,1)}, bf16[128,2176]{0,1:T(8,128)(2,1)S(1)}, u32[]{:S(2)}, u32[]{:S(2)}) collective-permute-start(bf16[128,2176]{0,1:T(8,128)(2,1)} %pad_maximum_fusion.2), channel_id=1, source_target_pairs={{0,2},{1,3},{4,6},{5,7},{8,10},{9,11},{12,14},{13,15},{16,18},{17,... | collective-permute-start | bytes 1671176 | tf_op jit(solution)/shard_map/ppermute | solution.py:76
  20.2 18.8 %collective-permute-start.11 = (bf16[1,4,2688]{2,1,0:T(4,128)(2,1)S(1)}, bf16[1,4,2688]{2,1,0:T(4,128)(2,1)S(1)}, u32[]{:S(2)}, u32[]{:S(2)}) collective-permute-start(bf16[1,4,2688]{2,1,0:T(4,128)(2,1)S(1)} %bitcast.126), channel_id=1, source_target_pairs={{0,3},{1,0},{2,1},{3,2},{4,7},{5,4},{6,5},{7,6},{8,11},{9,8},{10,9... | collective-permute-start | bytes 64520 | tf_op jit(solution)/shard_map/ppermute | solution.py:54
  20.3 19.0 %collective-permute-start.10 = (bf16[1,4,2688]{2,1,0:T(4,128)(2,1)S(1)}, bf16[1,4,2688]{2,1,0:T(4,128)(2,1)S(1)}, u32[]{:S(2)}, u32[]{:S(2)}) collective-permute-start(bf16[1,4,2688]{2,1,0:T(4,128)(2,1)S(1)} %bitcast.127), channel_id=1, source_target_pairs={{0,2},{1,3},{2,0},{3,1},{4,6},{5,7},{6,4},{7,5},{8,10},{9,11},{10,... | collective-permute-start | bytes 64520 | tf_op jit(solution)/shard_map/ppermute | solution.py:54
  21.1 18.1 %collective-permute-start.9 = (bf16[1,4,2688]{2,1,0:T(4,128)(2,1)S(1)}, bf16[1,4,2688]{2,1,0:T(4,128)(2,1)S(1)}, u32[]{:S(2)}, u32[]{:S(2)}) collective-permute-start(bf16[1,4,2688]{2,1,0:T(4,128)(2,1)S(1)} %bitcast.128), channel_id=1, source_target_pairs={{0,1},{1,2},{2,3},{3,0},{4,5},{5,6},{6,7},{7,4},{8,9},{9,10},{10,1... | collective-permute-start | bytes 64520 | tf_op jit(solution)/shard_map/ppermute | solution.py:54
  40.0 23.9 %collective-permute-start.1 = (bf16[128,2176]{0,1:T(8,128)(2,1)S(1)}, bf16[128,2176]{0,1:T(8,128)(2,1)S(1)}, u32[]{:S(2)}, u32[]{:S(2)}) collective-permute-start(bf16[128,2176]{0,1:T(8,128)(2,1)S(1)} %collective-permute-done), channel_id=1, source_target_pairs={{0,4},{1,5},{2,6},{3,7},{4,8},{5,9},{6,10},{7,11},{8,12},{9,13},{1... | collective-permute-start | bytes 1671176 | tf_op jit(solution)/shard_map/ppermute | solution.py:70
  44.0 22.0 %collective-permute-start.6 = (bf16[128,2176]{0,1:T(8,128)(2,1)S(1)}, bf16[128,2176]{0,1:T(8,128)(2,1)S(1)}, u32[]{:S(2)}, u32[]{:S(2)}) collective-permute-start(bf16[128,2176]{0,1:T(8,128)(2,1)S(1)} %collective-permute-done), channel_id=1, source_target_pairs={{2,0},{3,1},{6,4},{7,5},{10,8},{11,9},{14,12},{15,13},{18,16},{19,... | collective-permute-start | bytes 1671176 | tf_op jit(solution)/shard_map/ppermute | solution.py:76
  45.4 50.4 %collective-permute-start.14 = (bf16[4,4,2688]{2,1,0:T(4,128)(2,1)S(1)}, bf16[4,4,2688]{2,1,0:T(4,128)(2,1)S(1)}, u32[]{:S(2)}, u32[]{:S(2)}) collective-permute-start(bf16[4,4,2688]{2,1,0:T(4,128)(2,1)S(1)} %broadcast_select_fusion.2), channel_id=1, source_target_pairs={{0,12},{1,13},{2,14},{3,15},{4,0},{5,1},{6,2},{7,3},{8,4},{9,5},{1... | collective-permute-start | bytes 258056 | tf_op jit(solution)/shard_map/ppermute | solution.py:54
  48.1 48.3 %collective-permute-start.13 = (bf16[4,4,2688]{2,1,0:T(4,128)(2,1)S(1)}, bf16[4,4,2688]{2,1,0:T(4,128)(2,1)S(1)}, u32[]{:S(2)}, u32[]{:S(2)}) collective-permute-start(bf16[4,4,2688]{2,1,0:T(4,128)(2,1)S(1)} %broadcast_select_fusion.2), channel_id=1, source_target_pairs={{0,8},{1,9},{2,10},{3,11},{4,12},{5,13},{6,14},{7,15},{8,0},{9,1},... | collective-permute-start | bytes 258056 | tf_op jit(solution)/shard_map/ppermute | solution.py:54
  50.5 45.9 %collective-permute-start.12 = (bf16[4,4,2688]{2,1,0:T(4,128)(2,1)S(1)}, bf16[4,4,2688]{2,1,0:T(4,128)(2,1)S(1)}, u32[]{:S(2)}, u32[]{:S(2)}) collective-permute-start(bf16[4,4,2688]{2,1,0:T(4,128)(2,1)S(1)} %broadcast_select_fusion.2), channel_id=1, source_target_pairs={{0,4},{1,5},{2,6},{3,7},{4,8},{5,9},{6,10},{7,11},{8,12},{9,13},{1... | collective-permute-start | bytes 258056 | tf_op jit(solution)/shard_map/ppermute | solution.py:54
  63.9 26.3 %collective-permute-start.2 = (bf16[128,2176]{0,1:T(8,128)(2,1)S(1)}, bf16[128,2176]{0,1:T(8,128)(2,1)S(1)}, u32[]{:S(2)}, u32[]{:S(2)}) collective-permute-start(bf16[128,2176]{0,1:T(8,128)(2,1)S(1)} %collective-permute-done), channel_id=1, source_target_pairs={{0,2},{1,3},{4,6},{5,7},{8,10},{9,11},{12,14},{13,15},{16,18},{17,... | collective-permute-start | bytes 1671176 | tf_op jit(solution)/shard_map/ppermute | solution.py:76
  66.0 28.6 %collective-permute-start.3 = (bf16[128,2176]{0,1:T(8,128)(2,1)S(1)}, bf16[128,2176]{0,1:T(8,128)(2,1)S(1)}, u32[]{:S(2)}, u32[]{:S(2)}) collective-permute-start(bf16[128,2176]{0,1:T(8,128)(2,1)S(1)} %collective-permute-done.1), channel_id=1, source_target_pairs={{2,0},{3,1},{6,4},{7,5},{10,8},{11,9},{14,12},{15,13},{18,16},{19,... | collective-permute-start | bytes 1671176 | tf_op jit(solution)/shard_map/ppermute | solution.py:76
  90.2 9.2 %collective-permute-start.7 = (bf16[2,128,2176]{1,2,0:T(8,128)(2,1)}, bf16[2,128,2176]{1,2,0:T(8,128)(2,1)}, u32[]{:S(2)}, u32[]{:S(2)}) collective-permute-start(bf16[2,128,2176]{1,2,0:T(8,128)(2,1)} %pad_maximum_fusion.1), channel_id=1, source_target_pairs={{0,1},{1,0},{2,3},{3,2},{4,5},{5,4},{6,7},{7,6},{8,9},{9,8},{10,11... | collective-permute-start | bytes 3342344 | tf_op jit(solution)/shard_map/ppermute | solution.py:37
  95.7 5.0 %collective-permute-start.4 = (bf16[2,128,2176]{1,2,0:T(8,128)(2,1)}, bf16[2,128,2176]{1,2,0:T(8,128)(2,1)}, u32[]{:S(2)}, u32[]{:S(2)}) collective-permute-start(bf16[2,128,2176]{1,2,0:T(8,128)(2,1)} %pad_maximum_fusion), channel_id=1, source_target_pairs={{0,1},{1,0},{2,3},{3,2},{4,5},{5,4},{6,7},{7,6},{8,9},{9,8},{10,11... | collective-permute-start | bytes 3342344 | tf_op jit(solution)/shard_map/ppermute | solution.py:37
  95.8 7.7 %collective-permute-start.8 = (bf16[128,2176]{0,1:T(8,128)(2,1)}, bf16[128,2176]{0,1:T(8,128)(2,1)}, u32[]{:S(2)}, u32[]{:S(2)}) collective-permute-start(bf16[128,2176]{0,1:T(8,128)(2,1)} %pad_maximum_fusion.2), channel_id=1, source_target_pairs={{0,1},{1,0},{2,3},{3,2},{4,5},{5,4},{6,7},{7,6},{8,9},{9,8},{10,11... | collective-permute-start | bytes 1671176 | tf_op jit(solution)/shard_map/ppermute | solution.py:37
  103.1 4.4 %copy-start.6 = (s32[128]{0:T(128)S(1)}, s32[128]{0:T(128)}, u32[]{:S(2)}) copy-start(s32[128]{0:T(128)} %param.10) | copy-start | bytes 1540
  105.1 2.4 %copy-start.1 = (bf16[1280,2176]{0,1:T(8,128)(2,1)}, bf16[1280,2176]{0,1:T(8,128)(2,1)S(1)}, u32[]{:S(2)}) copy-start(bf16[1280,2176]{0,1:T(8,128)(2,1)S(1)} %fusion.19) | copy-start | bytes 16711684
  117.9 13.4 %collective-permute-start.17 = (bf16[1,4,2048]{2,1,0:T(4,128)(2,1)S(1)}, bf16[1,4,2048]{2,1,0:T(4,128)(2,1)S(1)}, u32[]{:S(2)}, u32[]{:S(2)}) collective-permute-start(bf16[1,4,2048]{2,1,0:T(4,128)(2,1)S(1)} %bitcast.143), channel_id=1, source_target_pairs={{0,3},{1,0},{2,1},{3,2},{4,7},{5,4},{6,5},{7,6},{8,11},{9,8},{10,9... | collective-permute-start | bytes 49160 | tf_op jit(solution)/shard_map/ppermute | solution.py:54
  118.0 13.4 %collective-permute-start.16 = (bf16[1,4,2048]{2,1,0:T(4,128)(2,1)S(1)}, bf16[1,4,2048]{2,1,0:T(4,128)(2,1)S(1)}, u32[]{:S(2)}, u32[]{:S(2)}) collective-permute-start(bf16[1,4,2048]{2,1,0:T(4,128)(2,1)S(1)} %bitcast.144), channel_id=1, source_target_pairs={{0,2},{1,3},{2,0},{3,1},{4,6},{5,7},{6,4},{7,5},{8,10},{9,11},{10,... | collective-permute-start | bytes 49160 | tf_op jit(solution)/shard_map/ppermute | solution.py:54
  119.8 11.6 %collective-permute-start.15 = (bf16[1,4,2048]{2,1,0:T(4,128)(2,1)S(1)}, bf16[1,4,2048]{2,1,0:T(4,128)(2,1)S(1)}, u32[]{:S(2)}, u32[]{:S(2)}) collective-permute-start(bf16[1,4,2048]{2,1,0:T(4,128)(2,1)S(1)} %bitcast.145), channel_id=1, source_target_pairs={{0,1},{1,2},{2,3},{3,0},{4,5},{5,6},{6,7},{7,4},{8,9},{9,10},{10,1... | collective-permute-start | bytes 49160 | tf_op jit(solution)/shard_map/ppermute | solution.py:54
  132.2 9.7 %collective-permute-start.20 = (bf16[4,4,2048]{2,1,0:T(4,128)(2,1)S(1)}, bf16[4,4,2048]{2,1,0:T(4,128)(2,1)S(1)}, u32[]{:S(2)}, u32[]{:S(2)}) collective-permute-start(bf16[4,4,2048]{2,1,0:T(4,128)(2,1)S(1)} %broadcast_select_fusion.3), channel_id=1, source_target_pairs={{0,12},{1,13},{2,14},{3,15},{4,0},{5,1},{6,2},{7,3},{8,4},{9,5},{1... | collective-permute-start | bytes 196616 | tf_op jit(solution)/shard_map/ppermute | solution.py:54
  139.1 8.0 %collective-permute-start.19 = (bf16[4,4,2048]{2,1,0:T(4,128)(2,1)S(1)}, bf16[4,4,2048]{2,1,0:T(4,128)(2,1)S(1)}, u32[]{:S(2)}, u32[]{:S(2)}) collective-permute-start(bf16[4,4,2048]{2,1,0:T(4,128)(2,1)S(1)} %broadcast_select_fusion.3), channel_id=1, source_target_pairs={{0,8},{1,9},{2,10},{3,11},{4,12},{5,13},{6,14},{7,15},{8,0},{9,1},... | collective-permute-start | bytes 196616 | tf_op jit(solution)/shard_map/ppermute | solution.py:54
  139.8 7.3 %collective-permute-start.18 = (bf16[4,4,2048]{2,1,0:T(4,128)(2,1)S(1)}, bf16[4,4,2048]{2,1,0:T(4,128)(2,1)S(1)}, u32[]{:S(2)}, u32[]{:S(2)}) collective-permute-start(bf16[4,4,2048]{2,1,0:T(4,128)(2,1)S(1)} %broadcast_select_fusion.3), channel_id=1, source_target_pairs={{0,4},{1,5},{2,6},{3,7},{4,8},{5,9},{6,10},{7,11},{8,12},{9,13},{1... | collective-permute-start | bytes 196616 | tf_op jit(solution)/shard_map/ppermute | solution.py:54
  148.2 6.6 %copy-start.5 = (f32[2688]{0:T(1024)S(1)}, f32[2688]{0:T(1024)}, u32[]{:S(2)}) copy-start(f32[2688]{0:T(1024)} %param.12) | copy-start | bytes 32260
  148.2 12.8 %copy-start = (bf16[2048,2688]{1,0:T(8,128)(2,1)S(1)}, bf16[2048,2688]{1,0:T(8,128)(2,1)}, u32[]{:S(2)}) copy-start(bf16[2048,2688]{1,0:T(8,128)(2,1)} %all-gather.2.cloned.1.call-done) | copy-start | bytes 33030148
  154.7 6.2 %copy-start.2 = (bf16[8,128,2,128]{3,1,2,0:T(8,128)(2,1)S(1)}, bf16[8,128,2,128]{3,1,2,0:T(8,128)(2,1)}, u32[]{:S(2)}) copy-start(bf16[8,128,2,128]{3,1,2,0:T(8,128)(2,1)} %fusion.12) | copy-start | bytes 1572868
  154.8 6.2 %copy-start.3 = (bf16[128,2688]{1,0:T(8,128)(2,1)S(1)}, bf16[128,2688]{1,0:T(8,128)(2,1)}, u32[]{:S(2)}) copy-start(bf16[128,2688]{1,0:T(8,128)(2,1)} %param.11) | copy-start | bytes 2064388
  159.6 4.0 %collective-permute-start.23 = (f32[1,3,64]{2,1,0:T(4,128)S(1)}, f32[1,3,64]{2,1,0:T(4,128)S(1)}, u32[]{:S(2)}, u32[]{:S(2)}) collective-permute-start(f32[1,3,64]{2,1,0:T(4,128)S(1)} %get-tuple-element.19), channel_id=1, source_target_pairs={{0,3},{1,0},{2,1},{3,2},{4,7},{5,4},{6,5},{7,6},{8,11},{9,8},{10,9... | collective-permute-start | bytes 2312 | tf_op jit(solution)/shard_map/ppermute | solution.py:54
  160.3 3.6 %collective-permute-start.22 = (f32[1,3,64]{2,1,0:T(4,128)S(1)}, f32[1,3,64]{2,1,0:T(4,128)S(1)}, u32[]{:S(2)}, u32[]{:S(2)}) collective-permute-start(f32[1,3,64]{2,1,0:T(4,128)S(1)} %get-tuple-element.19), channel_id=1, source_target_pairs={{0,2},{1,3},{2,0},{3,1},{4,6},{5,7},{6,4},{7,5},{8,10},{9,11},{10,... | collective-permute-start | bytes 2312 | tf_op jit(solution)/shard_map/ppermute | solution.py:54
  161.0 3.0 %collective-permute-start.21 = (f32[1,3,64]{2,1,0:T(4,128)S(1)}, f32[1,3,64]{2,1,0:T(4,128)S(1)}, u32[]{:S(2)}, u32[]{:S(2)}) collective-permute-start(f32[1,3,64]{2,1,0:T(4,128)S(1)} %get-tuple-element.19), channel_id=1, source_target_pairs={{0,1},{1,2},{2,3},{3,0},{4,5},{5,6},{6,7},{7,4},{8,9},{9,10},{10,1... | collective-permute-start | bytes 2312 | tf_op jit(solution)/shard_map/ppermute | solution.py:54
  164.7 4.1 %collective-permute-start.26 = (f32[4,3,64]{2,1,0:T(4,128)S(1)}, f32[4,3,64]{2,1,0:T(4,128)S(1)}, u32[]{:S(2)}, u32[]{:S(2)}) collective-permute-start(f32[4,3,64]{2,1,0:T(4,128)S(1)} %broadcast_select_fusion.4), channel_id=1, source_target_pairs={{0,12},{1,13},{2,14},{3,15},{4,0},{5,1},{6,2},{7,3},{8,4},{9,5},{1... | collective-permute-start | bytes 9224 | tf_op jit(solution)/shard_map/ppermute | solution.py:54
  166.2 4.6 %collective-permute-start.25 = (f32[4,3,64]{2,1,0:T(4,128)S(1)}, f32[4,3,64]{2,1,0:T(4,128)S(1)}, u32[]{:S(2)}, u32[]{:S(2)}) collective-permute-start(f32[4,3,64]{2,1,0:T(4,128)S(1)} %broadcast_select_fusion.4), channel_id=1, source_target_pairs={{0,8},{1,9},{2,10},{3,11},{4,12},{5,13},{6,14},{7,15},{8,0},{9,1},... | collective-permute-start | bytes 9224 | tf_op jit(solution)/shard_map/ppermute | solution.py:54
  166.7 5.4 %collective-permute-start.24 = (f32[4,3,64]{2,1,0:T(4,128)S(1)}, f32[4,3,64]{2,1,0:T(4,128)S(1)}, u32[]{:S(2)}, u32[]{:S(2)}) collective-permute-start(f32[4,3,64]{2,1,0:T(4,128)S(1)} %broadcast_select_fusion.4), channel_id=1, source_target_pairs={{0,4},{1,5},{2,6},{3,7},{4,8},{5,9},{6,10},{7,11},{8,12},{9,13},{1... | collective-permute-start | bytes 9224 | tf_op jit(solution)/shard_map/ppermute | solution.py:54
Sparse Core Ops, SparseCore 0:
  10.3 115.2 all-gather.1

commit v10 on v8

--- a/solution.py
+++ b/solution.py
@@ -177,14 +177,13 @@
     if len(cycle) <= RING_CHIPS:
         slots, sources = ring_gather(out_proj, cycle)
         partner_slots = [swap_cores(s) for s in slots]
-        chip_rows = CORES * out_proj.shape[0]
-        full_proj = jnp.concatenate(
-            [in_core_order(m, t, first_core) for m, t in zip(slots, partner_slots)], 0
-        )
+        shard_rows = out_proj.shape[0]
+        full_proj = jnp.concatenate(slots + partner_slots, 0)
+        shards = [s * CORES + core for s in sources] + [s * CORES + (1 - core) for s in sources]
 
         def slot_columns(rows_of_context):
             return jnp.concatenate(
-                [lax.dynamic_slice_in_dim(rows_of_context, s * chip_rows, chip_rows, 1) for s in sources], 1
+                [lax.dynamic_slice_in_dim(rows_of_context, s * shard_rows, shard_rows, 1) for s in shards], 1
             )
 
     else:
@@ -199,6 +198,7 @@
     seg_cols = jnp.broadcast_to(segment_ids.astype(jnp.bfloat16)[:, None], (token_rows, SEG_LANES))
     own = jnp.concatenate([joined_keys_values, seg_cols], 1)
     key_value_pair, key_seg = halo_window(own, kv_width, blocks, first_core)
+    key_value_pair, queries, full_proj = lax.optimization_barrier((key_value_pair, queries, full_proj))
     count_of_keys = key_value_pair.shape[0]
     query_pos = first_row + jnp.arange(token_rows, dtype=jnp.int32)
     key_pos = first_row - blocks * token_rows + jnp.arange(count_of_keys, dtype=jnp.int32)

time: 187 us -> 215 us (1.15)
  other arithmetic: 30.9 us -> 9.74 us
  starting transfers between devices: 36.9 us -> 56.5 us
  local copies, waits for them, and re-layouts: 13.2 us -> 29.9 us
  waiting for transfers between devices: 67 us -> 79.6 us
    unnamed x12 -> x5, other arithmetic: 21 us -> 1.53 us
    ppermute x3, waiting for transfers between devices: 9.67 us -> 26.3 us  [ring_gather(): current = lax.ppermute(current, SEQ, backward)]
    unnamed x37 -> x70, local copies, waits for them, and re-layouts: 1.62 us -> 17 us
    ppermute x3, starting transfers between devices: 2.9 us -> 10.6 us  [ring_gather(): current = lax.ppermute(current, SEQ, backward)]
    ppermute x18, starting transfers between devices: 15.9 us -> 22.2 us  [gather_rows(): received.append(lax.ppermute(data, SEQ, pairs))]
    ppermute x4, starting transfers between devices: 0.01 us -> 5.38 us  [ring_gather(): current = lax.ppermute(current, SEQ, forward)]
    ppermute x18, waiting for transfers between devices: 16.4 us -> 20.5 us  [gather_rows(): received.append(lax.ppermute(data, SEQ, pairs))]
    ppermute x2, waiting for transfers between devices: 3.62 us -> 0.01 us  [shift_chips(): lax.ppermute(value, SEQ, [(s, s + step) for s in range(count - step)])]
  transfers between devices with their start and end apart: 42 -> 42, of which waited for: 20 -> 16; matrix products, arithmetic and copies ran while one was open for 29% -> 16% of each run, Pallas kernels for 0% -> 0%
where the time goes in v10:
time: 215 us
  waiting for transfers between devices  79.6 us (37%)
  starting transfers between devices  56.5 us (26%)
  local copies, waits for them, and re-layouts  29.9 us (14%)
  matrix products  25.7 us (12%)
  between operations  13.2 us (6%)
  other arithmetic  9.74 us (5%)
    ppermute x3, waiting for transfers between devices, ring_gather(): current = lax.ppermute(current, SEQ, backward)  26.3 us
    ppermute x4, waiting for transfers between devices, ring_gather(): current = lax.ppermute(current, SEQ, forward)  24.4 us
    ppermute x18, starting transfers between devices, gather_rows(): received.append(lax.ppermute(data, SEQ, pairs))  22.2 us
    ppermute x18, waiting for transfers between devices, gather_rows(): received.append(lax.ppermute(data, SEQ, pairs))  20.5 us
    unnamed x70, local copies, waits for them, and re-layouts  17 us
    ppermute x3, starting transfers between devices, ring_gather(): current = lax.ppermute(current, SEQ, backward)  10.6 us
    ppermute x2, starting transfers between devices, shift_chips(): lax.ppermute(value, SEQ, [(s, s + step) for s in range(count - step)])  8.81 us
    ppermute x4, waiting for transfers between devices, across_pair(): return lax.ppermute(value, SEQ, pairs)  8.27 us
  transfers between devices with their start and end apart: 42, of which 16 were waited for; matrix products, arithmetic and copies ran while one was open for 16% of the time, Pallas kernels for 0%

profile of v10, /device:TPU:0, one launch (start us, length us, event | category | flops | bytes accessed | tf_op | source)
XLA Modules:
  0.0 214.6 jit_solution(9830728958314115009)
XLA Ops:
  0.7 1.0 slice.68
  1.7 3.0 %collective-permute-start.25 = (bf16[1,4,2688]{2,1,0:T(4,128)(2,1)S(1)}, bf16[1,4,2688]{2,1,0:T(4,128)(2,1)S(1)}, u32[]{:S(2)}, u32[]{:S(2)}) collective-permute-start(bf16[1,4,2688]{2,1,0:T(4,128)(2,1)S(1)} %bitcast.138), channel_id=1, source_target_pairs={{0,2},{1,3},{2,0},{3,1},{4,6},{5,7},{6,4},{7,5},{8,10},{9,11},{10,... | collective-permute-start | bytes 64520 | tf_op jit(solution)/shard_map/ppermute | solution.py:57
  4.8 1.7 collective-permute-start.26
  7.2 1.3 copy.17
  9.3 3.5 %collective-permute-start = (bf16[128,2176]{0,1:T(8,128)(2,1)}, bf16[128,2176]{0,1:T(8,128)(2,1)S(1)}, u32[]{:S(2)}, u32[]{:S(2)}) collective-permute-start(bf16[128,2176]{0,1:T(8,128)(2,1)} %pad_maximum_fusion.2), channel_id=1, source_target_pairs={{0,4},{1,5},{2,6},{3,7},{4,8},{5,9},{6,10},{7,11},{8,12},{9,13},{1... | collective-permute-start | bytes 1671176 | tf_op jit(solution)/shard_map/ppermute | solution.py:73
  12.9 1.6 collective-permute-start.9
  30.2 2.7 %collective-permute-start.28 = (bf16[4,4,2688]{2,1,0:T(4,128)(2,1)S(1)}, bf16[4,4,2688]{2,1,0:T(4,128)(2,1)S(1)}, u32[]{:S(2)}, u32[]{:S(2)}) collective-permute-start(bf16[4,4,2688]{2,1,0:T(4,128)(2,1)S(1)} %broadcast_select_fusion.3), channel_id=1, source_target_pairs={{0,8},{1,9},{2,10},{3,11},{4,12},{5,13},{6,14},{7,15},{8,0},{9,1},... | collective-permute-start | bytes 258056 | tf_op jit(solution)/shard_map/ppermute | solution.py:57
  33.1 9.3 %collective-permute-done.29 = bf16[4,4,2688]{2,1,0:T(4,128)(2,1)S(1)} collective-permute-done((bf16[4,4,2688]{2,1,0:T(4,128)(2,1)S(1)}, bf16[4,4,2688]{2,1,0:T(4,128)(2,1)S(1)}, u32[]{:S(2)}, u32[]{:S(2)}) %collective-permute-start.29) | collective-permute-done | bytes 86048 | tf_op jit(solution)/shard_map/ppermute | solution.py:57
  43.3 1.3 collective-permute-start.5
  44.7 1.3 collective-permute-start.6
  46.0 5.3 %collective-permute-start.1 = (bf16[128,2176]{0,1:T(8,128)(2,1)S(1)}, bf16[128,2176]{0,1:T(8,128)(2,1)S(1)}, u32[]{:S(2)}, u32[]{:S(2)}) collective-permute-start(bf16[128,2176]{0,1:T(8,128)(2,1)S(1)} %collective-permute-done), channel_id=1, source_target_pairs={{0,4},{1,5},{2,6},{3,7},{4,8},{5,9},{6,10},{7,11},{8,12},{9,13},{1... | collective-permute-start | bytes 1671176 | tf_op jit(solution)/shard_map/ppermute | solution.py:73
  52.6 3.5 %collective-permute-start.13 = (bf16[128,2688]{1,0:T(8,128)(2,1)}, bf16[128,2688]{1,0:T(8,128)(2,1)S(1)}, u32[]{:S(2)}, u32[]{:S(2)}) collective-permute-start(bf16[128,2688]{1,0:T(8,128)(2,1)} %param.15), channel_id=1, source_target_pairs={{0,2},{1,3},{2,6},{3,7},{4,0},{5,1},{6,10},{7,11},{8,4},{9,5},{10,... | collective-permute-start | bytes 2064392 | tf_op jit(solution)/shard_map/ppermute | solution.py:152
  56.1 2.0 constant_dynamic-update-slice_fusion.14
  58.1 4.1 %collective-permute-start.2 = (bf16[128,2176]{0,1:T(8,128)(2,1)S(1)}, bf16[128,2176]{0,1:T(8,128)(2,1)S(1)}, u32[]{:S(2)}, u32[]{:S(2)}) collective-permute-start(bf16[128,2176]{0,1:T(8,128)(2,1)S(1)} %collective-permute-done), channel_id=1, source_target_pairs={{0,2},{1,3},{4,6},{5,7},{8,10},{9,11},{12,14},{13,15},{16,18},{17,... | collective-permute-start | bytes 1671176 | tf_op jit(solution)/shard_map/ppermute | solution.py:79
  62.3 1.8 collective-permute-start.10
  64.0 1.3 collective-permute-start.3
  65.3 1.1 broadcast_select_fusion
  66.6 6.1 %collective-permute-done.13 = bf16[128,2688]{1,0:T(8,128)(2,1)S(1)} collective-permute-done((bf16[128,2688]{1,0:T(8,128)(2,1)}, bf16[128,2688]{1,0:T(8,128)(2,1)S(1)}, u32[]{:S(2)}, u32[]{:S(2)}) %collective-permute-start.13) | collective-permute-done | bytes 688160 | tf_op jit(solution)/shard_map/ppermute | solution.py:152
  72.7 8.2 %collective-permute-done.10 = bf16[128,2688]{1,0:T(8,128)(2,1)S(1)} collective-permute-done((bf16[128,2688]{1,0:T(8,128)(2,1)}, bf16[128,2688]{1,0:T(8,128)(2,1)S(1)}, u32[]{:S(2)}, u32[]{:S(2)}) %collective-permute-start.10) | collective-permute-done | bytes 688160 | tf_op jit(solution)/shard_map/ppermute | solution.py:147
  81.8 1.6 collective-permute-done.2
  83.4 6.7 %collective-permute-done.3 = bf16[128,2176]{0,1:T(8,128)(2,1)S(1)} collective-permute-done((bf16[128,2176]{0,1:T(8,128)(2,1)S(1)}, bf16[128,2176]{0,1:T(8,128)(2,1)S(1)}, u32[]{:S(2)}, u32[]{:S(2)}) %collective-permute-start.3) | collective-permute-done | bytes 557088 | tf_op jit(solution)/shard_map/ppermute | solution.py:79
  90.3 14.5 %collective-permute-done.11 = bf16[128,2688]{1,0:T(8,128)(2,1)S(1)} collective-permute-done((bf16[128,2688]{1,0:T(8,128)(2,1)S(1)}, bf16[128,2688]{1,0:T(8,128)(2,1)S(1)}, u32[]{:S(2)}, u32[]{:S(2)}) %collective-permute-start.11) | collective-permute-done | bytes 688160 | tf_op jit(solution)/shard_map/ppermute | solution.py:147
  105.7 2.0 collective-permute-start.12
  107.8 9.4 %collective-permute-done.14 = bf16[128,2688]{1,0:T(8,128)(2,1)S(1)} collective-permute-done((bf16[128,2688]{1,0:T(8,128)(2,1)S(1)}, bf16[128,2688]{1,0:T(8,128)(2,1)S(1)}, u32[]{:S(2)}, u32[]{:S(2)}) %collective-permute-start.14) | collective-permute-done | bytes 688160 | tf_op jit(solution)/shard_map/ppermute | solution.py:152
  117.2 1.7 collective-permute-done.12
  118.8 7.0 %collective-permute-start.15 = (bf16[128,2688]{1,0:T(8,128)(2,1)S(1)}, bf16[128,2688]{1,0:T(8,128)(2,1)S(1)}, u32[]{:S(2)}, u32[]{:S(2)}) collective-permute-start(bf16[128,2688]{1,0:T(8,128)(2,1)S(1)} %collective-permute-done.14), channel_id=1, source_target_pairs={{0,2},{1,3},{2,6},{3,7},{4,0},{5,1},{6,10},{7,11},{8,4},{9,5},{10,... | collective-permute-start | bytes 2064392 | tf_op jit(solution)/shard_map/ppermute | solution.py:152
  128.5 10.8 %collective-permute-done.15 = bf16[128,2688]{1,0:T(8,128)(2,1)S(1)} collective-permute-done((bf16[128,2688]{1,0:T(8,128)(2,1)S(1)}, bf16[128,2688]{1,0:T(8,128)(2,1)S(1)}, u32[]{:S(2)}, u32[]{:S(2)}) %collective-permute-start.15) | collective-permute-done | bytes 688160 | tf_op jit(solution)/shard_map/ppermute | solution.py:152
  147.3 1.6 fusion.14
  149.5 1.1 compare_and_fusion
  154.3 1.9 fusion.45
  156.2 1.2 reshape.338
  157.4 4.4 %fusion.48 = f32[8,2,128]{2,1,0:T(2,128)S(1)} fusion(pred[128,1152]{0,1:T(8,128)(4,1)S(1)} %compare_and_fusion, bf16[1152,8,128,1]{0,2,3,1:T(8,128)(2,1)S(1)} %bitcast.115, bf16[128,8,2,128]{3,2,1,0:T(2,128)(2,1)} %reshape.338), kind=kOutput, calls=%fused_computation.168 | convolution fusion | flops 613418112 | bytes 3039232 | tf_op jit(solution)/shard_map/sub | solution.py:226
  161.7 6.4 %fusion.7 = bf16[8,128,2,128]{3,1,2,0:T(8,128)(2,1)S(1)} fusion(bf16[1152,8,128,1]{0,2,3,1:T(8,128)(2,1)} %bitcast.117, f32[8,2,128]{2,1,0:T(2,128)S(1)} %fusion.48, pred[128,1152]{0,1:T(8,128)(4,1)S(1)} %compare_and_fusion, bf16[1152,8,128,1]{0,2,3,1:T(8,128)(2,1)S(1)} %bitcast.116, bf16[128,8,2,128]{3,2,1,0:T(2,128)(2,1)} %reshape.338), kind=kOutput, calls=%fused_computation.18 | convolution fusion | flops 1220021376 | bytes 5922816 | tf_op jit(solution)/shard_map/hgqk,khd->qhgd/dot_general | solution.py:228
  169.1 2.6 %collective-permute-start.31 = (bf16[1,4,2048]{2,1,0:T(4,128)(2,1)S(1)}, bf16[1,4,2048]{2,1,0:T(4,128)(2,1)S(1)}, u32[]{:S(2)}, u32[]{:S(2)}) collective-permute-start(bf16[1,4,2048]{2,1,0:T(4,128)(2,1)S(1)} %bitcast.147), channel_id=1, source_target_pairs={{0,2},{1,3},{2,0},{3,1},{4,6},{5,7},{6,4},{7,5},{8,10},{9,11},{10,... | collective-permute-start | bytes 49160 | tf_op jit(solution)/shard_map/ppermute | solution.py:57
  171.8 1.7 collective-permute-start.32
  173.8 1.1 collective-permute-done.30
  175.6 3.3 %collective-permute-start.35 = (bf16[4,4,2048]{2,1,0:T(4,128)(2,1)S(1)}, bf16[4,4,2048]{2,1,0:T(4,128)(2,1)S(1)}, u32[]{:S(2)}, u32[]{:S(2)}) collective-permute-start(bf16[4,4,2048]{2,1,0:T(4,128)(2,1)S(1)} %broadcast_select_fusion.4), channel_id=1, source_target_pairs={{0,12},{1,13},{2,14},{3,15},{4,0},{5,1},{6,2},{7,3},{8,4},{9,5},{1... | collective-permute-start | bytes 196616 | tf_op jit(solution)/shard_map/ppermute | solution.py:57
  179.0 1.2 collective-permute-start.33
  180.3 1.2 collective-permute-done.35
  181.4 4.5 %collective-permute-done.34 = bf16[4,4,2048]{2,1,0:T(4,128)(2,1)S(1)} collective-permute-done((bf16[4,4,2048]{2,1,0:T(4,128)(2,1)S(1)}, bf16[4,4,2048]{2,1,0:T(4,128)(2,1)S(1)}, u32[]{:S(2)}, u32[]{:S(2)}) %collective-permute-start.34) | collective-permute-done | bytes 65568 | tf_op jit(solution)/shard_map/ppermute | solution.py:57
  187.6 6.4 %multiply_reduce_fusion = (f32[64]{0:T(128)S(1)}, f32[64,2688]{1,0:T(8,128)S(1)}) fusion(bf16[64,2048]{1,0:T(8,128)(2,1)S(1)} %constant_dynamic-update-slice_fusion.32, bf16[2048,2688]{1,0:T(8,128)(2,1)} %constant_dynamic-update-slice_fusion, bf16[64,2688]{1,0:T(8,128)(2,1)S(1)} %gather.46, pred[64]{0:T(512)(128)(4,1)S(1)} %broadcast_in_dim.126), kind=kOutput, calls=%fused_computation.33 | convolution fusion | flops 705503168 | bytes 12304704 | tf_op jit(solution)/shard_map/dot_general | solution.py:234
  194.0 1.9 fusion.51
  196.2 1.1 collective-permute-start.38
  197.8 6.7 %fusion.6 = bf16[128,2688]{1,0:T(8,128)(2,1)} fusion(bf16[128,2048]{0,1:T(8,128)(2,1)S(1)} %constant_dynamic-update-slice_fusion.16, bf16[2048,2688]{1,0:T(8,128)(2,1)} %constant_dynamic-update-slice_fusion, bf16[128,2688]{1,0:T(8,128)(2,1)S(1)} %copy-done), kind=kOutput, calls=%fused_computation.16 | convolution fusion | flops 1410318336 | bytes 12910592 | tf_op jit(solution)/shard_map/dot_general | solution.py:238
  205.2 1.2 collective-permute-start.41
  207.0 2.0 collective-permute-start.39
  209.0 1.9 collective-permute-done.40
  211.0 1.5 collective-permute-done.39
  (184 shorter events, 32.9 us)
Async XLA Ops:
  0.6 14.9 %copy-start.8 = (s32[8]{0:T(128)S(1)}, s32[8]{0:T(128)}, u32[]{:S(2)}) copy-start(s32[8]{0:T(128)} %constant.258.clone) | copy-start | bytes 100
  0.6 22.1 %copy-start.4 = (s32[8]{0:T(128)S(1)}, s32[8]{0:T(128)}, u32[]{:S(2)}) copy-start(s32[8]{0:T(128)} %constant.259.clone) | copy-start | bytes 100
  0.7 13.9 %copy-start.1 = (bf16[128,2688]{1,0:T(8,128)(2,1)S(1)}, bf16[128,2688]{1,0:T(8,128)(2,1)}, u32[]{:S(2)}) copy-start(bf16[128,2688]{1,0:T(8,128)(2,1)} %param.15) | copy-start | bytes 2064388
  0.7 14.8 %copy-start.7 = (s32[64]{0:T(128)S(1)}, s32[64]{0:T(128)}, u32[]{:S(2)}) copy-start(s32[64]{0:T(128)} %param.17) | copy-start | bytes 772
  1.7 27.2 %collective-permute-start.25 = (bf16[1,4,2688]{2,1,0:T(4,128)(2,1)S(1)}, bf16[1,4,2688]{2,1,0:T(4,128)(2,1)S(1)}, u32[]{:S(2)}, u32[]{:S(2)}) collective-permute-start(bf16[1,4,2688]{2,1,0:T(4,128)(2,1)S(1)} %bitcast.138), channel_id=1, source_target_pairs={{0,2},{1,3},{2,0},{3,1},{4,6},{5,7},{6,4},{7,5},{8,10},{9,11},{10,... | collective-permute-start | bytes 64520 | tf_op jit(solution)/shard_map/ppermute | solution.py:57
  4.8 24.2 %collective-permute-start.24 = (bf16[1,4,2688]{2,1,0:T(4,128)(2,1)S(1)}, bf16[1,4,2688]{2,1,0:T(4,128)(2,1)S(1)}, u32[]{:S(2)}, u32[]{:S(2)}) collective-permute-start(bf16[1,4,2688]{2,1,0:T(4,128)(2,1)S(1)} %bitcast.139), channel_id=1, source_target_pairs={{0,1},{1,2},{2,3},{3,0},{4,5},{5,6},{6,7},{7,4},{8,9},{9,10},{10,1... | collective-permute-start | bytes 64520 | tf_op jit(solution)/shard_map/ppermute | solution.py:57
  4.8 24.2 %collective-permute-start.26 = (bf16[1,4,2688]{2,1,0:T(4,128)(2,1)S(1)}, bf16[1,4,2688]{2,1,0:T(4,128)(2,1)S(1)}, u32[]{:S(2)}, u32[]{:S(2)}) collective-permute-start(bf16[1,4,2688]{2,1,0:T(4,128)(2,1)S(1)} %bitcast.140), channel_id=1, source_target_pairs={{0,3},{1,0},{2,1},{3,2},{4,7},{5,4},{6,5},{7,6},{8,11},{9,8},{10,9... | collective-permute-start | bytes 64520 | tf_op jit(solution)/shard_map/ppermute | solution.py:57
  9.3 35.3 %collective-permute-start = (bf16[128,2176]{0,1:T(8,128)(2,1)}, bf16[128,2176]{0,1:T(8,128)(2,1)S(1)}, u32[]{:S(2)}, u32[]{:S(2)}) collective-permute-start(bf16[128,2176]{0,1:T(8,128)(2,1)} %pad_maximum_fusion.2), channel_id=1, source_target_pairs={{0,4},{1,5},{2,6},{3,7},{4,8},{5,9},{6,10},{7,11},{8,12},{9,13},{1... | collective-permute-start | bytes 1671176 | tf_op jit(solution)/shard_map/ppermute | solution.py:73
  12.9 39.7 %collective-permute-start.9 = (bf16[128,2688]{1,0:T(8,128)(2,1)}, bf16[128,2688]{1,0:T(8,128)(2,1)}, u32[]{:S(2)}, u32[]{:S(2)}) collective-permute-start(bf16[128,2688]{1,0:T(8,128)(2,1)} %param.15), channel_id=1, source_target_pairs={{0,4},{1,5},{2,0},{3,1},{4,8},{5,9},{6,2},{7,3},{8,12},{9,13},{10,... | collective-permute-start | bytes 2064392 | tf_op jit(solution)/shard_map/ppermute | solution.py:147
  29.8 12.6 %collective-permute-start.29 = (bf16[4,4,2688]{2,1,0:T(4,128)(2,1)S(1)}, bf16[4,4,2688]{2,1,0:T(4,128)(2,1)S(1)}, u32[]{:S(2)}, u32[]{:S(2)}) collective-permute-start(bf16[4,4,2688]{2,1,0:T(4,128)(2,1)S(1)} %broadcast_select_fusion.3), channel_id=1, source_target_pairs={{0,12},{1,13},{2,14},{3,15},{4,0},{5,1},{6,2},{7,3},{8,4},{9,5},{1... | collective-permute-start | bytes 258056 | tf_op jit(solution)/shard_map/ppermute | solution.py:57
  30.2 13.2 %collective-permute-start.28 = (bf16[4,4,2688]{2,1,0:T(4,128)(2,1)S(1)}, bf16[4,4,2688]{2,1,0:T(4,128)(2,1)S(1)}, u32[]{:S(2)}, u32[]{:S(2)}) collective-permute-start(bf16[4,4,2688]{2,1,0:T(4,128)(2,1)S(1)} %broadcast_select_fusion.3), channel_id=1, source_target_pairs={{0,8},{1,9},{2,10},{3,11},{4,12},{5,13},{6,14},{7,15},{8,0},{9,1},... | collective-permute-start | bytes 258056 | tf_op jit(solution)/shard_map/ppermute | solution.py:57
  32.9 13.1 %collective-permute-start.27 = (bf16[4,4,2688]{2,1,0:T(4,128)(2,1)S(1)}, bf16[4,4,2688]{2,1,0:T(4,128)(2,1)S(1)}, u32[]{:S(2)}, u32[]{:S(2)}) collective-permute-start(bf16[4,4,2688]{2,1,0:T(4,128)(2,1)S(1)} %broadcast_select_fusion.3), channel_id=1, source_target_pairs={{0,4},{1,5},{2,6},{3,7},{4,8},{5,9},{6,10},{7,11},{8,12},{9,13},{1... | collective-permute-start | bytes 258056 | tf_op jit(solution)/shard_map/ppermute | solution.py:57
  42.4 104.9 %collective-permute-start.8 = (bf16[128,2176]{0,1:T(8,128)(2,1)}, bf16[128,2176]{0,1:T(8,128)(2,1)}, u32[]{:S(2)}, u32[]{:S(2)}) collective-permute-start(bf16[128,2176]{0,1:T(8,128)(2,1)} %pad_maximum_fusion.2), channel_id=1, source_target_pairs={{0,1},{1,0},{2,3},{3,2},{4,5},{5,4},{6,7},{7,6},{8,9},{9,8},{10,11... | collective-permute-start | bytes 1671176 | tf_op jit(solution)/shard_map/ppermute | solution.py:40
  43.3 14.8 %collective-permute-start.5 = (bf16[128,2176]{0,1:T(8,128)(2,1)}, bf16[128,2176]{0,1:T(8,128)(2,1)S(1)}, u32[]{:S(2)}, u32[]{:S(2)}) collective-permute-start(bf16[128,2176]{0,1:T(8,128)(2,1)} %pad_maximum_fusion.2), channel_id=1, source_target_pairs={{0,2},{1,3},{4,6},{5,7},{8,10},{9,11},{12,14},{13,15},{16,18},{17,... | collective-permute-start | bytes 1671176 | tf_op jit(solution)/shard_map/ppermute | solution.py:79
  44.7 17.6 %collective-permute-start.6 = (bf16[128,2176]{0,1:T(8,128)(2,1)S(1)}, bf16[128,2176]{0,1:T(8,128)(2,1)}, u32[]{:S(2)}, u32[]{:S(2)}) collective-permute-start(bf16[128,2176]{0,1:T(8,128)(2,1)S(1)} %collective-permute-done), channel_id=1, source_target_pairs={{2,0},{3,1},{6,4},{7,5},{10,8},{11,9},{14,12},{15,13},{18,16},{19,... | collective-permute-start | bytes 1671176 | tf_op jit(solution)/shard_map/ppermute | solution.py:79
  46.0 18.1 %collective-permute-start.1 = (bf16[128,2176]{0,1:T(8,128)(2,1)S(1)}, bf16[128,2176]{0,1:T(8,128)(2,1)S(1)}, u32[]{:S(2)}, u32[]{:S(2)}) collective-permute-start(bf16[128,2176]{0,1:T(8,128)(2,1)S(1)} %collective-permute-done), channel_id=1, source_target_pairs={{0,4},{1,5},{2,6},{3,7},{4,8},{5,9},{6,10},{7,11},{8,12},{9,13},{1... | collective-permute-start | bytes 1671176 | tf_op jit(solution)/shard_map/ppermute | solution.py:73
  52.6 20.1 %copy-start.2 = (bf16[128,2688]{1,0:T(8,128)(2,1)S(1)}, bf16[128,2688]{1,0:T(8,128)(2,1)}, u32[]{:S(2)}) copy-start(bf16[128,2688]{1,0:T(8,128)(2,1)} %param.15) | copy-start | bytes 2064388
  52.6 20.1 %collective-permute-start.13 = (bf16[128,2688]{1,0:T(8,128)(2,1)}, bf16[128,2688]{1,0:T(8,128)(2,1)S(1)}, u32[]{:S(2)}, u32[]{:S(2)}) collective-permute-start(bf16[128,2688]{1,0:T(8,128)(2,1)} %param.15), channel_id=1, source_target_pairs={{0,2},{1,3},{2,6},{3,7},{4,0},{5,1},{6,10},{7,11},{8,4},{9,5},{10,... | collective-permute-start | bytes 2064392 | tf_op jit(solution)/shard_map/ppermute | solution.py:152
  58.1 25.3 %collective-permute-start.2 = (bf16[128,2176]{0,1:T(8,128)(2,1)S(1)}, bf16[128,2176]{0,1:T(8,128)(2,1)S(1)}, u32[]{:S(2)}, u32[]{:S(2)}) collective-permute-start(bf16[128,2176]{0,1:T(8,128)(2,1)S(1)} %collective-permute-done), channel_id=1, source_target_pairs={{0,2},{1,3},{4,6},{5,7},{8,10},{9,11},{12,14},{13,15},{16,18},{17,... | collective-permute-start | bytes 1671176 | tf_op jit(solution)/shard_map/ppermute | solution.py:79
  62.3 18.6 %collective-permute-start.10 = (bf16[128,2688]{1,0:T(8,128)(2,1)}, bf16[128,2688]{1,0:T(8,128)(2,1)S(1)}, u32[]{:S(2)}, u32[]{:S(2)}) collective-permute-start(bf16[128,2688]{1,0:T(8,128)(2,1)} %collective-permute-done.9), channel_id=1, source_target_pairs={{0,4},{1,5},{2,0},{3,1},{4,8},{5,9},{6,2},{7,3},{8,12},{9,13},{10,... | collective-permute-start | bytes 2064392 | tf_op jit(solution)/shard_map/ppermute | solution.py:147
  64.0 26.0 %collective-permute-start.3 = (bf16[128,2176]{0,1:T(8,128)(2,1)S(1)}, bf16[128,2176]{0,1:T(8,128)(2,1)S(1)}, u32[]{:S(2)}, u32[]{:S(2)}) collective-permute-start(bf16[128,2176]{0,1:T(8,128)(2,1)S(1)} %collective-permute-done.1), channel_id=1, source_target_pairs={{2,0},{3,1},{6,4},{7,5},{10,8},{11,9},{14,12},{15,13},{18,16},{19,... | collective-permute-start | bytes 1671176 | tf_op jit(solution)/shard_map/ppermute | solution.py:79
  72.7 67.6 %collective-permute-start.16 = (bf16[128,2688]{1,0:T(8,128)(2,1)S(1)}, bf16[128,2688]{1,0:T(8,128)(2,1)S(1)}, u32[]{:S(2)}, u32[]{:S(2)}) collective-permute-start(bf16[128,2688]{1,0:T(8,128)(2,1)S(1)} %copy-done.2), channel_id=1, source_target_pairs={{0,1},{1,0},{2,3},{3,2},{4,5},{5,4},{6,7},{7,6},{8,9},{9,8},{10,11... | collective-permute-start | bytes 2064392 | tf_op jit(solution)/shard_map/ppermute | solution.py:40
  80.9 70.6 %collective-permute-start.21 = (bf16[128,2688]{1,0:T(8,128)(2,1)S(1)}, bf16[128,2688]{1,0:T(8,128)(2,1)S(1)}, u32[]{:S(2)}, u32[]{:S(2)}) collective-permute-start(bf16[128,2688]{1,0:T(8,128)(2,1)S(1)} %collective-permute-done.13), channel_id=1, source_target_pairs={{0,1},{1,0},{2,3},{3,2},{4,5},{5,4},{6,7},{7,6},{8,9},{9,8},{10,11... | collective-permute-start | bytes 2064392 | tf_op jit(solution)/shard_map/ppermute | solution.py:40
  83.4 22.3 %collective-permute-start.7 = (bf16[2,128,2176]{1,2,0:T(8,128)(2,1)S(1)}, bf16[2,128,2176]{1,2,0:T(8,128)(2,1)S(1)}, u32[]{:S(2)}, u32[]{:S(2)}) collective-permute-start(bf16[2,128,2176]{1,2,0:T(8,128)(2,1)S(1)} %pad_maximum_fusion.1), channel_id=1, source_target_pairs={{0,1},{1,0},{2,3},{3,2},{4,5},{5,4},{6,7},{7,6},{8,9},{9,8},{10,11... | collective-permute-start | bytes 3342344 | tf_op jit(solution)/shard_map/ppermute | solution.py:40
  90.1 14.7 %collective-permute-start.11 = (bf16[128,2688]{1,0:T(8,128)(2,1)S(1)}, bf16[128,2688]{1,0:T(8,128)(2,1)S(1)}, u32[]{:S(2)}, u32[]{:S(2)}) collective-permute-start(bf16[128,2688]{1,0:T(8,128)(2,1)S(1)} %collective-permute-done.10), channel_id=1, source_target_pairs={{0,4},{1,5},{2,0},{3,1},{4,8},{5,9},{6,2},{7,3},{8,12},{9,13},{10,... | collective-permute-start | bytes 2064392 | tf_op jit(solution)/shard_map/ppermute | solution.py:147
  104.8 12.4 %collective-permute-start.14 = (bf16[128,2688]{1,0:T(8,128)(2,1)S(1)}, bf16[128,2688]{1,0:T(8,128)(2,1)S(1)}, u32[]{:S(2)}, u32[]{:S(2)}) collective-permute-start(bf16[128,2688]{1,0:T(8,128)(2,1)S(1)} %collective-permute-done.13), channel_id=1, source_target_pairs={{0,2},{1,3},{2,6},{3,7},{4,0},{5,1},{6,10},{7,11},{8,4},{9,5},{10,... | collective-permute-start | bytes 2064392 | tf_op jit(solution)/shard_map/ppermute | solution.py:152
  105.7 13.1 %collective-permute-start.12 = (bf16[128,2688]{1,0:T(8,128)(2,1)S(1)}, bf16[128,2688]{1,0:T(8,128)(2,1)S(1)}, u32[]{:S(2)}, u32[]{:S(2)}) collective-permute-start(bf16[128,2688]{1,0:T(8,128)(2,1)S(1)} %collective-permute-done.11), channel_id=1, source_target_pairs={{0,4},{1,5},{2,0},{3,1},{4,8},{5,9},{6,2},{7,3},{8,12},{9,13},{10,... | collective-permute-start | bytes 2064392 | tf_op jit(solution)/shard_map/ppermute | solution.py:147
  117.2 24.5 %collective-permute-start.17 = (bf16[128,2688]{1,0:T(8,128)(2,1)}, bf16[128,2688]{1,0:T(8,128)(2,1)S(1)}, u32[]{:S(2)}, u32[]{:S(2)}) collective-permute-start(bf16[128,2688]{1,0:T(8,128)(2,1)} %collective-permute-done.9), channel_id=1, source_target_pairs={{0,1},{1,0},{2,3},{3,2},{4,5},{5,4},{6,7},{7,6},{8,9},{9,8},{10,11... | collective-permute-start | bytes 2064392 | tf_op jit(solution)/shard_map/ppermute | solution.py:40
  118.8 20.5 %collective-permute-start.15 = (bf16[128,2688]{1,0:T(8,128)(2,1)S(1)}, bf16[128,2688]{1,0:T(8,128)(2,1)S(1)}, u32[]{:S(2)}, u32[]{:S(2)}) collective-permute-start(bf16[128,2688]{1,0:T(8,128)(2,1)S(1)} %collective-permute-done.14), channel_id=1, source_target_pairs={{0,2},{1,3},{2,6},{3,7},{4,0},{5,1},{6,10},{7,11},{8,4},{9,5},{10,... | collective-permute-start | bytes 2064392 | tf_op jit(solution)/shard_map/ppermute | solution.py:152
  139.3 3.3 %collective-permute-start.18 = (bf16[128,2688]{1,0:T(8,128)(2,1)S(1)}, bf16[128,2688]{1,0:T(8,128)(2,1)S(1)}, u32[]{:S(2)}, u32[]{:S(2)}) collective-permute-start(bf16[128,2688]{1,0:T(8,128)(2,1)S(1)} %collective-permute-done.10), channel_id=1, source_target_pairs={{0,1},{1,0},{2,3},{3,2},{4,5},{5,4},{6,7},{7,6},{8,9},{9,8},{10,11... | collective-permute-start | bytes 2064392 | tf_op jit(solution)/shard_map/ppermute | solution.py:40
  140.3 5.2 %collective-permute-start.4 = (bf16[2,128,2176]{1,2,0:T(8,128)(2,1)S(1)}, bf16[2,128,2176]{1,2,0:T(8,128)(2,1)S(1)}, u32[]{:S(2)}, u32[]{:S(2)}) collective-permute-start(bf16[2,128,2176]{1,2,0:T(8,128)(2,1)S(1)} %pad_maximum_fusion), channel_id=1, source_target_pairs={{0,1},{1,0},{2,3},{3,2},{4,5},{5,4},{6,7},{7,6},{8,9},{9,8},{10,11... | collective-permute-start | bytes 3342344 | tf_op jit(solution)/shard_map/ppermute | solution.py:40
  141.7 2.5 %collective-permute-start.19 = (bf16[128,2688]{1,0:T(8,128)(2,1)S(1)}, bf16[128,2688]{1,0:T(8,128)(2,1)S(1)}, u32[]{:S(2)}, u32[]{:S(2)}) collective-permute-start(bf16[128,2688]{1,0:T(8,128)(2,1)S(1)} %collective-permute-done.11), channel_id=1, source_target_pairs={{0,1},{1,0},{2,3},{3,2},{4,5},{5,4},{6,7},{7,6},{8,9},{9,8},{10,11... | collective-permute-start | bytes 2064392 | tf_op jit(solution)/shard_map/ppermute | solution.py:40
  142.6 9.8 %collective-permute-start.22 = (bf16[128,2688]{1,0:T(8,128)(2,1)S(1)}, bf16[128,2688]{1,0:T(8,128)(2,1)S(1)}, u32[]{:S(2)}, u32[]{:S(2)}) collective-permute-start(bf16[128,2688]{1,0:T(8,128)(2,1)S(1)} %collective-permute-done.14), channel_id=1, source_target_pairs={{0,1},{1,0},{2,3},{3,2},{4,5},{5,4},{6,7},{7,6},{8,9},{9,8},{10,11... | collective-permute-start | bytes 2064392 | tf_op jit(solution)/shard_map/ppermute | solution.py:40
  144.2 9.2 %collective-permute-start.23 = (bf16[128,2688]{1,0:T(8,128)(2,1)S(1)}, bf16[128,2688]{1,0:T(8,128)(2,1)S(1)}, u32[]{:S(2)}, u32[]{:S(2)}) collective-permute-start(bf16[128,2688]{1,0:T(8,128)(2,1)S(1)} %collective-permute-done.15), channel_id=1, source_target_pairs={{0,1},{1,0},{2,3},{3,2},{4,5},{5,4},{6,7},{7,6},{8,9},{9,8},{10,11... | collective-permute-start | bytes 2064392 | tf_op jit(solution)/shard_map/ppermute | solution.py:40
  145.5 5.1 %collective-permute-start.20 = (bf16[128,2688]{1,0:T(8,128)(2,1)S(1)}, bf16[128,2688]{1,0:T(8,128)(2,1)S(1)}, u32[]{:S(2)}, u32[]{:S(2)}) collective-permute-start(bf16[128,2688]{1,0:T(8,128)(2,1)S(1)} %collective-permute-done.12), channel_id=1, source_target_pairs={{0,1},{1,0},{2,3},{3,2},{4,5},{5,4},{6,7},{7,6},{8,9},{9,8},{10,11... | collective-permute-start | bytes 2064392 | tf_op jit(solution)/shard_map/ppermute | solution.py:40
  169.1 4.6 %collective-permute-start.31 = (bf16[1,4,2048]{2,1,0:T(4,128)(2,1)S(1)}, bf16[1,4,2048]{2,1,0:T(4,128)(2,1)S(1)}, u32[]{:S(2)}, u32[]{:S(2)}) collective-permute-start(bf16[1,4,2048]{2,1,0:T(4,128)(2,1)S(1)} %bitcast.147), channel_id=1, source_target_pairs={{0,2},{1,3},{2,0},{3,1},{4,6},{5,7},{6,4},{7,5},{8,10},{9,11},{10,... | collective-permute-start | bytes 49160 | tf_op jit(solution)/shard_map/ppermute | solution.py:57
  171.7 3.2 %collective-permute-start.30 = (bf16[1,4,2048]{2,1,0:T(4,128)(2,1)S(1)}, bf16[1,4,2048]{2,1,0:T(4,128)(2,1)S(1)}, u32[]{:S(2)}, u32[]{:S(2)}) collective-permute-start(bf16[1,4,2048]{2,1,0:T(4,128)(2,1)S(1)} %bitcast.148), channel_id=1, source_target_pairs={{0,1},{1,2},{2,3},{3,0},{4,5},{5,6},{6,7},{7,4},{8,9},{9,10},{10,1... | collective-permute-start | bytes 49160 | tf_op jit(solution)/shard_map/ppermute | solution.py:57
  171.8 3.1 %collective-permute-start.32 = (bf16[1,4,2048]{2,1,0:T(4,128)(2,1)S(1)}, bf16[1,4,2048]{2,1,0:T(4,128)(2,1)S(1)}, u32[]{:S(2)}, u32[]{:S(2)}) collective-permute-start(bf16[1,4,2048]{2,1,0:T(4,128)(2,1)S(1)} %bitcast.149), channel_id=1, source_target_pairs={{0,3},{1,0},{2,1},{3,2},{4,7},{5,4},{6,5},{7,6},{8,11},{9,8},{10,9... | collective-permute-start | bytes 49160 | tf_op jit(solution)/shard_map/ppermute | solution.py:57
  175.6 5.8 %collective-permute-start.35 = (bf16[4,4,2048]{2,1,0:T(4,128)(2,1)S(1)}, bf16[4,4,2048]{2,1,0:T(4,128)(2,1)S(1)}, u32[]{:S(2)}, u32[]{:S(2)}) collective-permute-start(bf16[4,4,2048]{2,1,0:T(4,128)(2,1)S(1)} %broadcast_select_fusion.4), channel_id=1, source_target_pairs={{0,12},{1,13},{2,14},{3,15},{4,0},{5,1},{6,2},{7,3},{8,4},{9,5},{1... | collective-permute-start | bytes 196616 | tf_op jit(solution)/shard_map/ppermute | solution.py:57
  179.0 6.9 %collective-permute-start.34 = (bf16[4,4,2048]{2,1,0:T(4,128)(2,1)S(1)}, bf16[4,4,2048]{2,1,0:T(4,128)(2,1)S(1)}, u32[]{:S(2)}, u32[]{:S(2)}) collective-permute-start(bf16[4,4,2048]{2,1,0:T(4,128)(2,1)S(1)} %broadcast_select_fusion.4), channel_id=1, source_target_pairs={{0,8},{1,9},{2,10},{3,11},{4,12},{5,13},{6,14},{7,15},{8,0},{9,1},... | collective-permute-start | bytes 196616 | tf_op jit(solution)/shard_map/ppermute | solution.py:57
  179.0 6.9 %collective-permute-start.33 = (bf16[4,4,2048]{2,1,0:T(4,128)(2,1)S(1)}, bf16[4,4,2048]{2,1,0:T(4,128)(2,1)S(1)}, u32[]{:S(2)}, u32[]{:S(2)}) collective-permute-start(bf16[4,4,2048]{2,1,0:T(4,128)(2,1)S(1)} %broadcast_select_fusion.4), channel_id=1, source_target_pairs={{0,4},{1,5},{2,6},{3,7},{4,8},{5,9},{6,10},{7,11},{8,12},{9,13},{1... | collective-permute-start | bytes 196616 | tf_op jit(solution)/shard_map/ppermute | solution.py:57
  186.9 7.0 %slice-start = ((s8[5505024]{0:T(1024)(128)(4,1)}), s8[1310720]{0:T(1024)(128)(4,1)S(1)}, s32[]{:S(2)}) async-start(s8[5505024]{0:T(1024)(128)(4,1)} %bitcast.111), calls=%async_computation | async-start | bytes 2621440
  196.2 8.3 %collective-permute-start.38 = (f32[1,3,64]{2,1,0:T(4,128)S(1)}, f32[1,3,64]{2,1,0:T(4,128)S(1)}, u32[]{:S(2)}, u32[]{:S(2)}) collective-permute-start(f32[1,3,64]{2,1,0:T(4,128)S(1)} %get-tuple-element.27), channel_id=1, source_target_pairs={{0,3},{1,0},{2,1},{3,2},{4,7},{5,4},{6,5},{7,6},{8,11},{9,8},{10,9... | collective-permute-start | bytes 2312 | tf_op jit(solution)/shard_map/ppermute | solution.py:57
  197.3 7.2 %collective-permute-start.37 = (f32[1,3,64]{2,1,0:T(4,128)S(1)}, f32[1,3,64]{2,1,0:T(4,128)S(1)}, u32[]{:S(2)}, u32[]{:S(2)}) collective-permute-start(f32[1,3,64]{2,1,0:T(4,128)S(1)} %get-tuple-element.27), channel_id=1, source_target_pairs={{0,2},{1,3},{2,0},{3,1},{4,6},{5,7},{6,4},{7,5},{8,10},{9,11},{10,... | collective-permute-start | bytes 2312 | tf_op jit(solution)/shard_map/ppermute | solution.py:57
  197.6 6.9 %collective-permute-start.36 = (f32[1,3,64]{2,1,0:T(4,128)S(1)}, f32[1,3,64]{2,1,0:T(4,128)S(1)}, u32[]{:S(2)}, u32[]{:S(2)}) collective-permute-start(f32[1,3,64]{2,1,0:T(4,128)S(1)} %get-tuple-element.27), channel_id=1, source_target_pairs={{0,1},{1,2},{2,3},{3,0},{4,5},{5,6},{6,7},{7,4},{8,9},{9,10},{10,1... | collective-permute-start | bytes 2312 | tf_op jit(solution)/shard_map/ppermute | solution.py:57
  205.2 3.8 %collective-permute-start.41 = (f32[4,3,64]{2,1,0:T(4,128)S(1)}, f32[4,3,64]{2,1,0:T(4,128)S(1)}, u32[]{:S(2)}, u32[]{:S(2)}) collective-permute-start(f32[4,3,64]{2,1,0:T(4,128)S(1)} %broadcast_select_fusion.5), channel_id=1, source_target_pairs={{0,12},{1,13},{2,14},{3,15},{4,0},{5,1},{6,2},{7,3},{8,4},{9,5},{1... | collective-permute-start | bytes 9224 | tf_op jit(solution)/shard_map/ppermute | solution.py:57
  206.4 4.5 %collective-permute-start.40 = (f32[4,3,64]{2,1,0:T(4,128)S(1)}, f32[4,3,64]{2,1,0:T(4,128)S(1)}, u32[]{:S(2)}, u32[]{:S(2)}) collective-permute-start(f32[4,3,64]{2,1,0:T(4,128)S(1)} %broadcast_select_fusion.5), channel_id=1, source_target_pairs={{0,8},{1,9},{2,10},{3,11},{4,12},{5,13},{6,14},{7,15},{8,0},{9,1},... | collective-permute-start | bytes 9224 | tf_op jit(solution)/shard_map/ppermute | solution.py:57
  207.0 5.4 %collective-permute-start.39 = (f32[4,3,64]{2,1,0:T(4,128)S(1)}, f32[4,3,64]{2,1,0:T(4,128)S(1)}, u32[]{:S(2)}, u32[]{:S(2)}) collective-permute-start(f32[4,3,64]{2,1,0:T(4,128)S(1)} %broadcast_select_fusion.5), channel_id=1, source_target_pairs={{0,4},{1,5},{2,6},{3,7},{4,8},{5,9},{6,10},{7,11},{8,12},{9,13},{1... | collective-permute-start | bytes 9224 | tf_op jit(solution)/shard_map/ppermute | solution.py:57
  (5 other events, 19.2 us)

commit v11 on v7

--- a/solution.py
+++ b/solution.py
@@ -10,7 +10,7 @@
 HEAD_SIZE = 128
 ATTENTION_SPAN = 1024
 SCORE_DEV = 4
-SEG_LANES = 128
+DOCS = 4
 LANES = 128
 CORES = 2
 SEQ = ("chip", "core")
@@ -76,7 +76,7 @@
     return lax.ppermute(value, SEQ, pairs)
 
 
-def halo_window(own, kv_width, blocks, first_core):
+def halo_window(own, blocks, first_core):
     assert blocks == 4 * CORES
     odd = (lax.axis_index("chip") % 2) == 1
     back2 = shift_chips(own, 2)
@@ -97,7 +97,7 @@
     token_rows = own.shape[0]
     core = lax.axis_index("core")
     window = lax.dynamic_slice_in_dim(sequence, core * token_rows, (blocks + 1) * token_rows, 0)
-    return window[:, :kv_width], window[:, kv_width].astype(jnp.int32)
+    return window
 
 
 def normalize(hidden, norm_gain):
@@ -123,13 +123,22 @@
     stride = token_rows // score_count
     scored_residual = gather_rows(residual.reshape(score_count, stride, width)[:, stride - 1, :])
 
-    seg_cols = jnp.broadcast_to(segment_ids.astype(jnp.bfloat16)[:, None], (token_rows, SEG_LANES))
-    own = jnp.concatenate([joined_keys_values, seg_cols], 1)
-    key_value_pair, key_seg = halo_window(own, kv_width, blocks, first_core)
+    values = jnp.arange(DOCS, dtype=jnp.int32)
+    here = first_row + jnp.arange(token_rows, dtype=jnp.int32)
+    first_seen = jnp.min(
+        jnp.where(segment_ids[None, :] == values[:, None], here[None, :], jnp.iinfo(jnp.int32).max), axis=1
+    )
+    segment_start = jnp.min(gather_rows(first_seen).reshape(-1, DOCS), axis=0)
+    first_segment = segment_ids[0]
+    first_start = jnp.take(segment_start, first_segment)
+    key_value_pair = halo_window(joined_keys_values, blocks, first_core)
     count_of_keys = key_value_pair.shape[0]
-    query_pos = first_row + jnp.arange(token_rows, dtype=jnp.int32)
-    key_pos = first_row - blocks * token_rows + jnp.arange(count_of_keys, dtype=jnp.int32)
-    allowed = (segment_ids[:, None] == key_seg[None, :]) & (key_pos[None, :] >= 0)
+    rim_rows = blocks * token_rows
+    query_pos = here
+    key_pos = first_row - rim_rows + jnp.arange(count_of_keys, dtype=jnp.int32)
+    rim_same = (segment_ids[:, None] == first_segment) & (key_pos[None, :rim_rows] >= first_start)
+    own_same = segment_ids[:, None] == segment_ids[None, :]
+    allowed = jnp.concatenate([rim_same, own_same], 1) & (key_pos[None, :] >= 0)
     allowed = (
         allowed
         & (key_pos[None, :] <= query_pos[:, None])

time: 164 us -> 176 us (1.073)
  waiting for transfers between devices: 53.2 us -> 61.2 us
  between operations: 14.6 us -> 17.2 us
    ppermute x18 -> x24, starting transfers between devices: 21.6 us -> 32.8 us  [gather_rows(): received.append(lax.ppermute(data, SEQ, pairs))]
    ppermute x3, starting transfers between devices: 10.9 us -> 0.58 us  [swap_cores(): return lax.ppermute(value, 'core', [(0, 1), (1, 0)])]
    ppermute x18 -> x24, waiting for transfers between devices: 9.72 us -> 14.5 us  [gather_rows(): received.append(lax.ppermute(data, SEQ, pairs))]
    ppermute x2, waiting for transfers between devices: 15.4 us -> 19.6 us  [shift_chips(): lax.ppermute(value, SEQ, [(s, s + step) for s in range(count - step)])]
    gather x8 -> x10, local copies, waits for them, and re-layouts: 4.77 us -> 5.28 us  [gather_rows(): data = jnp.take(stacked, order, axis=0)]
  transfers between devices with their start and end apart: 28 -> 34, of which waited for: 10 -> 13; matrix products, arithmetic and copies ran while one was open for 20% -> 19% of each run, Pallas kernels for 0% -> 0%
where the time goes in v11:
time: 176 us
  waiting for transfers between devices  61.2 us (35%)
  starting transfers between devices  50.4 us (29%)
  matrix products  23.7 us (13%)
  between operations  17.2 us (10%)
  local copies, waits for them, and re-layouts  13.5 us (8%)
  other arithmetic  9.72 us (6%)
    ppermute x24, starting transfers between devices, gather_rows(): received.append(lax.ppermute(data, SEQ, pairs))  32.8 us
    ppermute x4, waiting for transfers between devices, across_pair(): return lax.ppermute(value, SEQ, pairs)  26.4 us
    ppermute x2, waiting for transfers between devices, shift_chips(): lax.ppermute(value, SEQ, [(s, s + step) for s in range(count - step)])  19.6 us
    ppermute x24, waiting for transfers between devices, gather_rows(): received.append(lax.ppermute(data, SEQ, pairs))  14.5 us
    ppermute x4, starting transfers between devices, across_pair(): return lax.ppermute(value, SEQ, pairs)  9.2 us
    ppermute x2, starting transfers between devices, shift_chips(): lax.ppermute(value, SEQ, [(s, s + step) for s in range(count - step)])  7.74 us
    dot_general x1, matrix products, local(): jnp.einsum('hgqk,khd->qhgd', weights, heads_for_values, preferred_element...  6.49 us
    dot_general x1, matrix products, local(): jnp.dot(scored_context, full_proj, preferred_element_type=jnp.float32)  6.49 us
  transfers between devices with their start and end apart: 34, of which 13 were waited for; matrix products, arithmetic and copies ran while one was open for 19% of the time, Pallas kernels for 0%

profile of v11, /device:TPU:0, one launch (start us, length us, event | category | flops | bytes accessed | tf_op | source)
XLA Modules:
  0.0 175.7 jit_solution(17369413989084611955)
XLA Ops:
  7.9 1.3 copy.26
  9.2 5.0 %collective-permute-start = (bf16[128,2048]{0,1:T(8,128)(2,1)S(1)}, bf16[128,2048]{0,1:T(8,128)(2,1)S(1)}, u32[]{:S(2)}, u32[]{:S(2)}) collective-permute-start(bf16[128,2048]{0,1:T(8,128)(2,1)S(1)} %copy.26), channel_id=1, source_target_pairs={{0,4},{1,5},{2,6},{3,7},{4,8},{5,9},{6,10},{7,11},{8,12},{9,13},{1... | collective-permute-start | bytes 1572872 | tf_op jit(solution)/shard_map/ppermute | solution.py:70
  14.2 3.5 %collective-permute-start.5 = (bf16[128,2048]{0,1:T(8,128)(2,1)S(1)}, bf16[128,2048]{0,1:T(8,128)(2,1)S(1)}, u32[]{:S(2)}, u32[]{:S(2)}) collective-permute-start(bf16[128,2048]{0,1:T(8,128)(2,1)S(1)} %copy.26), channel_id=1, source_target_pairs={{0,2},{1,3},{4,6},{5,7},{8,10},{9,11},{12,14},{13,15},{16,18},{17,... | collective-permute-start | bytes 1572872 | tf_op jit(solution)/shard_map/ppermute | solution.py:76
  17.7 0.8 select_reduce_fusion.2
  18.6 1.7 collective-permute-start.11
  22.3 1.4 reshape.376
  23.7 1.0 slice.78
  25.3 7.1 %collective-permute-start.15 = (bf16[1,4,2688]{2,1,0:T(4,128)(2,1)S(1)}, bf16[1,4,2688]{2,1,0:T(4,128)(2,1)S(1)}, u32[]{:S(2)}, u32[]{:S(2)}) collective-permute-start(bf16[1,4,2688]{2,1,0:T(4,128)(2,1)S(1)} %bitcast.127), channel_id=1, source_target_pairs={{0,1},{1,2},{2,3},{3,0},{4,5},{5,6},{6,7},{7,4},{8,9},{9,10},{10,1... | collective-permute-start | bytes 64520 | tf_op jit(solution)/shard_map/ppermute | solution.py:54
  32.4 3.8 %collective-permute-done.10 = s32[1,4]{1,0:T(1,128)S(1)} collective-permute-done((s32[1,4]{1,0:T(1,128)S(1)}, s32[1,4]{1,0:T(1,128)S(1)}, u32[]{:S(2)}, u32[]{:S(2)}) %collective-permute-start.10) | collective-permute-done | bytes 48 | tf_op jit(solution)/shard_map/ppermute | solution.py:54
  36.8 1.5 collective-permute-start.12
  38.4 1.1 collective-permute-start.13
  39.5 2.8 %collective-permute-done.12 = s32[4,4]{1,0:T(4,128)S(1)} collective-permute-done((s32[4,4]{1,0:T(4,128)S(1)}, s32[4,4]{1,0:T(4,128)S(1)}, u32[]{:S(2)}, u32[]{:S(2)}) %collective-permute-start.12) | collective-permute-done | bytes 96 | tf_op jit(solution)/shard_map/ppermute | solution.py:54
  42.9 2.5 %collective-permute-start.16 = (bf16[1,4,2688]{2,1,0:T(4,128)(2,1)S(1)}, bf16[1,4,2688]{2,1,0:T(4,128)(2,1)S(1)}, u32[]{:S(2)}, u32[]{:S(2)}) collective-permute-start(bf16[1,4,2688]{2,1,0:T(4,128)(2,1)S(1)} %bitcast.128), channel_id=1, source_target_pairs={{0,2},{1,3},{2,0},{3,1},{4,6},{5,7},{6,4},{7,5},{8,10},{9,11},{10,... | collective-permute-start | bytes 64520 | tf_op jit(solution)/shard_map/ppermute | solution.py:54
  48.2 2.1 %fusion.16 = pred[128,1152]{0,1:T(8,128)(4,1)} fusion(pred[128,128]{0,1:T(8,128)(4,1)S(1)} %broadcast_compare_fusion, pred[128,1024]{0,1:T(8,128)(4,1)S(1)} %broadcast_and_fusion, s32[128]{0:T(128)S(1)} %get-tuple-element.38, s32[128]{0:T(128)S(1)} %get-tuple-element.37, s32[1152]{0:T(1024)S(1)} %iota_add_fusion, pred[1152]{0:T(1024)(128)(4,1)S(1)} %broadcast_compare_fusion.1), kind=kLoop, calls=%fused_computation.38 | loop fusion | flops 884736 | bytes 301696 | tf_op jit(solution)/shard_map/and | solution.py:143
  51.5 2.8 %collective-permute-start.1 = (bf16[128,2048]{0,1:T(8,128)(2,1)S(1)}, bf16[128,2048]{0,1:T(8,128)(2,1)S(1)}, u32[]{:S(2)}, u32[]{:S(2)}) collective-permute-start(bf16[128,2048]{0,1:T(8,128)(2,1)S(1)} %collective-permute-done), channel_id=1, source_target_pairs={{0,4},{1,5},{2,6},{3,7},{4,8},{5,9},{6,10},{7,11},{8,12},{9,13},{1... | collective-permute-start | bytes 1572872 | tf_op jit(solution)/shard_map/ppermute | solution.py:70
  54.3 1.3 collective-permute-start.6
  55.6 0.7 broadcast_select_fusion.2
  56.7 1.5 collective-permute-start.19
  58.2 19.6 %collective-permute-done.1 = bf16[128,2048]{0,1:T(8,128)(2,1)S(1)} collective-permute-done((bf16[128,2048]{0,1:T(8,128)(2,1)S(1)}, bf16[128,2048]{0,1:T(8,128)(2,1)S(1)}, u32[]{:S(2)}, u32[]{:S(2)}) %collective-permute-start.1) | collective-permute-done | bytes 524320 | tf_op jit(solution)/shard_map/ppermute | solution.py:70
  77.8 3.2 %collective-permute-start.2 = (bf16[128,2048]{0,1:T(8,128)(2,1)S(1)}, bf16[128,2048]{0,1:T(8,128)(2,1)S(1)}, u32[]{:S(2)}, u32[]{:S(2)}) collective-permute-start(bf16[128,2048]{0,1:T(8,128)(2,1)S(1)} %collective-permute-done), channel_id=1, source_target_pairs={{0,2},{1,3},{4,6},{5,7},{8,10},{9,11},{12,14},{13,15},{16,18},{17,... | collective-permute-start | bytes 1572872 | tf_op jit(solution)/shard_map/ppermute | solution.py:76
  81.0 0.7 collective-permute-done.6
  81.7 1.3 collective-permute-start.3
  83.2 13.0 %collective-permute-done.2 = bf16[128,2048]{0,1:T(8,128)(2,1)S(1)} collective-permute-done((bf16[128,2048]{0,1:T(8,128)(2,1)S(1)}, bf16[128,2048]{0,1:T(8,128)(2,1)S(1)}, u32[]{:S(2)}, u32[]{:S(2)}) %collective-permute-start.2) | collective-permute-done | bytes 524320 | tf_op jit(solution)/shard_map/ppermute | solution.py:76
  96.1 12.7 %collective-permute-done.3 = bf16[128,2048]{0,1:T(8,128)(2,1)S(1)} collective-permute-done((bf16[128,2048]{0,1:T(8,128)(2,1)S(1)}, bf16[128,2048]{0,1:T(8,128)(2,1)S(1)}, u32[]{:S(2)}, u32[]{:S(2)}) %collective-permute-start.3) | collective-permute-done | bytes 524320 | tf_op jit(solution)/shard_map/ppermute | solution.py:76
  109.2 3.0 %collective-permute-start.20 = (bf16[4,4,2688]{2,1,0:T(4,128)(2,1)}, bf16[4,4,2688]{2,1,0:T(4,128)(2,1)}, u32[]{:S(2)}, u32[]{:S(2)}) collective-permute-start(bf16[4,4,2688]{2,1,0:T(4,128)(2,1)} %broadcast_select_fusion.2), channel_id=1, source_target_pairs={{0,12},{1,13},{2,14},{3,15},{4,0},{5,1},{6,2},{7,3},{8,4},{9,5},{1... | collective-permute-start | bytes 258056 | tf_op jit(solution)/shard_map/ppermute | solution.py:54
  114.2 1.9 %constant_dynamic-slice_fusion = (bf16[1152,1024]{0,1:T(8,128)(2,1)S(1)}, bf16[1152,1024]{0,1:T(8,128)(2,1)}) fusion(bf16[1280,2048]{0,1:T(8,128)(2,1)S(1)} %fusion.14, s32[]{:T(128)S(6)} %select_n.282, s32[]{:T(128)S(6)} %add.215), kind=kLoop, calls=%fused_computation.125 | loop fusion | bytes 9437192 | tf_op jit(solution)/shard_map/slice | solution.py:148
  116.1 3.6 %fusion.51 = f32[8,2,128]{2,1,0:T(2,128)S(1)} fusion(pred[128,1152]{0,1:T(8,128)(4,1)S(1)} %copy-done.2, bf16[1152,8,128,1]{0,2,3,1:T(8,128)(2,1)S(1)} %bitcast.120, bf16[128,8,2,128]{3,2,1,0:T(2,128)(2,1)S(1)} %reshape.376), kind=kOutput, calls=%fused_computation.133 | convolution fusion | flops 613418112 | bytes 3039232 | tf_op jit(solution)/shard_map/sub | solution.py:162
  119.8 6.5 %fusion.7 = bf16[8,128,2,128]{3,1,2,0:T(8,128)(2,1)S(1)} fusion(bf16[1152,8,128,1]{0,2,3,1:T(8,128)(2,1)} %bitcast.122, f32[8,2,128]{2,1,0:T(2,128)S(1)} %fusion.51, pred[128,1152]{0,1:T(8,128)(4,1)} %fusion.16, bf16[1152,8,128,1]{0,2,3,1:T(8,128)(2,1)S(1)} %bitcast.121, bf16[128,8,2,128]{3,2,1,0:T(2,128)(2,1)S(1)} %reshape.376), kind=kOutput, calls=%fused_computation.20 | convolution fusion | flops 1220021376 | bytes 5922816 | tf_op jit(solution)/shard_map/hgqk,khd->qhgd/dot_general | solution.py:164
  127.4 1.7 collective-permute-start.23
  129.1 1.3 pad_maximum_fusion.2
  130.4 0.8 gather_fusion.3
  132.1 1.5 collective-permute-start.24
  133.6 1.3 collective-permute-start.25
  134.9 2.6 %collective-permute-start.26 = (bf16[4,4,2048]{2,1,0:T(4,128)(2,1)S(1)}, bf16[4,4,2048]{2,1,0:T(4,128)(2,1)S(1)}, u32[]{:S(2)}, u32[]{:S(2)}) collective-permute-start(bf16[4,4,2048]{2,1,0:T(4,128)(2,1)S(1)} %broadcast_select_fusion.3), channel_id=1, source_target_pairs={{0,12},{1,13},{2,14},{3,15},{4,0},{5,1},{6,2},{7,3},{8,4},{9,5},{1... | collective-permute-start | bytes 196616 | tf_op jit(solution)/shard_map/ppermute | solution.py:54
  137.6 1.5 collective-permute-done.24
  139.1 2.6 %collective-permute-done.25 = bf16[4,4,2048]{2,1,0:T(4,128)(2,1)S(1)} collective-permute-done((bf16[4,4,2048]{2,1,0:T(4,128)(2,1)S(1)}, bf16[4,4,2048]{2,1,0:T(4,128)(2,1)S(1)}, u32[]{:S(2)}, u32[]{:S(2)}) %collective-permute-start.25) | collective-permute-done | bytes 65568 | tf_op jit(solution)/shard_map/ppermute | solution.py:54
  142.0 0.8 gather_fusion.5
  142.9 6.5 %multiply_reduce_fusion = (f32[64]{0:T(128)S(1)}, f32[64,2688]{1,0:T(8,128)S(1)}) fusion(bf16[2048,2688]{1,0:T(8,128)(2,1)} %all-gather.2.cloned.1.call-done, bf16[64,2048]{1,0:T(8,128)(2,1)S(1)} %gather.72, pred[64]{0:T(512)(128)(4,1)S(1)} %broadcast_in_dim.166, bf16[64,2688]{1,0:T(8,128)(2,1)S(1)} %gather.67), kind=kOutput, calls=%fused_computation.35 | convolution fusion | flops 705634240 | bytes 12304704 | tf_op jit(solution)/shard_map/dot_general | solution.py:170
  149.4 4.5 %fusion.54 = (f32[64]{0:T(128)S(1)}, f32[64,1024]{1,0:T(8,128)S(1)}) fusion(bf16[1024,2688]{1,0:T(8,128)(2,1)} %param.14, f32[64,2688]{1,0:T(8,128)S(1)} %get-tuple-element.34, f32[2688]{0:T(1024)S(1)} %copy-done.3, f32[64]{0:T(128)S(1)} %add_rsqrt_fusion), kind=kOutput, calls=%fused_computation.134 | convolution fusion | flops 352903104 | bytes 6466560 | tf_op jit(solution)/shard_map/dot_general | solution.py:177
  154.3 1.0 collective-permute-start.28
  155.3 1.4 collective-permute-start.29
  156.7 2.5 %fusion.6 = bf16[128,2688]{1,0:T(8,128)(2,1)} fusion(bf16[128,2048]{0,1:T(8,128)(2,1)S(1)} %bitcast.119, bf16[2048,2688]{1,0:T(8,128)(2,1)S(1)} %copy-done, bf16[128,2688]{1,0:T(8,128)(2,1)S(1)} %copy-done.1), kind=kOutput, calls=%fused_computation.18 | convolution fusion | flops 1410318336 | bytes 12910592 | tf_op jit(solution)/shard_map/dot_general | solution.py:174
  159.9 1.3 collective-permute-start.30
  161.2 1.8 %collective-permute-start.31 = (f32[4,3,64]{2,1,0:T(4,128)S(1)}, f32[4,3,64]{2,1,0:T(4,128)S(1)}, u32[]{:S(2)}, u32[]{:S(2)}) collective-permute-start(f32[4,3,64]{2,1,0:T(4,128)S(1)} %broadcast_select_fusion.4), channel_id=1, source_target_pairs={{0,8},{1,9},{2,10},{3,11},{4,12},{5,13},{6,14},{7,15},{8,0},{9,1},... | collective-permute-start | bytes 9224 | tf_op jit(solution)/shard_map/ppermute | solution.py:54
  163.0 0.7 collective-permute-start.32
  163.9 1.6 collective-permute-done.30
  165.8 0.9 collective-permute-done.32
  167.5 0.8 broadcast_subtract_fusion
  (116 shorter events, 14.1 us)
Async XLA Ops:
  7.2 18.0 %copy-start.4 = (s32[128]{0:T(128)S(1)}, s32[128]{0:T(128)}, u32[]{:S(2)}) copy-start(s32[128]{0:T(128)} %param.10) | copy-start | bytes 1540
  7.2 18.0 %copy-start.5 = (s32[64]{0:T(128)S(1)}, s32[64]{0:T(128)}, u32[]{:S(2)}) copy-start(s32[64]{0:T(128)} %param.15) | copy-start | bytes 772
  7.2 135.7 %all-gather.2.cloned.1.call-start = ((), (), s32[]{:S(2)}) async-start(), calls=%async_computation | async-start | bytes 11698176 | tf_op jit(solution)/shard_map/all_gather | solution.py:121
  9.2 42.3 %collective-permute-start = (bf16[128,2048]{0,1:T(8,128)(2,1)S(1)}, bf16[128,2048]{0,1:T(8,128)(2,1)S(1)}, u32[]{:S(2)}, u32[]{:S(2)}) collective-permute-start(bf16[128,2048]{0,1:T(8,128)(2,1)S(1)} %copy.26), channel_id=1, source_target_pairs={{0,4},{1,5},{2,6},{3,7},{4,8},{5,9},{6,10},{7,11},{8,12},{9,13},{1... | collective-permute-start | bytes 1572872 | tf_op jit(solution)/shard_map/ppermute | solution.py:70
  14.2 42.5 %collective-permute-start.5 = (bf16[128,2048]{0,1:T(8,128)(2,1)S(1)}, bf16[128,2048]{0,1:T(8,128)(2,1)S(1)}, u32[]{:S(2)}, u32[]{:S(2)}) collective-permute-start(bf16[128,2048]{0,1:T(8,128)(2,1)S(1)} %copy.26), channel_id=1, source_target_pairs={{0,2},{1,3},{4,6},{5,7},{8,10},{9,11},{12,14},{13,15},{16,18},{17,... | collective-permute-start | bytes 1572872 | tf_op jit(solution)/shard_map/ppermute | solution.py:76
  18.5 6.8 %collective-permute-start.9 = (s32[1,4]{1,0:T(1,128)S(1)}, s32[1,4]{1,0:T(1,128)S(1)}, u32[]{:S(2)}, u32[]{:S(2)}) collective-permute-start(s32[1,4]{1,0:T(1,128)S(1)} %bitcast.163), channel_id=1, source_target_pairs={{0,1},{1,2},{2,3},{3,0},{4,5},{5,6},{6,7},{7,4},{8,9},{9,10},{10,1... | collective-permute-start | bytes 56 | tf_op jit(solution)/shard_map/ppermute | solution.py:54
  18.5 17.6 %collective-permute-start.10 = (s32[1,4]{1,0:T(1,128)S(1)}, s32[1,4]{1,0:T(1,128)S(1)}, u32[]{:S(2)}, u32[]{:S(2)}) collective-permute-start(s32[1,4]{1,0:T(1,128)S(1)} %bitcast.164), channel_id=1, source_target_pairs={{0,2},{1,3},{2,0},{3,1},{4,6},{5,7},{6,4},{7,5},{8,10},{9,11},{10,... | collective-permute-start | bytes 56 | tf_op jit(solution)/shard_map/ppermute | solution.py:54
  18.6 17.6 %collective-permute-start.11 = (s32[1,4]{1,0:T(1,128)S(1)}, s32[1,4]{1,0:T(1,128)S(1)}, u32[]{:S(2)}, u32[]{:S(2)}) collective-permute-start(s32[1,4]{1,0:T(1,128)S(1)} %bitcast.165), channel_id=1, source_target_pairs={{0,3},{1,0},{2,1},{3,2},{4,7},{5,4},{6,5},{7,6},{8,11},{9,8},{10,9... | collective-permute-start | bytes 56 | tf_op jit(solution)/shard_map/ppermute | solution.py:54
  25.3 25.0 %collective-permute-start.15 = (bf16[1,4,2688]{2,1,0:T(4,128)(2,1)S(1)}, bf16[1,4,2688]{2,1,0:T(4,128)(2,1)S(1)}, u32[]{:S(2)}, u32[]{:S(2)}) collective-permute-start(bf16[1,4,2688]{2,1,0:T(4,128)(2,1)S(1)} %bitcast.127), channel_id=1, source_target_pairs={{0,1},{1,2},{2,3},{3,0},{4,5},{5,6},{6,7},{7,4},{8,9},{9,10},{10,1... | collective-permute-start | bytes 64520 | tf_op jit(solution)/shard_map/ppermute | solution.py:54
  36.8 5.5 %collective-permute-start.12 = (s32[4,4]{1,0:T(4,128)S(1)}, s32[4,4]{1,0:T(4,128)S(1)}, u32[]{:S(2)}, u32[]{:S(2)}) collective-permute-start(s32[4,4]{1,0:T(4,128)S(1)} %broadcast_select_fusion.5), channel_id=1, source_target_pairs={{0,4},{1,5},{2,6},{3,7},{4,8},{5,9},{6,10},{7,11},{8,12},{9,13},{1... | collective-permute-start | bytes 200 | tf_op jit(solution)/shard_map/ppermute | solution.py:54
  38.4 4.5 %collective-permute-start.13 = (s32[4,4]{1,0:T(4,128)S(1)}, s32[4,4]{1,0:T(4,128)S(1)}, u32[]{:S(2)}, u32[]{:S(2)}) collective-permute-start(s32[4,4]{1,0:T(4,128)S(1)} %broadcast_select_fusion.5), channel_id=1, source_target_pairs={{0,8},{1,9},{2,10},{3,11},{4,12},{5,13},{6,14},{7,15},{8,0},{9,1},... | collective-permute-start | bytes 200 | tf_op jit(solution)/shard_map/ppermute | solution.py:54
  42.3 3.8 %collective-permute-start.14 = (s32[4,4]{1,0:T(4,128)S(1)}, s32[4,4]{1,0:T(4,128)S(1)}, u32[]{:S(2)}, u32[]{:S(2)}) collective-permute-start(s32[4,4]{1,0:T(4,128)S(1)} %broadcast_select_fusion.5), channel_id=1, source_target_pairs={{0,12},{1,13},{2,14},{3,15},{4,0},{5,1},{6,2},{7,3},{8,4},{9,5},{1... | collective-permute-start | bytes 200 | tf_op jit(solution)/shard_map/ppermute | solution.py:54
  42.9 7.9 %collective-permute-start.16 = (bf16[1,4,2688]{2,1,0:T(4,128)(2,1)S(1)}, bf16[1,4,2688]{2,1,0:T(4,128)(2,1)S(1)}, u32[]{:S(2)}, u32[]{:S(2)}) collective-permute-start(bf16[1,4,2688]{2,1,0:T(4,128)(2,1)S(1)} %bitcast.128), channel_id=1, source_target_pairs={{0,2},{1,3},{2,0},{3,1},{4,6},{5,7},{6,4},{7,5},{8,10},{9,11},{10,... | collective-permute-start | bytes 64520 | tf_op jit(solution)/shard_map/ppermute | solution.py:54
  46.1 4.7 %collective-permute-start.17 = (bf16[1,4,2688]{2,1,0:T(4,128)(2,1)S(1)}, bf16[1,4,2688]{2,1,0:T(4,128)(2,1)S(1)}, u32[]{:S(2)}, u32[]{:S(2)}) collective-permute-start(bf16[1,4,2688]{2,1,0:T(4,128)(2,1)S(1)} %bitcast.129), channel_id=1, source_target_pairs={{0,3},{1,0},{2,1},{3,2},{4,7},{5,4},{6,5},{7,6},{8,11},{9,8},{10,9... | collective-permute-start | bytes 64520 | tf_op jit(solution)/shard_map/ppermute | solution.py:54
  50.3 63.5 %collective-permute-start.8 = (bf16[128,2048]{0,1:T(8,128)(2,1)S(1)}, bf16[128,2048]{0,1:T(8,128)(2,1)S(1)}, u32[]{:S(2)}, u32[]{:S(2)}) collective-permute-start(bf16[128,2048]{0,1:T(8,128)(2,1)S(1)} %copy.26), channel_id=1, source_target_pairs={{0,1},{1,0},{2,3},{3,2},{4,5},{5,4},{6,7},{7,6},{8,9},{9,8},{10,11... | collective-permute-start | bytes 1572872 | tf_op jit(solution)/shard_map/ppermute | solution.py:37
  51.5 26.2 %collective-permute-start.1 = (bf16[128,2048]{0,1:T(8,128)(2,1)S(1)}, bf16[128,2048]{0,1:T(8,128)(2,1)S(1)}, u32[]{:S(2)}, u32[]{:S(2)}) collective-permute-start(bf16[128,2048]{0,1:T(8,128)(2,1)S(1)} %collective-permute-done), channel_id=1, source_target_pairs={{0,4},{1,5},{2,6},{3,7},{4,8},{5,9},{6,10},{7,11},{8,12},{9,13},{1... | collective-permute-start | bytes 1572872 | tf_op jit(solution)/shard_map/ppermute | solution.py:70
  54.3 27.4 %collective-permute-start.6 = (bf16[128,2048]{0,1:T(8,128)(2,1)S(1)}, bf16[128,2048]{0,1:T(8,128)(2,1)S(1)}, u32[]{:S(2)}, u32[]{:S(2)}) collective-permute-start(bf16[128,2048]{0,1:T(8,128)(2,1)S(1)} %collective-permute-done), channel_id=1, source_target_pairs={{2,0},{3,1},{6,4},{7,5},{10,8},{11,9},{14,12},{15,13},{18,16},{19,... | collective-permute-start | bytes 1572872 | tf_op jit(solution)/shard_map/ppermute | solution.py:76
  56.4 71.0 %collective-permute-start.18 = (bf16[4,4,2688]{2,1,0:T(4,128)(2,1)}, bf16[4,4,2688]{2,1,0:T(4,128)(2,1)}, u32[]{:S(2)}, u32[]{:S(2)}) collective-permute-start(bf16[4,4,2688]{2,1,0:T(4,128)(2,1)} %broadcast_select_fusion.2), channel_id=1, source_target_pairs={{0,4},{1,5},{2,6},{3,7},{4,8},{5,9},{6,10},{7,11},{8,12},{9,13},{1... | collective-permute-start | bytes 258056 | tf_op jit(solution)/shard_map/ppermute | solution.py:54
  56.7 72.4 %collective-permute-start.19 = (bf16[4,4,2688]{2,1,0:T(4,128)(2,1)}, bf16[4,4,2688]{2,1,0:T(4,128)(2,1)}, u32[]{:S(2)}, u32[]{:S(2)}) collective-permute-start(bf16[4,4,2688]{2,1,0:T(4,128)(2,1)} %broadcast_select_fusion.2), channel_id=1, source_target_pairs={{0,8},{1,9},{2,10},{3,11},{4,12},{5,13},{6,14},{7,15},{8,0},{9,1},... | collective-permute-start | bytes 258056 | tf_op jit(solution)/shard_map/ppermute | solution.py:54
  77.8 18.4 %collective-permute-start.2 = (bf16[128,2048]{0,1:T(8,128)(2,1)S(1)}, bf16[128,2048]{0,1:T(8,128)(2,1)S(1)}, u32[]{:S(2)}, u32[]{:S(2)}) collective-permute-start(bf16[128,2048]{0,1:T(8,128)(2,1)S(1)} %collective-permute-done), channel_id=1, source_target_pairs={{0,2},{1,3},{4,6},{5,7},{8,10},{9,11},{12,14},{13,15},{16,18},{17,... | collective-permute-start | bytes 1572872 | tf_op jit(solution)/shard_map/ppermute | solution.py:76
  81.7 27.1 %collective-permute-start.3 = (bf16[128,2048]{0,1:T(8,128)(2,1)S(1)}, bf16[128,2048]{0,1:T(8,128)(2,1)S(1)}, u32[]{:S(2)}, u32[]{:S(2)}) collective-permute-start(bf16[128,2048]{0,1:T(8,128)(2,1)S(1)} %collective-permute-done.1), channel_id=1, source_target_pairs={{2,0},{3,1},{6,4},{7,5},{10,8},{11,9},{14,12},{15,13},{18,16},{19,... | collective-permute-start | bytes 1572872 | tf_op jit(solution)/shard_map/ppermute | solution.py:76
  96.1 13.0 %collective-permute-start.7 = (bf16[2,128,2048]{1,2,0:T(8,128)(2,1)S(1)}, bf16[2,128,2048]{1,2,0:T(8,128)(2,1)S(1)}, u32[]{:S(2)}, u32[]{:S(2)}) collective-permute-start(bf16[2,128,2048]{1,2,0:T(8,128)(2,1)S(1)} %pad_maximum_fusion.1), channel_id=1, source_target_pairs={{0,1},{1,0},{2,3},{3,2},{4,5},{5,4},{6,7},{7,6},{8,9},{9,8},{10,11... | collective-permute-start | bytes 3145736 | tf_op jit(solution)/shard_map/ppermute | solution.py:37
  109.0 3.3 %collective-permute-start.4 = (bf16[2,128,2048]{1,2,0:T(8,128)(2,1)S(1)}, bf16[2,128,2048]{1,2,0:T(8,128)(2,1)S(1)}, u32[]{:S(2)}, u32[]{:S(2)}) collective-permute-start(bf16[2,128,2048]{1,2,0:T(8,128)(2,1)S(1)} %pad_maximum_fusion), channel_id=1, source_target_pairs={{0,1},{1,0},{2,3},{3,2},{4,5},{5,4},{6,7},{7,6},{8,9},{9,8},{10,11... | collective-permute-start | bytes 3145736 | tf_op jit(solution)/shard_map/ppermute | solution.py:37
  109.2 19.9 %collective-permute-start.20 = (bf16[4,4,2688]{2,1,0:T(4,128)(2,1)}, bf16[4,4,2688]{2,1,0:T(4,128)(2,1)}, u32[]{:S(2)}, u32[]{:S(2)}) collective-permute-start(bf16[4,4,2688]{2,1,0:T(4,128)(2,1)} %broadcast_select_fusion.2), channel_id=1, source_target_pairs={{0,12},{1,13},{2,14},{3,15},{4,0},{5,1},{6,2},{7,3},{8,4},{9,5},{1... | collective-permute-start | bytes 258056 | tf_op jit(solution)/shard_map/ppermute | solution.py:54
  114.2 1.9 %copy-start.2 = (pred[128,1152]{0,1:T(8,128)(4,1)S(1)}, pred[128,1152]{0,1:T(8,128)(4,1)}, u32[]{:S(2)}) copy-start(pred[128,1152]{0,1:T(8,128)(4,1)} %fusion.16) | copy-start | bytes 442372
  127.2 4.1 %collective-permute-start.21 = (bf16[1,4,2048]{2,1,0:T(4,128)(2,1)S(1)}, bf16[1,4,2048]{2,1,0:T(4,128)(2,1)S(1)}, u32[]{:S(2)}, u32[]{:S(2)}) collective-permute-start(bf16[1,4,2048]{2,1,0:T(4,128)(2,1)S(1)} %bitcast.133), channel_id=1, source_target_pairs={{0,1},{1,2},{2,3},{3,0},{4,5},{5,6},{6,7},{7,4},{8,9},{9,10},{10,1... | collective-permute-start | bytes 49160 | tf_op jit(solution)/shard_map/ppermute | solution.py:54
  127.3 4.0 %collective-permute-start.22 = (bf16[1,4,2048]{2,1,0:T(4,128)(2,1)S(1)}, bf16[1,4,2048]{2,1,0:T(4,128)(2,1)S(1)}, u32[]{:S(2)}, u32[]{:S(2)}) collective-permute-start(bf16[1,4,2048]{2,1,0:T(4,128)(2,1)S(1)} %bitcast.134), channel_id=1, source_target_pairs={{0,2},{1,3},{2,0},{3,1},{4,6},{5,7},{6,4},{7,5},{8,10},{9,11},{10,... | collective-permute-start | bytes 49160 | tf_op jit(solution)/shard_map/ppermute | solution.py:54
  127.4 3.9 %collective-permute-start.23 = (bf16[1,4,2048]{2,1,0:T(4,128)(2,1)S(1)}, bf16[1,4,2048]{2,1,0:T(4,128)(2,1)S(1)}, u32[]{:S(2)}, u32[]{:S(2)}) collective-permute-start(bf16[1,4,2048]{2,1,0:T(4,128)(2,1)S(1)} %bitcast.135), channel_id=1, source_target_pairs={{0,3},{1,0},{2,1},{3,2},{4,7},{5,4},{6,5},{7,6},{8,11},{9,8},{10,9... | collective-permute-start | bytes 49160 | tf_op jit(solution)/shard_map/ppermute | solution.py:54
  132.1 7.0 %collective-permute-start.24 = (bf16[4,4,2048]{2,1,0:T(4,128)(2,1)S(1)}, bf16[4,4,2048]{2,1,0:T(4,128)(2,1)S(1)}, u32[]{:S(2)}, u32[]{:S(2)}) collective-permute-start(bf16[4,4,2048]{2,1,0:T(4,128)(2,1)S(1)} %broadcast_select_fusion.3), channel_id=1, source_target_pairs={{0,4},{1,5},{2,6},{3,7},{4,8},{5,9},{6,10},{7,11},{8,12},{9,13},{1... | collective-permute-start | bytes 196616 | tf_op jit(solution)/shard_map/ppermute | solution.py:54
  133.6 8.1 %collective-permute-start.25 = (bf16[4,4,2048]{2,1,0:T(4,128)(2,1)S(1)}, bf16[4,4,2048]{2,1,0:T(4,128)(2,1)S(1)}, u32[]{:S(2)}, u32[]{:S(2)}) collective-permute-start(bf16[4,4,2048]{2,1,0:T(4,128)(2,1)S(1)} %broadcast_select_fusion.3), channel_id=1, source_target_pairs={{0,8},{1,9},{2,10},{3,11},{4,12},{5,13},{6,14},{7,15},{8,0},{9,1},... | collective-permute-start | bytes 196616 | tf_op jit(solution)/shard_map/ppermute | solution.py:54
  134.9 6.8 %collective-permute-start.26 = (bf16[4,4,2048]{2,1,0:T(4,128)(2,1)S(1)}, bf16[4,4,2048]{2,1,0:T(4,128)(2,1)S(1)}, u32[]{:S(2)}, u32[]{:S(2)}) collective-permute-start(bf16[4,4,2048]{2,1,0:T(4,128)(2,1)S(1)} %broadcast_select_fusion.3), channel_id=1, source_target_pairs={{0,12},{1,13},{2,14},{3,15},{4,0},{5,1},{6,2},{7,3},{8,4},{9,5},{1... | collective-permute-start | bytes 196616 | tf_op jit(solution)/shard_map/ppermute | solution.py:54
  142.9 6.6 %copy-start.3 = (f32[2688]{0:T(1024)S(1)}, f32[2688]{0:T(1024)}, u32[]{:S(2)}) copy-start(f32[2688]{0:T(1024)} %param.12) | copy-start | bytes 32260
  142.9 13.8 %copy-start = (bf16[2048,2688]{1,0:T(8,128)(2,1)S(1)}, bf16[2048,2688]{1,0:T(8,128)(2,1)}, u32[]{:S(2)}) copy-start(bf16[2048,2688]{1,0:T(8,128)(2,1)} %all-gather.2.cloned.1.call-done) | copy-start | bytes 33030148
  149.4 7.3 %copy-start.1 = (bf16[128,2688]{1,0:T(8,128)(2,1)S(1)}, bf16[128,2688]{1,0:T(8,128)(2,1)}, u32[]{:S(2)}) copy-start(bf16[128,2688]{1,0:T(8,128)(2,1)} %param.11) | copy-start | bytes 2064388
  154.2 5.1 %collective-permute-start.27 = (f32[1,3,64]{2,1,0:T(4,128)S(1)}, f32[1,3,64]{2,1,0:T(4,128)S(1)}, u32[]{:S(2)}, u32[]{:S(2)}) collective-permute-start(f32[1,3,64]{2,1,0:T(4,128)S(1)} %get-tuple-element.32), channel_id=1, source_target_pairs={{0,1},{1,2},{2,3},{3,0},{4,5},{5,6},{6,7},{7,4},{8,9},{9,10},{10,1... | collective-permute-start | bytes 2312 | tf_op jit(solution)/shard_map/ppermute | solution.py:54
  154.3 4.9 %collective-permute-start.28 = (f32[1,3,64]{2,1,0:T(4,128)S(1)}, f32[1,3,64]{2,1,0:T(4,128)S(1)}, u32[]{:S(2)}, u32[]{:S(2)}) collective-permute-start(f32[1,3,64]{2,1,0:T(4,128)S(1)} %get-tuple-element.32), channel_id=1, source_target_pairs={{0,2},{1,3},{2,0},{3,1},{4,6},{5,7},{6,4},{7,5},{8,10},{9,11},{10,... | collective-permute-start | bytes 2312 | tf_op jit(solution)/shard_map/ppermute | solution.py:54
  155.3 3.9 %collective-permute-start.29 = (f32[1,3,64]{2,1,0:T(4,128)S(1)}, f32[1,3,64]{2,1,0:T(4,128)S(1)}, u32[]{:S(2)}, u32[]{:S(2)}) collective-permute-start(f32[1,3,64]{2,1,0:T(4,128)S(1)} %get-tuple-element.32), channel_id=1, source_target_pairs={{0,3},{1,0},{2,1},{3,2},{4,7},{5,4},{6,5},{7,6},{8,11},{9,8},{10,9... | collective-permute-start | bytes 2312 | tf_op jit(solution)/shard_map/ppermute | solution.py:54
  159.9 5.5 %collective-permute-start.30 = (f32[4,3,64]{2,1,0:T(4,128)S(1)}, f32[4,3,64]{2,1,0:T(4,128)S(1)}, u32[]{:S(2)}, u32[]{:S(2)}) collective-permute-start(f32[4,3,64]{2,1,0:T(4,128)S(1)} %broadcast_select_fusion.4), channel_id=1, source_target_pairs={{0,4},{1,5},{2,6},{3,7},{4,8},{5,9},{6,10},{7,11},{8,12},{9,13},{1... | collective-permute-start | bytes 9224 | tf_op jit(solution)/shard_map/ppermute | solution.py:54
  161.2 4.6 %collective-permute-start.31 = (f32[4,3,64]{2,1,0:T(4,128)S(1)}, f32[4,3,64]{2,1,0:T(4,128)S(1)}, u32[]{:S(2)}, u32[]{:S(2)}) collective-permute-start(f32[4,3,64]{2,1,0:T(4,128)S(1)} %broadcast_select_fusion.4), channel_id=1, source_target_pairs={{0,8},{1,9},{2,10},{3,11},{4,12},{5,13},{6,14},{7,15},{8,0},{9,1},... | collective-permute-start | bytes 9224 | tf_op jit(solution)/shard_map/ppermute | solution.py:54
  163.0 3.7 %collective-permute-start.32 = (f32[4,3,64]{2,1,0:T(4,128)S(1)}, f32[4,3,64]{2,1,0:T(4,128)S(1)}, u32[]{:S(2)}, u32[]{:S(2)}) collective-permute-start(f32[4,3,64]{2,1,0:T(4,128)S(1)} %broadcast_select_fusion.4), channel_id=1, source_target_pairs={{0,12},{1,13},{2,14},{3,15},{4,0},{5,1},{6,2},{7,3},{8,4},{9,5},{1... | collective-permute-start | bytes 9224 | tf_op jit(solution)/shard_map/ppermute | solution.py:54
Sparse Core Ops, SparseCore 0:
  10.3 116.6 all-gather.1

commit v12 on v7

--- a/solution.py
+++ b/solution.py
@@ -121,7 +121,6 @@
     full_proj = lax.all_gather(out_proj, SEQ, axis=0, tiled=True)
     score_count = SCORE_DEV
     stride = token_rows // score_count
-    scored_residual = gather_rows(residual.reshape(score_count, stride, width)[:, stride - 1, :])
 
     seg_cols = jnp.broadcast_to(segment_ids.astype(jnp.bfloat16)[:, None], (token_rows, SEG_LANES))
     own = jnp.concatenate([joined_keys_values, seg_cols], 1)
@@ -157,7 +156,17 @@
     )
     context = context.reshape(token_rows, QUERY_HEADS * HEAD_SIZE).astype(jnp.bfloat16)
 
-    scored_context = gather_rows(context.reshape(score_count, stride, -1)[:, stride - 1, :])
+    scored = gather_rows(
+        jnp.concatenate(
+            [
+                context.reshape(score_count, stride, -1)[:, stride - 1, :],
+                residual.reshape(score_count, stride, width)[:, stride - 1, :],
+            ],
+            1,
+        )
+    )
+    context_width = context.shape[1]
+    scored_context, scored_residual = scored[:, :context_width], scored[:, context_width:]
     picked = scored_residual.astype(jnp.float32) + jnp.dot(
         scored_context, full_proj, preferred_element_type=jnp.float32
     )

time: 164 us -> 173 us (1.055)
  waiting for transfers between devices: 53.2 us -> 61.3 us
  starting transfers between devices: 49 us -> 44.2 us
  other arithmetic: 10.5 us -> 13.2 us
  local copies, waits for them, and re-layouts: 12.5 us -> 15 us
    ppermute x2, waiting for transfers between devices: 15.4 us -> 26.3 us  [shift_chips(): lax.ppermute(value, SEQ, [(s, s + step) for s in range(count - step)])]
    ppermute x3, starting transfers between devices: 10.9 us -> 0.08 us  [swap_cores(): return lax.ppermute(value, 'core', [(0, 1), (1, 0)])]
    ppermute x4, waiting for transfers between devices: 27.3 us -> 20 us  [across_pair(): return lax.ppermute(value, SEQ, pairs)]
    ppermute x18 -> x12, waiting for transfers between devices: 9.72 us -> 14.3 us  [gather_rows(): received.append(lax.ppermute(data, SEQ, pairs))]
    ppermute x2, starting transfers between devices: 8.45 us -> 12.7 us  [shift_chips(): lax.ppermute(value, SEQ, [(s, s + step) for s in range(count - step)])]
    ppermute x4, starting transfers between devices: 8.1 us -> 10.6 us  [across_pair(): return lax.ppermute(value, SEQ, pairs)]
    reshape x1, local copies, waits for them, and re-layouts: 0.37 us -> 2.19 us  [local(): queries.reshape(token_rows, KEY_VALUE_HEADS, queries_per_group, HEAD_SIZE)]
    gather x8 -> x5, local copies, waits for them, and re-layouts: 4.77 us -> 3.53 us  [gather_rows(): data = jnp.take(stacked, order, axis=0)]
  transfers between devices with their start and end apart: 28 -> 22, of which waited for: 10 -> 9; matrix products, arithmetic and copies ran while one was open for 20% -> 22% of each run, Pallas kernels for 0% -> 0%
where the time goes in v12:
time: 173 us
  waiting for transfers between devices  61.3 us (35%)
  starting transfers between devices  44.2 us (26%)
  matrix products  24.3 us (14%)
  local copies, waits for them, and re-layouts  15 us (9%)
  between operations  14.5 us (8%)
  other arithmetic  13.2 us (8%)
    ppermute x2, waiting for transfers between devices, shift_chips(): lax.ppermute(value, SEQ, [(s, s + step) for s in range(count - step)])  26.3 us
    ppermute x12, starting transfers between devices, gather_rows(): received.append(lax.ppermute(data, SEQ, pairs))  20.7 us
    ppermute x4, waiting for transfers between devices, across_pair(): return lax.ppermute(value, SEQ, pairs)  20 us
    ppermute x12, waiting for transfers between devices, gather_rows(): received.append(lax.ppermute(data, SEQ, pairs))  14.3 us
    ppermute x2, starting transfers between devices, shift_chips(): lax.ppermute(value, SEQ, [(s, s + step) for s in range(count - step)])  12.7 us
    ppermute x4, starting transfers between devices, across_pair(): return lax.ppermute(value, SEQ, pairs)  10.6 us
    dot_general x1, matrix products, local(): jnp.einsum('hgqk,khd->qhgd', weights, heads_for_values, preferred_element...  6.58 us
    dot_general x1, matrix products, local(): jnp.dot(scored_context, full_proj, preferred_element_type=jnp.float32)  6.4 us
  transfers between devices with their start and end apart: 22, of which 9 were waited for; matrix products, arithmetic and copies ran while one was open for 22% of the time, Pallas kernels for 0%

profile of v12, /device:TPU:0, one launch (start us, length us, event | category | flops | bytes accessed | tf_op | source)
XLA Modules:
  0.0 172.6 jit_solution(3284282911223743743)
XLA Ops:
  7.2 0.7 all-gather.2.cloned.1.call-update
  7.9 1.3 copy.16
  9.2 0.7 convert_element_type.43
  9.9 5.0 %collective-permute-start = (bf16[128,2176]{0,1:T(8,128)(2,1)S(1)}, bf16[128,2176]{0,1:T(8,128)(2,1)S(1)}, u32[]{:S(2)}, u32[]{:S(2)}) collective-permute-start(bf16[128,2176]{0,1:T(8,128)(2,1)S(1)} %pad_maximum_fusion.3), channel_id=1, source_target_pairs={{0,4},{1,5},{2,6},{3,7},{4,8},{5,9},{6,10},{7,11},{8,12},{9,13},{1... | collective-permute-start | bytes 1671176 | tf_op jit(solution)/shard_map/ppermute | solution.py:70
  14.9 3.5 %collective-permute-start.5 = (bf16[128,2176]{0,1:T(8,128)(2,1)S(1)}, bf16[128,2176]{0,1:T(8,128)(2,1)S(1)}, u32[]{:S(2)}, u32[]{:S(2)}) collective-permute-start(bf16[128,2176]{0,1:T(8,128)(2,1)S(1)} %pad_maximum_fusion.3), channel_id=1, source_target_pairs={{0,2},{1,3},{4,6},{5,7},{8,10},{9,11},{12,14},{13,15},{16,18},{17,... | collective-permute-start | bytes 1671176 | tf_op jit(solution)/shard_map/ppermute | solution.py:76
  18.5 13.9 %collective-permute-done = bf16[128,2176]{0,1:T(8,128)(2,1)S(1)} collective-permute-done((bf16[128,2176]{0,1:T(8,128)(2,1)S(1)}, bf16[128,2176]{0,1:T(8,128)(2,1)S(1)}, u32[]{:S(2)}, u32[]{:S(2)}) %collective-permute-start) | collective-permute-done | bytes 557088 | tf_op jit(solution)/shard_map/ppermute | solution.py:70
  32.4 7.7 %collective-permute-start.1 = (bf16[128,2176]{0,1:T(8,128)(2,1)S(1)}, bf16[128,2176]{0,1:T(8,128)(2,1)S(1)}, u32[]{:S(2)}, u32[]{:S(2)}) collective-permute-start(bf16[128,2176]{0,1:T(8,128)(2,1)S(1)} %collective-permute-done), channel_id=1, source_target_pairs={{0,4},{1,5},{2,6},{3,7},{4,8},{5,9},{6,10},{7,11},{8,12},{9,13},{1... | collective-permute-start | bytes 1671176 | tf_op jit(solution)/shard_map/ppermute | solution.py:70
  40.2 1.3 collective-permute-start.6
  42.6 0.6 pad_clamp_fusion.1
  43.8 4.6 %collective-permute-start.2 = (bf16[128,2176]{0,1:T(8,128)(2,1)S(1)}, bf16[128,2176]{0,1:T(8,128)(2,1)S(1)}, u32[]{:S(2)}, u32[]{:S(2)}) collective-permute-start(bf16[128,2176]{0,1:T(8,128)(2,1)S(1)} %collective-permute-done), channel_id=1, source_target_pairs={{0,2},{1,3},{4,6},{5,7},{8,10},{9,11},{12,14},{13,15},{16,18},{17,... | collective-permute-start | bytes 1671176 | tf_op jit(solution)/shard_map/ppermute | solution.py:76
  48.4 12.4 %collective-permute-done.1 = bf16[128,2176]{0,1:T(8,128)(2,1)S(1)} collective-permute-done((bf16[128,2176]{0,1:T(8,128)(2,1)S(1)}, bf16[128,2176]{0,1:T(8,128)(2,1)S(1)}, u32[]{:S(2)}, u32[]{:S(2)}) %collective-permute-start.1) | collective-permute-done | bytes 557088 | tf_op jit(solution)/shard_map/ppermute | solution.py:70
  60.8 1.3 collective-permute-start.3
  62.2 1.1 pad_maximum_fusion.1
  63.3 20.0 %collective-permute-done.3 = bf16[128,2176]{0,1:T(8,128)(2,1)S(1)} collective-permute-done((bf16[128,2176]{0,1:T(8,128)(2,1)S(1)}, bf16[128,2176]{0,1:T(8,128)(2,1)S(1)}, u32[]{:S(2)}, u32[]{:S(2)}) %collective-permute-start.3) | collective-permute-done | bytes 557088 | tf_op jit(solution)/shard_map/ppermute | solution.py:76
  83.3 1.1 pad_maximum_fusion
  84.4 0.6 compare_and_fusion.1
  85.0 2.2 %reshape.306 = bf16[128,8,2,128]{3,2,1,0:T(2,128)(2,1)} reshape(bf16[128,2048]{1,0:T(8,128)(2,1)} %param.8) | data formatting | bytes 1048576 | tf_op jit(solution)/shard_map/reshape | solution.py:137
  87.2 1.0 slice.72
  88.2 0.6 copy.46
  89.4 1.3 slice_bitcast_fusion
  90.7 1.3 slice_bitcast_fusion.2
  93.5 1.6 fusion.14
  95.2 1.9 %constant_dynamic-slice_fusion = (bf16[1152,1024]{0,1:T(8,128)(2,1)S(1)}, bf16[1152,1024]{0,1:T(8,128)(2,1)}) fusion(bf16[1280,2176]{0,1:T(8,128)(2,1)S(1)} %fusion.14, s32[]{:T(128)S(6)} %select_n.199, s32[]{:T(128)S(6)} %add.176), kind=kLoop, calls=%fused_computation.107 | loop fusion | bytes 9437192 | tf_op jit(solution)/shard_map/slice | solution.py:138
  97.1 1.1 compare_and_fusion
  98.2 4.3 %fusion.49 = f32[8,2,128]{2,1,0:T(2,128)} fusion(pred[128,1152]{0,1:T(8,128)(4,1)S(1)} %compare_and_fusion, bf16[1152,8,128,1]{0,2,3,1:T(8,128)(2,1)S(1)} %bitcast.95, bf16[128,8,2,128]{3,2,1,0:T(2,128)(2,1)S(1)} %copy-done.2), kind=kOutput, calls=%fused_computation.114 | convolution fusion | flops 613418112 | bytes 3039232 | tf_op jit(solution)/shard_map/sub | solution.py:152
  102.5 6.6 %fusion.7 = bf16[8,128,2,128]{3,1,2,0:T(8,128)(2,1)S(1)} fusion(bf16[1152,8,128,1]{0,2,3,1:T(8,128)(2,1)} %bitcast.97, f32[8,2,128]{2,1,0:T(2,128)} %fusion.49, pred[128,1152]{0,1:T(8,128)(4,1)S(1)} %compare_and_fusion, bf16[1152,8,128,1]{0,2,3,1:T(8,128)(2,1)S(1)} %bitcast.96, bf16[128,8,2,128]{3,2,1,0:T(2,128)(2,1)S(1)} %copy-done.2), kind=kOutput, calls=%fused_computation.16 | convolution fusion | flops 1220021376 | bytes 5922816 | tf_op jit(solution)/shard_map/hgqk,khd->qhgd/dot_general | solution.py:154
  110.1 0.7 collective-permute-start.9
  110.8 1.4 collective-permute-start.11
  112.6 1.0 collective-permute-done.9
  113.6 1.2 collective-permute-done.10
  114.9 0.8 gather_fusion
  115.9 5.5 %collective-permute-start.12 = (bf16[4,4,4736]{2,1,0:T(4,128)(2,1)S(1)}, bf16[4,4,4736]{2,1,0:T(4,128)(2,1)S(1)}, u32[]{:S(2)}, u32[]{:S(2)}) collective-permute-start(bf16[4,4,4736]{2,1,0:T(4,128)(2,1)S(1)} %broadcast_select_fusion.3), channel_id=1, source_target_pairs={{0,4},{1,5},{2,6},{3,7},{4,8},{5,9},{6,10},{7,11},{8,12},{9,13},{1... | collective-permute-start | bytes 454664 | tf_op jit(solution)/shard_map/ppermute | solution.py:54
  121.3 4.1 %collective-permute-start.13 = (bf16[4,4,4736]{2,1,0:T(4,128)(2,1)S(1)}, bf16[4,4,4736]{2,1,0:T(4,128)(2,1)S(1)}, u32[]{:S(2)}, u32[]{:S(2)}) collective-permute-start(bf16[4,4,4736]{2,1,0:T(4,128)(2,1)S(1)} %broadcast_select_fusion.3), channel_id=1, source_target_pairs={{0,8},{1,9},{2,10},{3,11},{4,12},{5,13},{6,14},{7,15},{8,0},{9,1},... | collective-permute-start | bytes 454664 | tf_op jit(solution)/shard_map/ppermute | solution.py:54
  125.4 0.9 collective-permute-start.14
  126.4 3.1 %collective-permute-done.12 = bf16[4,4,4736]{2,1,0:T(4,128)(2,1)S(1)} collective-permute-done((bf16[4,4,4736]{2,1,0:T(4,128)(2,1)S(1)}, bf16[4,4,4736]{2,1,0:T(4,128)(2,1)S(1)}, u32[]{:S(2)}, u32[]{:S(2)}) %collective-permute-start.12) | collective-permute-done | bytes 151584 | tf_op jit(solution)/shard_map/ppermute | solution.py:54
  129.5 6.7 %collective-permute-done.13 = bf16[4,4,4736]{2,1,0:T(4,128)(2,1)S(1)} collective-permute-done((bf16[4,4,4736]{2,1,0:T(4,128)(2,1)S(1)}, bf16[4,4,4736]{2,1,0:T(4,128)(2,1)S(1)}, u32[]{:S(2)}, u32[]{:S(2)}) %collective-permute-start.13) | collective-permute-done | bytes 151584 | tf_op jit(solution)/shard_map/ppermute | solution.py:54
  136.7 1.2 gather_fusion.1
  138.3 6.4 %multiply_reduce_fusion = (f32[64]{0:T(128)S(1)}, f32[64,2688]{1,0:T(8,128)S(1)}) fusion(bf16[2048,2688]{1,0:T(8,128)(2,1)} %all-gather.2.cloned.1.call-done, bf16[64,4736]{1,0:T(8,128)(2,1)S(1)} %broadcast_select_fusion), kind=kOutput, calls=%fused_computation.31 | convolution fusion | flops 705331136 | bytes 12304640 | tf_op jit(solution)/shard_map/dot_general | solution.py:170
  144.7 4.5 %fusion.52 = (f32[64]{0:T(128)S(1)}, f32[64,1024]{1,0:T(8,128)S(1)}) fusion(bf16[1024,2688]{1,0:T(8,128)(2,1)} %param.14, f32[64,2688]{1,0:T(8,128)S(1)} %get-tuple-element.21, f32[2688]{0:T(1024)S(1)} %copy-done.4, f32[64]{0:T(128)S(1)} %add_rsqrt_fusion), kind=kOutput, calls=%fused_computation.115 | convolution fusion | flops 352903104 | bytes 6466560 | tf_op jit(solution)/shard_map/dot_general | solution.py:177
  150.2 1.4 collective-permute-start.17
  151.5 2.5 %fusion.6 = bf16[128,2688]{1,0:T(8,128)(2,1)} fusion(bf16[128,2048]{0,1:T(8,128)(2,1)S(1)} %bitcast.94, bf16[2048,2688]{1,0:T(8,128)(2,1)S(1)} %copy-done, bf16[128,2688]{1,0:T(8,128)(2,1)S(1)} %copy-done.1), kind=kOutput, calls=%fused_computation.14 | convolution fusion | flops 1410318336 | bytes 12910592 | tf_op jit(solution)/shard_map/dot_general | solution.py:174
  154.1 0.7 gather_fusion.2
  154.9 3.8 %collective-permute-start.18 = (f32[4,3,64]{2,1,0:T(4,128)S(1)}, f32[4,3,64]{2,1,0:T(4,128)S(1)}, u32[]{:S(2)}, u32[]{:S(2)}) collective-permute-start(f32[4,3,64]{2,1,0:T(4,128)S(1)} %broadcast_select_fusion.4), channel_id=1, source_target_pairs={{0,4},{1,5},{2,6},{3,7},{4,8},{5,9},{6,10},{7,11},{8,12},{9,13},{1... | collective-permute-start | bytes 9224 | tf_op jit(solution)/shard_map/ppermute | solution.py:54
  158.7 1.1 collective-permute-start.19
  159.8 1.3 collective-permute-start.20
  161.2 2.0 %collective-permute-done.19 = f32[4,3,64]{2,1,0:T(4,128)S(1)} collective-permute-done((f32[4,3,64]{2,1,0:T(4,128)S(1)}, f32[4,3,64]{2,1,0:T(4,128)S(1)}, u32[]{:S(2)}, u32[]{:S(2)}) %collective-permute-start.19) | collective-permute-done | bytes 3104 | tf_op jit(solution)/shard_map/ppermute | solution.py:54
  163.5 0.7 gather_fusion.3
  164.4 0.8 broadcast_subtract_fusion
  (90 shorter events, 8.8 us)
Async XLA Ops:
  7.2 131.1 %all-gather.2.cloned.1.call-start = ((), (), s32[]{:S(2)}) async-start(), calls=%async_computation | async-start | bytes 11698176 | tf_op jit(solution)/shard_map/all_gather | solution.py:121
  9.9 22.5 %collective-permute-start = (bf16[128,2176]{0,1:T(8,128)(2,1)S(1)}, bf16[128,2176]{0,1:T(8,128)(2,1)S(1)}, u32[]{:S(2)}, u32[]{:S(2)}) collective-permute-start(bf16[128,2176]{0,1:T(8,128)(2,1)S(1)} %pad_maximum_fusion.3), channel_id=1, source_target_pairs={{0,4},{1,5},{2,6},{3,7},{4,8},{5,9},{6,10},{7,11},{8,12},{9,13},{1... | collective-permute-start | bytes 1671176 | tf_op jit(solution)/shard_map/ppermute | solution.py:70
  14.9 47.2 %collective-permute-start.5 = (bf16[128,2176]{0,1:T(8,128)(2,1)S(1)}, bf16[128,2176]{0,1:T(8,128)(2,1)S(1)}, u32[]{:S(2)}, u32[]{:S(2)}) collective-permute-start(bf16[128,2176]{0,1:T(8,128)(2,1)S(1)} %pad_maximum_fusion.3), channel_id=1, source_target_pairs={{0,2},{1,3},{4,6},{5,7},{8,10},{9,11},{12,14},{13,15},{16,18},{17,... | collective-permute-start | bytes 1671176 | tf_op jit(solution)/shard_map/ppermute | solution.py:76
  18.4 75.1 %collective-permute-start.8 = (bf16[128,2176]{0,1:T(8,128)(2,1)S(1)}, bf16[128,2176]{0,1:T(8,128)(2,1)}, u32[]{:S(2)}, u32[]{:S(2)}) collective-permute-start(bf16[128,2176]{0,1:T(8,128)(2,1)S(1)} %pad_maximum_fusion.3), channel_id=1, source_target_pairs={{0,1},{1,0},{2,3},{3,2},{4,5},{5,4},{6,7},{7,6},{8,9},{9,8},{10,11... | collective-permute-start | bytes 1671176 | tf_op jit(solution)/shard_map/ppermute | solution.py:37
  32.4 28.4 %collective-permute-start.1 = (bf16[128,2176]{0,1:T(8,128)(2,1)S(1)}, bf16[128,2176]{0,1:T(8,128)(2,1)S(1)}, u32[]{:S(2)}, u32[]{:S(2)}) collective-permute-start(bf16[128,2176]{0,1:T(8,128)(2,1)S(1)} %collective-permute-done), channel_id=1, source_target_pairs={{0,4},{1,5},{2,6},{3,7},{4,8},{5,9},{6,10},{7,11},{8,12},{9,13},{1... | collective-permute-start | bytes 1671176 | tf_op jit(solution)/shard_map/ppermute | solution.py:70
  40.2 21.9 %collective-permute-start.6 = (bf16[128,2176]{0,1:T(8,128)(2,1)S(1)}, bf16[128,2176]{0,1:T(8,128)(2,1)S(1)}, u32[]{:S(2)}, u32[]{:S(2)}) collective-permute-start(bf16[128,2176]{0,1:T(8,128)(2,1)S(1)} %collective-permute-done), channel_id=1, source_target_pairs={{2,0},{3,1},{6,4},{7,5},{10,8},{11,9},{14,12},{15,13},{18,16},{19,... | collective-permute-start | bytes 1671176 | tf_op jit(solution)/shard_map/ppermute | solution.py:76
  43.8 19.5 %collective-permute-start.2 = (bf16[128,2176]{0,1:T(8,128)(2,1)S(1)}, bf16[128,2176]{0,1:T(8,128)(2,1)S(1)}, u32[]{:S(2)}, u32[]{:S(2)}) collective-permute-start(bf16[128,2176]{0,1:T(8,128)(2,1)S(1)} %collective-permute-done), channel_id=1, source_target_pairs={{0,2},{1,3},{4,6},{5,7},{8,10},{9,11},{12,14},{13,15},{16,18},{17,... | collective-permute-start | bytes 1671176 | tf_op jit(solution)/shard_map/ppermute | solution.py:76
  60.8 22.5 %collective-permute-start.3 = (bf16[128,2176]{0,1:T(8,128)(2,1)S(1)}, bf16[128,2176]{0,1:T(8,128)(2,1)S(1)}, u32[]{:S(2)}, u32[]{:S(2)}) collective-permute-start(bf16[128,2176]{0,1:T(8,128)(2,1)S(1)} %collective-permute-done.1), channel_id=1, source_target_pairs={{2,0},{3,1},{6,4},{7,5},{10,8},{11,9},{14,12},{15,13},{18,16},{19,... | collective-permute-start | bytes 1671176 | tf_op jit(solution)/shard_map/ppermute | solution.py:76
  63.3 25.6 %copy-start.11 = (s32[64]{0:T(128)S(1)}, s32[64]{0:T(128)}, u32[]{:S(2)}) copy-start(s32[64]{0:T(128)} %param.15) | copy-start | bytes 772
  63.3 26.1 %collective-permute-start.7 = (bf16[2,128,2176]{1,2,0:T(8,128)(2,1)}, bf16[2,128,2176]{1,2,0:T(8,128)(2,1)}, u32[]{:S(2)}, u32[]{:S(2)}) collective-permute-start(bf16[2,128,2176]{1,2,0:T(8,128)(2,1)} %pad_maximum_fusion.1), channel_id=1, source_target_pairs={{0,1},{1,0},{2,3},{3,2},{4,5},{5,4},{6,7},{7,6},{8,9},{9,8},{10,11... | collective-permute-start | bytes 3342344 | tf_op jit(solution)/shard_map/ppermute | solution.py:37
  84.4 6.2 %collective-permute-start.4 = (bf16[2,128,2176]{1,2,0:T(8,128)(2,1)}, bf16[2,128,2176]{1,2,0:T(8,128)(2,1)}, u32[]{:S(2)}, u32[]{:S(2)}) collective-permute-start(bf16[2,128,2176]{1,2,0:T(8,128)(2,1)} %pad_maximum_fusion), channel_id=1, source_target_pairs={{0,1},{1,0},{2,3},{3,2},{4,5},{5,4},{6,7},{7,6},{8,9},{9,8},{10,11... | collective-permute-start | bytes 3342344 | tf_op jit(solution)/shard_map/ppermute | solution.py:37
  95.2 1.9 %copy-start.6 = (pred[1152]{0:T(1024)(128)(4,1)S(1)}, pred[1152]{0:T(1024)(128)(4,1)}, u32[]{:S(2)}) copy-start(pred[1152]{0:T(1024)(128)(4,1)} %broadcast_compare_fusion) | copy-start | bytes 3460
  95.2 1.9 %copy-start.7 = (s32[128]{0:T(128)S(1)}, s32[128]{0:T(128)}, u32[]{:S(2)}) copy-start(s32[128]{0:T(128)} %param.10) | copy-start | bytes 1540
  95.2 1.9 %copy-start.9 = (s32[128]{0:T(128)S(1)}, s32[128]{0:T(128)}, u32[]{:S(2)}) copy-start(s32[128]{0:T(128)} %get-tuple-element.24) | copy-start | bytes 1540
  95.2 1.9 %copy-start.10 = (s32[128]{0:T(128)S(1)}, s32[128]{0:T(128)}, u32[]{:S(2)}) copy-start(s32[128]{0:T(128)} %get-tuple-element.25) | copy-start | bytes 1540
  95.2 3.0 %copy-start.2 = (bf16[128,8,2,128]{3,2,1,0:T(2,128)(2,1)S(1)}, bf16[128,8,2,128]{3,2,1,0:T(2,128)(2,1)}, u32[]{:S(2)}) copy-start(bf16[128,8,2,128]{3,2,1,0:T(2,128)(2,1)} %reshape.306) | copy-start | bytes 1572868
  109.1 1.0 copy-start.3
  109.1 6.6 %copy-start.5 = (pred[4]{0:T(512)(128)(4,1)S(1)}, pred[4]{0:T(512)(128)(4,1)}, u32[]{:S(2)}) copy-start(pred[4]{0:T(512)(128)(4,1)} %compare_and_fusion.1) | copy-start | bytes 16
  110.1 3.4 %collective-permute-start.9 = (bf16[1,4,4736]{2,1,0:T(4,128)(2,1)S(1)}, bf16[1,4,4736]{2,1,0:T(4,128)(2,1)S(1)}, u32[]{:S(2)}, u32[]{:S(2)}) collective-permute-start(bf16[1,4,4736]{2,1,0:T(4,128)(2,1)S(1)} %get-tuple-element.14), channel_id=1, source_target_pairs={{0,1},{1,2},{2,3},{3,0},{4,5},{5,6},{6,7},{7,4},{8,9},{9,10},{10,1... | collective-permute-start | bytes 113672 | tf_op jit(solution)/shard_map/ppermute | solution.py:54
  110.8 4.0 %collective-permute-start.10 = (bf16[1,4,4736]{2,1,0:T(4,128)(2,1)S(1)}, bf16[1,4,4736]{2,1,0:T(4,128)(2,1)S(1)}, u32[]{:S(2)}, u32[]{:S(2)}) collective-permute-start(bf16[1,4,4736]{2,1,0:T(4,128)(2,1)S(1)} %get-tuple-element.14), channel_id=1, source_target_pairs={{0,2},{1,3},{2,0},{3,1},{4,6},{5,7},{6,4},{7,5},{8,10},{9,11},{10,... | collective-permute-start | bytes 113672 | tf_op jit(solution)/shard_map/ppermute | solution.py:54
  110.8 4.0 %collective-permute-start.11 = (bf16[1,4,4736]{2,1,0:T(4,128)(2,1)S(1)}, bf16[1,4,4736]{2,1,0:T(4,128)(2,1)S(1)}, u32[]{:S(2)}, u32[]{:S(2)}) collective-permute-start(bf16[1,4,4736]{2,1,0:T(4,128)(2,1)S(1)} %get-tuple-element.14), channel_id=1, source_target_pairs={{0,3},{1,0},{2,1},{3,2},{4,7},{5,4},{6,5},{7,6},{8,11},{9,8},{10,9... | collective-permute-start | bytes 113672 | tf_op jit(solution)/shard_map/ppermute | solution.py:54
  115.9 13.7 %collective-permute-start.12 = (bf16[4,4,4736]{2,1,0:T(4,128)(2,1)S(1)}, bf16[4,4,4736]{2,1,0:T(4,128)(2,1)S(1)}, u32[]{:S(2)}, u32[]{:S(2)}) collective-permute-start(bf16[4,4,4736]{2,1,0:T(4,128)(2,1)S(1)} %broadcast_select_fusion.3), channel_id=1, source_target_pairs={{0,4},{1,5},{2,6},{3,7},{4,8},{5,9},{6,10},{7,11},{8,12},{9,13},{1... | collective-permute-start | bytes 454664 | tf_op jit(solution)/shard_map/ppermute | solution.py:54
  121.3 14.9 %collective-permute-start.13 = (bf16[4,4,4736]{2,1,0:T(4,128)(2,1)S(1)}, bf16[4,4,4736]{2,1,0:T(4,128)(2,1)S(1)}, u32[]{:S(2)}, u32[]{:S(2)}) collective-permute-start(bf16[4,4,4736]{2,1,0:T(4,128)(2,1)S(1)} %broadcast_select_fusion.3), channel_id=1, source_target_pairs={{0,8},{1,9},{2,10},{3,11},{4,12},{5,13},{6,14},{7,15},{8,0},{9,1},... | collective-permute-start | bytes 454664 | tf_op jit(solution)/shard_map/ppermute | solution.py:54
  125.4 10.8 %collective-permute-start.14 = (bf16[4,4,4736]{2,1,0:T(4,128)(2,1)S(1)}, bf16[4,4,4736]{2,1,0:T(4,128)(2,1)S(1)}, u32[]{:S(2)}, u32[]{:S(2)}) collective-permute-start(bf16[4,4,4736]{2,1,0:T(4,128)(2,1)S(1)} %broadcast_select_fusion.3), channel_id=1, source_target_pairs={{0,12},{1,13},{2,14},{3,15},{4,0},{5,1},{6,2},{7,3},{8,4},{9,5},{1... | collective-permute-start | bytes 454664 | tf_op jit(solution)/shard_map/ppermute | solution.py:54
  138.2 6.5 %copy-start.4 = (f32[2688]{0:T(1024)S(1)}, f32[2688]{0:T(1024)}, u32[]{:S(2)}) copy-start(f32[2688]{0:T(1024)} %param.12) | copy-start | bytes 32260
  138.3 13.3 %copy-start = (bf16[2048,2688]{1,0:T(8,128)(2,1)S(1)}, bf16[2048,2688]{1,0:T(8,128)(2,1)}, u32[]{:S(2)}) copy-start(bf16[2048,2688]{1,0:T(8,128)(2,1)} %all-gather.2.cloned.1.call-done) | copy-start | bytes 33030148
  144.7 4.5 %copy-start.8 = (s32[64]{0:T(128)S(1)}, s32[64]{0:T(128)}, u32[]{:S(2)}) copy-start(s32[64]{0:T(128)} %broadcast_subtract_fusion.1) | copy-start | bytes 772
  144.7 6.8 %copy-start.1 = (bf16[128,2688]{1,0:T(8,128)(2,1)S(1)}, bf16[128,2688]{1,0:T(8,128)(2,1)}, u32[]{:S(2)}) copy-start(bf16[128,2688]{1,0:T(8,128)(2,1)} %param.11) | copy-start | bytes 2064388
  149.5 4.6 %collective-permute-start.15 = (f32[1,3,64]{2,1,0:T(4,128)S(1)}, f32[1,3,64]{2,1,0:T(4,128)S(1)}, u32[]{:S(2)}, u32[]{:S(2)}) collective-permute-start(f32[1,3,64]{2,1,0:T(4,128)S(1)} %get-tuple-element.19), channel_id=1, source_target_pairs={{0,1},{1,2},{2,3},{3,0},{4,5},{5,6},{6,7},{7,4},{8,9},{9,10},{10,1... | collective-permute-start | bytes 2312 | tf_op jit(solution)/shard_map/ppermute | solution.py:54
  149.7 4.4 %collective-permute-start.16 = (f32[1,3,64]{2,1,0:T(4,128)S(1)}, f32[1,3,64]{2,1,0:T(4,128)S(1)}, u32[]{:S(2)}, u32[]{:S(2)}) collective-permute-start(f32[1,3,64]{2,1,0:T(4,128)S(1)} %get-tuple-element.19), channel_id=1, source_target_pairs={{0,2},{1,3},{2,0},{3,1},{4,6},{5,7},{6,4},{7,5},{8,10},{9,11},{10,... | collective-permute-start | bytes 2312 | tf_op jit(solution)/shard_map/ppermute | solution.py:54
  150.2 3.9 %collective-permute-start.17 = (f32[1,3,64]{2,1,0:T(4,128)S(1)}, f32[1,3,64]{2,1,0:T(4,128)S(1)}, u32[]{:S(2)}, u32[]{:S(2)}) collective-permute-start(f32[1,3,64]{2,1,0:T(4,128)S(1)} %get-tuple-element.19), channel_id=1, source_target_pairs={{0,3},{1,0},{2,1},{3,2},{4,7},{5,4},{6,5},{7,6},{8,11},{9,8},{10,9... | collective-permute-start | bytes 2312 | tf_op jit(solution)/shard_map/ppermute | solution.py:54
  154.9 6.3 %collective-permute-start.18 = (f32[4,3,64]{2,1,0:T(4,128)S(1)}, f32[4,3,64]{2,1,0:T(4,128)S(1)}, u32[]{:S(2)}, u32[]{:S(2)}) collective-permute-start(f32[4,3,64]{2,1,0:T(4,128)S(1)} %broadcast_select_fusion.4), channel_id=1, source_target_pairs={{0,4},{1,5},{2,6},{3,7},{4,8},{5,9},{6,10},{7,11},{8,12},{9,13},{1... | collective-permute-start | bytes 9224 | tf_op jit(solution)/shard_map/ppermute | solution.py:54
  158.7 4.5 %collective-permute-start.19 = (f32[4,3,64]{2,1,0:T(4,128)S(1)}, f32[4,3,64]{2,1,0:T(4,128)S(1)}, u32[]{:S(2)}, u32[]{:S(2)}) collective-permute-start(f32[4,3,64]{2,1,0:T(4,128)S(1)} %broadcast_select_fusion.4), channel_id=1, source_target_pairs={{0,8},{1,9},{2,10},{3,11},{4,12},{5,13},{6,14},{7,15},{8,0},{9,1},... | collective-permute-start | bytes 9224 | tf_op jit(solution)/shard_map/ppermute | solution.py:54
  159.8 3.7 %collective-permute-start.20 = (f32[4,3,64]{2,1,0:T(4,128)S(1)}, f32[4,3,64]{2,1,0:T(4,128)S(1)}, u32[]{:S(2)}, u32[]{:S(2)}) collective-permute-start(f32[4,3,64]{2,1,0:T(4,128)S(1)} %broadcast_select_fusion.4), channel_id=1, source_target_pairs={{0,12},{1,13},{2,14},{3,15},{4,0},{5,1},{6,2},{7,3},{8,4},{9,5},{1... | collective-permute-start | bytes 9224 | tf_op jit(solution)/shard_map/ppermute | solution.py:54
Sparse Core Ops, SparseCore 0:
  10.3 116.8 all-gather.1

commit v13 on v7

--- a/solution.py
+++ b/solution.py
@@ -158,11 +158,13 @@
     context = context.reshape(token_rows, QUERY_HEADS * HEAD_SIZE).astype(jnp.bfloat16)
 
     scored_context = gather_rows(context.reshape(score_count, stride, -1)[:, stride - 1, :])
-    picked = scored_residual.astype(jnp.float32) + jnp.dot(
-        scored_context, full_proj, preferred_element_type=jnp.float32
-    )
+    both = jnp.dot(
+        jnp.concatenate([scored_context, context], 0), full_proj, preferred_element_type=jnp.float32
+    )
+    scored_total = scored_context.shape[0]
+    picked = scored_residual.astype(jnp.float32) + both[:scored_total]
     normed = normalize(picked, norm_gain)
-    projected = jnp.dot(context, full_proj, preferred_element_type=jnp.float32)
+    projected = both[scored_total:]
     hidden = residual.astype(jnp.float32) + projected
     layer_out = hidden.astype(jnp.bfloat16)
     logits = lax.dot_general(

time: 164 us -> 162 us (0.988)
  matrix products: 23.5 us -> 18.7 us
    dot_general x1, matrix products: 4.52 us -> 1.89 us  [local(): lax.dot_general(normed, head_weight, (((1,), (1,)), ((), ())), preferred_...]
    dot_general x2 -> x1, matrix products: 9.03 us -> 6.8 us  [local(): jnp.dot(jnp.concatenate([scored_context, context], 0), full_proj, preferr...]
  transfers between devices with their start and end apart: 28 -> 28, of which waited for: 10 -> 11; matrix products, arithmetic and copies ran while one was open for 20% -> 19% of each run, Pallas kernels for 0% -> 0%
where the time goes in v13:
time: 162 us; the launch traced here: 161 us
  waiting for transfers between devices  53.9 us (33%)
  starting transfers between devices  49.7 us (31%)
  matrix products  18.7 us (12%)
  between operations  14.6 us (9%)
  local copies, waits for them, and re-layouts  12.4 us (8%)
  other arithmetic  11.9 us (7%)
    ppermute x4, waiting for transfers between devices, across_pair(): return lax.ppermute(value, SEQ, pairs)  27.3 us
    ppermute x18, starting transfers between devices, gather_rows(): received.append(lax.ppermute(data, SEQ, pairs))  21.8 us
    ppermute x2, waiting for transfers between devices, shift_chips(): lax.ppermute(value, SEQ, [(s, s + step) for s in range(count - step)])  15.6 us
    ppermute x3, starting transfers between devices, swap_cores(): return lax.ppermute(value, 'core', [(0, 1), (1, 0)])  11.4 us
    ppermute x18, waiting for transfers between devices, gather_rows(): received.append(lax.ppermute(data, SEQ, pairs))  10.4 us
    ppermute x2, starting transfers between devices, shift_chips(): lax.ppermute(value, SEQ, [(s, s + step) for s in range(count - step)])  8.45 us
    ppermute x4, starting transfers between devices, across_pair(): return lax.ppermute(value, SEQ, pairs)  8.04 us
    dot_general x1, matrix products, local(): jnp.dot(jnp.concatenate([scored_context, context], 0), full_proj, preferr...  6.8 us
  transfers between devices with their start and end apart: 28, of which 11 were waited for; matrix products, arithmetic and copies ran while one was open for 19% of the time, Pallas kernels for 0%

profile of v13, /device:TPU:0, one launch (start us, length us, event | category | flops | bytes accessed | tf_op | source)
XLA Modules:
  0.0 161.1 jit_solution(10229100973929339645)
XLA Ops:
  7.2 0.7 all-gather.2.cloned.1.call-update
  7.9 1.3 copy.16
  9.2 0.7 convert_element_type.43
  10.0 5.0 %collective-permute-start = (bf16[128,2176]{0,1:T(8,128)(2,1)S(1)}, bf16[128,2176]{0,1:T(8,128)(2,1)S(1)}, u32[]{:S(2)}, u32[]{:S(2)}) collective-permute-start(bf16[128,2176]{0,1:T(8,128)(2,1)S(1)} %pad_maximum_fusion.2), channel_id=1, source_target_pairs={{0,4},{1,5},{2,6},{3,7},{4,8},{5,9},{6,10},{7,11},{8,12},{9,13},{1... | collective-permute-start | bytes 1671176 | tf_op jit(solution)/shard_map/ppermute | solution.py:70
  14.9 3.5 %collective-permute-start.5 = (bf16[128,2176]{0,1:T(8,128)(2,1)S(1)}, bf16[128,2176]{0,1:T(8,128)(2,1)S(1)}, u32[]{:S(2)}, u32[]{:S(2)}) collective-permute-start(bf16[128,2176]{0,1:T(8,128)(2,1)S(1)} %pad_maximum_fusion.2), channel_id=1, source_target_pairs={{0,2},{1,3},{4,6},{5,7},{8,10},{9,11},{12,14},{13,15},{16,18},{17,... | collective-permute-start | bytes 1671176 | tf_op jit(solution)/shard_map/ppermute | solution.py:76
  18.4 1.0 slice.77
  19.5 1.7 %collective-permute-start.17 = (bf16[1,4,2688]{2,1,0:T(4,128)(2,1)S(1)}, bf16[1,4,2688]{2,1,0:T(4,128)(2,1)S(1)}, u32[]{:S(2)}, u32[]{:S(2)}) collective-permute-start(bf16[1,4,2688]{2,1,0:T(4,128)(2,1)S(1)} %bitcast.113), channel_id=1, source_target_pairs={{0,3},{1,0},{2,1},{3,2},{4,7},{5,4},{6,5},{7,6},{8,11},{9,8},{10,9... | collective-permute-start | bytes 64520 | tf_op jit(solution)/shard_map/ppermute | solution.py:54
  22.4 0.6 pad_clamp_fusion
  24.2 0.7 broadcast_in_dim.140
  24.8 11.3 %collective-permute-start.8 = (bf16[128,2176]{0,1:T(8,128)(2,1)S(1)}, bf16[128,2176]{0,1:T(8,128)(2,1)S(1)}, u32[]{:S(2)}, u32[]{:S(2)}) collective-permute-start(bf16[128,2176]{0,1:T(8,128)(2,1)S(1)} %pad_maximum_fusion.2), channel_id=1, source_target_pairs={{0,1},{1,0},{2,3},{3,2},{4,5},{5,4},{6,7},{7,6},{8,9},{9,8},{10,11... | collective-permute-start | bytes 1671176 | tf_op jit(solution)/shard_map/ppermute | solution.py:37
  36.1 1.9 %collective-permute-done.16 = bf16[1,4,2688]{2,1,0:T(4,128)(2,1)S(1)} collective-permute-done((bf16[1,4,2688]{2,1,0:T(4,128)(2,1)S(1)}, bf16[1,4,2688]{2,1,0:T(4,128)(2,1)S(1)}, u32[]{:S(2)}, u32[]{:S(2)}) %collective-permute-start.16) | collective-permute-done | bytes 21536 | tf_op jit(solution)/shard_map/ppermute | solution.py:54
  38.3 0.7 gather_fusion.2
  39.1 3.5 %collective-permute-start.1 = (bf16[128,2176]{0,1:T(8,128)(2,1)S(1)}, bf16[128,2176]{0,1:T(8,128)(2,1)S(1)}, u32[]{:S(2)}, u32[]{:S(2)}) collective-permute-start(bf16[128,2176]{0,1:T(8,128)(2,1)S(1)} %collective-permute-done), channel_id=1, source_target_pairs={{0,4},{1,5},{2,6},{3,7},{4,8},{5,9},{6,10},{7,11},{8,12},{9,13},{1... | collective-permute-start | bytes 1671176 | tf_op jit(solution)/shard_map/ppermute | solution.py:70
  42.6 1.3 collective-permute-start.6
  43.9 0.7 broadcast_select_fusion.5
  44.6 1.5 collective-permute-start.18
  46.2 0.8 collective-permute-start.19
  46.9 15.6 %collective-permute-done.1 = bf16[128,2176]{0,1:T(8,128)(2,1)S(1)} collective-permute-done((bf16[128,2176]{0,1:T(8,128)(2,1)S(1)}, bf16[128,2176]{0,1:T(8,128)(2,1)S(1)}, u32[]{:S(2)}, u32[]{:S(2)}) %collective-permute-start.1) | collective-permute-done | bytes 557088 | tf_op jit(solution)/shard_map/ppermute | solution.py:70
  62.5 2.0 %collective-permute-start.2 = (bf16[128,2176]{0,1:T(8,128)(2,1)S(1)}, bf16[128,2176]{0,1:T(8,128)(2,1)S(1)}, u32[]{:S(2)}, u32[]{:S(2)}) collective-permute-start(bf16[128,2176]{0,1:T(8,128)(2,1)S(1)} %collective-permute-done), channel_id=1, source_target_pairs={{0,2},{1,3},{4,6},{5,7},{8,10},{9,11},{12,14},{13,15},{16,18},{17,... | collective-permute-start | bytes 1671176 | tf_op jit(solution)/shard_map/ppermute | solution.py:76
  64.5 1.3 collective-permute-start.3
  66.0 22.9 %collective-permute-done.2 = bf16[128,2176]{0,1:T(8,128)(2,1)S(1)} collective-permute-done((bf16[128,2176]{0,1:T(8,128)(2,1)S(1)}, bf16[128,2176]{0,1:T(8,128)(2,1)S(1)}, u32[]{:S(2)}, u32[]{:S(2)}) %collective-permute-start.2) | collective-permute-done | bytes 557088 | tf_op jit(solution)/shard_map/ppermute | solution.py:76
  88.9 4.3 %collective-permute-done.3 = bf16[128,2176]{0,1:T(8,128)(2,1)S(1)} collective-permute-done((bf16[128,2176]{0,1:T(8,128)(2,1)S(1)}, bf16[128,2176]{0,1:T(8,128)(2,1)S(1)}, u32[]{:S(2)}, u32[]{:S(2)}) %collective-permute-start.3) | collective-permute-done | bytes 557088 | tf_op jit(solution)/shard_map/ppermute | solution.py:76
  93.7 4.8 %collective-permute-start.20 = (bf16[4,4,2688]{2,1,0:T(4,128)(2,1)}, bf16[4,4,2688]{2,1,0:T(4,128)(2,1)}, u32[]{:S(2)}, u32[]{:S(2)}) collective-permute-start(bf16[4,4,2688]{2,1,0:T(4,128)(2,1)} %broadcast_select_fusion.5), channel_id=1, source_target_pairs={{0,12},{1,13},{2,14},{3,15},{4,0},{5,1},{6,2},{7,3},{8,4},{9,5},{1... | collective-permute-start | bytes 258056 | tf_op jit(solution)/shard_map/ppermute | solution.py:54
  100.7 1.9 %constant_dynamic-slice_fusion = (bf16[1152,1024]{0,1:T(8,128)(2,1)S(1)}, bf16[1152,1024]{0,1:T(8,128)(2,1)}) fusion(bf16[1280,2176]{0,1:T(8,128)(2,1)S(1)} %fusion.14, s32[]{:T(128)S(6)} %select_n.241, s32[]{:T(128)S(6)} %add.187), kind=kLoop, calls=%fused_computation.116 | loop fusion | bytes 9437192 | tf_op jit(solution)/shard_map/slice | solution.py:139
  102.6 1.1 compare_and_fusion
  103.7 3.7 %fusion.52 = f32[8,2,128]{2,1,0:T(2,128)S(1)} fusion(pred[128,1152]{0,1:T(8,128)(4,1)S(1)} %compare_and_fusion, bf16[1152,8,128,1]{0,2,3,1:T(8,128)(2,1)S(1)} %bitcast.103, bf16[128,8,2,128]{3,2,1,0:T(2,128)(2,1)S(1)} %reshape.322), kind=kOutput, calls=%fused_computation.125 | convolution fusion | flops 613418112 | bytes 3039232 | tf_op jit(solution)/shard_map/sub | solution.py:153
  107.3 6.3 %fusion.7 = bf16[8,128,2,128]{3,1,2,0:T(8,128)(2,1)S(1)} fusion(bf16[1152,8,128,1]{0,2,3,1:T(8,128)(2,1)} %bitcast.105, f32[8,2,128]{2,1,0:T(2,128)S(1)} %fusion.52, pred[128,1152]{0,1:T(8,128)(4,1)} %copy-done.2, bf16[1152,8,128,1]{0,2,3,1:T(8,128)(2,1)S(1)} %bitcast.104, bf16[128,8,2,128]{3,2,1,0:T(2,128)(2,1)S(1)} %reshape.322), kind=kOutput, calls=%fused_computation.17 | convolution fusion | flops 1220021376 | bytes 5922816 | tf_op jit(solution)/shard_map/hgqk,khd->qhgd/dot_general | solution.py:155
  115.1 1.4 collective-permute-start.11
  116.5 1.4 pad_maximum_fusion.3
  117.9 1.0 gather_fusion.3
  119.0 0.7 gather_fusion
  120.0 2.7 %collective-permute-start.13 = (bf16[4,4,2048]{2,1,0:T(4,128)(2,1)S(1)}, bf16[4,4,2048]{2,1,0:T(4,128)(2,1)S(1)}, u32[]{:S(2)}, u32[]{:S(2)}) collective-permute-start(bf16[4,4,2048]{2,1,0:T(4,128)(2,1)S(1)} %broadcast_select_fusion.6), channel_id=1, source_target_pairs={{0,8},{1,9},{2,10},{3,11},{4,12},{5,13},{6,14},{7,15},{8,0},{9,1},... | collective-permute-start | bytes 196616 | tf_op jit(solution)/shard_map/ppermute | solution.py:54
  122.7 1.3 collective-permute-start.14
  124.1 2.6 %collective-permute-done.12 = bf16[4,4,2048]{2,1,0:T(4,128)(2,1)S(1)} collective-permute-done((bf16[4,4,2048]{2,1,0:T(4,128)(2,1)S(1)}, bf16[4,4,2048]{2,1,0:T(4,128)(2,1)S(1)}, u32[]{:S(2)}, u32[]{:S(2)}) %collective-permute-start.12) | collective-permute-done | bytes 65568 | tf_op jit(solution)/shard_map/ppermute | solution.py:54
  126.7 1.8 %collective-permute-done.13 = bf16[4,4,2048]{2,1,0:T(4,128)(2,1)S(1)} collective-permute-done((bf16[4,4,2048]{2,1,0:T(4,128)(2,1)S(1)}, bf16[4,4,2048]{2,1,0:T(4,128)(2,1)S(1)}, u32[]{:S(2)}, u32[]{:S(2)}) %collective-permute-start.13) | collective-permute-done | bytes 65568 | tf_op jit(solution)/shard_map/ppermute | solution.py:54
  128.8 0.9 gather_fusion.1
  130.2 6.8 %fusion.15 = f32[192,2688]{1,0:T(8,128)S(1)} fusion(bf16[2048,2688]{1,0:T(8,128)(2,1)} %all-gather.2.cloned.1.call-done, bf16[128,2048]{0,1:T(8,128)(2,1)S(1)} %bitcast.109, bf16[64,2048]{0,1:T(8,128)(2,1)S(1)} %copy.21), kind=kOutput, calls=%fused_computation.31 | convolution fusion | flops 2115502080 | bytes 13860864 | tf_op jit(solution)/shard_map/dot_general | solution.py:161
  137.3 1.9 %fusion.55 = (f32[64]{0:T(128)S(1)}, f32[64,1024]{1,0:T(8,128)S(1)}) fusion(bf16[1024,2688]{1,0:T(8,128)(2,1)S(1)} %bitcast.100, f32[192,2688]{1,0:T(8,128)S(1)} %fusion.15, f32[2688]{0:T(1024)S(1)} %copy-done.3, f32[64]{0:T(128)S(1)} %add_rsqrt_fusion, bf16[64,2688]{1,0:T(8,128)(2,1)S(1)} %gather.51, pred[64]{0:T(512)(128)(4,1)S(1)} %broadcast_in_dim.123), kind=kOutput, calls=%fused_computation.126 | convolution fusion | flops 353419200 | bytes 6812928 | tf_op jit(solution)/shard_map/dot_general | solution.py:170
  139.7 1.3 collective-permute-start.22
  141.0 1.4 collective-permute-start.23
  142.4 1.0 fusion.6
  143.7 0.7 gather_fusion.4
  144.5 1.5 collective-permute-start.24
  146.0 2.3 %collective-permute-start.25 = (f32[4,3,64]{2,1,0:T(4,128)S(1)}, f32[4,3,64]{2,1,0:T(4,128)S(1)}, u32[]{:S(2)}, u32[]{:S(2)}) collective-permute-start(f32[4,3,64]{2,1,0:T(4,128)S(1)} %broadcast_select_fusion.7), channel_id=1, source_target_pairs={{0,8},{1,9},{2,10},{3,11},{4,12},{5,13},{6,14},{7,15},{8,0},{9,1},... | collective-permute-start | bytes 9224 | tf_op jit(solution)/shard_map/ppermute | solution.py:54
  148.5 1.5 collective-permute-done.24
  150.5 1.4 collective-permute-done.26
  152.0 0.7 gather_fusion.5
  152.9 0.8 broadcast_subtract_fusion
  (111 shorter events, 10.7 us)
Async XLA Ops:
  7.2 15.8 %copy-start.9 = (s32[64]{0:T(128)S(1)}, s32[64]{0:T(128)}, u32[]{:S(2)}) copy-start(s32[64]{0:T(128)} %param.15) | copy-start | bytes 772
  7.2 16.4 %copy-start.1 = (bf16[128,2048]{1,0:T(8,128)(2,1)S(1)}, bf16[128,2048]{1,0:T(8,128)(2,1)}, u32[]{:S(2)}) copy-start(bf16[128,2048]{1,0:T(8,128)(2,1)} %param.8) | copy-start | bytes 1572868
  7.2 123.0 %all-gather.2.cloned.1.call-start = ((), (), s32[]{:S(2)}) async-start(), calls=%async_computation | async-start | bytes 11698176 | tf_op jit(solution)/shard_map/all_gather | solution.py:121
  10.0 29.1 %collective-permute-start = (bf16[128,2176]{0,1:T(8,128)(2,1)S(1)}, bf16[128,2176]{0,1:T(8,128)(2,1)S(1)}, u32[]{:S(2)}, u32[]{:S(2)}) collective-permute-start(bf16[128,2176]{0,1:T(8,128)(2,1)S(1)} %pad_maximum_fusion.2), channel_id=1, source_target_pairs={{0,4},{1,5},{2,6},{3,7},{4,8},{5,9},{6,10},{7,11},{8,12},{9,13},{1... | collective-permute-start | bytes 1671176 | tf_op jit(solution)/shard_map/ppermute | solution.py:70
  14.9 31.2 %collective-permute-start.5 = (bf16[128,2176]{0,1:T(8,128)(2,1)S(1)}, bf16[128,2176]{0,1:T(8,128)(2,1)S(1)}, u32[]{:S(2)}, u32[]{:S(2)}) collective-permute-start(bf16[128,2176]{0,1:T(8,128)(2,1)S(1)} %pad_maximum_fusion.2), channel_id=1, source_target_pairs={{0,2},{1,3},{4,6},{5,7},{8,10},{9,11},{12,14},{13,15},{16,18},{17,... | collective-permute-start | bytes 1671176 | tf_op jit(solution)/shard_map/ppermute | solution.py:76
  19.4 5.5 %collective-permute-start.15 = (bf16[1,4,2688]{2,1,0:T(4,128)(2,1)S(1)}, bf16[1,4,2688]{2,1,0:T(4,128)(2,1)S(1)}, u32[]{:S(2)}, u32[]{:S(2)}) collective-permute-start(bf16[1,4,2688]{2,1,0:T(4,128)(2,1)S(1)} %bitcast.111), channel_id=1, source_target_pairs={{0,1},{1,2},{2,3},{3,0},{4,5},{5,6},{6,7},{7,4},{8,9},{9,10},{10,1... | collective-permute-start | bytes 64520 | tf_op jit(solution)/shard_map/ppermute | solution.py:54
  19.4 18.6 %collective-permute-start.16 = (bf16[1,4,2688]{2,1,0:T(4,128)(2,1)S(1)}, bf16[1,4,2688]{2,1,0:T(4,128)(2,1)S(1)}, u32[]{:S(2)}, u32[]{:S(2)}) collective-permute-start(bf16[1,4,2688]{2,1,0:T(4,128)(2,1)S(1)} %bitcast.112), channel_id=1, source_target_pairs={{0,2},{1,3},{2,0},{3,1},{4,6},{5,7},{6,4},{7,5},{8,10},{9,11},{10,... | collective-permute-start | bytes 64520 | tf_op jit(solution)/shard_map/ppermute | solution.py:54
  19.5 18.7 %collective-permute-start.17 = (bf16[1,4,2688]{2,1,0:T(4,128)(2,1)S(1)}, bf16[1,4,2688]{2,1,0:T(4,128)(2,1)S(1)}, u32[]{:S(2)}, u32[]{:S(2)}) collective-permute-start(bf16[1,4,2688]{2,1,0:T(4,128)(2,1)S(1)} %bitcast.113), channel_id=1, source_target_pairs={{0,3},{1,0},{2,1},{3,2},{4,7},{5,4},{6,5},{7,6},{8,11},{9,8},{10,9... | collective-permute-start | bytes 64520 | tf_op jit(solution)/shard_map/ppermute | solution.py:54
  24.8 75.3 %collective-permute-start.8 = (bf16[128,2176]{0,1:T(8,128)(2,1)S(1)}, bf16[128,2176]{0,1:T(8,128)(2,1)S(1)}, u32[]{:S(2)}, u32[]{:S(2)}) collective-permute-start(bf16[128,2176]{0,1:T(8,128)(2,1)S(1)} %pad_maximum_fusion.2), channel_id=1, source_target_pairs={{0,1},{1,0},{2,3},{3,2},{4,5},{5,4},{6,7},{7,6},{8,9},{9,8},{10,11... | collective-permute-start | bytes 1671176 | tf_op jit(solution)/shard_map/ppermute | solution.py:37
  39.1 23.4 %collective-permute-start.1 = (bf16[128,2176]{0,1:T(8,128)(2,1)S(1)}, bf16[128,2176]{0,1:T(8,128)(2,1)S(1)}, u32[]{:S(2)}, u32[]{:S(2)}) collective-permute-start(bf16[128,2176]{0,1:T(8,128)(2,1)S(1)} %collective-permute-done), channel_id=1, source_target_pairs={{0,4},{1,5},{2,6},{3,7},{4,8},{5,9},{6,10},{7,11},{8,12},{9,13},{1... | collective-permute-start | bytes 1671176 | tf_op jit(solution)/shard_map/ppermute | solution.py:70
  42.6 21.9 %collective-permute-start.6 = (bf16[128,2176]{0,1:T(8,128)(2,1)S(1)}, bf16[128,2176]{0,1:T(8,128)(2,1)S(1)}, u32[]{:S(2)}, u32[]{:S(2)}) collective-permute-start(bf16[128,2176]{0,1:T(8,128)(2,1)S(1)} %collective-permute-done), channel_id=1, source_target_pairs={{2,0},{3,1},{6,4},{7,5},{10,8},{11,9},{14,12},{15,13},{18,16},{19,... | collective-permute-start | bytes 1671176 | tf_op jit(solution)/shard_map/ppermute | solution.py:76
  44.6 70.4 %collective-permute-start.18 = (bf16[4,4,2688]{2,1,0:T(4,128)(2,1)}, bf16[4,4,2688]{2,1,0:T(4,128)(2,1)}, u32[]{:S(2)}, u32[]{:S(2)}) collective-permute-start(bf16[4,4,2688]{2,1,0:T(4,128)(2,1)} %broadcast_select_fusion.5), channel_id=1, source_target_pairs={{0,4},{1,5},{2,6},{3,7},{4,8},{5,9},{6,10},{7,11},{8,12},{9,13},{1... | collective-permute-start | bytes 258056 | tf_op jit(solution)/shard_map/ppermute | solution.py:54
  46.2 70.3 %collective-permute-start.19 = (bf16[4,4,2688]{2,1,0:T(4,128)(2,1)}, bf16[4,4,2688]{2,1,0:T(4,128)(2,1)}, u32[]{:S(2)}, u32[]{:S(2)}) collective-permute-start(bf16[4,4,2688]{2,1,0:T(4,128)(2,1)} %broadcast_select_fusion.5), channel_id=1, source_target_pairs={{0,8},{1,9},{2,10},{3,11},{4,12},{5,13},{6,14},{7,15},{8,0},{9,1},... | collective-permute-start | bytes 258056 | tf_op jit(solution)/shard_map/ppermute | solution.py:54
  62.5 26.4 %collective-permute-start.2 = (bf16[128,2176]{0,1:T(8,128)(2,1)S(1)}, bf16[128,2176]{0,1:T(8,128)(2,1)S(1)}, u32[]{:S(2)}, u32[]{:S(2)}) collective-permute-start(bf16[128,2176]{0,1:T(8,128)(2,1)S(1)} %collective-permute-done), channel_id=1, source_target_pairs={{0,2},{1,3},{4,6},{5,7},{8,10},{9,11},{12,14},{13,15},{16,18},{17,... | collective-permute-start | bytes 1671176 | tf_op jit(solution)/shard_map/ppermute | solution.py:76
  64.5 28.8 %collective-permute-start.3 = (bf16[128,2176]{0,1:T(8,128)(2,1)S(1)}, bf16[128,2176]{0,1:T(8,128)(2,1)S(1)}, u32[]{:S(2)}, u32[]{:S(2)}) collective-permute-start(bf16[128,2176]{0,1:T(8,128)(2,1)S(1)} %collective-permute-done.1), channel_id=1, source_target_pairs={{2,0},{3,1},{6,4},{7,5},{10,8},{11,9},{14,12},{15,13},{18,16},{19,... | collective-permute-start | bytes 1671176 | tf_op jit(solution)/shard_map/ppermute | solution.py:76
  88.9 4.7 %collective-permute-start.7 = (bf16[2,128,2176]{1,2,0:T(8,128)(2,1)S(1)}, bf16[2,128,2176]{1,2,0:T(8,128)(2,1)S(1)}, u32[]{:S(2)}, u32[]{:S(2)}) collective-permute-start(bf16[2,128,2176]{1,2,0:T(8,128)(2,1)S(1)} %pad_maximum_fusion.1), channel_id=1, source_target_pairs={{0,1},{1,0},{2,3},{3,2},{4,5},{5,4},{6,7},{7,6},{8,9},{9,8},{10,11... | collective-permute-start | bytes 3342344 | tf_op jit(solution)/shard_map/ppermute | solution.py:37
  93.5 5.1 %collective-permute-start.4 = (bf16[2,128,2176]{1,2,0:T(8,128)(2,1)S(1)}, bf16[2,128,2176]{1,2,0:T(8,128)(2,1)S(1)}, u32[]{:S(2)}, u32[]{:S(2)}) collective-permute-start(bf16[2,128,2176]{1,2,0:T(8,128)(2,1)S(1)} %pad_maximum_fusion), channel_id=1, source_target_pairs={{0,1},{1,0},{2,3},{3,2},{4,5},{5,4},{6,7},{7,6},{8,9},{9,8},{10,11... | collective-permute-start | bytes 3342344 | tf_op jit(solution)/shard_map/ppermute | solution.py:37
  93.7 22.8 %collective-permute-start.20 = (bf16[4,4,2688]{2,1,0:T(4,128)(2,1)}, bf16[4,4,2688]{2,1,0:T(4,128)(2,1)}, u32[]{:S(2)}, u32[]{:S(2)}) collective-permute-start(bf16[4,4,2688]{2,1,0:T(4,128)(2,1)} %broadcast_select_fusion.5), channel_id=1, source_target_pairs={{0,12},{1,13},{2,14},{3,15},{4,0},{5,1},{6,2},{7,3},{8,4},{9,5},{1... | collective-permute-start | bytes 258056 | tf_op jit(solution)/shard_map/ppermute | solution.py:54
  100.7 1.9 %copy-start.4 = (s32[128]{0:T(128)S(1)}, s32[128]{0:T(128)}, u32[]{:S(2)}) copy-start(s32[128]{0:T(128)} %param.10) | copy-start | bytes 1540
  100.7 1.9 %copy-start.7 = (s32[128]{0:T(128)S(1)}, s32[128]{0:T(128)}, u32[]{:S(2)}) copy-start(s32[128]{0:T(128)} %get-tuple-element.24) | copy-start | bytes 1540
  100.7 1.9 %copy-start.8 = (s32[128]{0:T(128)S(1)}, s32[128]{0:T(128)}, u32[]{:S(2)}) copy-start(s32[128]{0:T(128)} %get-tuple-element.25) | copy-start | bytes 1540
  103.7 3.7 %copy-start.2 = (pred[128,1152]{0,1:T(8,128)(4,1)}, pred[128,1152]{0,1:T(8,128)(4,1)S(1)}, u32[]{:S(2)}) copy-start(pred[128,1152]{0,1:T(8,128)(4,1)S(1)} %compare_and_fusion) | copy-start | bytes 442372
  114.6 4.3 %collective-permute-start.9 = (bf16[1,4,2048]{2,1,0:T(4,128)(2,1)S(1)}, bf16[1,4,2048]{2,1,0:T(4,128)(2,1)S(1)}, u32[]{:S(2)}, u32[]{:S(2)}) collective-permute-start(bf16[1,4,2048]{2,1,0:T(4,128)(2,1)S(1)} %bitcast.117), channel_id=1, source_target_pairs={{0,1},{1,2},{2,3},{3,0},{4,5},{5,6},{6,7},{7,4},{8,9},{9,10},{10,1... | collective-permute-start | bytes 49160 | tf_op jit(solution)/shard_map/ppermute | solution.py:54
  114.9 4.0 %collective-permute-start.10 = (bf16[1,4,2048]{2,1,0:T(4,128)(2,1)S(1)}, bf16[1,4,2048]{2,1,0:T(4,128)(2,1)S(1)}, u32[]{:S(2)}, u32[]{:S(2)}) collective-permute-start(bf16[1,4,2048]{2,1,0:T(4,128)(2,1)S(1)} %bitcast.118), channel_id=1, source_target_pairs={{0,2},{1,3},{2,0},{3,1},{4,6},{5,7},{6,4},{7,5},{8,10},{9,11},{10,... | collective-permute-start | bytes 49160 | tf_op jit(solution)/shard_map/ppermute | solution.py:54
  115.1 3.9 %collective-permute-start.11 = (bf16[1,4,2048]{2,1,0:T(4,128)(2,1)S(1)}, bf16[1,4,2048]{2,1,0:T(4,128)(2,1)S(1)}, u32[]{:S(2)}, u32[]{:S(2)}) collective-permute-start(bf16[1,4,2048]{2,1,0:T(4,128)(2,1)S(1)} %bitcast.119), channel_id=1, source_target_pairs={{0,3},{1,0},{2,1},{3,2},{4,7},{5,4},{6,5},{7,6},{8,11},{9,8},{10,9... | collective-permute-start | bytes 49160 | tf_op jit(solution)/shard_map/ppermute | solution.py:54
  119.9 6.8 %collective-permute-start.12 = (bf16[4,4,2048]{2,1,0:T(4,128)(2,1)S(1)}, bf16[4,4,2048]{2,1,0:T(4,128)(2,1)S(1)}, u32[]{:S(2)}, u32[]{:S(2)}) collective-permute-start(bf16[4,4,2048]{2,1,0:T(4,128)(2,1)S(1)} %broadcast_select_fusion.6), channel_id=1, source_target_pairs={{0,4},{1,5},{2,6},{3,7},{4,8},{5,9},{6,10},{7,11},{8,12},{9,13},{1... | collective-permute-start | bytes 196616 | tf_op jit(solution)/shard_map/ppermute | solution.py:54
  120.0 8.5 %collective-permute-start.13 = (bf16[4,4,2048]{2,1,0:T(4,128)(2,1)S(1)}, bf16[4,4,2048]{2,1,0:T(4,128)(2,1)S(1)}, u32[]{:S(2)}, u32[]{:S(2)}) collective-permute-start(bf16[4,4,2048]{2,1,0:T(4,128)(2,1)S(1)} %broadcast_select_fusion.6), channel_id=1, source_target_pairs={{0,8},{1,9},{2,10},{3,11},{4,12},{5,13},{6,14},{7,15},{8,0},{9,1},... | collective-permute-start | bytes 196616 | tf_op jit(solution)/shard_map/ppermute | solution.py:54
  122.7 5.8 %collective-permute-start.14 = (bf16[4,4,2048]{2,1,0:T(4,128)(2,1)S(1)}, bf16[4,4,2048]{2,1,0:T(4,128)(2,1)S(1)}, u32[]{:S(2)}, u32[]{:S(2)}) collective-permute-start(bf16[4,4,2048]{2,1,0:T(4,128)(2,1)S(1)} %broadcast_select_fusion.6), channel_id=1, source_target_pairs={{0,12},{1,13},{2,14},{3,15},{4,0},{5,1},{6,2},{7,3},{8,4},{9,5},{1... | collective-permute-start | bytes 196616 | tf_op jit(solution)/shard_map/ppermute | solution.py:54
  129.7 7.5 %slice-start = ((s8[5505024]{0:T(1024)(128)(4,1)}), s8[1310720]{0:T(1024)(128)(4,1)S(1)}, s32[]{:S(2)}) async-start(s8[5505024]{0:T(1024)(128)(4,1)} %bitcast.99), calls=%async_computation.1 | async-start | bytes 2621440
  130.1 7.1 %slice-start.1 = ((s8[5505024]{0:T(1024)(128)(4,1)}), s8[4194304]{0:T(1024)(128)(4,1)S(1)}, s32[]{:S(2)}) async-start(s8[5505024]{0:T(1024)(128)(4,1)} %bitcast.99), calls=%async_computation.2 | async-start | bytes 8388608
  130.2 7.1 %copy-start.3 = (f32[2688]{0:T(1024)S(1)}, f32[2688]{0:T(1024)}, u32[]{:S(2)}) copy-start(f32[2688]{0:T(1024)} %param.12) | copy-start | bytes 32260
  137.3 1.9 %copy-start.6 = (s32[64]{0:T(128)S(1)}, s32[64]{0:T(128)}, u32[]{:S(2)}) copy-start(s32[64]{0:T(128)} %broadcast_subtract_fusion.1) | copy-start | bytes 772
  137.3 5.1 %copy-start = (bf16[128,2688]{1,0:T(8,128)(2,1)S(1)}, bf16[128,2688]{1,0:T(8,128)(2,1)}, u32[]{:S(2)}) copy-start(bf16[128,2688]{1,0:T(8,128)(2,1)} %param.11) | copy-start | bytes 2064388
  139.2 13.5 %copy-start.5 = (pred[16]{0:T(512)(128)(4,1)S(1)}, pred[16]{0:T(512)(128)(4,1)}, u32[]{:S(2)}) copy-start(pred[16]{0:T(512)(128)(4,1)} %broadcast_in_dim.140) | copy-start | bytes 52
  139.5 3.9 %collective-permute-start.21 = (f32[1,3,64]{2,1,0:T(4,128)S(1)}, f32[1,3,64]{2,1,0:T(4,128)S(1)}, u32[]{:S(2)}, u32[]{:S(2)}) collective-permute-start(f32[1,3,64]{2,1,0:T(4,128)S(1)} %get-tuple-element.21), channel_id=1, source_target_pairs={{0,1},{1,2},{2,3},{3,0},{4,5},{5,6},{6,7},{7,4},{8,9},{9,10},{10,1... | collective-permute-start | bytes 2312 | tf_op jit(solution)/shard_map/ppermute | solution.py:54
  139.7 3.7 %collective-permute-start.22 = (f32[1,3,64]{2,1,0:T(4,128)S(1)}, f32[1,3,64]{2,1,0:T(4,128)S(1)}, u32[]{:S(2)}, u32[]{:S(2)}) collective-permute-start(f32[1,3,64]{2,1,0:T(4,128)S(1)} %get-tuple-element.21), channel_id=1, source_target_pairs={{0,2},{1,3},{2,0},{3,1},{4,6},{5,7},{6,4},{7,5},{8,10},{9,11},{10,... | collective-permute-start | bytes 2312 | tf_op jit(solution)/shard_map/ppermute | solution.py:54
  141.0 2.7 %collective-permute-start.23 = (f32[1,3,64]{2,1,0:T(4,128)S(1)}, f32[1,3,64]{2,1,0:T(4,128)S(1)}, u32[]{:S(2)}, u32[]{:S(2)}) collective-permute-start(f32[1,3,64]{2,1,0:T(4,128)S(1)} %get-tuple-element.21), channel_id=1, source_target_pairs={{0,3},{1,0},{2,1},{3,2},{4,7},{5,4},{6,5},{7,6},{8,11},{9,8},{10,9... | collective-permute-start | bytes 2312 | tf_op jit(solution)/shard_map/ppermute | solution.py:54
  144.5 5.5 %collective-permute-start.24 = (f32[4,3,64]{2,1,0:T(4,128)S(1)}, f32[4,3,64]{2,1,0:T(4,128)S(1)}, u32[]{:S(2)}, u32[]{:S(2)}) collective-permute-start(f32[4,3,64]{2,1,0:T(4,128)S(1)} %broadcast_select_fusion.7), channel_id=1, source_target_pairs={{0,4},{1,5},{2,6},{3,7},{4,8},{5,9},{6,10},{7,11},{8,12},{9,13},{1... | collective-permute-start | bytes 9224 | tf_op jit(solution)/shard_map/ppermute | solution.py:54
  146.0 4.6 %collective-permute-start.25 = (f32[4,3,64]{2,1,0:T(4,128)S(1)}, f32[4,3,64]{2,1,0:T(4,128)S(1)}, u32[]{:S(2)}, u32[]{:S(2)}) collective-permute-start(f32[4,3,64]{2,1,0:T(4,128)S(1)} %broadcast_select_fusion.7), channel_id=1, source_target_pairs={{0,8},{1,9},{2,10},{3,11},{4,12},{5,13},{6,14},{7,15},{8,0},{9,1},... | collective-permute-start | bytes 9224 | tf_op jit(solution)/shard_map/ppermute | solution.py:54
  148.3 3.7 %collective-permute-start.26 = (f32[4,3,64]{2,1,0:T(4,128)S(1)}, f32[4,3,64]{2,1,0:T(4,128)S(1)}, u32[]{:S(2)}, u32[]{:S(2)}) collective-permute-start(f32[4,3,64]{2,1,0:T(4,128)S(1)} %broadcast_select_fusion.7), channel_id=1, source_target_pairs={{0,12},{1,13},{2,14},{3,15},{4,0},{5,1},{6,2},{7,3},{8,4},{9,5},{1... | collective-permute-start | bytes 9224 | tf_op jit(solution)/shard_map/ppermute | solution.py:54
Sparse Core Ops, SparseCore 0:
  10.3 114.2 all-gather.1

commit v14 on v13

--- a/solution.py
+++ b/solution.py
@@ -94,10 +94,7 @@
     for mine, theirs in ((back4, far[1]), (back3, far[0]), (back2, near[1]), (back1, near[0]), (own, partner_own)):
         pieces.append(in_core_order(mine, theirs, first_core))
     sequence = jnp.concatenate(pieces, 0)
-    token_rows = own.shape[0]
-    core = lax.axis_index("core")
-    window = lax.dynamic_slice_in_dim(sequence, core * token_rows, (blocks + 1) * token_rows, 0)
-    return window[:, :kv_width], window[:, kv_width].astype(jnp.int32)
+    return sequence[:, :kv_width], sequence[:, kv_width].astype(jnp.int32)
 
 
 def normalize(hidden, norm_gain):
@@ -128,7 +125,7 @@
     key_value_pair, key_seg = halo_window(own, kv_width, blocks, first_core)
     count_of_keys = key_value_pair.shape[0]
     query_pos = first_row + jnp.arange(token_rows, dtype=jnp.int32)
-    key_pos = first_row - blocks * token_rows + jnp.arange(count_of_keys, dtype=jnp.int32)
+    key_pos = (lax.axis_index("chip") * CORES - blocks) * token_rows + jnp.arange(count_of_keys, dtype=jnp.int32)
     allowed = (segment_ids[:, None] == key_seg[None, :]) & (key_pos[None, :] >= 0)
     allowed = (
         allowed

time: 162 us -> 162 us (level)
  no operation moved by 1% of the time
where the time goes in v14:
time: 162 us
  waiting for transfers between devices  53.9 us (33%)
  starting transfers between devices  50.4 us (31%)
  matrix products  19.9 us (12%)
  between operations  14.6 us (9%)
  local copies, waits for them, and re-layouts  12 us (7%)
  other arithmetic  11.2 us (7%)
    ppermute x4, waiting for transfers between devices, across_pair(): return lax.ppermute(value, SEQ, pairs)  27.3 us
    ppermute x18, starting transfers between devices, gather_rows(): received.append(lax.ppermute(data, SEQ, pairs))  21.9 us
    ppermute x2, waiting for transfers between devices, shift_chips(): lax.ppermute(value, SEQ, [(s, s + step) for s in range(count - step)])  15.6 us
    ppermute x3, starting transfers between devices, swap_cores(): return lax.ppermute(value, 'core', [(0, 1), (1, 0)])  11.9 us
    ppermute x18, waiting for transfers between devices, gather_rows(): received.append(lax.ppermute(data, SEQ, pairs))  10.3 us
    ppermute x2, starting transfers between devices, shift_chips(): lax.ppermute(value, SEQ, [(s, s + step) for s in range(count - step)])  8.45 us
    ppermute x4, starting transfers between devices, across_pair(): return lax.ppermute(value, SEQ, pairs)  8.04 us
    dot_general x1, matrix products, local(): jnp.einsum('hgqk,khd->qhgd', weights, heads_for_values, preferred_element...  7.21 us
  transfers between devices with their start and end apart: 28, of which 11 were waited for; matrix products, arithmetic and copies ran while one was open for 19% of the time, Pallas kernels for 0%

profile of v14, /device:TPU:0, one launch (start us, length us, event | category | flops | bytes accessed | tf_op | source)
XLA Modules:
  0.0 162.0 jit_solution(7764582298259689151)
XLA Ops:
  7.2 0.7 all-gather.2.cloned.1.call-update
  7.9 1.3 copy.16
  9.2 0.7 convert_element_type.43
  10.0 5.0 %collective-permute-start = (bf16[128,2176]{0,1:T(8,128)(2,1)S(1)}, bf16[128,2176]{0,1:T(8,128)(2,1)S(1)}, u32[]{:S(2)}, u32[]{:S(2)}) collective-permute-start(bf16[128,2176]{0,1:T(8,128)(2,1)S(1)} %pad_maximum_fusion.2), channel_id=1, source_target_pairs={{0,4},{1,5},{2,6},{3,7},{4,8},{5,9},{6,10},{7,11},{8,12},{9,13},{1... | collective-permute-start | bytes 1671176 | tf_op jit(solution)/shard_map/ppermute | solution.py:70
  14.9 3.5 %collective-permute-start.5 = (bf16[128,2176]{0,1:T(8,128)(2,1)S(1)}, bf16[128,2176]{0,1:T(8,128)(2,1)S(1)}, u32[]{:S(2)}, u32[]{:S(2)}) collective-permute-start(bf16[128,2176]{0,1:T(8,128)(2,1)S(1)} %pad_maximum_fusion.2), channel_id=1, source_target_pairs={{0,2},{1,3},{4,6},{5,7},{8,10},{9,11},{12,14},{13,15},{16,18},{17,... | collective-permute-start | bytes 1671176 | tf_op jit(solution)/shard_map/ppermute | solution.py:76
  18.4 1.0 slice.80
  19.5 1.7 %collective-permute-start.17 = (bf16[1,4,2688]{2,1,0:T(4,128)(2,1)S(1)}, bf16[1,4,2688]{2,1,0:T(4,128)(2,1)S(1)}, u32[]{:S(2)}, u32[]{:S(2)}) collective-permute-start(bf16[1,4,2688]{2,1,0:T(4,128)(2,1)S(1)} %bitcast.113), channel_id=1, source_target_pairs={{0,3},{1,0},{2,1},{3,2},{4,7},{5,4},{6,5},{7,6},{8,11},{9,8},{10,9... | collective-permute-start | bytes 64520 | tf_op jit(solution)/shard_map/ppermute | solution.py:54
  21.8 0.6 pad_clamp_fusion.1
  23.7 0.6 broadcast_in_dim.140
  24.3 11.9 %collective-permute-start.8 = (bf16[128,2176]{0,1:T(8,128)(2,1)S(1)}, bf16[128,2176]{0,1:T(8,128)(2,1)S(1)}, u32[]{:S(2)}, u32[]{:S(2)}) collective-permute-start(bf16[128,2176]{0,1:T(8,128)(2,1)S(1)} %pad_maximum_fusion.2), channel_id=1, source_target_pairs={{0,1},{1,0},{2,3},{3,2},{4,5},{5,4},{6,7},{7,6},{8,9},{9,8},{10,11... | collective-permute-start | bytes 1671176 | tf_op jit(solution)/shard_map/ppermute | solution.py:37
  36.1 1.9 %collective-permute-done.16 = bf16[1,4,2688]{2,1,0:T(4,128)(2,1)S(1)} collective-permute-done((bf16[1,4,2688]{2,1,0:T(4,128)(2,1)S(1)}, bf16[1,4,2688]{2,1,0:T(4,128)(2,1)S(1)}, u32[]{:S(2)}, u32[]{:S(2)}) %collective-permute-start.16) | collective-permute-done | bytes 21536 | tf_op jit(solution)/shard_map/ppermute | solution.py:54
  38.3 0.7 gather_fusion.2
  39.1 3.5 %collective-permute-start.1 = (bf16[128,2176]{0,1:T(8,128)(2,1)S(1)}, bf16[128,2176]{0,1:T(8,128)(2,1)S(1)}, u32[]{:S(2)}, u32[]{:S(2)}) collective-permute-start(bf16[128,2176]{0,1:T(8,128)(2,1)S(1)} %collective-permute-done), channel_id=1, source_target_pairs={{0,4},{1,5},{2,6},{3,7},{4,8},{5,9},{6,10},{7,11},{8,12},{9,13},{1... | collective-permute-start | bytes 1671176 | tf_op jit(solution)/shard_map/ppermute | solution.py:70
  42.6 1.3 collective-permute-start.6
  43.9 0.7 broadcast_select_fusion.5
  44.6 1.5 collective-permute-start.18
  46.1 0.8 collective-permute-start.19
  46.9 15.6 %collective-permute-done.1 = bf16[128,2176]{0,1:T(8,128)(2,1)S(1)} collective-permute-done((bf16[128,2176]{0,1:T(8,128)(2,1)S(1)}, bf16[128,2176]{0,1:T(8,128)(2,1)S(1)}, u32[]{:S(2)}, u32[]{:S(2)}) %collective-permute-start.1) | collective-permute-done | bytes 557088 | tf_op jit(solution)/shard_map/ppermute | solution.py:70
  62.5 2.0 %collective-permute-start.2 = (bf16[128,2176]{0,1:T(8,128)(2,1)S(1)}, bf16[128,2176]{0,1:T(8,128)(2,1)S(1)}, u32[]{:S(2)}, u32[]{:S(2)}) collective-permute-start(bf16[128,2176]{0,1:T(8,128)(2,1)S(1)} %collective-permute-done), channel_id=1, source_target_pairs={{0,2},{1,3},{4,6},{5,7},{8,10},{9,11},{12,14},{13,15},{16,18},{17,... | collective-permute-start | bytes 1671176 | tf_op jit(solution)/shard_map/ppermute | solution.py:76
  64.5 1.3 collective-permute-start.3
  66.0 22.9 %collective-permute-done.2 = bf16[128,2176]{0,1:T(8,128)(2,1)S(1)} collective-permute-done((bf16[128,2176]{0,1:T(8,128)(2,1)S(1)}, bf16[128,2176]{0,1:T(8,128)(2,1)S(1)}, u32[]{:S(2)}, u32[]{:S(2)}) %collective-permute-start.2) | collective-permute-done | bytes 557088 | tf_op jit(solution)/shard_map/ppermute | solution.py:76
  88.9 4.3 %collective-permute-done.3 = bf16[128,2176]{0,1:T(8,128)(2,1)S(1)} collective-permute-done((bf16[128,2176]{0,1:T(8,128)(2,1)S(1)}, bf16[128,2176]{0,1:T(8,128)(2,1)S(1)}, u32[]{:S(2)}, u32[]{:S(2)}) %collective-permute-start.3) | collective-permute-done | bytes 557088 | tf_op jit(solution)/shard_map/ppermute | solution.py:76
  93.7 4.8 %collective-permute-start.20 = (bf16[4,4,2688]{2,1,0:T(4,128)(2,1)}, bf16[4,4,2688]{2,1,0:T(4,128)(2,1)}, u32[]{:S(2)}, u32[]{:S(2)}) collective-permute-start(bf16[4,4,2688]{2,1,0:T(4,128)(2,1)} %broadcast_select_fusion.5), channel_id=1, source_target_pairs={{0,12},{1,13},{2,14},{3,15},{4,0},{5,1},{6,2},{7,3},{8,4},{9,5},{1... | collective-permute-start | bytes 258056 | tf_op jit(solution)/shard_map/ppermute | solution.py:54
  100.7 1.1 compare_and_fusion
  101.8 2.0 %fusion.51 = (bf16[1280,1024]{0,1:T(8,128)(2,1)S(1)}, bf16[1280,1024]{0,1:T(8,128)(2,1)}) fusion(bf16[1280,2176]{0,1:T(8,128)(2,1)S(1)} %fusion.14), kind=kLoop, calls=%fused_computation.123 | loop fusion | bytes 10485760 | tf_op jit(solution)/shard_map/slice | solution.py:136
  103.8 4.0 %fusion.53 = f32[8,2,128]{2,1,0:T(2,128)S(1)} fusion(pred[128,1280]{0,1:T(8,128)(4,1)S(1)} %compare_and_fusion, bf16[1280,8,128,1]{0,2,3,1:T(8,128)(2,1)S(1)} %bitcast.103, bf16[128,8,2,128]{3,2,1,0:T(2,128)(2,1)S(1)} %reshape.322), kind=kOutput, calls=%fused_computation.125 | convolution fusion | flops 681575680 | bytes 3317760 | tf_op jit(solution)/shard_map/sub | solution.py:150
  107.8 7.2 %fusion.9 = bf16[8,128,2,128]{3,1,2,0:T(8,128)(2,1)S(1)} fusion(bf16[1280,8,128,1]{0,2,3,1:T(8,128)(2,1)} %bitcast.105, f32[8,2,128]{2,1,0:T(2,128)S(1)} %fusion.53, pred[128,1280]{0,1:T(8,128)(4,1)} %copy-done.3, bf16[1280,8,128,1]{0,2,3,1:T(8,128)(2,1)S(1)} %bitcast.104, bf16[128,8,2,128]{3,2,1,0:T(2,128)(2,1)} %copy-done.2), kind=kOutput, calls=%fused_computation.18 | convolution fusion | flops 1355549952 | bytes 6463488 | tf_op jit(solution)/shard_map/hgqk,khd->qhgd/dot_general | solution.py:152
  116.4 1.5 collective-permute-start.11
  117.8 1.3 pad_maximum_fusion.3
  119.1 0.9 gather_fusion.3
  120.1 0.7 gather_fusion
  121.2 2.7 %collective-permute-start.13 = (bf16[4,4,2048]{2,1,0:T(4,128)(2,1)S(1)}, bf16[4,4,2048]{2,1,0:T(4,128)(2,1)S(1)}, u32[]{:S(2)}, u32[]{:S(2)}) collective-permute-start(bf16[4,4,2048]{2,1,0:T(4,128)(2,1)S(1)} %broadcast_select_fusion.6), channel_id=1, source_target_pairs={{0,8},{1,9},{2,10},{3,11},{4,12},{5,13},{6,14},{7,15},{8,0},{9,1},... | collective-permute-start | bytes 196616 | tf_op jit(solution)/shard_map/ppermute | solution.py:54
  123.9 1.2 collective-permute-start.14
  125.2 2.4 %collective-permute-done.12 = bf16[4,4,2048]{2,1,0:T(4,128)(2,1)S(1)} collective-permute-done((bf16[4,4,2048]{2,1,0:T(4,128)(2,1)S(1)}, bf16[4,4,2048]{2,1,0:T(4,128)(2,1)S(1)}, u32[]{:S(2)}, u32[]{:S(2)}) %collective-permute-start.12) | collective-permute-done | bytes 65568 | tf_op jit(solution)/shard_map/ppermute | solution.py:54
  127.6 2.0 %collective-permute-done.13 = bf16[4,4,2048]{2,1,0:T(4,128)(2,1)S(1)} collective-permute-done((bf16[4,4,2048]{2,1,0:T(4,128)(2,1)S(1)}, bf16[4,4,2048]{2,1,0:T(4,128)(2,1)S(1)}, u32[]{:S(2)}, u32[]{:S(2)}) %collective-permute-start.13) | collective-permute-done | bytes 65568 | tf_op jit(solution)/shard_map/ppermute | solution.py:54
  129.8 0.8 gather_fusion.1
  131.1 6.8 %fusion.15 = f32[192,2688]{1,0:T(8,128)S(1)} fusion(bf16[2048,2688]{1,0:T(8,128)(2,1)} %all-gather.2.cloned.1.call-done, bf16[128,2048]{0,1:T(8,128)(2,1)S(1)} %bitcast.109, bf16[64,2048]{0,1:T(8,128)(2,1)S(1)} %copy.21), kind=kOutput, calls=%fused_computation.31 | convolution fusion | flops 2115502080 | bytes 13860864 | tf_op jit(solution)/shard_map/dot_general | solution.py:158
  138.3 1.9 %fusion.56 = (f32[64]{0:T(128)S(1)}, f32[64,1024]{1,0:T(8,128)S(1)}) fusion(bf16[1024,2688]{1,0:T(8,128)(2,1)S(1)} %bitcast.100, f32[192,2688]{1,0:T(8,128)S(1)} %fusion.15, f32[2688]{0:T(1024)S(1)} %copy-done.4, f32[64]{0:T(128)S(1)} %add_rsqrt_fusion, bf16[64,2688]{1,0:T(8,128)(2,1)S(1)} %gather.51, pred[64]{0:T(512)(128)(4,1)S(1)} %broadcast_in_dim.123), kind=kOutput, calls=%fused_computation.126 | convolution fusion | flops 353419200 | bytes 6812928 | tf_op jit(solution)/shard_map/dot_general | solution.py:167
  140.8 1.4 collective-permute-start.22
  142.2 1.4 collective-permute-start.23
  143.6 1.0 fusion.8
  144.9 0.7 gather_fusion.4
  145.7 1.4 collective-permute-start.24
  147.0 2.3 %collective-permute-start.25 = (f32[4,3,64]{2,1,0:T(4,128)S(1)}, f32[4,3,64]{2,1,0:T(4,128)S(1)}, u32[]{:S(2)}, u32[]{:S(2)}) collective-permute-start(f32[4,3,64]{2,1,0:T(4,128)S(1)} %broadcast_select_fusion.7), channel_id=1, source_target_pairs={{0,8},{1,9},{2,10},{3,11},{4,12},{5,13},{6,14},{7,15},{8,0},{9,1},... | collective-permute-start | bytes 9224 | tf_op jit(solution)/shard_map/ppermute | solution.py:54
  149.6 1.6 collective-permute-done.24
  151.6 1.4 collective-permute-done.26
  153.8 0.8 broadcast_subtract_fusion
  154.6 0.6 dynamic_slice.3
  (113 shorter events, 10.4 us)
Async XLA Ops:
  7.2 15.2 %copy-start.10 = (s32[64]{0:T(128)S(1)}, s32[64]{0:T(128)}, u32[]{:S(2)}) copy-start(s32[64]{0:T(128)} %param.15) | copy-start | bytes 772
  7.2 15.9 %copy-start.1 = (bf16[128,2048]{1,0:T(8,128)(2,1)S(1)}, bf16[128,2048]{1,0:T(8,128)(2,1)}, u32[]{:S(2)}) copy-start(bf16[128,2048]{1,0:T(8,128)(2,1)} %param.8) | copy-start | bytes 1572868
  7.2 123.9 %all-gather.2.cloned.1.call-start = ((), (), s32[]{:S(2)}) async-start(), calls=%async_computation | async-start | bytes 11698176 | tf_op jit(solution)/shard_map/all_gather | solution.py:118
  10.0 29.1 %collective-permute-start = (bf16[128,2176]{0,1:T(8,128)(2,1)S(1)}, bf16[128,2176]{0,1:T(8,128)(2,1)S(1)}, u32[]{:S(2)}, u32[]{:S(2)}) collective-permute-start(bf16[128,2176]{0,1:T(8,128)(2,1)S(1)} %pad_maximum_fusion.2), channel_id=1, source_target_pairs={{0,4},{1,5},{2,6},{3,7},{4,8},{5,9},{6,10},{7,11},{8,12},{9,13},{1... | collective-permute-start | bytes 1671176 | tf_op jit(solution)/shard_map/ppermute | solution.py:70
  14.9 31.2 %collective-permute-start.5 = (bf16[128,2176]{0,1:T(8,128)(2,1)S(1)}, bf16[128,2176]{0,1:T(8,128)(2,1)S(1)}, u32[]{:S(2)}, u32[]{:S(2)}) collective-permute-start(bf16[128,2176]{0,1:T(8,128)(2,1)S(1)} %pad_maximum_fusion.2), channel_id=1, source_target_pairs={{0,2},{1,3},{4,6},{5,7},{8,10},{9,11},{12,14},{13,15},{16,18},{17,... | collective-permute-start | bytes 1671176 | tf_op jit(solution)/shard_map/ppermute | solution.py:76
  19.4 4.9 %collective-permute-start.15 = (bf16[1,4,2688]{2,1,0:T(4,128)(2,1)S(1)}, bf16[1,4,2688]{2,1,0:T(4,128)(2,1)S(1)}, u32[]{:S(2)}, u32[]{:S(2)}) collective-permute-start(bf16[1,4,2688]{2,1,0:T(4,128)(2,1)S(1)} %bitcast.111), channel_id=1, source_target_pairs={{0,1},{1,2},{2,3},{3,0},{4,5},{5,6},{6,7},{7,4},{8,9},{9,10},{10,1... | collective-permute-start | bytes 64520 | tf_op jit(solution)/shard_map/ppermute | solution.py:54
  19.4 18.6 %collective-permute-start.16 = (bf16[1,4,2688]{2,1,0:T(4,128)(2,1)S(1)}, bf16[1,4,2688]{2,1,0:T(4,128)(2,1)S(1)}, u32[]{:S(2)}, u32[]{:S(2)}) collective-permute-start(bf16[1,4,2688]{2,1,0:T(4,128)(2,1)S(1)} %bitcast.112), channel_id=1, source_target_pairs={{0,2},{1,3},{2,0},{3,1},{4,6},{5,7},{6,4},{7,5},{8,10},{9,11},{10,... | collective-permute-start | bytes 64520 | tf_op jit(solution)/shard_map/ppermute | solution.py:54
  19.5 18.7 %collective-permute-start.17 = (bf16[1,4,2688]{2,1,0:T(4,128)(2,1)S(1)}, bf16[1,4,2688]{2,1,0:T(4,128)(2,1)S(1)}, u32[]{:S(2)}, u32[]{:S(2)}) collective-permute-start(bf16[1,4,2688]{2,1,0:T(4,128)(2,1)S(1)} %bitcast.113), channel_id=1, source_target_pairs={{0,3},{1,0},{2,1},{3,2},{4,7},{5,4},{6,5},{7,6},{8,11},{9,8},{10,9... | collective-permute-start | bytes 64520 | tf_op jit(solution)/shard_map/ppermute | solution.py:54
  23.4 80.3 %copy-start.2 = (bf16[128,8,2,128]{3,2,1,0:T(2,128)(2,1)}, bf16[128,8,2,128]{3,2,1,0:T(2,128)(2,1)S(1)}, u32[]{:S(2)}) copy-start(bf16[128,8,2,128]{3,2,1,0:T(2,128)(2,1)S(1)} %reshape.322) | copy-start | bytes 1572868
  24.3 75.9 %collective-permute-start.8 = (bf16[128,2176]{0,1:T(8,128)(2,1)S(1)}, bf16[128,2176]{0,1:T(8,128)(2,1)S(1)}, u32[]{:S(2)}, u32[]{:S(2)}) collective-permute-start(bf16[128,2176]{0,1:T(8,128)(2,1)S(1)} %pad_maximum_fusion.2), channel_id=1, source_target_pairs={{0,1},{1,0},{2,3},{3,2},{4,5},{5,4},{6,7},{7,6},{8,9},{9,8},{10,11... | collective-permute-start | bytes 1671176 | tf_op jit(solution)/shard_map/ppermute | solution.py:37
  39.1 23.4 %collective-permute-start.1 = (bf16[128,2176]{0,1:T(8,128)(2,1)S(1)}, bf16[128,2176]{0,1:T(8,128)(2,1)S(1)}, u32[]{:S(2)}, u32[]{:S(2)}) collective-permute-start(bf16[128,2176]{0,1:T(8,128)(2,1)S(1)} %collective-permute-done), channel_id=1, source_target_pairs={{0,4},{1,5},{2,6},{3,7},{4,8},{5,9},{6,10},{7,11},{8,12},{9,13},{1... | collective-permute-start | bytes 1671176 | tf_op jit(solution)/shard_map/ppermute | solution.py:70
  42.6 21.9 %collective-permute-start.6 = (bf16[128,2176]{0,1:T(8,128)(2,1)S(1)}, bf16[128,2176]{0,1:T(8,128)(2,1)S(1)}, u32[]{:S(2)}, u32[]{:S(2)}) collective-permute-start(bf16[128,2176]{0,1:T(8,128)(2,1)S(1)} %collective-permute-done), channel_id=1, source_target_pairs={{2,0},{3,1},{6,4},{7,5},{10,8},{11,9},{14,12},{15,13},{18,16},{19,... | collective-permute-start | bytes 1671176 | tf_op jit(solution)/shard_map/ppermute | solution.py:76
  44.6 71.8 %collective-permute-start.18 = (bf16[4,4,2688]{2,1,0:T(4,128)(2,1)}, bf16[4,4,2688]{2,1,0:T(4,128)(2,1)}, u32[]{:S(2)}, u32[]{:S(2)}) collective-permute-start(bf16[4,4,2688]{2,1,0:T(4,128)(2,1)} %broadcast_select_fusion.5), channel_id=1, source_target_pairs={{0,4},{1,5},{2,6},{3,7},{4,8},{5,9},{6,10},{7,11},{8,12},{9,13},{1... | collective-permute-start | bytes 258056 | tf_op jit(solution)/shard_map/ppermute | solution.py:54
  46.1 71.7 %collective-permute-start.19 = (bf16[4,4,2688]{2,1,0:T(4,128)(2,1)}, bf16[4,4,2688]{2,1,0:T(4,128)(2,1)}, u32[]{:S(2)}, u32[]{:S(2)}) collective-permute-start(bf16[4,4,2688]{2,1,0:T(4,128)(2,1)} %broadcast_select_fusion.5), channel_id=1, source_target_pairs={{0,8},{1,9},{2,10},{3,11},{4,12},{5,13},{6,14},{7,15},{8,0},{9,1},... | collective-permute-start | bytes 258056 | tf_op jit(solution)/shard_map/ppermute | solution.py:54
  62.5 26.4 %collective-permute-start.2 = (bf16[128,2176]{0,1:T(8,128)(2,1)S(1)}, bf16[128,2176]{0,1:T(8,128)(2,1)S(1)}, u32[]{:S(2)}, u32[]{:S(2)}) collective-permute-start(bf16[128,2176]{0,1:T(8,128)(2,1)S(1)} %collective-permute-done), channel_id=1, source_target_pairs={{0,2},{1,3},{4,6},{5,7},{8,10},{9,11},{12,14},{13,15},{16,18},{17,... | collective-permute-start | bytes 1671176 | tf_op jit(solution)/shard_map/ppermute | solution.py:76
  64.5 28.8 %collective-permute-start.3 = (bf16[128,2176]{0,1:T(8,128)(2,1)S(1)}, bf16[128,2176]{0,1:T(8,128)(2,1)S(1)}, u32[]{:S(2)}, u32[]{:S(2)}) collective-permute-start(bf16[128,2176]{0,1:T(8,128)(2,1)S(1)} %collective-permute-done.1), channel_id=1, source_target_pairs={{2,0},{3,1},{6,4},{7,5},{10,8},{11,9},{14,12},{15,13},{18,16},{19,... | collective-permute-start | bytes 1671176 | tf_op jit(solution)/shard_map/ppermute | solution.py:76
  88.9 4.7 %collective-permute-start.7 = (bf16[2,128,2176]{1,2,0:T(8,128)(2,1)S(1)}, bf16[2,128,2176]{1,2,0:T(8,128)(2,1)S(1)}, u32[]{:S(2)}, u32[]{:S(2)}) collective-permute-start(bf16[2,128,2176]{1,2,0:T(8,128)(2,1)S(1)} %pad_maximum_fusion.1), channel_id=1, source_target_pairs={{0,1},{1,0},{2,3},{3,2},{4,5},{5,4},{6,7},{7,6},{8,9},{9,8},{10,11... | collective-permute-start | bytes 3342344 | tf_op jit(solution)/shard_map/ppermute | solution.py:37
  93.5 5.1 %collective-permute-start.4 = (bf16[2,128,2176]{1,2,0:T(8,128)(2,1)S(1)}, bf16[2,128,2176]{1,2,0:T(8,128)(2,1)S(1)}, u32[]{:S(2)}, u32[]{:S(2)}) collective-permute-start(bf16[2,128,2176]{1,2,0:T(8,128)(2,1)S(1)} %pad_maximum_fusion), channel_id=1, source_target_pairs={{0,1},{1,0},{2,3},{3,2},{4,5},{5,4},{6,7},{7,6},{8,9},{9,8},{10,11... | collective-permute-start | bytes 3342344 | tf_op jit(solution)/shard_map/ppermute | solution.py:37
  93.7 24.2 %collective-permute-start.20 = (bf16[4,4,2688]{2,1,0:T(4,128)(2,1)}, bf16[4,4,2688]{2,1,0:T(4,128)(2,1)}, u32[]{:S(2)}, u32[]{:S(2)}) collective-permute-start(bf16[4,4,2688]{2,1,0:T(4,128)(2,1)} %broadcast_select_fusion.5), channel_id=1, source_target_pairs={{0,12},{1,13},{2,14},{3,15},{4,0},{5,1},{6,2},{7,3},{8,4},{9,5},{1... | collective-permute-start | bytes 258056 | tf_op jit(solution)/shard_map/ppermute | solution.py:54
  99.8 0.9 copy-start.5
  99.8 0.9 copy-start.8
  99.8 0.9 copy-start.9
  101.8 6.0 %copy-start.3 = (pred[128,1280]{0,1:T(8,128)(4,1)}, pred[128,1280]{0,1:T(8,128)(4,1)S(1)}, u32[]{:S(2)}) copy-start(pred[128,1280]{0,1:T(8,128)(4,1)S(1)} %compare_and_fusion) | copy-start | bytes 491524
  116.0 4.1 %collective-permute-start.9 = (bf16[1,4,2048]{2,1,0:T(4,128)(2,1)S(1)}, bf16[1,4,2048]{2,1,0:T(4,128)(2,1)S(1)}, u32[]{:S(2)}, u32[]{:S(2)}) collective-permute-start(bf16[1,4,2048]{2,1,0:T(4,128)(2,1)S(1)} %bitcast.117), channel_id=1, source_target_pairs={{0,1},{1,2},{2,3},{3,0},{4,5},{5,6},{6,7},{7,4},{8,9},{9,10},{10,1... | collective-permute-start | bytes 49160 | tf_op jit(solution)/shard_map/ppermute | solution.py:54
  116.2 3.8 %collective-permute-start.10 = (bf16[1,4,2048]{2,1,0:T(4,128)(2,1)S(1)}, bf16[1,4,2048]{2,1,0:T(4,128)(2,1)S(1)}, u32[]{:S(2)}, u32[]{:S(2)}) collective-permute-start(bf16[1,4,2048]{2,1,0:T(4,128)(2,1)S(1)} %bitcast.118), channel_id=1, source_target_pairs={{0,2},{1,3},{2,0},{3,1},{4,6},{5,7},{6,4},{7,5},{8,10},{9,11},{10,... | collective-permute-start | bytes 49160 | tf_op jit(solution)/shard_map/ppermute | solution.py:54
  116.4 3.7 %collective-permute-start.11 = (bf16[1,4,2048]{2,1,0:T(4,128)(2,1)S(1)}, bf16[1,4,2048]{2,1,0:T(4,128)(2,1)S(1)}, u32[]{:S(2)}, u32[]{:S(2)}) collective-permute-start(bf16[1,4,2048]{2,1,0:T(4,128)(2,1)S(1)} %bitcast.119), channel_id=1, source_target_pairs={{0,3},{1,0},{2,1},{3,2},{4,7},{5,4},{6,5},{7,6},{8,11},{9,8},{10,9... | collective-permute-start | bytes 49160 | tf_op jit(solution)/shard_map/ppermute | solution.py:54
  121.0 6.6 %collective-permute-start.12 = (bf16[4,4,2048]{2,1,0:T(4,128)(2,1)S(1)}, bf16[4,4,2048]{2,1,0:T(4,128)(2,1)S(1)}, u32[]{:S(2)}, u32[]{:S(2)}) collective-permute-start(bf16[4,4,2048]{2,1,0:T(4,128)(2,1)S(1)} %broadcast_select_fusion.6), channel_id=1, source_target_pairs={{0,4},{1,5},{2,6},{3,7},{4,8},{5,9},{6,10},{7,11},{8,12},{9,13},{1... | collective-permute-start | bytes 196616 | tf_op jit(solution)/shard_map/ppermute | solution.py:54
  121.2 8.4 %collective-permute-start.13 = (bf16[4,4,2048]{2,1,0:T(4,128)(2,1)S(1)}, bf16[4,4,2048]{2,1,0:T(4,128)(2,1)S(1)}, u32[]{:S(2)}, u32[]{:S(2)}) collective-permute-start(bf16[4,4,2048]{2,1,0:T(4,128)(2,1)S(1)} %broadcast_select_fusion.6), channel_id=1, source_target_pairs={{0,8},{1,9},{2,10},{3,11},{4,12},{5,13},{6,14},{7,15},{8,0},{9,1},... | collective-permute-start | bytes 196616 | tf_op jit(solution)/shard_map/ppermute | solution.py:54
  123.9 5.7 %collective-permute-start.14 = (bf16[4,4,2048]{2,1,0:T(4,128)(2,1)S(1)}, bf16[4,4,2048]{2,1,0:T(4,128)(2,1)S(1)}, u32[]{:S(2)}, u32[]{:S(2)}) collective-permute-start(bf16[4,4,2048]{2,1,0:T(4,128)(2,1)S(1)} %broadcast_select_fusion.6), channel_id=1, source_target_pairs={{0,12},{1,13},{2,14},{3,15},{4,0},{5,1},{6,2},{7,3},{8,4},{9,5},{1... | collective-permute-start | bytes 196616 | tf_op jit(solution)/shard_map/ppermute | solution.py:54
  130.6 7.6 %slice-start = ((s8[5505024]{0:T(1024)(128)(4,1)}), s8[1310720]{0:T(1024)(128)(4,1)S(1)}, s32[]{:S(2)}) async-start(s8[5505024]{0:T(1024)(128)(4,1)} %bitcast.99), calls=%async_computation.1 | async-start | bytes 2621440
  131.1 7.1 %slice-start.1 = ((s8[5505024]{0:T(1024)(128)(4,1)}), s8[4194304]{0:T(1024)(128)(4,1)S(1)}, s32[]{:S(2)}) async-start(s8[5505024]{0:T(1024)(128)(4,1)} %bitcast.99), calls=%async_computation.2 | async-start | bytes 8388608
  131.1 7.1 %copy-start.4 = (f32[2688]{0:T(1024)S(1)}, f32[2688]{0:T(1024)}, u32[]{:S(2)}) copy-start(f32[2688]{0:T(1024)} %param.12) | copy-start | bytes 32260
  138.3 1.9 %copy-start.7 = (s32[64]{0:T(128)S(1)}, s32[64]{0:T(128)}, u32[]{:S(2)}) copy-start(s32[64]{0:T(128)} %broadcast_subtract_fusion.1) | copy-start | bytes 772
  138.3 5.3 %copy-start = (bf16[128,2688]{1,0:T(8,128)(2,1)S(1)}, bf16[128,2688]{1,0:T(8,128)(2,1)}, u32[]{:S(2)}) copy-start(bf16[128,2688]{1,0:T(8,128)(2,1)} %param.11) | copy-start | bytes 2064388
  140.2 13.4 %copy-start.6 = (pred[16]{0:T(512)(128)(4,1)S(1)}, pred[16]{0:T(512)(128)(4,1)}, u32[]{:S(2)}) copy-start(pred[16]{0:T(512)(128)(4,1)} %broadcast_in_dim.140) | copy-start | bytes 52
  140.4 4.1 %collective-permute-start.21 = (f32[1,3,64]{2,1,0:T(4,128)S(1)}, f32[1,3,64]{2,1,0:T(4,128)S(1)}, u32[]{:S(2)}, u32[]{:S(2)}) collective-permute-start(f32[1,3,64]{2,1,0:T(4,128)S(1)} %get-tuple-element.21), channel_id=1, source_target_pairs={{0,1},{1,2},{2,3},{3,0},{4,5},{5,6},{6,7},{7,4},{8,9},{9,10},{10,1... | collective-permute-start | bytes 2312 | tf_op jit(solution)/shard_map/ppermute | solution.py:54
  140.8 3.7 %collective-permute-start.22 = (f32[1,3,64]{2,1,0:T(4,128)S(1)}, f32[1,3,64]{2,1,0:T(4,128)S(1)}, u32[]{:S(2)}, u32[]{:S(2)}) collective-permute-start(f32[1,3,64]{2,1,0:T(4,128)S(1)} %get-tuple-element.21), channel_id=1, source_target_pairs={{0,2},{1,3},{2,0},{3,1},{4,6},{5,7},{6,4},{7,5},{8,10},{9,11},{10,... | collective-permute-start | bytes 2312 | tf_op jit(solution)/shard_map/ppermute | solution.py:54
  142.2 2.7 %collective-permute-start.23 = (f32[1,3,64]{2,1,0:T(4,128)S(1)}, f32[1,3,64]{2,1,0:T(4,128)S(1)}, u32[]{:S(2)}, u32[]{:S(2)}) collective-permute-start(f32[1,3,64]{2,1,0:T(4,128)S(1)} %get-tuple-element.21), channel_id=1, source_target_pairs={{0,3},{1,0},{2,1},{3,2},{4,7},{5,4},{6,5},{7,6},{8,11},{9,8},{10,9... | collective-permute-start | bytes 2312 | tf_op jit(solution)/shard_map/ppermute | solution.py:54
  145.7 5.5 %collective-permute-start.24 = (f32[4,3,64]{2,1,0:T(4,128)S(1)}, f32[4,3,64]{2,1,0:T(4,128)S(1)}, u32[]{:S(2)}, u32[]{:S(2)}) collective-permute-start(f32[4,3,64]{2,1,0:T(4,128)S(1)} %broadcast_select_fusion.7), channel_id=1, source_target_pairs={{0,4},{1,5},{2,6},{3,7},{4,8},{5,9},{6,10},{7,11},{8,12},{9,13},{1... | collective-permute-start | bytes 9224 | tf_op jit(solution)/shard_map/ppermute | solution.py:54
  147.0 4.5 %collective-permute-start.25 = (f32[4,3,64]{2,1,0:T(4,128)S(1)}, f32[4,3,64]{2,1,0:T(4,128)S(1)}, u32[]{:S(2)}, u32[]{:S(2)}) collective-permute-start(f32[4,3,64]{2,1,0:T(4,128)S(1)} %broadcast_select_fusion.7), channel_id=1, source_target_pairs={{0,8},{1,9},{2,10},{3,11},{4,12},{5,13},{6,14},{7,15},{8,0},{9,1},... | collective-permute-start | bytes 9224 | tf_op jit(solution)/shard_map/ppermute | solution.py:54
  149.4 3.7 %collective-permute-start.26 = (f32[4,3,64]{2,1,0:T(4,128)S(1)}, f32[4,3,64]{2,1,0:T(4,128)S(1)}, u32[]{:S(2)}, u32[]{:S(2)}) collective-permute-start(f32[4,3,64]{2,1,0:T(4,128)S(1)} %broadcast_select_fusion.7), channel_id=1, source_target_pairs={{0,12},{1,13},{2,14},{3,15},{4,0},{5,1},{6,2},{7,3},{8,4},{9,5},{1... | collective-permute-start | bytes 9224 | tf_op jit(solution)/shard_map/ppermute | solution.py:54
Sparse Core Ops, SparseCore 0:
  10.3 114.2 all-gather.1

commit v15 on v13

--- a/solution.py
+++ b/solution.py
@@ -179,7 +179,7 @@
     shard_max = jnp.max(logits, axis=1)
     shard_total = jnp.sum(jnp.exp(logits - shard_max[:, None]), axis=1)
     shard_pick = jnp.sum(jnp.where(local_ids[:, None] == vocab_ids[None, :], logits, 0.0), axis=1)
-    stats = gather_rows(jnp.stack([shard_max, shard_total, shard_pick], 0))
+    stats = gather_rows(jnp.stack([shard_max, shard_total, shard_pick], 0), radix=16)
     stats = stats.reshape(-1, 3, shard_max.shape[0])
     all_max, all_total, all_pick = stats[:, 0], stats[:, 1], stats[:, 2]
     global_max = jnp.max(all_max, axis=0)

time: 162 us -> 174 us (1.074)
  starting transfers between devices: 49.7 us -> 64 us
  waiting for transfers between devices: 53.9 us -> 51.4 us
    ppermute x18 -> x27, starting transfers between devices: 21.8 us -> 36.5 us  [gather_rows(): received.append(lax.ppermute(data, SEQ, pairs))]
    ppermute x18 -> x27, waiting for transfers between devices: 10.4 us -> 7.82 us  [gather_rows(): received.append(lax.ppermute(data, SEQ, pairs))]
    gather x8 -> x7, local copies, waits for them, and re-layouts: 4.89 us -> 4.2 us  [gather_rows(): data = jnp.take(stacked, order, axis=0)]
  transfers between devices with their start and end apart: 28 -> 37, of which waited for: 11 -> 9; matrix products, arithmetic and copies ran while one was open for 19% -> 18% of each run, Pallas kernels for 0% -> 0%
where the time goes in v15:
time: 174 us; the launch traced here: 173 us
  starting transfers between devices  64 us (37%)
  waiting for transfers between devices  51.4 us (30%)
  matrix products  18.7 us (11%)
  between operations  14.6 us (8%)
  other arithmetic  12.9 us (7%)
  local copies, waits for them, and re-layouts  11.1 us (6%)
    ppermute x27, starting transfers between devices, gather_rows(): received.append(lax.ppermute(data, SEQ, pairs))  36.5 us
    ppermute x4, waiting for transfers between devices, across_pair(): return lax.ppermute(value, SEQ, pairs)  27.3 us
    ppermute x2, waiting for transfers between devices, shift_chips(): lax.ppermute(value, SEQ, [(s, s + step) for s in range(count - step)])  15.6 us
    ppermute x3, starting transfers between devices, swap_cores(): return lax.ppermute(value, 'core', [(0, 1), (1, 0)])  10.9 us
    ppermute x2, starting transfers between devices, shift_chips(): lax.ppermute(value, SEQ, [(s, s + step) for s in range(count - step)])  8.45 us
    ppermute x4, starting transfers between devices, across_pair(): return lax.ppermute(value, SEQ, pairs)  8.04 us
    ppermute x27, waiting for transfers between devices, gather_rows(): received.append(lax.ppermute(data, SEQ, pairs))  7.82 us
    dot_general x1, matrix products, local(): jnp.dot(jnp.concatenate([scored_context, context], 0), full_proj, preferr...  6.8 us
  transfers between devices with their start and end apart: 37, of which 9 were waited for; matrix products, arithmetic and copies ran while one was open for 18% of the time, Pallas kernels for 0%

profile of v15, /device:TPU:0, one launch (start us, length us, event | category | flops | bytes accessed | tf_op | source)
XLA Modules:
  0.0 172.7 jit_solution(13766113945187363545)
XLA Ops:
  7.9 1.3 copy.16
  10.0 5.0 %collective-permute-start = (bf16[128,2176]{0,1:T(8,128)(2,1)S(1)}, bf16[128,2176]{0,1:T(8,128)(2,1)S(1)}, u32[]{:S(2)}, u32[]{:S(2)}) collective-permute-start(bf16[128,2176]{0,1:T(8,128)(2,1)S(1)} %pad_maximum_fusion.2), channel_id=1, source_target_pairs={{0,4},{1,5},{2,6},{3,7},{4,8},{5,9},{6,10},{7,11},{8,12},{9,13},{1... | collective-permute-start | bytes 1671176 | tf_op jit(solution)/shard_map/ppermute | solution.py:70
  14.9 3.5 %collective-permute-start.5 = (bf16[128,2176]{0,1:T(8,128)(2,1)S(1)}, bf16[128,2176]{0,1:T(8,128)(2,1)S(1)}, u32[]{:S(2)}, u32[]{:S(2)}) collective-permute-start(bf16[128,2176]{0,1:T(8,128)(2,1)S(1)} %pad_maximum_fusion.2), channel_id=1, source_target_pairs={{0,2},{1,3},{4,6},{5,7},{8,10},{9,11},{12,14},{13,15},{16,18},{17,... | collective-permute-start | bytes 1671176 | tf_op jit(solution)/shard_map/ppermute | solution.py:76
  18.4 1.0 slice.75
  19.5 1.7 collective-permute-start.17
  25.3 10.9 %collective-permute-start.8 = (bf16[128,2176]{0,1:T(8,128)(2,1)S(1)}, bf16[128,2176]{0,1:T(8,128)(2,1)S(1)}, u32[]{:S(2)}, u32[]{:S(2)}) collective-permute-start(bf16[128,2176]{0,1:T(8,128)(2,1)S(1)} %pad_maximum_fusion.2), channel_id=1, source_target_pairs={{0,1},{1,0},{2,3},{3,2},{4,5},{5,4},{6,7},{7,6},{8,9},{9,8},{10,11... | collective-permute-start | bytes 1671176 | tf_op jit(solution)/shard_map/ppermute | solution.py:37
  36.1 1.9 %collective-permute-done.16 = bf16[1,4,2688]{2,1,0:T(4,128)(2,1)S(1)} collective-permute-done((bf16[1,4,2688]{2,1,0:T(4,128)(2,1)S(1)}, bf16[1,4,2688]{2,1,0:T(4,128)(2,1)S(1)}, u32[]{:S(2)}, u32[]{:S(2)}) %collective-permute-start.16) | collective-permute-done | bytes 21536 | tf_op jit(solution)/shard_map/ppermute | solution.py:54
  38.3 0.7 gather_fusion.2
  39.1 3.5 %collective-permute-start.1 = (bf16[128,2176]{0,1:T(8,128)(2,1)S(1)}, bf16[128,2176]{0,1:T(8,128)(2,1)S(1)}, u32[]{:S(2)}, u32[]{:S(2)}) collective-permute-start(bf16[128,2176]{0,1:T(8,128)(2,1)S(1)} %collective-permute-done), channel_id=1, source_target_pairs={{0,4},{1,5},{2,6},{3,7},{4,8},{5,9},{6,10},{7,11},{8,12},{9,13},{1... | collective-permute-start | bytes 1671176 | tf_op jit(solution)/shard_map/ppermute | solution.py:70
  42.6 1.3 collective-permute-start.6
  43.9 0.7 broadcast_select_fusion.5
  44.6 1.5 collective-permute-start.18
  46.2 0.8 collective-permute-start.19
  46.9 15.6 %collective-permute-done.1 = bf16[128,2176]{0,1:T(8,128)(2,1)S(1)} collective-permute-done((bf16[128,2176]{0,1:T(8,128)(2,1)S(1)}, bf16[128,2176]{0,1:T(8,128)(2,1)S(1)}, u32[]{:S(2)}, u32[]{:S(2)}) %collective-permute-start.1) | collective-permute-done | bytes 557088 | tf_op jit(solution)/shard_map/ppermute | solution.py:70
  62.5 2.0 %collective-permute-start.2 = (bf16[128,2176]{0,1:T(8,128)(2,1)S(1)}, bf16[128,2176]{0,1:T(8,128)(2,1)S(1)}, u32[]{:S(2)}, u32[]{:S(2)}) collective-permute-start(bf16[128,2176]{0,1:T(8,128)(2,1)S(1)} %collective-permute-done), channel_id=1, source_target_pairs={{0,2},{1,3},{4,6},{5,7},{8,10},{9,11},{12,14},{13,15},{16,18},{17,... | collective-permute-start | bytes 1671176 | tf_op jit(solution)/shard_map/ppermute | solution.py:76
  64.5 1.3 collective-permute-start.3
  66.0 22.9 %collective-permute-done.2 = bf16[128,2176]{0,1:T(8,128)(2,1)S(1)} collective-permute-done((bf16[128,2176]{0,1:T(8,128)(2,1)S(1)}, bf16[128,2176]{0,1:T(8,128)(2,1)S(1)}, u32[]{:S(2)}, u32[]{:S(2)}) %collective-permute-start.2) | collective-permute-done | bytes 557088 | tf_op jit(solution)/shard_map/ppermute | solution.py:76
  88.9 4.3 %collective-permute-done.3 = bf16[128,2176]{0,1:T(8,128)(2,1)S(1)} collective-permute-done((bf16[128,2176]{0,1:T(8,128)(2,1)S(1)}, bf16[128,2176]{0,1:T(8,128)(2,1)S(1)}, u32[]{:S(2)}, u32[]{:S(2)}) %collective-permute-start.3) | collective-permute-done | bytes 557088 | tf_op jit(solution)/shard_map/ppermute | solution.py:76
  93.7 4.8 %collective-permute-start.20 = (bf16[4,4,2688]{2,1,0:T(4,128)(2,1)}, bf16[4,4,2688]{2,1,0:T(4,128)(2,1)}, u32[]{:S(2)}, u32[]{:S(2)}) collective-permute-start(bf16[4,4,2688]{2,1,0:T(4,128)(2,1)} %broadcast_select_fusion.5), channel_id=1, source_target_pairs={{0,12},{1,13},{2,14},{3,15},{4,0},{5,1},{6,2},{7,3},{8,4},{9,5},{1... | collective-permute-start | bytes 258056 | tf_op jit(solution)/shard_map/ppermute | solution.py:54
  100.7 1.9 %constant_dynamic-slice_fusion = (bf16[1152,1024]{0,1:T(8,128)(2,1)S(1)}, bf16[1152,1024]{0,1:T(8,128)(2,1)}) fusion(bf16[1280,2176]{0,1:T(8,128)(2,1)S(1)} %fusion.14, s32[]{:T(128)S(6)} %select_n.251, s32[]{:T(128)S(6)} %add.217), kind=kLoop, calls=%fused_computation.139 | loop fusion | bytes 9437192 | tf_op jit(solution)/shard_map/slice | solution.py:139
  102.6 1.1 compare_and_fusion
  103.7 3.7 %fusion.54 = f32[8,2,128]{2,1,0:T(2,128)S(1)} fusion(pred[128,1152]{0,1:T(8,128)(4,1)S(1)} %compare_and_fusion, bf16[1152,8,128,1]{0,2,3,1:T(8,128)(2,1)S(1)} %bitcast.124, bf16[128,8,2,128]{3,2,1,0:T(2,128)(2,1)S(1)} %reshape.363), kind=kOutput, calls=%fused_computation.148 | convolution fusion | flops 613418112 | bytes 3039232 | tf_op jit(solution)/shard_map/sub | solution.py:153
  107.4 6.3 %fusion.7 = bf16[8,128,2,128]{3,1,2,0:T(8,128)(2,1)S(1)} fusion(bf16[1152,8,128,1]{0,2,3,1:T(8,128)(2,1)} %bitcast.126, f32[8,2,128]{2,1,0:T(2,128)S(1)} %fusion.54, pred[128,1152]{0,1:T(8,128)(4,1)} %copy-done.2, bf16[1152,8,128,1]{0,2,3,1:T(8,128)(2,1)S(1)} %bitcast.125, bf16[128,8,2,128]{3,2,1,0:T(2,128)(2,1)S(1)} %reshape.363), kind=kOutput, calls=%fused_computation.16 | convolution fusion | flops 1220021376 | bytes 5922816 | tf_op jit(solution)/shard_map/hgqk,khd->qhgd/dot_general | solution.py:155
  115.1 1.5 collective-permute-start.11
  116.5 1.4 pad_maximum_fusion.3
  117.9 1.0 gather_fusion.3
  119.1 0.7 gather_fusion
  120.0 2.7 %collective-permute-start.13 = (bf16[4,4,2048]{2,1,0:T(4,128)(2,1)S(1)}, bf16[4,4,2048]{2,1,0:T(4,128)(2,1)S(1)}, u32[]{:S(2)}, u32[]{:S(2)}) collective-permute-start(bf16[4,4,2048]{2,1,0:T(4,128)(2,1)S(1)} %broadcast_select_fusion.6), channel_id=1, source_target_pairs={{0,8},{1,9},{2,10},{3,11},{4,12},{5,13},{6,14},{7,15},{8,0},{9,1},... | collective-permute-start | bytes 196616 | tf_op jit(solution)/shard_map/ppermute | solution.py:54
  122.7 1.3 collective-permute-start.14
  124.1 2.6 %collective-permute-done.12 = bf16[4,4,2048]{2,1,0:T(4,128)(2,1)S(1)} collective-permute-done((bf16[4,4,2048]{2,1,0:T(4,128)(2,1)S(1)}, bf16[4,4,2048]{2,1,0:T(4,128)(2,1)S(1)}, u32[]{:S(2)}, u32[]{:S(2)}) %collective-permute-start.12) | collective-permute-done | bytes 65568 | tf_op jit(solution)/shard_map/ppermute | solution.py:54
  126.7 1.8 %collective-permute-done.13 = bf16[4,4,2048]{2,1,0:T(4,128)(2,1)S(1)} collective-permute-done((bf16[4,4,2048]{2,1,0:T(4,128)(2,1)S(1)}, bf16[4,4,2048]{2,1,0:T(4,128)(2,1)S(1)}, u32[]{:S(2)}, u32[]{:S(2)}) %collective-permute-start.13) | collective-permute-done | bytes 65568 | tf_op jit(solution)/shard_map/ppermute | solution.py:54
  128.8 0.9 gather_fusion.1
  130.2 6.8 %fusion.15 = f32[192,2688]{1,0:T(8,128)S(1)} fusion(bf16[2048,2688]{1,0:T(8,128)(2,1)} %all-gather.2.cloned.1.call-done, bf16[128,2048]{0,1:T(8,128)(2,1)S(1)} %bitcast.130, bf16[64,2048]{0,1:T(8,128)(2,1)S(1)} %copy.21), kind=kOutput, calls=%fused_computation.30 | convolution fusion | flops 2115502080 | bytes 13860864 | tf_op jit(solution)/shard_map/dot_general | solution.py:161
  137.4 1.9 %fusion.57 = (f32[64]{0:T(128)S(1)}, f32[64,1024]{1,0:T(8,128)S(1)}) fusion(bf16[1024,2688]{1,0:T(8,128)(2,1)S(1)} %bitcast.121, f32[192,2688]{1,0:T(8,128)S(1)} %fusion.15, f32[2688]{0:T(1024)S(1)} %copy-done.3, f32[64]{0:T(128)S(1)} %add_rsqrt_fusion, bf16[64,2688]{1,0:T(8,128)(2,1)S(1)} %gather.43, pred[64]{0:T(512)(128)(4,1)S(1)} %broadcast_in_dim.105), kind=kOutput, calls=%fused_computation.149 | convolution fusion | flops 353419200 | bytes 6812928 | tf_op jit(solution)/shard_map/dot_general | solution.py:170
  139.7 1.3 collective-permute-start.22
  141.0 2.2 %collective-permute-start.23 = (f32[1,3,64]{2,1,0:T(4,128)S(1)}, f32[1,3,64]{2,1,0:T(4,128)S(1)}, u32[]{:S(2)}, u32[]{:S(2)}) collective-permute-start(f32[1,3,64]{2,1,0:T(4,128)S(1)} %fusion.33), channel_id=1, source_target_pairs={{0,3},{1,4},{2,5},{3,6},{4,7},{5,8},{6,9},{7,10},{8,11},{9,12},{10... | collective-permute-start | bytes 2312 | tf_op jit(solution)/shard_map/ppermute | solution.py:54
  143.2 1.8 %collective-permute-start.25 = (f32[1,3,64]{2,1,0:T(4,128)S(1)}, f32[1,3,64]{2,1,0:T(4,128)S(1)}, u32[]{:S(2)}, u32[]{:S(2)}) collective-permute-start(f32[1,3,64]{2,1,0:T(4,128)S(1)} %fusion.33), channel_id=1, source_target_pairs={{0,5},{1,6},{2,7},{3,8},{4,9},{5,10},{6,11},{7,12},{8,13},{9,14},{... | collective-permute-start | bytes 2312 | tf_op jit(solution)/shard_map/ppermute | solution.py:54
  145.1 1.0 fusion.6
  146.0 1.9 %collective-permute-start.26 = (f32[1,3,64]{2,1,0:T(4,128)S(1)}, f32[1,3,64]{2,1,0:T(4,128)S(1)}, u32[]{:S(2)}, u32[]{:S(2)}) collective-permute-start(f32[1,3,64]{2,1,0:T(4,128)S(1)} %fusion.33), channel_id=1, source_target_pairs={{0,6},{1,7},{2,8},{3,9},{4,10},{5,11},{6,12},{7,13},{8,14},{9,15},... | collective-permute-start | bytes 2312 | tf_op jit(solution)/shard_map/ppermute | solution.py:54
  148.0 4.0 %collective-permute-start.27 = (f32[1,3,64]{2,1,0:T(4,128)S(1)}, f32[1,3,64]{2,1,0:T(4,128)S(1)}, u32[]{:S(2)}, u32[]{:S(2)}) collective-permute-start(f32[1,3,64]{2,1,0:T(4,128)S(1)} %fusion.33), channel_id=1, source_target_pairs={{0,7},{1,8},{2,9},{3,10},{4,11},{5,12},{6,13},{7,14},{8,15},{9,0},... | collective-permute-start | bytes 2312 | tf_op jit(solution)/shard_map/ppermute | solution.py:54
  152.7 1.2 collective-permute-start.30
  153.9 3.8 %collective-permute-start.31 = (f32[1,3,64]{2,1,0:T(4,128)S(1)}, f32[1,3,64]{2,1,0:T(4,128)S(1)}, u32[]{:S(2)}, u32[]{:S(2)}) collective-permute-start(f32[1,3,64]{2,1,0:T(4,128)S(1)} %fusion.33), channel_id=1, source_target_pairs={{0,11},{1,12},{2,13},{3,14},{4,15},{5,0},{6,1},{7,2},{8,3},{9,4},{... | collective-permute-start | bytes 2312 | tf_op jit(solution)/shard_map/ppermute | solution.py:54
  157.7 0.9 collective-permute-start.32
  158.6 2.7 %collective-permute-start.34 = (f32[1,3,64]{2,1,0:T(4,128)S(1)}, f32[1,3,64]{2,1,0:T(4,128)S(1)}, u32[]{:S(2)}, u32[]{:S(2)}) collective-permute-start(f32[1,3,64]{2,1,0:T(4,128)S(1)} %fusion.33), channel_id=1, source_target_pairs={{0,14},{1,15},{2,0},{3,1},{4,2},{5,3},{6,4},{7,5},{8,6},{9,7},{10,... | collective-permute-start | bytes 2312 | tf_op jit(solution)/shard_map/ppermute | solution.py:54
  161.3 0.9 collective-permute-start.35
  162.6 0.9 collective-permute-done.35
  163.5 0.7 gather_fusion.4
  164.4 0.8 broadcast_subtract_fusion
  (141 shorter events, 13.7 us)
Async XLA Ops:
  7.2 16.4 %copy-start.9 = (s32[64]{0:T(128)S(1)}, s32[64]{0:T(128)}, u32[]{:S(2)}) copy-start(s32[64]{0:T(128)} %param.15) | copy-start | bytes 772
  7.2 17.5 %copy-start.1 = (bf16[128,2048]{1,0:T(8,128)(2,1)S(1)}, bf16[128,2048]{1,0:T(8,128)(2,1)}, u32[]{:S(2)}) copy-start(bf16[128,2048]{1,0:T(8,128)(2,1)} %param.8) | copy-start | bytes 1572868
  7.2 123.0 %all-gather.2.cloned.1.call-start = ((), (), s32[]{:S(2)}) async-start(), calls=%async_computation | async-start | bytes 11698176 | tf_op jit(solution)/shard_map/all_gather | solution.py:121
  10.0 29.1 %collective-permute-start = (bf16[128,2176]{0,1:T(8,128)(2,1)S(1)}, bf16[128,2176]{0,1:T(8,128)(2,1)S(1)}, u32[]{:S(2)}, u32[]{:S(2)}) collective-permute-start(bf16[128,2176]{0,1:T(8,128)(2,1)S(1)} %pad_maximum_fusion.2), channel_id=1, source_target_pairs={{0,4},{1,5},{2,6},{3,7},{4,8},{5,9},{6,10},{7,11},{8,12},{9,13},{1... | collective-permute-start | bytes 1671176 | tf_op jit(solution)/shard_map/ppermute | solution.py:70
  14.9 31.2 %collective-permute-start.5 = (bf16[128,2176]{0,1:T(8,128)(2,1)S(1)}, bf16[128,2176]{0,1:T(8,128)(2,1)S(1)}, u32[]{:S(2)}, u32[]{:S(2)}) collective-permute-start(bf16[128,2176]{0,1:T(8,128)(2,1)S(1)} %pad_maximum_fusion.2), channel_id=1, source_target_pairs={{0,2},{1,3},{4,6},{5,7},{8,10},{9,11},{12,14},{13,15},{16,18},{17,... | collective-permute-start | bytes 1671176 | tf_op jit(solution)/shard_map/ppermute | solution.py:76
  19.4 5.9 %collective-permute-start.15 = (bf16[1,4,2688]{2,1,0:T(4,128)(2,1)S(1)}, bf16[1,4,2688]{2,1,0:T(4,128)(2,1)S(1)}, u32[]{:S(2)}, u32[]{:S(2)}) collective-permute-start(bf16[1,4,2688]{2,1,0:T(4,128)(2,1)S(1)} %bitcast.132), channel_id=1, source_target_pairs={{0,1},{1,2},{2,3},{3,0},{4,5},{5,6},{6,7},{7,4},{8,9},{9,10},{10,1... | collective-permute-start | bytes 64520 | tf_op jit(solution)/shard_map/ppermute | solution.py:54
  19.4 18.6 %collective-permute-start.16 = (bf16[1,4,2688]{2,1,0:T(4,128)(2,1)S(1)}, bf16[1,4,2688]{2,1,0:T(4,128)(2,1)S(1)}, u32[]{:S(2)}, u32[]{:S(2)}) collective-permute-start(bf16[1,4,2688]{2,1,0:T(4,128)(2,1)S(1)} %bitcast.133), channel_id=1, source_target_pairs={{0,2},{1,3},{2,0},{3,1},{4,6},{5,7},{6,4},{7,5},{8,10},{9,11},{10,... | collective-permute-start | bytes 64520 | tf_op jit(solution)/shard_map/ppermute | solution.py:54
  19.5 18.7 %collective-permute-start.17 = (bf16[1,4,2688]{2,1,0:T(4,128)(2,1)S(1)}, bf16[1,4,2688]{2,1,0:T(4,128)(2,1)S(1)}, u32[]{:S(2)}, u32[]{:S(2)}) collective-permute-start(bf16[1,4,2688]{2,1,0:T(4,128)(2,1)S(1)} %bitcast.134), channel_id=1, source_target_pairs={{0,3},{1,0},{2,1},{3,2},{4,7},{5,4},{6,5},{7,6},{8,11},{9,8},{10,9... | collective-permute-start | bytes 64520 | tf_op jit(solution)/shard_map/ppermute | solution.py:54
  25.3 74.9 %collective-permute-start.8 = (bf16[128,2176]{0,1:T(8,128)(2,1)S(1)}, bf16[128,2176]{0,1:T(8,128)(2,1)S(1)}, u32[]{:S(2)}, u32[]{:S(2)}) collective-permute-start(bf16[128,2176]{0,1:T(8,128)(2,1)S(1)} %pad_maximum_fusion.2), channel_id=1, source_target_pairs={{0,1},{1,0},{2,3},{3,2},{4,5},{5,4},{6,7},{7,6},{8,9},{9,8},{10,11... | collective-permute-start | bytes 1671176 | tf_op jit(solution)/shard_map/ppermute | solution.py:37
  39.1 23.4 %collective-permute-start.1 = (bf16[128,2176]{0,1:T(8,128)(2,1)S(1)}, bf16[128,2176]{0,1:T(8,128)(2,1)S(1)}, u32[]{:S(2)}, u32[]{:S(2)}) collective-permute-start(bf16[128,2176]{0,1:T(8,128)(2,1)S(1)} %collective-permute-done), channel_id=1, source_target_pairs={{0,4},{1,5},{2,6},{3,7},{4,8},{5,9},{6,10},{7,11},{8,12},{9,13},{1... | collective-permute-start | bytes 1671176 | tf_op jit(solution)/shard_map/ppermute | solution.py:70
  42.6 21.9 %collective-permute-start.6 = (bf16[128,2176]{0,1:T(8,128)(2,1)S(1)}, bf16[128,2176]{0,1:T(8,128)(2,1)S(1)}, u32[]{:S(2)}, u32[]{:S(2)}) collective-permute-start(bf16[128,2176]{0,1:T(8,128)(2,1)S(1)} %collective-permute-done), channel_id=1, source_target_pairs={{2,0},{3,1},{6,4},{7,5},{10,8},{11,9},{14,12},{15,13},{18,16},{19,... | collective-permute-start | bytes 1671176 | tf_op jit(solution)/shard_map/ppermute | solution.py:76
  44.6 70.5 %collective-permute-start.18 = (bf16[4,4,2688]{2,1,0:T(4,128)(2,1)}, bf16[4,4,2688]{2,1,0:T(4,128)(2,1)}, u32[]{:S(2)}, u32[]{:S(2)}) collective-permute-start(bf16[4,4,2688]{2,1,0:T(4,128)(2,1)} %broadcast_select_fusion.5), channel_id=1, source_target_pairs={{0,4},{1,5},{2,6},{3,7},{4,8},{5,9},{6,10},{7,11},{8,12},{9,13},{1... | collective-permute-start | bytes 258056 | tf_op jit(solution)/shard_map/ppermute | solution.py:54
  46.2 70.4 %collective-permute-start.19 = (bf16[4,4,2688]{2,1,0:T(4,128)(2,1)}, bf16[4,4,2688]{2,1,0:T(4,128)(2,1)}, u32[]{:S(2)}, u32[]{:S(2)}) collective-permute-start(bf16[4,4,2688]{2,1,0:T(4,128)(2,1)} %broadcast_select_fusion.5), channel_id=1, source_target_pairs={{0,8},{1,9},{2,10},{3,11},{4,12},{5,13},{6,14},{7,15},{8,0},{9,1},... | collective-permute-start | bytes 258056 | tf_op jit(solution)/shard_map/ppermute | solution.py:54
  62.5 26.4 %collective-permute-start.2 = (bf16[128,2176]{0,1:T(8,128)(2,1)S(1)}, bf16[128,2176]{0,1:T(8,128)(2,1)S(1)}, u32[]{:S(2)}, u32[]{:S(2)}) collective-permute-start(bf16[128,2176]{0,1:T(8,128)(2,1)S(1)} %collective-permute-done), channel_id=1, source_target_pairs={{0,2},{1,3},{4,6},{5,7},{8,10},{9,11},{12,14},{13,15},{16,18},{17,... | collective-permute-start | bytes 1671176 | tf_op jit(solution)/shard_map/ppermute | solution.py:76
  64.5 28.8 %collective-permute-start.3 = (bf16[128,2176]{0,1:T(8,128)(2,1)S(1)}, bf16[128,2176]{0,1:T(8,128)(2,1)S(1)}, u32[]{:S(2)}, u32[]{:S(2)}) collective-permute-start(bf16[128,2176]{0,1:T(8,128)(2,1)S(1)} %collective-permute-done.1), channel_id=1, source_target_pairs={{2,0},{3,1},{6,4},{7,5},{10,8},{11,9},{14,12},{15,13},{18,16},{19,... | collective-permute-start | bytes 1671176 | tf_op jit(solution)/shard_map/ppermute | solution.py:76
  88.9 4.7 %collective-permute-start.7 = (bf16[2,128,2176]{1,2,0:T(8,128)(2,1)S(1)}, bf16[2,128,2176]{1,2,0:T(8,128)(2,1)S(1)}, u32[]{:S(2)}, u32[]{:S(2)}) collective-permute-start(bf16[2,128,2176]{1,2,0:T(8,128)(2,1)S(1)} %pad_maximum_fusion.1), channel_id=1, source_target_pairs={{0,1},{1,0},{2,3},{3,2},{4,5},{5,4},{6,7},{7,6},{8,9},{9,8},{10,11... | collective-permute-start | bytes 3342344 | tf_op jit(solution)/shard_map/ppermute | solution.py:37
  93.5 5.1 %collective-permute-start.4 = (bf16[2,128,2176]{1,2,0:T(8,128)(2,1)S(1)}, bf16[2,128,2176]{1,2,0:T(8,128)(2,1)S(1)}, u32[]{:S(2)}, u32[]{:S(2)}) collective-permute-start(bf16[2,128,2176]{1,2,0:T(8,128)(2,1)S(1)} %pad_maximum_fusion), channel_id=1, source_target_pairs={{0,1},{1,0},{2,3},{3,2},{4,5},{5,4},{6,7},{7,6},{8,9},{9,8},{10,11... | collective-permute-start | bytes 3342344 | tf_op jit(solution)/shard_map/ppermute | solution.py:37
  93.7 22.9 %collective-permute-start.20 = (bf16[4,4,2688]{2,1,0:T(4,128)(2,1)}, bf16[4,4,2688]{2,1,0:T(4,128)(2,1)}, u32[]{:S(2)}, u32[]{:S(2)}) collective-permute-start(bf16[4,4,2688]{2,1,0:T(4,128)(2,1)} %broadcast_select_fusion.5), channel_id=1, source_target_pairs={{0,12},{1,13},{2,14},{3,15},{4,0},{5,1},{6,2},{7,3},{8,4},{9,5},{1... | collective-permute-start | bytes 258056 | tf_op jit(solution)/shard_map/ppermute | solution.py:54
  100.7 1.9 %copy-start.4 = (s32[128]{0:T(128)S(1)}, s32[128]{0:T(128)}, u32[]{:S(2)}) copy-start(s32[128]{0:T(128)} %param.10) | copy-start | bytes 1540
  100.7 1.9 %copy-start.7 = (s32[128]{0:T(128)S(1)}, s32[128]{0:T(128)}, u32[]{:S(2)}) copy-start(s32[128]{0:T(128)} %get-tuple-element.22) | copy-start | bytes 1540
  103.7 3.7 %copy-start.2 = (pred[128,1152]{0,1:T(8,128)(4,1)}, pred[128,1152]{0,1:T(8,128)(4,1)S(1)}, u32[]{:S(2)}) copy-start(pred[128,1152]{0,1:T(8,128)(4,1)S(1)} %compare_and_fusion) | copy-start | bytes 442372
  114.7 4.3 %collective-permute-start.9 = (bf16[1,4,2048]{2,1,0:T(4,128)(2,1)S(1)}, bf16[1,4,2048]{2,1,0:T(4,128)(2,1)S(1)}, u32[]{:S(2)}, u32[]{:S(2)}) collective-permute-start(bf16[1,4,2048]{2,1,0:T(4,128)(2,1)S(1)} %bitcast.138), channel_id=1, source_target_pairs={{0,1},{1,2},{2,3},{3,0},{4,5},{5,6},{6,7},{7,4},{8,9},{9,10},{10,1... | collective-permute-start | bytes 49160 | tf_op jit(solution)/shard_map/ppermute | solution.py:54
  114.9 4.1 %collective-permute-start.10 = (bf16[1,4,2048]{2,1,0:T(4,128)(2,1)S(1)}, bf16[1,4,2048]{2,1,0:T(4,128)(2,1)S(1)}, u32[]{:S(2)}, u32[]{:S(2)}) collective-permute-start(bf16[1,4,2048]{2,1,0:T(4,128)(2,1)S(1)} %bitcast.139), channel_id=1, source_target_pairs={{0,2},{1,3},{2,0},{3,1},{4,6},{5,7},{6,4},{7,5},{8,10},{9,11},{10,... | collective-permute-start | bytes 49160 | tf_op jit(solution)/shard_map/ppermute | solution.py:54
  115.1 3.9 %collective-permute-start.11 = (bf16[1,4,2048]{2,1,0:T(4,128)(2,1)S(1)}, bf16[1,4,2048]{2,1,0:T(4,128)(2,1)S(1)}, u32[]{:S(2)}, u32[]{:S(2)}) collective-permute-start(bf16[1,4,2048]{2,1,0:T(4,128)(2,1)S(1)} %bitcast.140), channel_id=1, source_target_pairs={{0,3},{1,0},{2,1},{3,2},{4,7},{5,4},{6,5},{7,6},{8,11},{9,8},{10,9... | collective-permute-start | bytes 49160 | tf_op jit(solution)/shard_map/ppermute | solution.py:54
  119.9 6.8 %collective-permute-start.12 = (bf16[4,4,2048]{2,1,0:T(4,128)(2,1)S(1)}, bf16[4,4,2048]{2,1,0:T(4,128)(2,1)S(1)}, u32[]{:S(2)}, u32[]{:S(2)}) collective-permute-start(bf16[4,4,2048]{2,1,0:T(4,128)(2,1)S(1)} %broadcast_select_fusion.6), channel_id=1, source_target_pairs={{0,4},{1,5},{2,6},{3,7},{4,8},{5,9},{6,10},{7,11},{8,12},{9,13},{1... | collective-permute-start | bytes 196616 | tf_op jit(solution)/shard_map/ppermute | solution.py:54
  120.0 8.6 %collective-permute-start.13 = (bf16[4,4,2048]{2,1,0:T(4,128)(2,1)S(1)}, bf16[4,4,2048]{2,1,0:T(4,128)(2,1)S(1)}, u32[]{:S(2)}, u32[]{:S(2)}) collective-permute-start(bf16[4,4,2048]{2,1,0:T(4,128)(2,1)S(1)} %broadcast_select_fusion.6), channel_id=1, source_target_pairs={{0,8},{1,9},{2,10},{3,11},{4,12},{5,13},{6,14},{7,15},{8,0},{9,1},... | collective-permute-start | bytes 196616 | tf_op jit(solution)/shard_map/ppermute | solution.py:54
  122.7 5.9 %collective-permute-start.14 = (bf16[4,4,2048]{2,1,0:T(4,128)(2,1)S(1)}, bf16[4,4,2048]{2,1,0:T(4,128)(2,1)S(1)}, u32[]{:S(2)}, u32[]{:S(2)}) collective-permute-start(bf16[4,4,2048]{2,1,0:T(4,128)(2,1)S(1)} %broadcast_select_fusion.6), channel_id=1, source_target_pairs={{0,12},{1,13},{2,14},{3,15},{4,0},{5,1},{6,2},{7,3},{8,4},{9,5},{1... | collective-permute-start | bytes 196616 | tf_op jit(solution)/shard_map/ppermute | solution.py:54
  129.8 7.5 %slice-start = ((s8[5505024]{0:T(1024)(128)(4,1)}), s8[1310720]{0:T(1024)(128)(4,1)S(1)}, s32[]{:S(2)}) async-start(s8[5505024]{0:T(1024)(128)(4,1)} %bitcast.120), calls=%async_computation.1 | async-start | bytes 2621440
  130.2 7.1 %slice-start.1 = ((s8[5505024]{0:T(1024)(128)(4,1)}), s8[4194304]{0:T(1024)(128)(4,1)S(1)}, s32[]{:S(2)}) async-start(s8[5505024]{0:T(1024)(128)(4,1)} %bitcast.120), calls=%async_computation.2 | async-start | bytes 8388608
  130.2 7.1 %copy-start.3 = (f32[2688]{0:T(1024)S(1)}, f32[2688]{0:T(1024)}, u32[]{:S(2)}) copy-start(f32[2688]{0:T(1024)} %param.12) | copy-start | bytes 32260
  137.4 1.9 %copy-start.6 = (s32[64]{0:T(128)S(1)}, s32[64]{0:T(128)}, u32[]{:S(2)}) copy-start(s32[64]{0:T(128)} %broadcast_subtract_fusion.1) | copy-start | bytes 772
  137.4 7.7 %copy-start = (bf16[128,2688]{1,0:T(8,128)(2,1)S(1)}, bf16[128,2688]{1,0:T(8,128)(2,1)}, u32[]{:S(2)}) copy-start(bf16[128,2688]{1,0:T(8,128)(2,1)} %param.11) | copy-start | bytes 2064388
  139.3 25.0 %copy-start.5 = (pred[16]{0:T(512)(128)(4,1)S(1)}, pred[16]{0:T(512)(128)(4,1)}, u32[]{:S(2)}) copy-start(pred[16]{0:T(512)(128)(4,1)} %compare_and_fusion.1) | copy-start | bytes 52
  139.5 6.5 %collective-permute-start.21 = (f32[1,3,64]{2,1,0:T(4,128)S(1)}, f32[1,3,64]{2,1,0:T(4,128)S(1)}, u32[]{:S(2)}, u32[]{:S(2)}) collective-permute-start(f32[1,3,64]{2,1,0:T(4,128)S(1)} %fusion.33), channel_id=1, source_target_pairs={{0,1},{1,2},{2,3},{3,4},{4,5},{5,6},{6,7},{7,8},{8,9},{9,10},{10,1... | collective-permute-start | bytes 2312 | tf_op jit(solution)/shard_map/ppermute | solution.py:54
  139.7 8.3 %collective-permute-start.22 = (f32[1,3,64]{2,1,0:T(4,128)S(1)}, f32[1,3,64]{2,1,0:T(4,128)S(1)}, u32[]{:S(2)}, u32[]{:S(2)}) collective-permute-start(f32[1,3,64]{2,1,0:T(4,128)S(1)} %fusion.33), channel_id=1, source_target_pairs={{0,2},{1,3},{2,4},{3,5},{4,6},{5,7},{6,8},{7,9},{8,10},{9,11},{10,... | collective-permute-start | bytes 2312 | tf_op jit(solution)/shard_map/ppermute | solution.py:54
  141.0 11.0 %collective-permute-start.23 = (f32[1,3,64]{2,1,0:T(4,128)S(1)}, f32[1,3,64]{2,1,0:T(4,128)S(1)}, u32[]{:S(2)}, u32[]{:S(2)}) collective-permute-start(f32[1,3,64]{2,1,0:T(4,128)S(1)} %fusion.33), channel_id=1, source_target_pairs={{0,3},{1,4},{2,5},{3,6},{4,7},{5,8},{6,9},{7,10},{8,11},{9,12},{10... | collective-permute-start | bytes 2312 | tf_op jit(solution)/shard_map/ppermute | solution.py:54
  143.2 9.4 %collective-permute-start.24 = (f32[1,3,64]{2,1,0:T(4,128)S(1)}, f32[1,3,64]{2,1,0:T(4,128)S(1)}, u32[]{:S(2)}, u32[]{:S(2)}) collective-permute-start(f32[1,3,64]{2,1,0:T(4,128)S(1)} %fusion.33), channel_id=1, source_target_pairs={{0,4},{1,5},{2,6},{3,7},{4,8},{5,9},{6,10},{7,11},{8,12},{9,13},{1... | collective-permute-start | bytes 2312 | tf_op jit(solution)/shard_map/ppermute | solution.py:54
  143.2 9.5 %collective-permute-start.25 = (f32[1,3,64]{2,1,0:T(4,128)S(1)}, f32[1,3,64]{2,1,0:T(4,128)S(1)}, u32[]{:S(2)}, u32[]{:S(2)}) collective-permute-start(f32[1,3,64]{2,1,0:T(4,128)S(1)} %fusion.33), channel_id=1, source_target_pairs={{0,5},{1,6},{2,7},{3,8},{4,9},{5,10},{6,11},{7,12},{8,13},{9,14},{... | collective-permute-start | bytes 2312 | tf_op jit(solution)/shard_map/ppermute | solution.py:54
  146.0 7.9 %collective-permute-start.26 = (f32[1,3,64]{2,1,0:T(4,128)S(1)}, f32[1,3,64]{2,1,0:T(4,128)S(1)}, u32[]{:S(2)}, u32[]{:S(2)}) collective-permute-start(f32[1,3,64]{2,1,0:T(4,128)S(1)} %fusion.33), channel_id=1, source_target_pairs={{0,6},{1,7},{2,8},{3,9},{4,10},{5,11},{6,12},{7,13},{8,14},{9,15},... | collective-permute-start | bytes 2312 | tf_op jit(solution)/shard_map/ppermute | solution.py:54
  148.0 9.7 %collective-permute-start.27 = (f32[1,3,64]{2,1,0:T(4,128)S(1)}, f32[1,3,64]{2,1,0:T(4,128)S(1)}, u32[]{:S(2)}, u32[]{:S(2)}) collective-permute-start(f32[1,3,64]{2,1,0:T(4,128)S(1)} %fusion.33), channel_id=1, source_target_pairs={{0,7},{1,8},{2,9},{3,10},{4,11},{5,12},{6,13},{7,14},{8,15},{9,0},... | collective-permute-start | bytes 2312 | tf_op jit(solution)/shard_map/ppermute | solution.py:54
  152.0 6.6 %collective-permute-start.28 = (f32[1,3,64]{2,1,0:T(4,128)S(1)}, f32[1,3,64]{2,1,0:T(4,128)S(1)}, u32[]{:S(2)}, u32[]{:S(2)}) collective-permute-start(f32[1,3,64]{2,1,0:T(4,128)S(1)} %fusion.33), channel_id=1, source_target_pairs={{0,8},{1,9},{2,10},{3,11},{4,12},{5,13},{6,14},{7,15},{8,0},{9,1},... | collective-permute-start | bytes 2312 | tf_op jit(solution)/shard_map/ppermute | solution.py:54
  152.6 6.0 %collective-permute-start.29 = (f32[1,3,64]{2,1,0:T(4,128)S(1)}, f32[1,3,64]{2,1,0:T(4,128)S(1)}, u32[]{:S(2)}, u32[]{:S(2)}) collective-permute-start(f32[1,3,64]{2,1,0:T(4,128)S(1)} %fusion.33), channel_id=1, source_target_pairs={{0,9},{1,10},{2,11},{3,12},{4,13},{5,14},{6,15},{7,0},{8,1},{9,2},... | collective-permute-start | bytes 2312 | tf_op jit(solution)/shard_map/ppermute | solution.py:54
  152.7 8.6 %collective-permute-start.30 = (f32[1,3,64]{2,1,0:T(4,128)S(1)}, f32[1,3,64]{2,1,0:T(4,128)S(1)}, u32[]{:S(2)}, u32[]{:S(2)}) collective-permute-start(f32[1,3,64]{2,1,0:T(4,128)S(1)} %fusion.33), channel_id=1, source_target_pairs={{0,10},{1,11},{2,12},{3,13},{4,14},{5,15},{6,0},{7,1},{8,2},{9,3},... | collective-permute-start | bytes 2312 | tf_op jit(solution)/shard_map/ppermute | solution.py:54
  153.9 8.3 %collective-permute-start.31 = (f32[1,3,64]{2,1,0:T(4,128)S(1)}, f32[1,3,64]{2,1,0:T(4,128)S(1)}, u32[]{:S(2)}, u32[]{:S(2)}) collective-permute-start(f32[1,3,64]{2,1,0:T(4,128)S(1)} %fusion.33), channel_id=1, source_target_pairs={{0,11},{1,12},{2,13},{3,14},{4,15},{5,0},{6,1},{7,2},{8,3},{9,4},{... | collective-permute-start | bytes 2312 | tf_op jit(solution)/shard_map/ppermute | solution.py:54
  157.7 4.5 %collective-permute-start.32 = (f32[1,3,64]{2,1,0:T(4,128)S(1)}, f32[1,3,64]{2,1,0:T(4,128)S(1)}, u32[]{:S(2)}, u32[]{:S(2)}) collective-permute-start(f32[1,3,64]{2,1,0:T(4,128)S(1)} %fusion.33), channel_id=1, source_target_pairs={{0,12},{1,13},{2,14},{3,15},{4,0},{5,1},{6,2},{7,3},{8,4},{9,5},{1... | collective-permute-start | bytes 2312 | tf_op jit(solution)/shard_map/ppermute | solution.py:54
  158.6 3.6 %collective-permute-start.33 = (f32[1,3,64]{2,1,0:T(4,128)S(1)}, f32[1,3,64]{2,1,0:T(4,128)S(1)}, u32[]{:S(2)}, u32[]{:S(2)}) collective-permute-start(f32[1,3,64]{2,1,0:T(4,128)S(1)} %fusion.33), channel_id=1, source_target_pairs={{0,13},{1,14},{2,15},{3,0},{4,1},{5,2},{6,3},{7,4},{8,5},{9,6},{10... | collective-permute-start | bytes 2312 | tf_op jit(solution)/shard_map/ppermute | solution.py:54
  158.6 4.0 %collective-permute-start.34 = (f32[1,3,64]{2,1,0:T(4,128)S(1)}, f32[1,3,64]{2,1,0:T(4,128)S(1)}, u32[]{:S(2)}, u32[]{:S(2)}) collective-permute-start(f32[1,3,64]{2,1,0:T(4,128)S(1)} %fusion.33), channel_id=1, source_target_pairs={{0,14},{1,15},{2,0},{3,1},{4,2},{5,3},{6,4},{7,5},{8,6},{9,7},{10,... | collective-permute-start | bytes 2312 | tf_op jit(solution)/shard_map/ppermute | solution.py:54
  161.3 2.2 %collective-permute-start.35 = (f32[1,3,64]{2,1,0:T(4,128)S(1)}, f32[1,3,64]{2,1,0:T(4,128)S(1)}, u32[]{:S(2)}, u32[]{:S(2)}) collective-permute-start(f32[1,3,64]{2,1,0:T(4,128)S(1)} %fusion.33), channel_id=1, source_target_pairs={{0,15},{1,0},{2,1},{3,2},{4,3},{5,4},{6,5},{7,6},{8,7},{9,8},{10,9... | collective-permute-start | bytes 2312 | tf_op jit(solution)/shard_map/ppermute | solution.py:54
  (1 other events, 1.9 us)
Sparse Core Ops, SparseCore 0:
  10.3 114.2 all-gather.1

commit v16 on v13

--- a/solution.py
+++ b/solution.py
@@ -121,11 +121,14 @@
     full_proj = lax.all_gather(out_proj, SEQ, axis=0, tiled=True)
     score_count = SCORE_DEV
     stride = token_rows // score_count
-    scored_residual = gather_rows(residual.reshape(score_count, stride, width)[:, stride - 1, :])
 
     seg_cols = jnp.broadcast_to(segment_ids.astype(jnp.bfloat16)[:, None], (token_rows, SEG_LANES))
     own = jnp.concatenate([joined_keys_values, seg_cols], 1)
     key_value_pair, key_seg = halo_window(own, kv_width, blocks, first_core)
+    residual_rows, key_value_pair = lax.optimization_barrier(
+        (residual.reshape(score_count, stride, width)[:, stride - 1, :], key_value_pair)
+    )
+    scored_residual = gather_rows(residual_rows)
     count_of_keys = key_value_pair.shape[0]
     query_pos = first_row + jnp.arange(token_rows, dtype=jnp.int32)
     key_pos = first_row - blocks * token_rows + jnp.arange(count_of_keys, dtype=jnp.int32)

time: 162 us -> 170 us (1.049)
  local copies, waits for them, and re-layouts: 12.4 us -> 17.4 us
  waiting for transfers between devices: 53.9 us -> 55.8 us
    ppermute x2, waiting for transfers between devices: 15.6 us -> 27.4 us  [shift_chips(): lax.ppermute(value, SEQ, [(s, s + step) for s in range(count - step)])]
    ppermute x3, starting transfers between devices: 11.4 us -> 0.08 us  [swap_cores(): return lax.ppermute(value, 'core', [(0, 1), (1, 0)])]
    ppermute x4, waiting for transfers between devices: 27.3 us -> 20 us  [across_pair(): return lax.ppermute(value, SEQ, pairs)]
    ppermute x2, starting transfers between devices: 8.45 us -> 12.7 us  [shift_chips(): lax.ppermute(value, SEQ, [(s, s + step) for s in range(count - step)])]
    ppermute x18, starting transfers between devices: 21.8 us -> 25.7 us  [gather_rows(): received.append(lax.ppermute(data, SEQ, pairs))]
    ppermute x18, waiting for transfers between devices: 10.4 us -> 7.75 us  [gather_rows(): received.append(lax.ppermute(data, SEQ, pairs))]
    ppermute x4, starting transfers between devices: 8.04 us -> 10.6 us  [across_pair(): return lax.ppermute(value, SEQ, pairs)]
    reshape x1, local copies, waits for them, and re-layouts: 0.37 us -> 2.19 us  [local(): queries.reshape(token_rows, KEY_VALUE_HEADS, queries_per_group, HEAD_SIZE)]
  transfers between devices with their start and end apart: 28 -> 28, of which waited for: 11 -> 10; matrix products, arithmetic and copies ran while one was open for 19% -> 22% of each run, Pallas kernels for 0% -> 0%
where the time goes in v16:
time: 170 us
  waiting for transfers between devices  55.8 us (33%)
  starting transfers between devices  49.1 us (29%)
  matrix products  19.6 us (12%)
  local copies, waits for them, and re-layouts  17.4 us (10%)
  between operations  14.6 us (9%)
  other arithmetic  13.3 us (8%)
    ppermute x2, waiting for transfers between devices, shift_chips(): lax.ppermute(value, SEQ, [(s, s + step) for s in range(count - step)])  27.4 us
    ppermute x18, starting transfers between devices, gather_rows(): received.append(lax.ppermute(data, SEQ, pairs))  25.7 us
    ppermute x4, waiting for transfers between devices, across_pair(): return lax.ppermute(value, SEQ, pairs)  20 us
    ppermute x2, starting transfers between devices, shift_chips(): lax.ppermute(value, SEQ, [(s, s + step) for s in range(count - step)])  12.7 us
    ppermute x4, starting transfers between devices, across_pair(): return lax.ppermute(value, SEQ, pairs)  10.6 us
    ppermute x18, waiting for transfers between devices, gather_rows(): received.append(lax.ppermute(data, SEQ, pairs))  7.75 us
    dot_general x1, matrix products, local(): jnp.dot(jnp.concatenate([scored_context, context], 0), full_proj, preferr...  6.8 us
    dot_general x1, matrix products, local(): jnp.einsum('hgqk,khd->qhgd', weights, heads_for_values, preferred_element...  6.7 us
  transfers between devices with their start and end apart: 28, of which 10 were waited for; matrix products, arithmetic and copies ran while one was open for 22% of the time, Pallas kernels for 0%

profile of v16, /device:TPU:0, one launch (start us, length us, event | category | flops | bytes accessed | tf_op | source)
XLA Modules:
  0.0 169.9 jit_solution(3689486977762381076)
XLA Ops:
  7.2 0.7 all-gather.2.cloned.1.call-update
  7.9 1.3 copy.17
  9.9 5.0 %collective-permute-start = (bf16[128,2176]{0,1:T(8,128)(2,1)S(1)}, bf16[128,2176]{0,1:T(8,128)(2,1)S(1)}, u32[]{:S(2)}, u32[]{:S(2)}) collective-permute-start(bf16[128,2176]{0,1:T(8,128)(2,1)S(1)} %pad_maximum_fusion.2), channel_id=1, source_target_pairs={{0,4},{1,5},{2,6},{3,7},{4,8},{5,9},{6,10},{7,11},{8,12},{9,13},{1... | collective-permute-start | bytes 1671176 | tf_op jit(solution)/shard_map/ppermute | solution.py:70
  14.9 3.5 %collective-permute-start.5 = (bf16[128,2176]{0,1:T(8,128)(2,1)S(1)}, bf16[128,2176]{0,1:T(8,128)(2,1)S(1)}, u32[]{:S(2)}, u32[]{:S(2)}) collective-permute-start(bf16[128,2176]{0,1:T(8,128)(2,1)S(1)} %pad_maximum_fusion.2), channel_id=1, source_target_pairs={{0,2},{1,3},{4,6},{5,7},{8,10},{9,11},{12,14},{13,15},{16,18},{17,... | collective-permute-start | bytes 1671176 | tf_op jit(solution)/shard_map/ppermute | solution.py:76
  18.5 13.9 %collective-permute-done = bf16[128,2176]{0,1:T(8,128)(2,1)S(1)} collective-permute-done((bf16[128,2176]{0,1:T(8,128)(2,1)S(1)}, bf16[128,2176]{0,1:T(8,128)(2,1)S(1)}, u32[]{:S(2)}, u32[]{:S(2)}) %collective-permute-start) | collective-permute-done | bytes 557088 | tf_op jit(solution)/shard_map/ppermute | solution.py:70
  32.4 7.7 %collective-permute-start.1 = (bf16[128,2176]{0,1:T(8,128)(2,1)S(1)}, bf16[128,2176]{0,1:T(8,128)(2,1)S(1)}, u32[]{:S(2)}, u32[]{:S(2)}) collective-permute-start(bf16[128,2176]{0,1:T(8,128)(2,1)S(1)} %collective-permute-done), channel_id=1, source_target_pairs={{0,4},{1,5},{2,6},{3,7},{4,8},{5,9},{6,10},{7,11},{8,12},{9,13},{1... | collective-permute-start | bytes 1671176 | tf_op jit(solution)/shard_map/ppermute | solution.py:70
  40.2 1.3 collective-permute-start.6
  42.7 4.6 %collective-permute-start.2 = (bf16[128,2176]{0,1:T(8,128)(2,1)S(1)}, bf16[128,2176]{0,1:T(8,128)(2,1)S(1)}, u32[]{:S(2)}, u32[]{:S(2)}) collective-permute-start(bf16[128,2176]{0,1:T(8,128)(2,1)S(1)} %collective-permute-done), channel_id=1, source_target_pairs={{0,2},{1,3},{4,6},{5,7},{8,10},{9,11},{12,14},{13,15},{16,18},{17,... | collective-permute-start | bytes 1671176 | tf_op jit(solution)/shard_map/ppermute | solution.py:76
  47.3 13.5 %collective-permute-done.1 = bf16[128,2176]{0,1:T(8,128)(2,1)S(1)} collective-permute-done((bf16[128,2176]{0,1:T(8,128)(2,1)S(1)}, bf16[128,2176]{0,1:T(8,128)(2,1)S(1)}, u32[]{:S(2)}, u32[]{:S(2)}) %collective-permute-start.1) | collective-permute-done | bytes 557088 | tf_op jit(solution)/shard_map/ppermute | solution.py:70
  60.8 1.3 collective-permute-start.3
  62.2 1.1 pad_maximum_fusion.1
  63.3 20.0 %collective-permute-done.3 = bf16[128,2176]{0,1:T(8,128)(2,1)S(1)} collective-permute-done((bf16[128,2176]{0,1:T(8,128)(2,1)S(1)}, bf16[128,2176]{0,1:T(8,128)(2,1)S(1)}, u32[]{:S(2)}, u32[]{:S(2)}) %collective-permute-start.3) | collective-permute-done | bytes 557088 | tf_op jit(solution)/shard_map/ppermute | solution.py:76
  83.3 1.1 pad_maximum_fusion
  85.0 1.0 slice.72
  86.5 2.2 %reshape.323 = bf16[128,8,2,128]{3,2,1,0:T(2,128)(2,1)} reshape(bf16[128,2048]{1,0:T(8,128)(2,1)} %param.8) | data formatting | bytes 1048576 | tf_op jit(solution)/shard_map/reshape | solution.py:141
  89.3 1.3 slice_bitcast_fusion
  90.6 1.3 slice_bitcast_fusion.2
  93.4 1.6 fusion.14
  95.7 1.1 compare_and_fusion
  96.8 1.9 %fusion.51 = (bf16[1152,1024]{0,1:T(8,128)(2,1)S(1)}, bf16[1152,1024]{0,1:T(8,128)(2,1)}) fusion(bf16[1152,2048]{0,1:T(8,128)(2,1)S(1)} %constant_dynamic-slice_fusion), kind=kLoop, calls=%fused_computation.123 | loop fusion | bytes 9437184 | tf_op jit(solution)/shard_map/slice | solution.py:142
  98.6 4.2 %fusion.53 = f32[8,2,128]{2,1,0:T(2,128)} fusion(pred[128,1152]{0,1:T(8,128)(4,1)S(1)} %compare_and_fusion, bf16[1152,8,128,1]{0,2,3,1:T(8,128)(2,1)S(1)} %bitcast.103, bf16[128,8,2,128]{3,2,1,0:T(2,128)(2,1)S(1)} %copy-done.1), kind=kOutput, calls=%fused_computation.125 | convolution fusion | flops 613418112 | bytes 3039232 | tf_op jit(solution)/shard_map/sub | solution.py:156
  102.9 6.7 %fusion.7 = bf16[8,128,2,128]{3,1,2,0:T(8,128)(2,1)S(1)} fusion(bf16[1152,8,128,1]{0,2,3,1:T(8,128)(2,1)} %bitcast.105, f32[8,2,128]{2,1,0:T(2,128)} %fusion.53, pred[128,1152]{0,1:T(8,128)(4,1)S(1)} %compare_and_fusion, bf16[1152,8,128,1]{0,2,3,1:T(8,128)(2,1)S(1)} %bitcast.104, bf16[128,8,2,128]{3,2,1,0:T(2,128)(2,1)S(1)} %copy-done.1), kind=kOutput, calls=%fused_computation.17 | convolution fusion | flops 1220021376 | bytes 5922816 | tf_op jit(solution)/shard_map/hgqk,khd->qhgd/dot_general | solution.py:158
  110.9 1.5 collective-permute-start.11
  112.9 1.7 %collective-permute-start.16 = (bf16[1,4,2688]{2,1,0:T(4,128)(2,1)S(1)}, bf16[1,4,2688]{2,1,0:T(4,128)(2,1)S(1)}, u32[]{:S(2)}, u32[]{:S(2)}) collective-permute-start(bf16[1,4,2688]{2,1,0:T(4,128)(2,1)S(1)} %bitcast.112), channel_id=1, source_target_pairs={{0,2},{1,3},{2,0},{3,1},{4,6},{5,7},{6,4},{7,5},{8,10},{9,11},{10,... | collective-permute-start | bytes 64520 | tf_op jit(solution)/shard_map/ppermute | solution.py:54
  114.6 1.4 collective-permute-start.17
  116.0 0.7 gather_fusion
  117.0 5.3 %collective-permute-start.12 = (bf16[4,4,2048]{2,1,0:T(4,128)(2,1)S(1)}, bf16[4,4,2048]{2,1,0:T(4,128)(2,1)S(1)}, u32[]{:S(2)}, u32[]{:S(2)}) collective-permute-start(bf16[4,4,2048]{2,1,0:T(4,128)(2,1)S(1)} %broadcast_select_fusion.6), channel_id=1, source_target_pairs={{0,4},{1,5},{2,6},{3,7},{4,8},{5,9},{6,10},{7,11},{8,12},{9,13},{1... | collective-permute-start | bytes 196616 | tf_op jit(solution)/shard_map/ppermute | solution.py:54
  122.2 4.0 %collective-permute-start.13 = (bf16[4,4,2048]{2,1,0:T(4,128)(2,1)S(1)}, bf16[4,4,2048]{2,1,0:T(4,128)(2,1)S(1)}, u32[]{:S(2)}, u32[]{:S(2)}) collective-permute-start(bf16[4,4,2048]{2,1,0:T(4,128)(2,1)S(1)} %broadcast_select_fusion.6), channel_id=1, source_target_pairs={{0,8},{1,9},{2,10},{3,11},{4,12},{5,13},{6,14},{7,15},{8,0},{9,1},... | collective-permute-start | bytes 196616 | tf_op jit(solution)/shard_map/ppermute | solution.py:54
  126.3 0.9 collective-permute-start.14
  127.3 0.7 gather_fusion.2
  128.2 1.2 collective-permute-start.18
  129.4 2.7 %collective-permute-start.20 = (bf16[4,4,2688]{2,1,0:T(4,128)(2,1)S(1)}, bf16[4,4,2688]{2,1,0:T(4,128)(2,1)S(1)}, u32[]{:S(2)}, u32[]{:S(2)}) collective-permute-start(bf16[4,4,2688]{2,1,0:T(4,128)(2,1)S(1)} %broadcast_select_fusion.5), channel_id=1, source_target_pairs={{0,12},{1,13},{2,14},{3,15},{4,0},{5,1},{6,2},{7,3},{8,4},{9,5},{1... | collective-permute-start | bytes 258056 | tf_op jit(solution)/shard_map/ppermute | solution.py:54
  132.4 0.9 gather_fusion.1
  133.7 1.9 %collective-permute-done.18 = bf16[4,4,2688]{2,1,0:T(4,128)(2,1)S(1)} collective-permute-done((bf16[4,4,2688]{2,1,0:T(4,128)(2,1)S(1)}, bf16[4,4,2688]{2,1,0:T(4,128)(2,1)S(1)}, u32[]{:S(2)}, u32[]{:S(2)}) %collective-permute-start.18) | collective-permute-done | bytes 86048 | tf_op jit(solution)/shard_map/ppermute | solution.py:54
  135.6 2.3 %collective-permute-done.19 = bf16[4,4,2688]{2,1,0:T(4,128)(2,1)S(1)} collective-permute-done((bf16[4,4,2688]{2,1,0:T(4,128)(2,1)S(1)}, bf16[4,4,2688]{2,1,0:T(4,128)(2,1)S(1)}, u32[]{:S(2)}, u32[]{:S(2)}) %collective-permute-start.19) | collective-permute-done | bytes 86048 | tf_op jit(solution)/shard_map/ppermute | solution.py:54
  138.2 1.1 gather_fusion.3
  139.5 6.8 %fusion.15 = f32[192,2688]{1,0:T(8,128)S(1)} fusion(bf16[2048,2688]{1,0:T(8,128)(2,1)} %all-gather.2.cloned.1.call-done, bf16[128,2048]{0,1:T(8,128)(2,1)S(1)} %bitcast.109, bf16[64,2048]{0,1:T(8,128)(2,1)S(1)} %copy.22), kind=kOutput, calls=%fused_computation.31 | convolution fusion | flops 2115502080 | bytes 13860864 | tf_op jit(solution)/shard_map/dot_general | solution.py:164
  146.6 1.9 %fusion.56 = (f32[64]{0:T(128)S(1)}, f32[64,1024]{1,0:T(8,128)S(1)}) fusion(bf16[1024,2688]{1,0:T(8,128)(2,1)S(1)} %bitcast.100, f32[192,2688]{1,0:T(8,128)S(1)} %fusion.15, f32[2688]{0:T(1024)S(1)} %copy-done.4, f32[64]{0:T(128)S(1)} %add_rsqrt_fusion, bf16[64,2688]{1,0:T(8,128)(2,1)S(1)} %gather.51, pred[64]{0:T(512)(128)(4,1)S(1)} %broadcast_in_dim.126), kind=kOutput, calls=%fused_computation.126 | convolution fusion | flops 353419200 | bytes 6812928 | tf_op jit(solution)/shard_map/dot_general | solution.py:173
  149.2 1.4 collective-permute-start.23
  150.6 1.0 fusion.6
  151.8 0.7 collective-permute-done.22
  152.5 0.7 gather_fusion.4
  153.3 2.3 %collective-permute-start.24 = (f32[4,3,64]{2,1,0:T(4,128)S(1)}, f32[4,3,64]{2,1,0:T(4,128)S(1)}, u32[]{:S(2)}, u32[]{:S(2)}) collective-permute-start(f32[4,3,64]{2,1,0:T(4,128)S(1)} %broadcast_select_fusion.7), channel_id=1, source_target_pairs={{0,4},{1,5},{2,6},{3,7},{4,8},{5,9},{6,10},{7,11},{8,12},{9,13},{1... | collective-permute-start | bytes 9224 | tf_op jit(solution)/shard_map/ppermute | solution.py:54
  155.6 1.5 collective-permute-start.25
  157.1 0.9 collective-permute-start.26
  158.7 1.5 collective-permute-done.25
  160.8 0.7 gather_fusion.5
  161.6 0.8 broadcast_subtract_fusion
  (108 shorter events, 12.8 us)
Async XLA Ops:
  7.2 132.3 %all-gather.2.cloned.1.call-start = ((), (), s32[]{:S(2)}) async-start(), calls=%async_computation | async-start | bytes 11698176 | tf_op jit(solution)/shard_map/all_gather | solution.py:121
  9.9 22.5 %collective-permute-start = (bf16[128,2176]{0,1:T(8,128)(2,1)S(1)}, bf16[128,2176]{0,1:T(8,128)(2,1)S(1)}, u32[]{:S(2)}, u32[]{:S(2)}) collective-permute-start(bf16[128,2176]{0,1:T(8,128)(2,1)S(1)} %pad_maximum_fusion.2), channel_id=1, source_target_pairs={{0,4},{1,5},{2,6},{3,7},{4,8},{5,9},{6,10},{7,11},{8,12},{9,13},{1... | collective-permute-start | bytes 1671176 | tf_op jit(solution)/shard_map/ppermute | solution.py:70
  14.9 47.2 %collective-permute-start.5 = (bf16[128,2176]{0,1:T(8,128)(2,1)S(1)}, bf16[128,2176]{0,1:T(8,128)(2,1)S(1)}, u32[]{:S(2)}, u32[]{:S(2)}) collective-permute-start(bf16[128,2176]{0,1:T(8,128)(2,1)S(1)} %pad_maximum_fusion.2), channel_id=1, source_target_pairs={{0,2},{1,3},{4,6},{5,7},{8,10},{9,11},{12,14},{13,15},{16,18},{17,... | collective-permute-start | bytes 1671176 | tf_op jit(solution)/shard_map/ppermute | solution.py:76
  18.4 75.0 %collective-permute-start.8 = (bf16[128,2176]{0,1:T(8,128)(2,1)S(1)}, bf16[128,2176]{0,1:T(8,128)(2,1)}, u32[]{:S(2)}, u32[]{:S(2)}) collective-permute-start(bf16[128,2176]{0,1:T(8,128)(2,1)S(1)} %pad_maximum_fusion.2), channel_id=1, source_target_pairs={{0,1},{1,0},{2,3},{3,2},{4,5},{5,4},{6,7},{7,6},{8,9},{9,8},{10,11... | collective-permute-start | bytes 1671176 | tf_op jit(solution)/shard_map/ppermute | solution.py:37
  32.4 28.4 %collective-permute-start.1 = (bf16[128,2176]{0,1:T(8,128)(2,1)S(1)}, bf16[128,2176]{0,1:T(8,128)(2,1)S(1)}, u32[]{:S(2)}, u32[]{:S(2)}) collective-permute-start(bf16[128,2176]{0,1:T(8,128)(2,1)S(1)} %collective-permute-done), channel_id=1, source_target_pairs={{0,4},{1,5},{2,6},{3,7},{4,8},{5,9},{6,10},{7,11},{8,12},{9,13},{1... | collective-permute-start | bytes 1671176 | tf_op jit(solution)/shard_map/ppermute | solution.py:70
  40.2 21.9 %collective-permute-start.6 = (bf16[128,2176]{0,1:T(8,128)(2,1)S(1)}, bf16[128,2176]{0,1:T(8,128)(2,1)S(1)}, u32[]{:S(2)}, u32[]{:S(2)}) collective-permute-start(bf16[128,2176]{0,1:T(8,128)(2,1)S(1)} %collective-permute-done), channel_id=1, source_target_pairs={{2,0},{3,1},{6,4},{7,5},{10,8},{11,9},{14,12},{15,13},{18,16},{19,... | collective-permute-start | bytes 1671176 | tf_op jit(solution)/shard_map/ppermute | solution.py:76
  42.7 20.5 %collective-permute-start.2 = (bf16[128,2176]{0,1:T(8,128)(2,1)S(1)}, bf16[128,2176]{0,1:T(8,128)(2,1)S(1)}, u32[]{:S(2)}, u32[]{:S(2)}) collective-permute-start(bf16[128,2176]{0,1:T(8,128)(2,1)S(1)} %collective-permute-done), channel_id=1, source_target_pairs={{0,2},{1,3},{4,6},{5,7},{8,10},{9,11},{12,14},{13,15},{16,18},{17,... | collective-permute-start | bytes 1671176 | tf_op jit(solution)/shard_map/ppermute | solution.py:76
  60.8 22.5 %collective-permute-start.3 = (bf16[128,2176]{0,1:T(8,128)(2,1)S(1)}, bf16[128,2176]{0,1:T(8,128)(2,1)S(1)}, u32[]{:S(2)}, u32[]{:S(2)}) collective-permute-start(bf16[128,2176]{0,1:T(8,128)(2,1)S(1)} %collective-permute-done.1), channel_id=1, source_target_pairs={{2,0},{3,1},{6,4},{7,5},{10,8},{11,9},{14,12},{15,13},{18,16},{19,... | collective-permute-start | bytes 1671176 | tf_op jit(solution)/shard_map/ppermute | solution.py:76
  63.3 25.5 %copy-start.7 = (s32[64]{0:T(128)S(1)}, s32[64]{0:T(128)}, u32[]{:S(2)}) copy-start(s32[64]{0:T(128)} %param.15) | copy-start | bytes 772
  63.3 26.0 %collective-permute-start.7 = (bf16[2,128,2176]{1,2,0:T(8,128)(2,1)}, bf16[2,128,2176]{1,2,0:T(8,128)(2,1)}, u32[]{:S(2)}, u32[]{:S(2)}) collective-permute-start(bf16[2,128,2176]{1,2,0:T(8,128)(2,1)} %pad_maximum_fusion.1), channel_id=1, source_target_pairs={{0,1},{1,0},{2,3},{3,2},{4,5},{5,4},{6,7},{7,6},{8,9},{9,8},{10,11... | collective-permute-start | bytes 3342344 | tf_op jit(solution)/shard_map/ppermute | solution.py:37
  84.4 6.1 %collective-permute-start.4 = (bf16[2,128,2176]{1,2,0:T(8,128)(2,1)}, bf16[2,128,2176]{1,2,0:T(8,128)(2,1)}, u32[]{:S(2)}, u32[]{:S(2)}) collective-permute-start(bf16[2,128,2176]{1,2,0:T(8,128)(2,1)} %pad_maximum_fusion), channel_id=1, source_target_pairs={{0,1},{1,0},{2,3},{3,2},{4,5},{5,4},{6,7},{7,6},{8,9},{9,8},{10,11... | collective-permute-start | bytes 3342344 | tf_op jit(solution)/shard_map/ppermute | solution.py:37
  95.0 0.7 copy-start.5
  96.7 1.9 %copy-start.1 = (bf16[128,8,2,128]{3,2,1,0:T(2,128)(2,1)S(1)}, bf16[128,8,2,128]{3,2,1,0:T(2,128)(2,1)}, u32[]{:S(2)}) copy-start(bf16[128,8,2,128]{3,2,1,0:T(2,128)(2,1)} %reshape.323) | copy-start | bytes 1572868
  109.6 3.2 %copy-start.2 = (bf16[4,1,2688]{2,0,1:T(4,128)(2,1)S(1)}, bf16[4,1,2688]{2,0,1:T(4,128)(2,1)}, u32[]{:S(2)}) copy-start(bf16[4,1,2688]{2,0,1:T(4,128)(2,1)} %copy.49) | copy-start | bytes 64516
  109.6 7.2 %copy-start.3 = (pred[4]{0:T(512)(128)(4,1)S(1)}, pred[4]{0:T(512)(128)(4,1)}, u32[]{:S(2)}) copy-start(pred[4]{0:T(512)(128)(4,1)} %compare_and_fusion.1) | copy-start | bytes 16
  110.6 4.0 %collective-permute-start.9 = (bf16[1,4,2048]{2,1,0:T(4,128)(2,1)S(1)}, bf16[1,4,2048]{2,1,0:T(4,128)(2,1)S(1)}, u32[]{:S(2)}, u32[]{:S(2)}) collective-permute-start(bf16[1,4,2048]{2,1,0:T(4,128)(2,1)S(1)} %bitcast.120), channel_id=1, source_target_pairs={{0,1},{1,2},{2,3},{3,0},{4,5},{5,6},{6,7},{7,4},{8,9},{9,10},{10,1... | collective-permute-start | bytes 49160 | tf_op jit(solution)/shard_map/ppermute | solution.py:54
  110.9 5.1 %collective-permute-start.10 = (bf16[1,4,2048]{2,1,0:T(4,128)(2,1)S(1)}, bf16[1,4,2048]{2,1,0:T(4,128)(2,1)S(1)}, u32[]{:S(2)}, u32[]{:S(2)}) collective-permute-start(bf16[1,4,2048]{2,1,0:T(4,128)(2,1)S(1)} %bitcast.121), channel_id=1, source_target_pairs={{0,2},{1,3},{2,0},{3,1},{4,6},{5,7},{6,4},{7,5},{8,10},{9,11},{10,... | collective-permute-start | bytes 49160 | tf_op jit(solution)/shard_map/ppermute | solution.py:54
  110.9 5.1 %collective-permute-start.11 = (bf16[1,4,2048]{2,1,0:T(4,128)(2,1)S(1)}, bf16[1,4,2048]{2,1,0:T(4,128)(2,1)S(1)}, u32[]{:S(2)}, u32[]{:S(2)}) collective-permute-start(bf16[1,4,2048]{2,1,0:T(4,128)(2,1)S(1)} %bitcast.122), channel_id=1, source_target_pairs={{0,3},{1,0},{2,1},{3,2},{4,7},{5,4},{6,5},{7,6},{8,11},{9,8},{10,9... | collective-permute-start | bytes 49160 | tf_op jit(solution)/shard_map/ppermute | solution.py:54
  112.8 13.5 %collective-permute-start.15 = (bf16[1,4,2688]{2,1,0:T(4,128)(2,1)S(1)}, bf16[1,4,2688]{2,1,0:T(4,128)(2,1)S(1)}, u32[]{:S(2)}, u32[]{:S(2)}) collective-permute-start(bf16[1,4,2688]{2,1,0:T(4,128)(2,1)S(1)} %bitcast.111), channel_id=1, source_target_pairs={{0,1},{1,2},{2,3},{3,0},{4,5},{5,6},{6,7},{7,4},{8,9},{9,10},{10,1... | collective-permute-start | bytes 64520 | tf_op jit(solution)/shard_map/ppermute | solution.py:54
  112.9 14.3 %collective-permute-start.16 = (bf16[1,4,2688]{2,1,0:T(4,128)(2,1)S(1)}, bf16[1,4,2688]{2,1,0:T(4,128)(2,1)S(1)}, u32[]{:S(2)}, u32[]{:S(2)}) collective-permute-start(bf16[1,4,2688]{2,1,0:T(4,128)(2,1)S(1)} %bitcast.112), channel_id=1, source_target_pairs={{0,2},{1,3},{2,0},{3,1},{4,6},{5,7},{6,4},{7,5},{8,10},{9,11},{10,... | collective-permute-start | bytes 64520 | tf_op jit(solution)/shard_map/ppermute | solution.py:54
  114.6 12.6 %collective-permute-start.17 = (bf16[1,4,2688]{2,1,0:T(4,128)(2,1)S(1)}, bf16[1,4,2688]{2,1,0:T(4,128)(2,1)S(1)}, u32[]{:S(2)}, u32[]{:S(2)}) collective-permute-start(bf16[1,4,2688]{2,1,0:T(4,128)(2,1)S(1)} %bitcast.113), channel_id=1, source_target_pairs={{0,3},{1,0},{2,1},{3,2},{4,7},{5,4},{6,5},{7,6},{8,11},{9,8},{10,9... | collective-permute-start | bytes 64520 | tf_op jit(solution)/shard_map/ppermute | solution.py:54
  117.0 12.5 %collective-permute-start.12 = (bf16[4,4,2048]{2,1,0:T(4,128)(2,1)S(1)}, bf16[4,4,2048]{2,1,0:T(4,128)(2,1)S(1)}, u32[]{:S(2)}, u32[]{:S(2)}) collective-permute-start(bf16[4,4,2048]{2,1,0:T(4,128)(2,1)S(1)} %broadcast_select_fusion.6), channel_id=1, source_target_pairs={{0,4},{1,5},{2,6},{3,7},{4,8},{5,9},{6,10},{7,11},{8,12},{9,13},{1... | collective-permute-start | bytes 196616 | tf_op jit(solution)/shard_map/ppermute | solution.py:54
  122.2 9.9 %collective-permute-start.13 = (bf16[4,4,2048]{2,1,0:T(4,128)(2,1)S(1)}, bf16[4,4,2048]{2,1,0:T(4,128)(2,1)S(1)}, u32[]{:S(2)}, u32[]{:S(2)}) collective-permute-start(bf16[4,4,2048]{2,1,0:T(4,128)(2,1)S(1)} %broadcast_select_fusion.6), channel_id=1, source_target_pairs={{0,8},{1,9},{2,10},{3,11},{4,12},{5,13},{6,14},{7,15},{8,0},{9,1},... | collective-permute-start | bytes 196616 | tf_op jit(solution)/shard_map/ppermute | solution.py:54
  126.3 5.8 %collective-permute-start.14 = (bf16[4,4,2048]{2,1,0:T(4,128)(2,1)S(1)}, bf16[4,4,2048]{2,1,0:T(4,128)(2,1)S(1)}, u32[]{:S(2)}, u32[]{:S(2)}) collective-permute-start(bf16[4,4,2048]{2,1,0:T(4,128)(2,1)S(1)} %broadcast_select_fusion.6), channel_id=1, source_target_pairs={{0,12},{1,13},{2,14},{3,15},{4,0},{5,1},{6,2},{7,3},{8,4},{9,5},{1... | collective-permute-start | bytes 196616 | tf_op jit(solution)/shard_map/ppermute | solution.py:54
  128.2 7.4 %collective-permute-start.18 = (bf16[4,4,2688]{2,1,0:T(4,128)(2,1)S(1)}, bf16[4,4,2688]{2,1,0:T(4,128)(2,1)S(1)}, u32[]{:S(2)}, u32[]{:S(2)}) collective-permute-start(bf16[4,4,2688]{2,1,0:T(4,128)(2,1)S(1)} %broadcast_select_fusion.5), channel_id=1, source_target_pairs={{0,4},{1,5},{2,6},{3,7},{4,8},{5,9},{6,10},{7,11},{8,12},{9,13},{1... | collective-permute-start | bytes 258056 | tf_op jit(solution)/shard_map/ppermute | solution.py:54
  129.4 8.5 %collective-permute-start.19 = (bf16[4,4,2688]{2,1,0:T(4,128)(2,1)S(1)}, bf16[4,4,2688]{2,1,0:T(4,128)(2,1)S(1)}, u32[]{:S(2)}, u32[]{:S(2)}) collective-permute-start(bf16[4,4,2688]{2,1,0:T(4,128)(2,1)S(1)} %broadcast_select_fusion.5), channel_id=1, source_target_pairs={{0,8},{1,9},{2,10},{3,11},{4,12},{5,13},{6,14},{7,15},{8,0},{9,1},... | collective-permute-start | bytes 258056 | tf_op jit(solution)/shard_map/ppermute | solution.py:54
  129.4 8.5 %collective-permute-start.20 = (bf16[4,4,2688]{2,1,0:T(4,128)(2,1)S(1)}, bf16[4,4,2688]{2,1,0:T(4,128)(2,1)S(1)}, u32[]{:S(2)}, u32[]{:S(2)}) collective-permute-start(bf16[4,4,2688]{2,1,0:T(4,128)(2,1)S(1)} %broadcast_select_fusion.5), channel_id=1, source_target_pairs={{0,12},{1,13},{2,14},{3,15},{4,0},{5,1},{6,2},{7,3},{8,4},{9,5},{1... | collective-permute-start | bytes 258056 | tf_op jit(solution)/shard_map/ppermute | solution.py:54
  137.9 8.7 %slice-start = ((s8[5505024]{0:T(1024)(128)(4,1)}), s8[1310720]{0:T(1024)(128)(4,1)S(1)}, s32[]{:S(2)}) async-start(s8[5505024]{0:T(1024)(128)(4,1)} %bitcast.99), calls=%async_computation.1 | async-start | bytes 2621440
  139.4 7.1 %slice-start.1 = ((s8[5505024]{0:T(1024)(128)(4,1)}), s8[4194304]{0:T(1024)(128)(4,1)S(1)}, s32[]{:S(2)}) async-start(s8[5505024]{0:T(1024)(128)(4,1)} %bitcast.99), calls=%async_computation.2 | async-start | bytes 8388608
  139.5 7.1 %copy-start.4 = (f32[2688]{0:T(1024)S(1)}, f32[2688]{0:T(1024)}, u32[]{:S(2)}) copy-start(f32[2688]{0:T(1024)} %param.12) | copy-start | bytes 32260
  146.6 1.9 %copy-start.6 = (s32[64]{0:T(128)S(1)}, s32[64]{0:T(128)}, u32[]{:S(2)}) copy-start(s32[64]{0:T(128)} %broadcast_subtract_fusion.1) | copy-start | bytes 772
  146.6 4.0 %copy-start = (bf16[128,2688]{1,0:T(8,128)(2,1)S(1)}, bf16[128,2688]{1,0:T(8,128)(2,1)}, u32[]{:S(2)}) copy-start(bf16[128,2688]{1,0:T(8,128)(2,1)} %param.11) | copy-start | bytes 2064388
  148.8 3.1 %collective-permute-start.21 = (f32[1,3,64]{2,1,0:T(4,128)S(1)}, f32[1,3,64]{2,1,0:T(4,128)S(1)}, u32[]{:S(2)}, u32[]{:S(2)}) collective-permute-start(f32[1,3,64]{2,1,0:T(4,128)S(1)} %get-tuple-element.23), channel_id=1, source_target_pairs={{0,1},{1,2},{2,3},{3,0},{4,5},{5,6},{6,7},{7,4},{8,9},{9,10},{10,1... | collective-permute-start | bytes 2312 | tf_op jit(solution)/shard_map/ppermute | solution.py:54
  148.8 3.7 %collective-permute-start.22 = (f32[1,3,64]{2,1,0:T(4,128)S(1)}, f32[1,3,64]{2,1,0:T(4,128)S(1)}, u32[]{:S(2)}, u32[]{:S(2)}) collective-permute-start(f32[1,3,64]{2,1,0:T(4,128)S(1)} %get-tuple-element.23), channel_id=1, source_target_pairs={{0,2},{1,3},{2,0},{3,1},{4,6},{5,7},{6,4},{7,5},{8,10},{9,11},{10,... | collective-permute-start | bytes 2312 | tf_op jit(solution)/shard_map/ppermute | solution.py:54
  149.2 3.3 %collective-permute-start.23 = (f32[1,3,64]{2,1,0:T(4,128)S(1)}, f32[1,3,64]{2,1,0:T(4,128)S(1)}, u32[]{:S(2)}, u32[]{:S(2)}) collective-permute-start(f32[1,3,64]{2,1,0:T(4,128)S(1)} %get-tuple-element.23), channel_id=1, source_target_pairs={{0,3},{1,0},{2,1},{3,2},{4,7},{5,4},{6,5},{7,6},{8,11},{9,8},{10,9... | collective-permute-start | bytes 2312 | tf_op jit(solution)/shard_map/ppermute | solution.py:54
  153.3 5.5 %collective-permute-start.24 = (f32[4,3,64]{2,1,0:T(4,128)S(1)}, f32[4,3,64]{2,1,0:T(4,128)S(1)}, u32[]{:S(2)}, u32[]{:S(2)}) collective-permute-start(f32[4,3,64]{2,1,0:T(4,128)S(1)} %broadcast_select_fusion.7), channel_id=1, source_target_pairs={{0,4},{1,5},{2,6},{3,7},{4,8},{5,9},{6,10},{7,11},{8,12},{9,13},{1... | collective-permute-start | bytes 9224 | tf_op jit(solution)/shard_map/ppermute | solution.py:54
  155.6 4.6 %collective-permute-start.25 = (f32[4,3,64]{2,1,0:T(4,128)S(1)}, f32[4,3,64]{2,1,0:T(4,128)S(1)}, u32[]{:S(2)}, u32[]{:S(2)}) collective-permute-start(f32[4,3,64]{2,1,0:T(4,128)S(1)} %broadcast_select_fusion.7), channel_id=1, source_target_pairs={{0,8},{1,9},{2,10},{3,11},{4,12},{5,13},{6,14},{7,15},{8,0},{9,1},... | collective-permute-start | bytes 9224 | tf_op jit(solution)/shard_map/ppermute | solution.py:54
  157.1 3.7 %collective-permute-start.26 = (f32[4,3,64]{2,1,0:T(4,128)S(1)}, f32[4,3,64]{2,1,0:T(4,128)S(1)}, u32[]{:S(2)}, u32[]{:S(2)}) collective-permute-start(f32[4,3,64]{2,1,0:T(4,128)S(1)} %broadcast_select_fusion.7), channel_id=1, source_target_pairs={{0,12},{1,13},{2,14},{3,15},{4,0},{5,1},{6,2},{7,3},{8,4},{9,5},{1... | collective-permute-start | bytes 9224 | tf_op jit(solution)/shard_map/ppermute | solution.py:54
Sparse Core Ops, SparseCore 0:
  10.3 116.8 all-gather.1
